TPU v7x, 256 devices: a whole 4x4x8 slice. The times are simulated.
256 devices in a mesh: req: 32 (over y, z), head: 8 (over x, core).
Axes of the slice: x: 4, y: 4, z: 8, core: 2. Of those that a mesh axis runs over, the one named last changes fastest.
Arguments:
- tokens: bfloat16 [2048, 1024], P(('req', 'head')), may hold values from -6 to 6
- gains: float32 [2, 1024], replicated, may hold values from 0.1 to 1.9
- qkv_weight: bfloat16 [3, 1024, 1024], P(None, None, 'head'), may hold values from -0.1875 to 0.1875
- out_weight: bfloat16 [1024, 1024], replicated, may hold values from -0.1875 to 0.1875
- gate_up_weight: bfloat16 [2, 1024, 4096], P(None, None, 'head'), may hold values from -0.1875 to 0.1875
- down_weight: bfloat16 [4096, 1024], P('head'), may hold values from -0.09375 to 0.09375
- variate_bias: float32 [2, 16], replicated, may hold values from -4 to 4
- page_cache: bfloat16 [2, 640, 128, 1024], P(None, 'req', None, 'head'), may hold values from -210 to 210
- page_variates: int32 [640, 128], P('req'), may hold values from 0 to 3
- token_variates: int32 [2048], replicated, may hold values from 0 to 3
- cache_len: int32 [32], replicated, may hold values from 64 to 4096, as said below
- page_table: int32 [32, 32], replicated, may hold values from -1 to 639, as said below
- parents: int32 [32, 64], P('req'), may hold values from -1 to 55, as said below
- accepted: int32 [32, 8], P('req'), may hold values from -1 to 63, as said below
Outputs:
- mixed: bfloat16 [2048, 1024], P(('req', 'head'))
- attended: bfloat16 [2048, 1024], P('req', 'head')
- new_kv: bfloat16 [2, 32, 8, 1024], P(None, 'req', None, 'head')
Inputs may be any that keep to these rules, and one draw needn't show every extreme that they name: `cache_len`: exactly half of the requests have 128 // 2 to 128 cached positions, the others 4096 // 2 + 1 to 4096. `page_table`: entry [r, b] is the page holding request r's positions b * 128 to b * 128 + 127 for b below ceil(cache_len[r] / 128), and -1 from there on; no page is listed twice. `parents`: node i lies on level i // 8; nodes of level 0 have parent -1, every other node's parent lies on the level before. `accepted`: row r lists a path of request r's tree from a level-0 node downward, one node a level, then -1; its length is 1 to 8, and 8 in some row.
All inputs are finite; a program needn't handle non-finite values.
Results may differ from a plain program's by a relative error of at most 0.015.
The roundings to bfloat16 on the way count: a program that leaves them out, or rounds other values in their place, can miss the bound.
Values may be sent and summed in bfloat16 or wider, within the bound.
No kernel may reach another device: no remote copies, remote signals or barrier semaphores. Data moves between devices by JAX's collectives and lax.ppermute only.
A program may use at most 192 MiB of HBM per device.

v0:
```python
import math

import jax
import jax.numpy as jnp
from jax import lax
from jax.sharding import PartitionSpec as P

HD = 64
LEVELS = 8


epsilon = 1e-06
masked_score = -1e30
highest = lax.Precision.HIGHEST


def rms_scaled(rows, gain):
    values = rows.astype(jnp.float32)
    return values * lax.rsqrt(jnp.mean(values * values, axis=-1, keepdims=True) + epsilon) * gain


def merge_parts(first, second):
    max_one, total_one, out_one = first
    max_two, total_two, out_two = second
    highest_max = jnp.maximum(max_one, max_two)
    factor_one = jnp.exp(max_one - highest_max)
    factor_two = jnp.exp(max_two - highest_max)
    return (
        highest_max,
        total_one * factor_one + total_two * factor_two,
        out_one * factor_one[..., None] + out_two * factor_two[..., None],
    )


def shards(
    tokens,
    gains,
    qkv_weight,
    out_weight,
    gate_up_weight,
    down_weight,
    variate_bias,
    page_cache,
    page_variates,
    token_variates,
    cache_len,
    page_table,
    parents,
    accepted,
):
    scale = 1.0 / math.sqrt(HD)
    local_req, tree = parents.shape
    pool, page = page_variates.shape
    requests = cache_len.shape[0]
    qdl = qkv_weight.shape[2]
    head_local = qdl // HD
    head_slot = lax.axis_index("head")
    req_slot = lax.axis_index("req")
    bias_local = lax.dynamic_slice_in_dim(variate_bias, head_slot * head_local, head_local, 1)
    same_bias = bias_local[0]
    other_bias = bias_local[1]
    normed = rms_scaled(tokens, gains[0]).astype(jnp.bfloat16)
    projected = jnp.einsum(
        "td,cdq->ctq",
        lax.all_gather(normed, "head", axis=0, tiled=True),
        qkv_weight,
        preferred_element_type=jnp.float32,
    ).astype(jnp.bfloat16)
    query = projected[0]
    key_new = projected[1]
    value_new = projected[2]
    all_queries = lax.all_gather(query, "req", axis=0, tiled=True)
    global_ids = req_slot * pool + jnp.arange(pool, dtype=jnp.int32)
    matching = (page_table[:, :, None] == global_ids[None, None, :]).astype(jnp.int32)
    owner = jnp.sum(matching * jnp.arange(requests, dtype=jnp.int32)[:, None, None], axis=(0, 1))
    page_order = jnp.sum(
        matching * jnp.arange(page_table.shape[1], dtype=jnp.int32)[None, :, None], axis=(0, 1)
    )
    owner_len = jnp.sum(matching * cache_len[:, None, None], axis=(0, 1))
    in_use = jnp.sum(matching, axis=(0, 1))
    filled = jnp.clip(owner_len - page_order * page, 0, page) * in_use
    valid = jnp.arange(page, dtype=jnp.int32)[None, :] < filled[:, None]
    page_queries = jnp.take(all_queries.reshape(requests, tree, head_local, HD), owner, axis=0)
    query_variates = jnp.take(token_variates.reshape(requests, tree), owner, axis=0)
    cache_keys = page_cache[0].reshape(pool, page, head_local, HD)
    cache_values = page_cache[1].reshape(pool, page, head_local, HD)
    scores = (
        jnp.einsum("pthd,pkhd->pthk", page_queries, cache_keys, preferred_element_type=jnp.float32)
        * scale
    )
    same_page = query_variates[:, :, None] == page_variates[:, None, :]
    scores = scores + jnp.where(
        same_page[:, :, None, :], same_bias[None, None, :, None], other_bias[None, None, :, None]
    )
    keep = valid[:, None, None, :]
    page_max = jnp.max(jnp.where(keep, scores, masked_score), axis=-1)
    weights = jnp.where(keep, jnp.exp(scores - page_max[..., None]), 0.0).astype(jnp.bfloat16)
    page_total = jnp.sum(weights, axis=-1, dtype=jnp.float32)
    page_out = jnp.einsum(
        "pthk,pkhd->pthd", weights, cache_values, preferred_element_type=jnp.float32
    )
    member = (owner[None, :] == jnp.arange(requests, dtype=jnp.int32)[:, None]) & (
        in_use[None, :] > 0
    )
    request_max = jnp.max(jnp.where(member[:, :, None, None], page_max[None], masked_score), axis=1)
    owner_max = jnp.take(request_max, owner, axis=0)
    factor = jnp.where(in_use[:, None, None] > 0, jnp.exp(page_max - owner_max), 0.0)
    member_float = member.astype(jnp.float32)
    request_total = jnp.dot(
        member_float, (page_total * factor).reshape(pool, -1), precision=highest
    ).reshape(requests, tree, head_local)
    request_out = jnp.dot(
        member_float, (page_out * factor[..., None]).reshape(pool, -1), precision=highest
    ).reshape(requests, tree, head_local, HD)
    received = (
        lax.all_to_all(request_max, "req", split_axis=0, concat_axis=0, tiled=True),
        lax.all_to_all(request_total, "req", split_axis=0, concat_axis=0, tiled=True),
        lax.all_to_all(request_out, "req", split_axis=0, concat_axis=0, tiled=True),
    )
    sources = lax.axis_size("req")
    source_max, source_total, source_out = [
        member_part.reshape((sources, local_req) + member_part.shape[1:])
        for member_part in received
    ]
    largest = jnp.max(source_max, axis=0)
    source_factor = jnp.exp(source_max - largest[None])
    cached_part = (
        largest,
        jnp.sum(source_total * source_factor, axis=0),
        jnp.sum(source_out * source_factor[..., None], axis=0),
    )
    tree_query = query.reshape(local_req, tree, head_local, HD)
    tree_key = key_new.reshape(local_req, tree, head_local, HD)
    tree_value = value_new.reshape(local_req, tree, head_local, HD)
    nodes = jnp.arange(tree, dtype=jnp.int32)
    reach = (parents[:, :, None] == nodes[None, None, :]).astype(jnp.float32) + jnp.eye(
        tree, dtype=jnp.float32
    )[None]
    for step in range(LEVELS.bit_length()):
        reach = jnp.minimum(jnp.einsum("rij,rjk->rik", reach, reach, precision=highest), 1.0)
    allowed = reach > 0.5
    group_variates = lax.dynamic_slice_in_dim(
        token_variates, req_slot * local_req * tree, local_req * tree, 0
    ).reshape(local_req, tree)
    tree_scores = (
        jnp.einsum("rihd,rjhd->rihj", tree_query, tree_key, preferred_element_type=jnp.float32)
        * scale
    )
    same_tree = group_variates[:, :, None] == group_variates[:, None, :]
    tree_scores = tree_scores + jnp.where(
        same_tree[:, :, None, :], same_bias[None, None, :, None], other_bias[None, None, :, None]
    )
    keep_tree = allowed[:, :, None, :]
    tree_max = jnp.max(jnp.where(keep_tree, tree_scores, masked_score), axis=-1)
    tree_weights = jnp.where(keep_tree, jnp.exp(tree_scores - tree_max[..., None]), 0.0).astype(
        jnp.bfloat16
    )
    tree_total = jnp.sum(tree_weights, axis=-1, dtype=jnp.float32)
    tree_out = jnp.einsum(
        "rihj,rjhd->rihd", tree_weights, tree_value, preferred_element_type=jnp.float32
    )
    final_max, final_total, final_out = merge_parts(cached_part, (tree_max, tree_total, tree_out))
    attended = (
        (final_out / final_total[..., None]).astype(jnp.bfloat16).reshape(local_req * tree, qdl)
    )
    token_heads = lax.all_to_all(attended, "head", split_axis=0, concat_axis=1, tiled=True)
    attention_rows = jnp.dot(token_heads, out_weight, preferred_element_type=jnp.float32)
    hidden_state = (tokens.astype(jnp.float32) + attention_rows).astype(jnp.bfloat16)
    normed_two = rms_scaled(hidden_state, gains[1]).astype(jnp.bfloat16)
    both_parts = jnp.einsum(
        "td,cdf->ctf",
        lax.all_gather(normed_two, "head", axis=0, tiled=True),
        gate_up_weight,
        preferred_element_type=jnp.float32,
    )
    activated = (jax.nn.silu(both_parts[0]) * both_parts[1]).astype(jnp.bfloat16)
    ffn_rows = lax.psum_scatter(
        jnp.dot(activated, down_weight, preferred_element_type=jnp.float32).astype(jnp.bfloat16),
        "head",
        scatter_dimension=0,
        tiled=True,
    ).astype(jnp.float32)
    mixed = (hidden_state.astype(jnp.float32) + ffn_rows).astype(jnp.bfloat16)
    chosen = (accepted[:, :, None] == nodes[None, None, :]).astype(jnp.bfloat16)
    stacked = jnp.stack([key_new, value_new]).reshape(2, local_req, tree, qdl)
    new_kv = jnp.einsum(
        "rat,crtq->craq", chosen, stacked, preferred_element_type=jnp.float32
    ).astype(jnp.bfloat16)
    return (mixed, attended, new_kv)


def solution(mesh):
    return jax.shard_map(
        shards,
        mesh=mesh,
        in_specs=(
            P(("req", "head"), None),
            P(),
            P(None, None, "head"),
            P(),
            P(None, None, "head"),
            P("head", None),
            P(),
            P(None, "req", None, "head"),
            P("req", None),
            P(),
            P(),
            P(),
            P("req", None),
            P("req", None),
        ),
        out_specs=(P(("req", "head"), None), P("req", "head"), P(None, "req", None, "head")),
        check_vma=False,
    )
```

profile of v0, /device:TPU:1, one launch (start us, length us, event | category | flops | bytes accessed | tf_op | source)
XLA Modules:
  0.0 245.8 jit_solution(13211089157063011466)
XLA Ops:
  7.2 0.9 constant_dynamic-slice_fusion
  8.1 0.8 fusion.31
  9.0 2.3 fusion.21
  11.5 0.8 fusion.58
  12.3 0.8 reshape.491
  13.1 0.8 fusion.33
  13.9 15.8 %all_gather.9 = bf16[64,1024]{1,0:T(8,128)(2,1)S(1)} all-gather(bf16[8,1024]{1,0:T(8,128)(2,1)S(1)} %fusion.33), channel_id=1, replica_groups=mesh['req'=32,'head'=8] {'head'}, dimensions={0}, use_global_device_ids=true | all-gather | bytes 147456 | tf_op jit(solution)/shard_map/all_gather | solution.py:65
  29.7 1.4 fusion.11
  32.3 43.9 %all-gather = bf16[1,2048,128]{2,1,0:T(8,128)(2,1)} all-gather(bf16[1,64,128]{2,1,0:T(8,128)(2,1)S(1)} %get-tuple-element.28), channel_id=2, replica_groups=mesh['req'=32,'head'=8] {'req'}, dimensions={1}, use_global_device_ids=true | all-gather | bytes 540672 | tf_op jit(solution)/shard_map/all_gather | solution.py:72
  76.2 2.4 reshape.490
  78.7 1.3 copy.75
  80.5 2.7 %gather_fusion = bf16[20,64,2,64]{3,1,2,0:T(8,128)(2,1)} fusion(bf16[32,64,2,64]{3,1,2,0:T(8,128)(2,1)} %copy.75, s32[1024]{0:T(1024)S(1)} %pad_clamp_fusion), kind=kCustom, calls=%fused_computation | custom fusion | bytes 655440 | tf_op jit(solution)/shard_map/jit(_take)/gather | solution.py:83
  83.2 2.2 fusion.56
  85.5 1.1 copy.76
  86.9 2.0 select_reduce_fusion
  89.1 0.7 reshape.531
  89.8 6.7 %all-to-all-start.1 = ((f32[32,1,128]{2,1,0:T(1,128)}), f32[32,1,128]{2,1,0:T(1,128)}, u32[]{:S(2)}, u32[]{:S(2)}) async-start(f32[32,1,128]{2,1,0:T(1,128)} %reshape.531), calls=%async_computation.1 | async-start | bytes 32768 | tf_op jit(solution)/shard_map/all_to_all | solution.py:116
  97.4 0.7 copy.92
  98.1 0.8 convert_reduce_fusion
  98.9 0.7 copy.91
  99.6 2.2 copy.77
  101.8 1.8 fusion.2
  103.6 1.0 copy.79
  104.7 2.1 reshape.492
  106.8 2.1 dot_general.59
  109.0 3.3 %fusion = f32[32,64,2,64]{3,0,2,1:T(8,128)} fusion(f32[64,2,64,20]{2,1,0,3:T(2,128)S(1)} %dot_general.59, s32[20]{0:T(128)S(1)} %copy-done.15, pred[20]{0:T(512)(128)(4,1)S(1)} %copy-done.10), kind=kOutput, calls=%fused_computation.4 | convolution fusion | flops 62915840 | bytes 1704036 | tf_op jit(solution)/shard_map/dot_general | solution.py:112
  112.7 0.7 reshape.533
  113.4 9.0 %all-to-all-start.2 = ((f32[32,1,128]{2,1,0:T(1,128)}), f32[32,1,128]{2,1,0:T(1,128)S(1)}, u32[]{:S(2)}, u32[]{:S(2)}) async-start(f32[32,1,128]{2,1,0:T(1,128)} %reshape.533), calls=%async_computation.2 | async-start | bytes 32768 | tf_op jit(solution)/shard_map/all_to_all | solution.py:117
  122.4 0.8 fusion.34
  123.2 0.8 reshape.494
  124.0 0.8 dynamic_slice.7
  124.7 4.5 %copy.81 = f32[32,64,2,64]{3,2,1,0:T(2,128)} copy(f32[32,64,2,64]{3,0,2,1:T(8,128)} %fusion) | data formatting | bytes 2097152 | tf_op jit(solution)/shard_map/dot_general | solution.py:112
  129.2 4.2 %reshape.529 = f32[32,1,8192]{2,1,0:T(1,128)} reshape(f32[32,64,2,64]{3,2,1,0:T(2,128)} %copy.81) | data formatting | bytes 2097152
  133.5 9.5 %all-to-all-start = ((f32[32,1,8192]{2,1,0:T(1,128)}), f32[32,1,8192]{2,1,0:T(1,128)}, u32[]{:S(2)}, u32[]{:S(2)}) async-start(f32[32,1,8192]{2,1,0:T(1,128)} %reshape.529), calls=%async_computation | async-start | bytes 2097152 | tf_op jit(solution)/shard_map/all_to_all | solution.py:118
  145.1 1.4 reduce.9
  147.4 1.4 copy.83
  148.8 11.1 %all-to-all-done = f32[32,1,8192]{2,1,0:T(1,128)} async-done(((f32[32,1,8192]{2,1,0:T(1,128)}), f32[32,1,8192]{2,1,0:T(1,128)}, u32[]{:S(2)}, u32[]{:S(2)}) %all-to-all-start) | async-done | bytes 1048608 | tf_op jit(solution)/shard_map/all_to_all | solution.py:118
  159.9 4.4 %reduce.8 = f32[32,8192]{1,0:T(8,128)S(1)} reduce(f32[32,1,8192]{2,1,0:T(1,128)} %all-to-all-done, f32[]{:T(128)} %broadcast.354), dimensions={1}, to_apply=%all_to_all.23.reduce_sub_computation | reduce | bytes 2097156 | tf_op jit(solution)/shard_map/all_to_all | solution.py:118
  164.4 2.9 %reshape.530 = f32[32,64,2,64]{3,2,1,0:T(2,128)} reshape(f32[32,8192]{1,0:T(8,128)S(1)} %reduce.8) | data formatting | bytes 2097152
  167.3 4.2 %multiply_reduce_fusion = f32[64,2,64]{2,1,0:T(2,128)S(1)} fusion(f32[32,64,2,64]{3,2,1,0:T(2,128)} %reshape.530, f32[32,64,2]{2,1,0:T(8,128)} %copy.83), kind=kLoop, calls=%fused_computation.3 | loop fusion | flops 516096 | bytes 1097728 | tf_op jit(solution)/shard_map/reduce_sum | solution.py:130
  171.9 21.6 %all_to_all.34 = bf16[8,8,128]{2,1,0:T(8,128)(2,1)S(1)} all-to-all(bf16[8,8,128]{2,1,0:T(8,128)(2,1)S(1)} %all_to_all.26), channel_id=1, replica_groups=mesh['req'=32,'head'=8] {'head'}, dimensions={0} | all-to-all | bytes 32768 | tf_op jit(solution)/shard_map/all_to_all | solution.py:166
  193.5 2.1 multiply_reduce_fusion.1
  195.7 13.4 %all_gather.11 = bf16[64,1024]{1,0:T(8,128)(2,1)S(1)} all-gather(bf16[8,1024]{1,0:T(8,128)(2,1)S(1)} %multiply_convert_fusion), channel_id=1, replica_groups=mesh['req'=32,'head'=8] {'head'}, dimensions={0}, use_global_device_ids=true | all-gather | bytes 147456 | tf_op jit(solution)/shard_map/all_gather | solution.py:172
  209.6 0.9 convolution_convert_fusion
  210.6 0.8 fusion.15
  211.4 0.7 copy.97
  212.1 25.6 %reduce-scatter.2.cloned.1.call-done = bf16[8,1024]{1,0:T(8,128)(2,1)} async-done(((bf16[64,1024]{1,0:T(8,128)(2,1)}), bf16[8,1024]{1,0:T(8,128)(2,1)}) %reduce-scatter.2.cloned.1.call-update) | async-done | bytes 16400 | tf_op jit(solution)/shard_map/reduce_scatter | solution.py:177
  237.6 1.3 add_convert_fusion
  (94 shorter events, 7.7 us)
Async XLA Ops:
  7.2 201.9 %copy-start = (bf16[2,1024,512]{2,1,0:T(8,128)(2,1)S(1)}, bf16[2,1024,512]{2,1,0:T(8,128)(2,1)}, u32[]{:S(2)}) copy-start(bf16[2,1024,512]{2,1,0:T(8,128)(2,1)} %param.18) | copy-start | bytes 6291460
  8.1 78.8 %copy-start.16 = (f32[2]{0:T(128)}, f32[2]{0:T(128)S(1)}, u32[]{:S(2)}) copy-start(f32[2]{0:T(128)S(1)} %get-tuple-element.31) | copy-start | bytes 28
  8.1 78.8 %copy-start.18 = (f32[2]{0:T(128)}, f32[2]{0:T(128)S(1)}, u32[]{:S(2)}) copy-start(f32[2]{0:T(128)S(1)} %get-tuple-element.32) | copy-start | bytes 28
  11.3 67.4 %copy-start.14 = (s32[20]{0:T(128)}, s32[20]{0:T(128)S(1)}, u32[]{:S(2)}) copy-start(s32[20]{0:T(128)S(1)} %get-tuple-element.18) | copy-start | bytes 244
  11.3 85.8 %copy-start.9 = (pred[20]{0:T(512)(128)(4,1)}, pred[20]{0:T(512)(128)(4,1)S(1)}, u32[]{:S(2)}) copy-start(pred[20]{0:T(512)(128)(4,1)S(1)} %get-tuple-element.40) | copy-start | bytes 64
  11.3 85.8 %copy-start.12 = (pred[20]{0:T(512)(128)(4,1)}, pred[20]{0:T(512)(128)(4,1)S(1)}, u32[]{:S(2)}) copy-start(pred[20]{0:T(512)(128)(4,1)S(1)} %get-tuple-element.39) | copy-start | bytes 64
  31.0 0.6 copy-start.3
  31.7 0.6 copy-start.6
  85.5 1.2 copy-start.11
  89.8 23.6 %all-to-all-start.1 = ((f32[32,1,128]{2,1,0:T(1,128)}), f32[32,1,128]{2,1,0:T(1,128)}, u32[]{:S(2)}, u32[]{:S(2)}) async-start(f32[32,1,128]{2,1,0:T(1,128)} %reshape.531), calls=%async_computation.1 | async-start | bytes 32768 | tf_op jit(solution)/shard_map/all_to_all | solution.py:116
  106.8 2.1 copy-start.10
  106.8 2.1 copy-start.15
  108.9 3.4 %copy-start.1 = (f32[20,64,2]{0,2,1:T(2,128)S(1)}, f32[20,64,2]{0,2,1:T(2,128)}, u32[]{:S(2)}) copy-start(f32[20,64,2]{0,2,1:T(2,128)} %copy.92) | copy-start | bytes 30724
  108.9 3.4 %copy-start.2 = (f32[20,64,2]{0,2,1:T(2,128)S(1)}, f32[20,64,2]{0,2,1:T(2,128)}, u32[]{:S(2)}) copy-start(f32[20,64,2]{0,2,1:T(2,128)} %copy.91) | copy-start | bytes 30724
  108.9 3.3 %copy-start.13 = (pred[20]{0:T(512)(128)(4,1)S(1)}, pred[20]{0:T(512)(128)(4,1)}, u32[]{:S(2)}) copy-start(pred[20]{0:T(512)(128)(4,1)} %copy-done.12) | copy-start | bytes 64
  113.4 20.1 %all-to-all-start.2 = ((f32[32,1,128]{2,1,0:T(1,128)}), f32[32,1,128]{2,1,0:T(1,128)S(1)}, u32[]{:S(2)}, u32[]{:S(2)}) async-start(f32[32,1,128]{2,1,0:T(1,128)} %reshape.533), calls=%async_computation.2 | async-start | bytes 32768 | tf_op jit(solution)/shard_map/all_to_all | solution.py:117
  133.5 10.6 %copy-start.8 = (bf16[1,64,128]{2,1,0:T(8,128)(2,1)S(1)}, bf16[1,64,128]{2,1,0:T(8,128)(2,1)}, u32[]{:S(2)}) copy-start(bf16[1,64,128]{2,1,0:T(8,128)(2,1)} %get-tuple-element.26) | copy-start | bytes 49156
  133.5 10.7 %copy-start.7 = (bf16[1,64,128]{2,1,0:T(8,128)(2,1)S(1)}, bf16[1,64,128]{2,1,0:T(8,128)(2,1)}, u32[]{:S(2)}) copy-start(bf16[1,64,128]{2,1,0:T(8,128)(2,1)} %get-tuple-element.27) | copy-start | bytes 49156
  133.5 10.9 %copy-start.17 = (f32[2]{0:T(128)S(1)}, f32[2]{0:T(128)}, u32[]{:S(2)}) copy-start(f32[2]{0:T(128)} %copy-done.16) | copy-start | bytes 28
  133.5 10.9 %copy-start.19 = (f32[2]{0:T(128)S(1)}, f32[2]{0:T(128)}, u32[]{:S(2)}) copy-start(f32[2]{0:T(128)} %copy-done.18) | copy-start | bytes 28
  133.5 26.5 %all-to-all-start = ((f32[32,1,8192]{2,1,0:T(1,128)}), f32[32,1,8192]{2,1,0:T(1,128)}, u32[]{:S(2)}, u32[]{:S(2)}) async-start(f32[32,1,8192]{2,1,0:T(1,128)} %reshape.529), calls=%async_computation | async-start | bytes 2097152 | tf_op jit(solution)/shard_map/all_to_all | solution.py:118
  143.0 94.6 %reduce-scatter.2.cloned.1.call-start = ((), (), s32[]{:S(2)}) async-start(), calls=%async_computation.5 | async-start | bytes 147456 | tf_op jit(solution)/shard_map/reduce_scatter | solution.py:177
  167.3 26.2 %copy-start.5 = (bf16[8,1024]{1,0:T(8,128)(2,1)S(1)}, bf16[8,1024]{1,0:T(8,128)(2,1)}, u32[]{:S(2)}) copy-start(bf16[8,1024]{1,0:T(8,128)(2,1)} %param.14) | copy-start | bytes 49156
  195.7 13.9 %copy-start.20 = (bf16[512,1024]{1,0:T(8,128)(2,1)S(1)}, bf16[512,1024]{1,0:T(8,128)(2,1)}, u32[]{:S(2)}) copy-start(bf16[512,1024]{1,0:T(8,128)(2,1)} %param.19) | copy-start | bytes 3145732
  209.6 1.0 copy-start.4
  209.6 1.0 copy-start.21
Sparse Core Ops, SparseCore 0:
  210.7 26.8 reduce-scatter.1
where the time goes:
time: 248 us; the launch traced here: 246 us
  blocking collectives  94.7 us (38%)
  local copies, waits for them, and re-layouts  41.6 us (17%)
  waiting for transfers between devices  36.7 us (15%)
  starting transfers between devices  25.4 us (10%)
  other arithmetic  18.7 us (8%)
  between operations  14.6 us (6%)
  matrix products  14.1 us (6%)
    all_gather x1, blocking collectives, shards(): all_queries = lax.all_gather(query, 'req', axis=0, tiled=True)  43.9 us
    reduce_scatter x1, waiting for transfers between devices, shards(): lax.psum_scatter(jnp.dot(activated, down_weight, preferred_element_type=j...  25.6 us
    all_to_all x1, blocking collectives, shards(): lax.all_to_all(attended, 'head', split_axis=0, concat_axis=1, tiled=True)  21.6 us
    all_gather x1, blocking collectives, shards(): lax.all_gather(normed, 'head', axis=0, tiled=True)  15.8 us
    all_gather x1, blocking collectives, shards(): lax.all_gather(normed_two, 'head', axis=0, tiled=True)  13.4 us
    all_to_all x1, waiting for transfers between devices, shards(): lax.all_to_all(request_out, 'req', split_axis=0, concat_axis=0, tiled=True)  11.1 us
    unnamed x51, local copies, waits for them, and re-layouts  10 us
    all_to_all x1, starting transfers between devices, shards(): lax.all_to_all(request_out, 'req', split_axis=0, concat_axis=0, tiled=True)  9.5 us
  transfers between devices with their start and end apart: 4, of which 2 were waited for; matrix products, arithmetic and copies ran while one was open for 14% of the time, Pallas kernels for 0%

commit v1 on v0

--- a/solution.py
+++ b/solution.py
@@ -30,6 +30,11 @@
         total_one * factor_one + total_two * factor_two,
         out_one * factor_one[..., None] + out_two * factor_two[..., None],
     )
+
+
+def gather_rows(rows, axis_name, parts):
+    spread = jnp.broadcast_to(rows[None], (parts,) + rows.shape)
+    return lax.all_to_all(spread, axis_name, 0, 0, tiled=True)
 
 
 def shards(
@@ -59,17 +64,19 @@
     bias_local = lax.dynamic_slice_in_dim(variate_bias, head_slot * head_local, head_local, 1)
     same_bias = bias_local[0]
     other_bias = bias_local[1]
-    normed = rms_scaled(tokens, gains[0]).astype(jnp.bfloat16)
+    head_parts = lax.axis_size("head")
+    group_tokens = gather_rows(tokens, "head", head_parts).reshape(-1, tokens.shape[1])
+    normed = rms_scaled(group_tokens, gains[0]).astype(jnp.bfloat16)
     projected = jnp.einsum(
         "td,cdq->ctq",
-        lax.all_gather(normed, "head", axis=0, tiled=True),
+        normed,
         qkv_weight,
         preferred_element_type=jnp.float32,
     ).astype(jnp.bfloat16)
     query = projected[0]
     key_new = projected[1]
     value_new = projected[2]
-    all_queries = lax.all_gather(query, "req", axis=0, tiled=True)
+    all_queries = gather_rows(query, "req", requests // local_req)
     global_ids = req_slot * pool + jnp.arange(pool, dtype=jnp.int32)
     matching = (page_table[:, :, None] == global_ids[None, None, :]).astype(jnp.int32)
     owner = jnp.sum(matching * jnp.arange(requests, dtype=jnp.int32)[:, None, None], axis=(0, 1))
@@ -112,16 +119,15 @@
     request_out = jnp.dot(
         member_float, (page_out * factor[..., None]).reshape(pool, -1), precision=highest
     ).reshape(requests, tree, head_local, HD)
-    received = (
-        lax.all_to_all(request_max, "req", split_axis=0, concat_axis=0, tiled=True),
-        lax.all_to_all(request_total, "req", split_axis=0, concat_axis=0, tiled=True),
-        lax.all_to_all(request_out, "req", split_axis=0, concat_axis=0, tiled=True),
-    )
+    packed = jnp.concatenate(
+        [request_out, request_total[..., None], request_max[..., None]], axis=-1
+    )
+    received = lax.all_to_all(packed, "req", split_axis=0, concat_axis=0, tiled=True)
     sources = lax.axis_size("req")
-    source_max, source_total, source_out = [
-        member_part.reshape((sources, local_req) + member_part.shape[1:])
-        for member_part in received
-    ]
+    received = received.reshape((sources, local_req) + received.shape[1:])
+    source_out = received[..., :HD]
+    source_total = received[..., HD]
+    source_max = received[..., HD + 1]
     largest = jnp.max(source_max, axis=0)
     source_factor = jnp.exp(source_max - largest[None])
     cached_part = (
@@ -163,24 +169,30 @@
     attended = (
         (final_out / final_total[..., None]).astype(jnp.bfloat16).reshape(local_req * tree, qdl)
     )
-    token_heads = lax.all_to_all(attended, "head", split_axis=0, concat_axis=1, tiled=True)
+    group_rows = local_req * tree
+    token_heads = (
+        gather_rows(attended, "head", head_parts).transpose(1, 0, 2).reshape(group_rows, -1)
+    )
     attention_rows = jnp.dot(token_heads, out_weight, preferred_element_type=jnp.float32)
-    hidden_state = (tokens.astype(jnp.float32) + attention_rows).astype(jnp.bfloat16)
+    hidden_state = (group_tokens.astype(jnp.float32) + attention_rows).astype(jnp.bfloat16)
     normed_two = rms_scaled(hidden_state, gains[1]).astype(jnp.bfloat16)
     both_parts = jnp.einsum(
         "td,cdf->ctf",
-        lax.all_gather(normed_two, "head", axis=0, tiled=True),
+        normed_two,
         gate_up_weight,
         preferred_element_type=jnp.float32,
     )
     activated = (jax.nn.silu(both_parts[0]) * both_parts[1]).astype(jnp.bfloat16)
-    ffn_rows = lax.psum_scatter(
-        jnp.dot(activated, down_weight, preferred_element_type=jnp.float32).astype(jnp.bfloat16),
-        "head",
-        scatter_dimension=0,
-        tiled=True,
-    ).astype(jnp.float32)
-    mixed = (hidden_state.astype(jnp.float32) + ffn_rows).astype(jnp.bfloat16)
+    down_part = jnp.dot(activated, down_weight, preferred_element_type=jnp.float32).astype(
+        jnp.bfloat16
+    )
+    own_rows = tokens.shape[0]
+    down_parts = lax.all_to_all(
+        down_part.reshape(head_parts, own_rows, -1), "head", 0, 0, tiled=True
+    )
+    ffn_rows = jnp.sum(down_parts.astype(jnp.float32), axis=0)
+    own_hidden = lax.dynamic_slice_in_dim(hidden_state, head_slot * own_rows, own_rows, 0)
+    mixed = (own_hidden.astype(jnp.float32) + ffn_rows).astype(jnp.bfloat16)
     chosen = (accepted[:, :, None] == nodes[None, None, :]).astype(jnp.bfloat16)
     stacked = jnp.stack([key_new, value_new]).reshape(2, local_req, tree, qdl)
     new_kv = jnp.einsum(

time: 248 us -> 178 us (0.72)
  blocking collectives: 94.7 us -> 0 us
  waiting for transfers between devices: 36.7 us -> 69.8 us
  between operations: 14.6 us -> 1.18 us
  starting transfers between devices: 25.4 us -> 35.6 us
    all_gather x3 -> x0, blocking collectives: 73.1 us -> none  [the longest x1 43.9 us: shards(): all_queries = lax.all_gather(query, 'req', axis=0, tiled=True)]
    all_to_all x3 -> x5, waiting for transfers between devices: 11.1 us -> 69.8 us  [the longest x1 46.4 us: shards(): lax.all_to_all(packed, 'req', split_axis=0, concat_axis=0, tiled=True)]
    reduce_scatter x1 -> x0, waiting for transfers between devices: 25.6 us -> none  [shards(): lax.psum_scatter(jnp.dot(activated, down_weight, preferred_element_type=j...]
    all_to_all x1 -> x0, blocking collectives: 21.6 us -> none  [shards(): lax.all_to_all(attended, 'head', split_axis=0, concat_axis=1, tiled=True)]
    all_to_all x3 -> x5, starting transfers between devices: 25.2 us -> 35.6 us  [the longest x3 23.6 us: gather_rows(): return lax.all_to_all(spread, axis_name, 0, 0, tiled=True)]
    unnamed x51 -> x70, local copies, waits for them, and re-layouts: 10 us -> 1.99 us
    all_to_all x3 -> x0, other arithmetic: 6.54 us -> none  [the longest x1 4.45 us: shards(): lax.all_to_all(request_out, 'req', split_axis=0, concat_axis=0, tiled=True)]
    broadcast_in_dim x0 -> x5, local copies, waits for them, and re-layouts: none -> 6.06 us  [the longest x4 3.16 us: gather_rows(): spread = jnp.broadcast_to(rows[None], (parts,) + rows.shape)]
  transfers between devices with their start and end apart: 4 -> 5, of which waited for: 2 -> 4; matrix products, arithmetic and copies ran while one was open for 14% -> 9% of each run, Pallas kernels for 0% -> 0%
where the time goes in v1:
time: 178 us; the launch traced here: 177 us
  waiting for transfers between devices  69.8 us (39%)
  local copies, waits for them, and re-layouts  41.2 us (23%)
  starting transfers between devices  35.6 us (20%)
  other arithmetic  16.6 us (9%)
  matrix products  12.2 us (7%)
    all_to_all x1, waiting for transfers between devices, shards(): lax.all_to_all(packed, 'req', split_axis=0, concat_axis=0, tiled=True)  46.4 us
    all_to_all x3, starting transfers between devices, gather_rows(): return lax.all_to_all(spread, axis_name, 0, 0, tiled=True)  23.6 us
    all_to_all x3, waiting for transfers between devices, gather_rows(): return lax.all_to_all(spread, axis_name, 0, 0, tiled=True)  18.9 us
    all_to_all x1, starting transfers between devices, shards(): lax.all_to_all(packed, 'req', split_axis=0, concat_axis=0, tiled=True)  7.88 us
    all_to_all x1, waiting for transfers between devices, shards(): lax.all_to_all(down_part.reshape(head_parts, own_rows, -1), 'head', 0, 0,...  4.48 us
    all_to_all x1, local copies, waits for them, and re-layouts, shards(): lax.all_to_all(packed, 'req', split_axis=0, concat_axis=0, tiled=True)  4.35 us
    all_to_all x1, starting transfers between devices, shards(): lax.all_to_all(down_part.reshape(head_parts, own_rows, -1), 'head', 0, 0,...  4.13 us
    concatenate x1, other arithmetic, shards(): jnp.concatenate([request_out, request_total[..., None], request_max[...,...  4 us
  transfers between devices with their start and end apart: 5, of which 4 were waited for; matrix products, arithmetic and copies ran while one was open for 9% of the time, Pallas kernels for 0%

profile of v1, /device:TPU:1, one launch (start us, length us, event | category | flops | bytes accessed | tf_op | source)
XLA Modules:
  0.0 176.5 jit_solution(7175061981431263604)
XLA Ops:
  0.6 1.5 broadcast_in_dim.215
  2.2 6.5 %all-to-all-start = ((bf16[8,8,1024]{2,1,0:T(8,128)(2,1)}), bf16[8,8,1024]{2,1,0:T(8,128)(2,1)S(1)}, u32[]{:S(2)}, u32[]{:S(2)}) async-start(bf16[8,8,1024]{2,1,0:T(8,128)(2,1)} %broadcast_in_dim.215), calls=%async_computation | async-start | bytes 262144 | tf_op jit(solution)/shard_map/all_to_all | solution.py:37
  8.6 2.9 %fusion.23 = (s32[20]{0:T(128)}, s32[20]{0:T(128)}, s32[20]{0:T(128)S(1)}, s32[20]{0:T(128)S(1)}) fusion(s32[32,32]{1,0:T(8,128)} %param.25, s32[20]{0:T(128)S(1)} %iota_add_fusion, s32[32]{0:T(128)} %param.24), kind=kLoop, calls=%fused_computation.54 | loop fusion | flops 184240 | bytes 4624 | tf_op jit(solution)/shard_map/reduce_sum | solution.py:83
  12.7 0.8 reshape.532
  13.5 1.4 fusion.72
  14.8 1.4 fusion.70
  16.2 1.1 copy.145
  17.3 1.1 copy.146
  18.4 0.7 gather_fusion.1
  20.1 1.4 fusion.14
  22.7 0.9 broadcast_in_dim.219
  23.6 10.7 %all-to-all-start.1 = ((bf16[32,64,128]{2,1,0:T(8,128)(2,1)}), bf16[32,64,128]{2,1,0:T(8,128)(2,1)}, u32[]{:S(2)}, u32[]{:S(2)}) async-start(bf16[32,64,128]{2,1,0:T(8,128)(2,1)} %broadcast_in_dim.219), calls=%async_computation.1 | async-start | bytes 1048576 | tf_op jit(solution)/shard_map/all_to_all | solution.py:37
  34.6 0.9 broadcast_compare_fusion
  35.5 13.7 %all-to-all-done.1 = bf16[32,64,128]{2,1,0:T(8,128)(2,1)} async-done(((bf16[32,64,128]{2,1,0:T(8,128)(2,1)}), bf16[32,64,128]{2,1,0:T(8,128)(2,1)}, u32[]{:S(2)}, u32[]{:S(2)}) %all-to-all-start.1) | async-done | bytes 524320 | tf_op jit(solution)/shard_map/all_to_all | solution.py:37
  49.2 2.4 %reshape.531 = bf16[32,64,2,64]{3,2,1,0:T(2,128)(2,1)S(1)} reshape(bf16[32,64,128]{2,1,0:T(8,128)(2,1)} %all-to-all-done.1) | data formatting | bytes 1048576 | tf_op jit(solution)/shard_map/reshape | solution.py:90
  51.7 1.3 copy.144
  52.9 2.9 %gather_fusion = bf16[20,64,2,64]{3,1,2,0:T(8,128)(2,1)} fusion(bf16[32,64,2,64]{3,1,2,0:T(8,128)(2,1)} %copy.144, s32[1024]{0:T(1024)} %pad_clamp_fusion), kind=kCustom, calls=%fused_computation | custom fusion | bytes 655440 | tf_op jit(solution)/shard_map/jit(_take)/gather | solution.py:90
  55.8 2.0 %select_reduce_fusion = (f32[20,64,2]{1,2,0:T(2,128)S(1)}, f32[20,64,2,128]{3,1,2,0:T(8,128)S(1)}) fusion(pred[20,128]{1,0:T(8,128)(4,1)S(1)} %iota_compare_fusion, f32[2]{0:T(128)S(1)} %copy-done.31, f32[2]{0:T(128)S(1)} %copy-done.29, pred[20,64,128]{2,1,0:T(8,128)(4,1)} %broadcast_compare_fusion, bf16[20,128,2,64]{1,3,2,0:T(8,128)(2,1)} %bitcast.165, ...), kind=kOutput, calls=%fused_computation.15 | convolution fusion | flops 43742720 | bytes 2470436 | tf_op jit(solution)/shard_map/pthd,pkhd->pthk/dot_general | solution.py:95
  58.0 0.7 gather_fusion.2
  58.8 0.7 copy.152
  59.6 0.7 copy.151
  60.3 0.8 convert_reduce_fusion
  61.4 1.3 fusion.3
  62.7 1.0 copy.148
  63.7 2.1 %reshape.533 = f32[20,8192]{1,0:T(8,128)} reshape(f32[20,64,2,64]{3,2,1,0:T(2,128)S(1)} %copy.148) | data formatting | bytes 1310720 | tf_op jit(solution)/shard_map/reshape | solution.py:120
  65.9 2.1 %dot_general.59 = f32[64,2,64,20]{2,1,0,3:T(2,128)S(1)} reshape(f32[8192,20]{0,1:T(8,128)} %bitcast.163) | data formatting | bytes 1310720 | tf_op jit(solution)/shard_map/dot_general | solution.py:119
  68.0 3.3 %fusion.1 = f32[32,64,2,64]{3,0,2,1:T(8,128)} fusion(f32[64,2,64,20]{2,1,0,3:T(2,128)S(1)} %dot_general.59, s32[20]{0:T(128)S(1)} %copy-done.22, pred[20]{0:T(512)(128)(4,1)S(1)} %copy-done.15), kind=kOutput, calls=%fused_computation.6 | convolution fusion | flops 62915840 | bytes 1704036 | tf_op jit(solution)/shard_map/dot_general | solution.py:119
  71.4 0.9 select_multiply_fusion
  72.6 2.9 %copy.154 = f32[32,64,2,1]{3,0,2,1:T(8,128)} copy(f32[32,64,2,1]{1,0,3,2:T(8,128)S(1)} %convolution_bitcast_fusion.3) | data formatting | bytes 32768 | tf_op jit(solution)/shard_map/dot_general | solution.py:116
  75.5 2.9 %copy.155 = f32[32,64,2,1]{3,0,2,1:T(8,128)} copy(f32[32,64,2,1]{1,0,3,2:T(8,128)S(1)} %bitcast.166) | data formatting | bytes 32768 | tf_op jit(solution)/shard_map/broadcast_in_dim | solution.py:123
  78.4 4.0 %pad_maximum_fusion = f32[32,64,2,66]{3,0,2,1:T(8,128)S(1)} fusion(f32[32,64,2,1]{3,0,2,1:T(8,128)} %copy.155, f32[32,64,2,1]{3,0,2,1:T(8,128)} %copy.154, f32[32,64,2,64]{3,0,2,1:T(8,128)} %fusion.1), kind=kLoop, calls=%fused_computation.5 | loop fusion | flops 540672 | bytes 2162688 | tf_op jit(solution)/shard_map/concatenate | solution.py:122
  82.4 3.0 %copy.156 = f32[32,64,2,66]{3,2,1,0:T(2,128)} copy(f32[32,64,2,66]{3,0,2,1:T(8,128)S(1)} %pad_maximum_fusion) | data formatting | bytes 2162688 | tf_op jit(solution)/shard_map/concatenate | solution.py:122
  85.4 7.9 %all-to-all-start.2 = ((f32[32,64,2,66]{3,2,1,0:T(2,128)}), f32[32,64,2,66]{3,2,1,0:T(2,128)}, u32[]{:S(2)}, u32[]{:S(2)}) async-start(f32[32,64,2,66]{3,2,1,0:T(2,128)} %copy.156), calls=%async_computation.2 | async-start | bytes 4194304 | tf_op jit(solution)/shard_map/all_to_all | solution.py:125
  93.3 0.8 dynamic_slice.10
  95.6 46.4 %all-to-all-done.2 = f32[32,64,2,66]{3,2,1,0:T(2,128)} async-done(((f32[32,64,2,66]{3,2,1,0:T(2,128)}), f32[32,64,2,66]{3,2,1,0:T(2,128)}, u32[]{:S(2)}, u32[]{:S(2)}) %all-to-all-start.2) | async-done | bytes 1081376 | tf_op jit(solution)/shard_map/all_to_all | solution.py:125
  141.9 4.4 %copy.157 = f32[32,64,2,66]{1,0,3,2:T(8,128)} copy(f32[32,64,2,66]{3,2,1,0:T(2,128)} %all-to-all-done.2) | data formatting | bytes 2162688 | tf_op jit(solution)/shard_map/all_to_all | solution.py:125
  146.3 0.8 slice_reduce_fusion
  147.1 0.8 fusion.48
  147.9 0.8 exponential_bitcast_fusion
  148.7 2.1 %fusion = f32[64,2,64]{0,2,1:T(8,128)S(1)} fusion(f32[32,1,64,2,66]{2,0,4,3,1:T(8,128)} %bitcast.162, f32[32,64,2]{1,0,2:T(8,128)S(1)} %exponential_bitcast_fusion), kind=kLoop, calls=%fused_computation.4 | loop fusion | flops 516096 | bytes 1097728 | tf_op jit(solution)/shard_map/reduce_sum | solution.py:136
  151.0 0.7 broadcast_in_dim.249
  151.7 6.5 %all-to-all-start.3 = ((bf16[8,64,128]{2,1,0:T(8,128)(2,1)}), bf16[8,64,128]{2,1,0:T(8,128)(2,1)S(1)}, u32[]{:S(2)}, u32[]{:S(2)}) async-start(bf16[8,64,128]{2,1,0:T(8,128)(2,1)} %broadcast_in_dim.249), calls=%async_computation.3 | async-start | bytes 262144 | tf_op jit(solution)/shard_map/all_to_all | solution.py:37
  158.2 5.2 %all-to-all-done.3 = bf16[8,64,128]{2,1,0:T(8,128)(2,1)S(1)} async-done(((bf16[8,64,128]{2,1,0:T(8,128)(2,1)}), bf16[8,64,128]{2,1,0:T(8,128)(2,1)S(1)}, u32[]{:S(2)}, u32[]{:S(2)}) %all-to-all-start.3) | async-done | bytes 131104 | tf_op jit(solution)/shard_map/all_to_all | solution.py:37
  164.1 1.0 copy-done.2
  165.6 0.9 fusion.7
  166.5 4.1 %all-to-all-start.4 = ((bf16[8,8,1024]{2,1,0:T(8,128)(2,1)}), bf16[8,8,1024]{2,1,0:T(8,128)(2,1)S(1)}, u32[]{:S(2)}, u32[]{:S(2)}) async-start(bf16[8,8,1024]{2,1,0:T(8,128)(2,1)} %fusion.7), calls=%async_computation.4 | async-start | bytes 262144 | tf_op jit(solution)/shard_map/all_to_all | solution.py:190
  170.6 0.8 fusion.16
  171.4 4.5 %all-to-all-done.4 = bf16[8,8,1024]{2,1,0:T(8,128)(2,1)S(1)} async-done(((bf16[8,8,1024]{2,1,0:T(8,128)(2,1)}), bf16[8,8,1024]{2,1,0:T(8,128)(2,1)S(1)}, u32[]{:S(2)}, u32[]{:S(2)}) %all-to-all-start.4) | async-done | bytes 131104 | tf_op jit(solution)/shard_map/all_to_all | solution.py:190
  (109 shorter events, 8.0 us)
Async XLA Ops:
  0.6 162.8 %copy-start = (bf16[1024,1024]{1,0:T(8,128)(2,1)S(1)}, bf16[1024,1024]{1,0:T(8,128)(2,1)}, u32[]{:S(2)}) copy-start(bf16[1024,1024]{1,0:T(8,128)(2,1)} %param.17) | copy-start | bytes 6291460
  2.2 17.6 %all-to-all-start = ((bf16[8,8,1024]{2,1,0:T(8,128)(2,1)}), bf16[8,8,1024]{2,1,0:T(8,128)(2,1)S(1)}, u32[]{:S(2)}, u32[]{:S(2)}) async-start(bf16[8,8,1024]{2,1,0:T(8,128)(2,1)} %broadcast_in_dim.215), calls=%async_computation | async-start | bytes 262144 | tf_op jit(solution)/shard_map/all_to_all | solution.py:37
  11.5 0.6 copy-start.20
  11.5 0.6 copy-start.23
  17.3 1.8 %copy-start.27 = (f32[2,16]{1,0:T(2,128)S(1)}, f32[2,16]{1,0:T(2,128)}, u32[]{:S(2)}) copy-start(f32[2,16]{1,0:T(2,128)} %param.20) | copy-start | bytes 388
  17.3 2.7 %copy-start.12 = (f32[1,1024]{1,0:T(1,128)S(1)}, f32[1,1024]{1,0:T(1,128)}, u32[]{:S(2)}) copy-start(f32[1,1024]{1,0:T(1,128)} %get-tuple-element.35) | copy-start | bytes 12292
  19.8 3.8 %copy-start.3 = (bf16[8,8,1024]{2,1,0:T(8,128)(2,1)}, bf16[8,8,1024]{2,1,0:T(8,128)(2,1)S(1)}, u32[]{:S(2)}) copy-start(bf16[8,8,1024]{2,1,0:T(8,128)(2,1)S(1)} %all-to-all-done) | copy-start | bytes 393220
  20.0 14.3 %copy-start.24 = (s32[20]{0:T(128)S(1)}, s32[20]{0:T(128)}, u32[]{:S(2)}) copy-start(s32[20]{0:T(128)} %copy-done.23) | copy-start | bytes 244
  20.0 14.3 %copy-start.25 = (s32[20]{0:T(128)S(1)}, s32[20]{0:T(128)}, u32[]{:S(2)}) copy-start(s32[20]{0:T(128)} %get-tuple-element.21) | copy-start | bytes 244
  20.0 14.3 %copy-start.26 = (s32[20]{0:T(128)S(1)}, s32[20]{0:T(128)}, u32[]{:S(2)}) copy-start(s32[20]{0:T(128)} %get-tuple-element.22) | copy-start | bytes 244
  20.0 14.4 %copy-start.13 = (pred[20]{0:T(512)(128)(4,1)S(1)}, pred[20]{0:T(512)(128)(4,1)}, u32[]{:S(2)}) copy-start(pred[20]{0:T(512)(128)(4,1)} %get-tuple-element.45) | copy-start | bytes 64
  20.0 14.4 %copy-start.21 = (s32[20]{0:T(128)S(1)}, s32[20]{0:T(128)}, u32[]{:S(2)}) copy-start(s32[20]{0:T(128)} %copy-done.20) | copy-start | bytes 244
  20.0 14.5 %copy-start.17 = (pred[20]{0:T(512)(128)(4,1)S(1)}, pred[20]{0:T(512)(128)(4,1)}, u32[]{:S(2)}) copy-start(pred[20]{0:T(512)(128)(4,1)} %get-tuple-element.44) | copy-start | bytes 64
  20.0 14.5 %copy-start.16 = (s32[20,128]{1,0:T(8,128)S(1)}, s32[20,128]{1,0:T(8,128)}, u32[]{:S(2)}) copy-start(s32[20,128]{1,0:T(8,128)} %param.22) | copy-start | bytes 30724
  21.5 0.6 copy-start.6
  23.6 25.5 %all-to-all-start.1 = ((bf16[32,64,128]{2,1,0:T(8,128)(2,1)}), bf16[32,64,128]{2,1,0:T(8,128)(2,1)}, u32[]{:S(2)}, u32[]{:S(2)}) async-start(bf16[32,64,128]{2,1,0:T(8,128)(2,1)} %broadcast_in_dim.219), calls=%async_computation.1 | async-start | bytes 1048576 | tf_op jit(solution)/shard_map/all_to_all | solution.py:37
  51.6 4.1 %copy-start.18 = (pred[20]{0:T(512)(128)(4,1)S(1)}, pred[20]{0:T(512)(128)(4,1)}, u32[]{:S(2)}) copy-start(pred[20]{0:T(512)(128)(4,1)} %get-tuple-element.44) | copy-start | bytes 64
  51.6 4.1 %copy-start.29 = (f32[2]{0:T(128)S(1)}, f32[2]{0:T(128)}, u32[]{:S(2)}) copy-start(f32[2]{0:T(128)} %get-tuple-element.36) | copy-start | bytes 28
  51.6 4.1 %copy-start.31 = (f32[2]{0:T(128)S(1)}, f32[2]{0:T(128)}, u32[]{:S(2)}) copy-start(f32[2]{0:T(128)} %get-tuple-element.37) | copy-start | bytes 28
  57.8 0.9 copy-start.14
  60.3 1.1 copy-start.1
  65.9 2.1 %copy-start.15 = (pred[20]{0:T(512)(128)(4,1)S(1)}, pred[20]{0:T(512)(128)(4,1)}, u32[]{:S(2)}) copy-start(pred[20]{0:T(512)(128)(4,1)} %get-tuple-element.45) | copy-start | bytes 64
  65.9 2.1 %copy-start.22 = (s32[20]{0:T(128)S(1)}, s32[20]{0:T(128)}, u32[]{:S(2)}) copy-start(s32[20]{0:T(128)} %copy-done.20) | copy-start | bytes 244
  68.0 3.4 %copy-start.5 = (f32[20,64,2]{0,2,1:T(2,128)S(1)}, f32[20,64,2]{0,2,1:T(2,128)}, u32[]{:S(2)}) copy-start(f32[20,64,2]{0,2,1:T(2,128)} %copy.152) | copy-start | bytes 30724
  68.0 3.4 %copy-start.19 = (pred[20]{0:T(512)(128)(4,1)S(1)}, pred[20]{0:T(512)(128)(4,1)}, u32[]{:S(2)}) copy-start(pred[20]{0:T(512)(128)(4,1)} %get-tuple-element.44) | copy-start | bytes 64
  85.4 8.7 %copy-start.28 = (s32[1,64]{1,0:T(1,128)S(1)}, s32[1,64]{1,0:T(1,128)}, u32[]{:S(2)}) copy-start(s32[1,64]{1,0:T(1,128)} %param.26) | copy-start | bytes 772
  85.4 9.7 %copy-start.9 = (bf16[1,64,128]{2,1,0:T(8,128)(2,1)S(1)}, bf16[1,64,128]{2,1,0:T(8,128)(2,1)}, u32[]{:S(2)}) copy-start(bf16[1,64,128]{2,1,0:T(8,128)(2,1)} %get-tuple-element.30) | copy-start | bytes 49156
  85.4 9.8 %copy-start.8 = (bf16[1,64,128]{2,1,0:T(8,128)(2,1)S(1)}, bf16[1,64,128]{2,1,0:T(8,128)(2,1)}, u32[]{:S(2)}) copy-start(bf16[1,64,128]{2,1,0:T(8,128)(2,1)} %get-tuple-element.33) | copy-start | bytes 49156
  85.4 10.0 %copy-start.30 = (f32[2]{0:T(128)S(1)}, f32[2]{0:T(128)}, u32[]{:S(2)}) copy-start(f32[2]{0:T(128)} %get-tuple-element.36) | copy-start | bytes 28
  85.4 10.0 %copy-start.32 = (f32[2]{0:T(128)S(1)}, f32[2]{0:T(128)}, u32[]{:S(2)}) copy-start(f32[2]{0:T(128)} %get-tuple-element.37) | copy-start | bytes 28
  85.4 56.5 %all-to-all-start.2 = ((f32[32,64,2,66]{3,2,1,0:T(2,128)}), f32[32,64,2,66]{3,2,1,0:T(2,128)}, u32[]{:S(2)}, u32[]{:S(2)}) async-start(f32[32,64,2,66]{3,2,1,0:T(2,128)} %copy.156), calls=%async_computation.2 | async-start | bytes 4194304 | tf_op jit(solution)/shard_map/all_to_all | solution.py:125
  148.6 14.8 %copy-start.4 = (bf16[8,8,1024]{2,1,0:T(8,128)(2,1)S(1)}, bf16[8,8,1024]{2,1,0:T(8,128)(2,1)}, u32[]{:S(2)}) copy-start(bf16[8,8,1024]{2,1,0:T(8,128)(2,1)} %copy-done.3) | copy-start | bytes 393220
  151.0 13.0 %copy-start.10 = (bf16[64,128]{1,0:T(8,128)(2,1)}, bf16[64,128]{1,0:T(8,128)(2,1)S(1)}, u32[]{:S(2)}) copy-start(bf16[64,128]{1,0:T(8,128)(2,1)S(1)} %copy.165) | copy-start | bytes 49156
  151.7 11.7 %all-to-all-start.3 = ((bf16[8,64,128]{2,1,0:T(8,128)(2,1)}), bf16[8,64,128]{2,1,0:T(8,128)(2,1)S(1)}, u32[]{:S(2)}, u32[]{:S(2)}) async-start(bf16[8,64,128]{2,1,0:T(8,128)(2,1)} %broadcast_in_dim.249), calls=%async_computation.3 | async-start | bytes 262144 | tf_op jit(solution)/shard_map/all_to_all | solution.py:37
  158.2 5.9 %copy-start.11 = (f32[1,1024]{1,0:T(1,128)S(1)}, f32[1,1024]{1,0:T(1,128)}, u32[]{:S(2)}) copy-start(f32[1,1024]{1,0:T(1,128)} %get-tuple-element.34) | copy-start | bytes 12292
  163.4 1.6 copy-start.2
  164.0 1.5 copy-start.33
  165.5 5.1 %copy-start.7 = (bf16[3,64,128]{2,1,0:T(8,128)(2,1)S(1)}, bf16[3,64,128]{2,1,0:T(8,128)(2,1)}, u32[]{:S(2)}) copy-start(bf16[3,64,128]{2,1,0:T(8,128)(2,1)} %copy-done.6) | copy-start | bytes 147460
  165.6 5.1 %copy-start.34 = (s32[1,8]{1,0:T(1,128)S(1)}, s32[1,8]{1,0:T(1,128)}, u32[]{:S(2)}) copy-start(s32[1,8]{1,0:T(1,128)} %param.27) | copy-start | bytes 100
  166.5 9.4 %all-to-all-start.4 = ((bf16[8,8,1024]{2,1,0:T(8,128)(2,1)}), bf16[8,8,1024]{2,1,0:T(8,128)(2,1)S(1)}, u32[]{:S(2)}, u32[]{:S(2)}) async-start(bf16[8,8,1024]{2,1,0:T(8,128)(2,1)} %fusion.7), calls=%async_computation.4 | async-start | bytes 262144 | tf_op jit(solution)/shard_map/all_to_all | solution.py:190

commit v2 on v1

--- a/solution.py
+++ b/solution.py
@@ -119,15 +119,26 @@
     request_out = jnp.dot(
         member_float, (page_out * factor[..., None]).reshape(pool, -1), precision=highest
     ).reshape(requests, tree, head_local, HD)
+    out_width = tree * head_local * HD
+    stat_width = tree * head_local
     packed = jnp.concatenate(
-        [request_out, request_total[..., None], request_max[..., None]], axis=-1
+        [
+            request_out.reshape(requests, out_width),
+            request_total.reshape(requests, stat_width),
+            request_max.reshape(requests, stat_width),
+        ],
+        axis=-1,
     )
     received = lax.all_to_all(packed, "req", split_axis=0, concat_axis=0, tiled=True)
     sources = lax.axis_size("req")
-    received = received.reshape((sources, local_req) + received.shape[1:])
-    source_out = received[..., :HD]
-    source_total = received[..., HD]
-    source_max = received[..., HD + 1]
+    received = received.reshape(sources, local_req, -1)
+    source_out = received[..., :out_width].reshape(sources, local_req, tree, head_local, HD)
+    source_total = received[..., out_width : out_width + stat_width].reshape(
+        sources, local_req, tree, head_local
+    )
+    source_max = received[..., out_width + stat_width :].reshape(
+        sources, local_req, tree, head_local
+    )
     largest = jnp.max(source_max, axis=0)
     source_factor = jnp.exp(source_max - largest[None])
     cached_part = (

time: 178 us -> 149 us (0.84)
  waiting for transfers between devices: 69.8 us -> 46.7 us
  other arithmetic: 16.6 us -> 11 us
  starting transfers between devices: 35.6 us -> 38 us
  matrix products: 12.2 us -> 10.4 us
    all_to_all x1, waiting for transfers between devices: 46.4 us -> 23.2 us  [shards(): lax.all_to_all(packed, 'req', split_axis=0, concat_axis=0, tiled=True)]
    mul x0 -> x2, local copies, waits for them, and re-layouts: none -> 8.95 us  [shards(): source_out * source_factor[..., None]]
    dot_general x2 -> x0, local copies, waits for them, and re-layouts: 4.98 us -> none  [the longest x1 2.9 us: shards(): jnp.dot(member_float, (page_total * factor).reshape(pool, -1), precision=...]
    concatenate x1 -> x0, other arithmetic: 4 us -> none  [shards(): jnp.concatenate([request_out, request_total[..., None], request_max[...,...]
    concatenate x1 -> x0, local copies, waits for them, and re-layouts: 2.95 us -> none  [shards(): jnp.concatenate([request_out, request_total[..., None], request_max[...,...]
    broadcast_in_dim x1 -> x0, local copies, waits for them, and re-layouts: 2.89 us -> none  [shards(): request_max[..., None]]
    all_to_all x3, starting transfers between devices: 23.6 us -> 26.2 us  [gather_rows(): return lax.all_to_all(spread, axis_name, 0, 0, tiled=True)]
    all_to_all x1, local copies, waits for them, and re-layouts: 4.35 us -> 2.1 us  [shards(): lax.all_to_all(packed, 'req', split_axis=0, concat_axis=0, tiled=True)]
  transfers between devices with their start and end apart: 5 -> 5, of which waited for: 4 -> 4; matrix products, arithmetic and copies ran while one was open for 9% -> 10% of each run, Pallas kernels for 0% -> 0%
where the time goes in v2:
time: 149 us; the launch traced here: 148 us
  waiting for transfers between devices  46.7 us (31%)
  local copies, waits for them, and re-layouts  40.9 us (27%)
  starting transfers between devices  38 us (26%)
  other arithmetic  11 us (7%)
  matrix products  10.4 us (7%)
    all_to_all x3, starting transfers between devices, gather_rows(): return lax.all_to_all(spread, axis_name, 0, 0, tiled=True)  26.2 us
    all_to_all x1, waiting for transfers between devices, shards(): lax.all_to_all(packed, 'req', split_axis=0, concat_axis=0, tiled=True)  23.2 us
    all_to_all x3, waiting for transfers between devices, gather_rows(): return lax.all_to_all(spread, axis_name, 0, 0, tiled=True)  19 us
    mul x2, local copies, waits for them, and re-layouts, shards(): source_out * source_factor[..., None]  8.95 us
    all_to_all x1, starting transfers between devices, shards(): lax.all_to_all(packed, 'req', split_axis=0, concat_axis=0, tiled=True)  7.69 us
    all_to_all x1, waiting for transfers between devices, shards(): lax.all_to_all(down_part.reshape(head_parts, own_rows, -1), 'head', 0, 0,...  4.48 us
    all_to_all x1, starting transfers between devices, shards(): lax.all_to_all(down_part.reshape(head_parts, own_rows, -1), 'head', 0, 0,...  4.14 us
    reshape x2, local copies, waits for them, and re-layouts, shards(): all_queries.reshape(requests, tree, head_local, HD)  3.69 us
  transfers between devices with their start and end apart: 5, of which 4 were waited for; matrix products, arithmetic and copies ran while one was open for 10% of the time, Pallas kernels for 0%

profile of v2, /device:TPU:1, one launch (start us, length us, event | category | flops | bytes accessed | tf_op | source)
XLA Modules:
  0.0 148.2 jit_solution(6456724652282315898)
XLA Ops:
  0.6 1.5 %broadcast_in_dim.212 = bf16[8,8,1024]{2,1,0:T(8,128)(2,1)} broadcast(bf16[8,1024]{1,0:T(8,128)(2,1)} %param.14), dimensions={1,2} | broadcast | bytes 147456 | tf_op jit(solution)/shard_map/broadcast_in_dim | solution.py:36
  2.2 6.5 %all-to-all-start = ((bf16[8,8,1024]{2,1,0:T(8,128)(2,1)}), bf16[8,8,1024]{2,1,0:T(8,128)(2,1)S(1)}, u32[]{:S(2)}, u32[]{:S(2)}) async-start(bf16[8,8,1024]{2,1,0:T(8,128)(2,1)} %broadcast_in_dim.212), calls=%async_computation | async-start | bytes 262144 | tf_op jit(solution)/shard_map/all_to_all | solution.py:37
  8.6 0.7 constant_dynamic-slice_fusion
  9.9 2.9 %fusion.21 = (s32[20]{0:T(128)}, s32[20]{0:T(128)}, s32[20]{0:T(128)}, s32[20]{0:T(128)S(1)}) fusion(s32[32,32]{1,0:T(8,128)} %param.25, s32[20]{0:T(128)S(1)} %iota_add_fusion, s32[32]{0:T(128)} %param.24), kind=kLoop, calls=%fused_computation.51 | loop fusion | flops 184240 | bytes 4624 | tf_op jit(solution)/shard_map/reduce_sum | solution.py:83
  13.4 1.4 fusion.79
  14.8 0.8 reshape.546
  15.6 1.4 fusion.77
  17.0 1.1 copy.107
  18.1 1.1 copy.106
  19.2 0.7 gather_fusion.1
  20.2 1.4 fusion.11
  21.6 0.6 copy-done.7
  22.2 0.6 fusion.78
  22.9 0.9 broadcast_in_dim.216
  23.8 10.7 %all-to-all-start.1 = ((bf16[32,64,128]{2,1,0:T(8,128)(2,1)}), bf16[32,64,128]{2,1,0:T(8,128)(2,1)}, u32[]{:S(2)}, u32[]{:S(2)}) async-start(bf16[32,64,128]{2,1,0:T(8,128)(2,1)} %broadcast_in_dim.216), calls=%async_computation.1 | async-start | bytes 1048576 | tf_op jit(solution)/shard_map/all_to_all | solution.py:37
  34.7 0.9 broadcast_compare_fusion
  35.6 13.7 %all-to-all-done.1 = bf16[32,64,128]{2,1,0:T(8,128)(2,1)} async-done(((bf16[32,64,128]{2,1,0:T(8,128)(2,1)}), bf16[32,64,128]{2,1,0:T(8,128)(2,1)}, u32[]{:S(2)}, u32[]{:S(2)}) %all-to-all-start.1) | async-done | bytes 524320 | tf_op jit(solution)/shard_map/all_to_all | solution.py:37
  49.3 2.4 %reshape.545 = bf16[32,64,2,64]{3,2,1,0:T(2,128)(2,1)S(1)} reshape(bf16[32,64,128]{2,1,0:T(8,128)(2,1)} %all-to-all-done.1) | data formatting | bytes 1048576 | tf_op jit(solution)/shard_map/reshape | solution.py:90
  51.8 1.2 copy.105
  53.1 2.9 %gather_fusion = bf16[20,64,2,64]{3,1,2,0:T(8,128)(2,1)} fusion(bf16[32,64,2,64]{3,1,2,0:T(8,128)(2,1)} %copy.105, s32[1024]{0:T(1024)} %pad_clamp_fusion), kind=kCustom, calls=%fused_computation | custom fusion | bytes 655440 | tf_op jit(solution)/shard_map/jit(_take)/gather | solution.py:90
  56.0 2.0 %select_reduce_fusion = (f32[20,64,2]{1,2,0:T(2,128)S(1)}, f32[20,64,2,128]{3,1,2,0:T(8,128)S(1)}) fusion(pred[20,128]{1,0:T(8,128)(4,1)S(1)} %iota_compare_fusion, f32[2]{0:T(128)S(1)} %copy-done.28, f32[2]{0:T(128)S(1)} %copy-done.26, pred[20,64,128]{2,1,0:T(8,128)(4,1)} %broadcast_compare_fusion, bf16[20,128,2,64]{1,3,2,0:T(8,128)(2,1)} %bitcast.129, ...), kind=kOutput, calls=%fused_computation.10 | convolution fusion | flops 43742720 | bytes 2470436 | tf_op jit(solution)/shard_map/pthd,pkhd->pthk/dot_general | solution.py:95
  58.2 0.7 copy.113
  59.0 0.7 gather_fusion.2
  59.7 0.7 exponential_select_fusion
  60.4 0.7 copy.112
  61.2 1.4 convert_reduce_fusion
  62.6 1.1 fusion
  63.8 1.0 copy.109
  64.8 2.1 %reshape.547 = f32[20,8192]{1,0:T(8,128)} reshape(f32[20,64,2,64]{3,2,1,0:T(2,128)S(1)} %copy.109) | data formatting | bytes 1310720 | tf_op jit(solution)/shard_map/reshape | solution.py:120
  67.0 0.9 copy.110
  67.9 1.8 %fusion.73 = f32[32,8192]{1,0:T(8,128)S(1)} fusion(f32[20,8192]{1,0:T(8,128)} %reshape.547, s32[20]{0:T(128)S(1)} %copy-done.17, pred[20]{0:T(512)(128)(4,1)S(1)} %get-tuple-element.44), kind=kOutput, calls=%fused_computation.132 | convolution fusion | flops 62915840 | bytes 1704036 | tf_op jit(solution)/shard_map/dot_general | solution.py:119
  70.1 2.1 %copy.115 = f32[32,1,8448]{2,1,0:T(1,128)} copy(f32[32,1,8448]{2,0,1:T(8,128)S(1)} %maximum_bitcast_fusion) | data formatting | bytes 2162688 | tf_op jit(solution)/shard_map/all_to_all | solution.py:132
  72.2 7.7 %all-to-all-start.2 = ((f32[32,1,8448]{2,1,0:T(1,128)}), f32[32,1,8448]{2,1,0:T(1,128)S(1)}, u32[]{:S(2)}, u32[]{:S(2)}) async-start(f32[32,1,8448]{2,1,0:T(1,128)} %copy.115), calls=%async_computation.2 | async-start | bytes 2162688 | tf_op jit(solution)/shard_map/all_to_all | solution.py:132
  79.9 0.8 dynamic_slice.10
  82.2 23.2 %all-to-all-done.2 = f32[32,1,8448]{2,1,0:T(1,128)S(1)} async-done(((f32[32,1,8448]{2,1,0:T(1,128)}), f32[32,1,8448]{2,1,0:T(1,128)S(1)}, u32[]{:S(2)}, u32[]{:S(2)}) %all-to-all-start.2) | async-done | bytes 1081376 | tf_op jit(solution)/shard_map/all_to_all | solution.py:132
  106.2 1.8 %copy.117 = f32[32,64,2]{2,1,0:T(8,128)} copy(f32[32,64,2]{0,2,1:T(2,128)S(1)} %subtract_exponential_fusion) | data formatting | bytes 32768 | tf_op jit(solution)/shard_map/exp | solution.py:143
  108.1 4.7 %mul.216 = f32[32,64,2,64]{3,2,1,0:T(2,128)} broadcast(f32[32,64,2]{2,1,0:T(8,128)} %copy.117), dimensions={0,1,2} | broadcast | bytes 1064960 | tf_op jit(solution)/shard_map/mul | solution.py:147
  112.8 4.2 %mul.217 = f32[32,1,8192]{2,1,0:T(1,128)} reshape(f32[32,64,2,64]{3,2,1,0:T(2,128)} %mul.216) | data formatting | bytes 2097152 | tf_op jit(solution)/shard_map/mul | solution.py:147
  117.0 2.6 %fusion.14 = f32[8192]{0:T(1024)S(1)} fusion(f32[32,1,8192]{2,1,0:T(1,128)} %mul.217, f32[32,1,8448]{2,1,0:T(1,128)S(1)} %all-to-all-done.2), kind=kLoop, calls=%fused_computation.35 | loop fusion | flops 516096 | bytes 2129920 | tf_op jit(solution)/shard_map/reduce_sum | solution.py:147
  120.1 0.7 broadcast_in_dim.245
  120.7 9.0 %all-to-all-start.3 = ((bf16[8,64,128]{2,1,0:T(8,128)(2,1)}), bf16[8,64,128]{2,1,0:T(8,128)(2,1)S(1)}, u32[]{:S(2)}, u32[]{:S(2)}) async-start(bf16[8,64,128]{2,1,0:T(8,128)(2,1)} %broadcast_in_dim.245), calls=%async_computation.3 | async-start | bytes 262144 | tf_op jit(solution)/shard_map/all_to_all | solution.py:37
  129.8 5.2 %all-to-all-done.3 = bf16[8,64,128]{2,1,0:T(8,128)(2,1)S(1)} async-done(((bf16[8,64,128]{2,1,0:T(8,128)(2,1)}), bf16[8,64,128]{2,1,0:T(8,128)(2,1)S(1)}, u32[]{:S(2)}, u32[]{:S(2)}) %all-to-all-start.3) | async-done | bytes 131104 | tf_op jit(solution)/shard_map/all_to_all | solution.py:37
  135.7 1.0 copy-done.2
  137.2 0.9 fusion.4
  138.1 4.1 %all-to-all-start.4 = ((bf16[8,8,1024]{2,1,0:T(8,128)(2,1)}), bf16[8,8,1024]{2,1,0:T(8,128)(2,1)S(1)}, u32[]{:S(2)}, u32[]{:S(2)}) async-start(bf16[8,8,1024]{2,1,0:T(8,128)(2,1)} %fusion.4), calls=%async_computation.4 | async-start | bytes 262144 | tf_op jit(solution)/shard_map/all_to_all | solution.py:201
  142.3 0.8 fusion.13
  143.1 4.5 %all-to-all-done.4 = bf16[8,8,1024]{2,1,0:T(8,128)(2,1)S(1)} async-done(((bf16[8,8,1024]{2,1,0:T(8,128)(2,1)}), bf16[8,8,1024]{2,1,0:T(8,128)(2,1)S(1)}, u32[]{:S(2)}, u32[]{:S(2)}) %all-to-all-start.4) | async-done | bytes 131104 | tf_op jit(solution)/shard_map/all_to_all | solution.py:201
  147.6 0.6 add_convert_fusion
  (110 shorter events, 6.2 us)
Async XLA Ops:
  0.6 134.4 %copy-start = (bf16[1024,1024]{1,0:T(8,128)(2,1)S(1)}, bf16[1024,1024]{1,0:T(8,128)(2,1)}, u32[]{:S(2)}) copy-start(bf16[1024,1024]{1,0:T(8,128)(2,1)} %param.17) | copy-start | bytes 6291460
  2.2 17.8 %all-to-all-start = ((bf16[8,8,1024]{2,1,0:T(8,128)(2,1)}), bf16[8,8,1024]{2,1,0:T(8,128)(2,1)S(1)}, u32[]{:S(2)}, u32[]{:S(2)}) async-start(bf16[8,8,1024]{2,1,0:T(8,128)(2,1)} %broadcast_in_dim.212), calls=%async_computation | async-start | bytes 262144 | tf_op jit(solution)/shard_map/all_to_all | solution.py:37
  12.8 0.6 copy-start.15
  18.1 1.8 %copy-start.16 = (s32[20]{0:T(128)S(1)}, s32[20]{0:T(128)}, u32[]{:S(2)}) copy-start(s32[20]{0:T(128)} %copy-done.15) | copy-start | bytes 244
  18.1 1.8 %copy-start.22 = (s32[20]{0:T(128)S(1)}, s32[20]{0:T(128)}, u32[]{:S(2)}) copy-start(s32[20]{0:T(128)} %get-tuple-element.20) | copy-start | bytes 244
  18.1 2.0 %copy-start.14 = (f32[1,1024]{1,0:T(1,128)S(1)}, f32[1,1024]{1,0:T(1,128)}, u32[]{:S(2)}) copy-start(f32[1,1024]{1,0:T(1,128)} %get-tuple-element.34) | copy-start | bytes 12292
  19.9 14.7 %copy-start.19 = (pred[20]{0:T(512)(128)(4,1)}, pred[20]{0:T(512)(128)(4,1)S(1)}, u32[]{:S(2)}) copy-start(pred[20]{0:T(512)(128)(4,1)S(1)} %get-tuple-element.43) | copy-start | bytes 64
  19.9 3.8 %copy-start.3 = (bf16[8,8,1024]{2,1,0:T(8,128)(2,1)}, bf16[8,8,1024]{2,1,0:T(8,128)(2,1)S(1)}, u32[]{:S(2)}) copy-start(bf16[8,8,1024]{2,1,0:T(8,128)(2,1)S(1)} %all-to-all-done) | copy-start | bytes 393220
  20.1 14.3 %copy-start.23 = (s32[20]{0:T(128)S(1)}, s32[20]{0:T(128)}, u32[]{:S(2)}) copy-start(s32[20]{0:T(128)} %get-tuple-element.18) | copy-start | bytes 244
  20.2 14.3 %copy-start.24 = (s32[20]{0:T(128)S(1)}, s32[20]{0:T(128)}, u32[]{:S(2)}) copy-start(s32[20]{0:T(128)} %get-tuple-element.19) | copy-start | bytes 244
  20.2 14.5 %copy-start.18 = (s32[20,128]{1,0:T(8,128)S(1)}, s32[20,128]{1,0:T(8,128)}, u32[]{:S(2)}) copy-start(s32[20,128]{1,0:T(8,128)} %param.22) | copy-start | bytes 30724
  21.6 0.6 copy-start.7
  23.8 25.6 %all-to-all-start.1 = ((bf16[32,64,128]{2,1,0:T(8,128)(2,1)}), bf16[32,64,128]{2,1,0:T(8,128)(2,1)}, u32[]{:S(2)}, u32[]{:S(2)}) async-start(bf16[32,64,128]{2,1,0:T(8,128)(2,1)} %broadcast_in_dim.216), calls=%async_computation.1 | async-start | bytes 1048576 | tf_op jit(solution)/shard_map/all_to_all | solution.py:37
  51.8 4.1 %copy-start.20 = (pred[20]{0:T(512)(128)(4,1)S(1)}, pred[20]{0:T(512)(128)(4,1)}, u32[]{:S(2)}) copy-start(pred[20]{0:T(512)(128)(4,1)} %copy-done.19) | copy-start | bytes 64
  51.8 4.1 %copy-start.26 = (f32[2]{0:T(128)S(1)}, f32[2]{0:T(128)}, u32[]{:S(2)}) copy-start(f32[2]{0:T(128)} %get-tuple-element.35) | copy-start | bytes 28
  51.8 4.1 %copy-start.28 = (f32[2]{0:T(128)S(1)}, f32[2]{0:T(128)}, u32[]{:S(2)}) copy-start(f32[2]{0:T(128)} %get-tuple-element.36) | copy-start | bytes 28
  61.1 1.4 copy-start.1
  64.8 2.2 %copy-start.5 = (f32[32,64,2]{0,2,1:T(2,128)S(1)}, f32[32,64,2]{0,2,1:T(2,128)}, u32[]{:S(2)}) copy-start(f32[32,64,2]{0,2,1:T(2,128)} %copy.113) | copy-start | bytes 49156
  64.8 3.1 %copy-start.17 = (s32[20]{0:T(128)S(1)}, s32[20]{0:T(128)}, u32[]{:S(2)}) copy-start(s32[20]{0:T(128)} %copy-done.15) | copy-start | bytes 244
  66.9 2.7 %copy-start.6 = (f32[20,64,2]{0,2,1:T(2,128)S(1)}, f32[20,64,2]{0,2,1:T(2,128)}, u32[]{:S(2)}) copy-start(f32[20,64,2]{0,2,1:T(2,128)} %copy.112) | copy-start | bytes 30724
  66.9 2.8 %copy-start.21 = (pred[20]{0:T(512)(128)(4,1)S(1)}, pred[20]{0:T(512)(128)(4,1)}, u32[]{:S(2)}) copy-start(pred[20]{0:T(512)(128)(4,1)} %copy-done.19) | copy-start | bytes 64
  72.2 8.5 %copy-start.25 = (s32[1,64]{1,0:T(1,128)S(1)}, s32[1,64]{1,0:T(1,128)}, u32[]{:S(2)}) copy-start(s32[1,64]{1,0:T(1,128)} %param.26) | copy-start | bytes 772
  72.2 9.5 %copy-start.11 = (bf16[1,64,128]{2,1,0:T(8,128)(2,1)S(1)}, bf16[1,64,128]{2,1,0:T(8,128)(2,1)}, u32[]{:S(2)}) copy-start(bf16[1,64,128]{2,1,0:T(8,128)(2,1)} %get-tuple-element.29) | copy-start | bytes 49156
  72.2 9.6 %copy-start.10 = (bf16[1,64,128]{2,1,0:T(8,128)(2,1)S(1)}, bf16[1,64,128]{2,1,0:T(8,128)(2,1)}, u32[]{:S(2)}) copy-start(bf16[1,64,128]{2,1,0:T(8,128)(2,1)} %get-tuple-element.31) | copy-start | bytes 49156
  72.2 9.7 %copy-start.9 = (bf16[1,64,128]{2,1,0:T(8,128)(2,1)S(1)}, bf16[1,64,128]{2,1,0:T(8,128)(2,1)}, u32[]{:S(2)}) copy-start(bf16[1,64,128]{2,1,0:T(8,128)(2,1)} %get-tuple-element.32) | copy-start | bytes 49156
  72.2 9.8 %copy-start.27 = (f32[2]{0:T(128)S(1)}, f32[2]{0:T(128)}, u32[]{:S(2)}) copy-start(f32[2]{0:T(128)} %get-tuple-element.35) | copy-start | bytes 28
  72.2 9.8 %copy-start.29 = (f32[2]{0:T(128)S(1)}, f32[2]{0:T(128)}, u32[]{:S(2)}) copy-start(f32[2]{0:T(128)} %get-tuple-element.36) | copy-start | bytes 28
  72.2 33.2 %all-to-all-start.2 = ((f32[32,1,8448]{2,1,0:T(1,128)}), f32[32,1,8448]{2,1,0:T(1,128)S(1)}, u32[]{:S(2)}, u32[]{:S(2)}) async-start(f32[32,1,8448]{2,1,0:T(1,128)} %copy.115), calls=%async_computation.2 | async-start | bytes 2162688 | tf_op jit(solution)/shard_map/all_to_all | solution.py:132
  117.0 18.0 %copy-start.4 = (bf16[8,8,1024]{2,1,0:T(8,128)(2,1)S(1)}, bf16[8,8,1024]{2,1,0:T(8,128)(2,1)}, u32[]{:S(2)}) copy-start(bf16[8,8,1024]{2,1,0:T(8,128)(2,1)} %copy-done.3) | copy-start | bytes 393220
  120.1 15.6 %copy-start.12 = (bf16[64,128]{1,0:T(8,128)(2,1)}, bf16[64,128]{1,0:T(8,128)(2,1)S(1)}, u32[]{:S(2)}) copy-start(bf16[64,128]{1,0:T(8,128)(2,1)S(1)} %copy.127) | copy-start | bytes 49156
  120.7 14.3 %all-to-all-start.3 = ((bf16[8,64,128]{2,1,0:T(8,128)(2,1)}), bf16[8,64,128]{2,1,0:T(8,128)(2,1)S(1)}, u32[]{:S(2)}, u32[]{:S(2)}) async-start(bf16[8,64,128]{2,1,0:T(8,128)(2,1)} %broadcast_in_dim.245), calls=%async_computation.3 | async-start | bytes 262144 | tf_op jit(solution)/shard_map/all_to_all | solution.py:37
  129.8 5.9 %copy-start.13 = (f32[1,1024]{1,0:T(1,128)S(1)}, f32[1,1024]{1,0:T(1,128)}, u32[]{:S(2)}) copy-start(f32[1,1024]{1,0:T(1,128)} %get-tuple-element.33) | copy-start | bytes 12292
  135.0 1.6 %copy-start.2 = (bf16[2,1024,512]{2,1,0:T(8,128)(2,1)S(1)}, bf16[2,1024,512]{2,1,0:T(8,128)(2,1)}, u32[]{:S(2)}) copy-start(bf16[2,1024,512]{2,1,0:T(8,128)(2,1)} %param.18) | copy-start | bytes 6291460
  135.6 1.5 %copy-start.30 = (bf16[512,1024]{1,0:T(8,128)(2,1)S(1)}, bf16[512,1024]{1,0:T(8,128)(2,1)}, u32[]{:S(2)}) copy-start(bf16[512,1024]{1,0:T(8,128)(2,1)} %param.19) | copy-start | bytes 3145732
  137.2 5.1 %copy-start.8 = (bf16[3,64,128]{2,1,0:T(8,128)(2,1)S(1)}, bf16[3,64,128]{2,1,0:T(8,128)(2,1)}, u32[]{:S(2)}) copy-start(bf16[3,64,128]{2,1,0:T(8,128)(2,1)} %copy-done.7) | copy-start | bytes 147460
  137.2 5.1 %copy-start.31 = (s32[1,8]{1,0:T(1,128)S(1)}, s32[1,8]{1,0:T(1,128)}, u32[]{:S(2)}) copy-start(s32[1,8]{1,0:T(1,128)} %param.27) | copy-start | bytes 100
  138.1 9.4 %all-to-all-start.4 = ((bf16[8,8,1024]{2,1,0:T(8,128)(2,1)}), bf16[8,8,1024]{2,1,0:T(8,128)(2,1)S(1)}, u32[]{:S(2)}, u32[]{:S(2)}) async-start(bf16[8,8,1024]{2,1,0:T(8,128)(2,1)} %fusion.4), calls=%async_computation.4 | async-start | bytes 262144 | tf_op jit(solution)/shard_map/all_to_all | solution.py:201

commit v3 on v1

--- a/solution.py
+++ b/solution.py
@@ -87,53 +87,71 @@
     in_use = jnp.sum(matching, axis=(0, 1))
     filled = jnp.clip(owner_len - page_order * page, 0, page) * in_use
     valid = jnp.arange(page, dtype=jnp.int32)[None, :] < filled[:, None]
-    page_queries = jnp.take(all_queries.reshape(requests, tree, head_local, HD), owner, axis=0)
+    head_of_column = jnp.arange(qdl, dtype=jnp.int32) // HD
+    head_mask = jnp.arange(head_local, dtype=jnp.int32)[:, None] == head_of_column[None, :]
+    split_rows = head_local * tree
+    page_queries = jnp.take(all_queries.reshape(requests, tree, qdl), owner, axis=0)
+    split_queries = jnp.where(
+        head_mask[None, :, None, :], page_queries[:, None], jnp.zeros((), page_queries.dtype)
+    ).reshape(pool, split_rows, qdl)
     query_variates = jnp.take(token_variates.reshape(requests, tree), owner, axis=0)
-    cache_keys = page_cache[0].reshape(pool, page, head_local, HD)
-    cache_values = page_cache[1].reshape(pool, page, head_local, HD)
     scores = (
-        jnp.einsum("pthd,pkhd->pthk", page_queries, cache_keys, preferred_element_type=jnp.float32)
+        jnp.einsum(
+            "prd,pkd->prk", split_queries, page_cache[0], preferred_element_type=jnp.float32
+        )
         * scale
     )
     same_page = query_variates[:, :, None] == page_variates[:, None, :]
-    scores = scores + jnp.where(
-        same_page[:, :, None, :], same_bias[None, None, :, None], other_bias[None, None, :, None]
-    )
-    keep = valid[:, None, None, :]
+    page_bias = jnp.where(
+        same_page[:, None], same_bias[None, :, None, None], other_bias[None, :, None, None]
+    ).reshape(pool, split_rows, page)
+    scores = scores + page_bias
+    keep = valid[:, None, :]
     page_max = jnp.max(jnp.where(keep, scores, masked_score), axis=-1)
     weights = jnp.where(keep, jnp.exp(scores - page_max[..., None]), 0.0).astype(jnp.bfloat16)
     page_total = jnp.sum(weights, axis=-1, dtype=jnp.float32)
-    page_out = jnp.einsum(
-        "pthk,pkhd->pthd", weights, cache_values, preferred_element_type=jnp.float32
-    )
+    crossed_out = jnp.einsum(
+        "prk,pkc->prc", weights, page_cache[1], preferred_element_type=jnp.float32
+    ).reshape(pool, head_local, tree, qdl)
     member = (owner[None, :] == jnp.arange(requests, dtype=jnp.int32)[:, None]) & (
         in_use[None, :] > 0
     )
-    request_max = jnp.max(jnp.where(member[:, :, None, None], page_max[None], masked_score), axis=1)
+    request_max = jnp.max(jnp.where(member[:, :, None], page_max[None], masked_score), axis=1)
     owner_max = jnp.take(request_max, owner, axis=0)
-    factor = jnp.where(in_use[:, None, None] > 0, jnp.exp(page_max - owner_max), 0.0)
+    factor = jnp.where(in_use[:, None] > 0, jnp.exp(page_max - owner_max), 0.0)
     member_float = member.astype(jnp.float32)
-    request_total = jnp.dot(
-        member_float, (page_total * factor).reshape(pool, -1), precision=highest
-    ).reshape(requests, tree, head_local)
-    request_out = jnp.dot(
-        member_float, (page_out * factor[..., None]).reshape(pool, -1), precision=highest
-    ).reshape(requests, tree, head_local, HD)
-    packed = jnp.concatenate(
-        [request_out, request_total[..., None], request_max[..., None]], axis=-1
-    )
+    request_total = jnp.dot(member_float, page_total * factor, precision=highest)
+    scaled_out = jnp.sum(
+        jnp.where(
+            head_mask[None, :, None, :],
+            crossed_out * factor.reshape(pool, head_local, tree)[..., None],
+            0.0,
+        ),
+        axis=1,
+    )
+    request_out = jnp.dot(member_float, scaled_out.reshape(pool, -1), precision=highest)
+    out_width = tree * qdl
+    stat_width = tree * head_local
+    packed = jnp.concatenate([request_out, request_total, request_max], axis=-1)
     received = lax.all_to_all(packed, "req", split_axis=0, concat_axis=0, tiled=True)
     sources = lax.axis_size("req")
-    received = received.reshape((sources, local_req) + received.shape[1:])
-    source_out = received[..., :HD]
-    source_total = received[..., HD]
-    source_max = received[..., HD + 1]
+    received = received.reshape(sources, local_req, -1)
+    source_out = received[..., :out_width]
+    source_total = received[..., out_width : out_width + stat_width].reshape(
+        sources, local_req, head_local, tree
+    )
+    source_max = received[..., out_width + stat_width :].reshape(
+        sources, local_req, head_local, tree
+    )
     largest = jnp.max(source_max, axis=0)
     source_factor = jnp.exp(source_max - largest[None])
+    spread_factor = jnp.broadcast_to(
+        source_factor.transpose(0, 1, 3, 2)[..., None], (sources, local_req, tree, head_local, HD)
+    ).reshape(sources, local_req, out_width)
     cached_part = (
-        largest,
-        jnp.sum(source_total * source_factor, axis=0),
-        jnp.sum(source_out * source_factor[..., None], axis=0),
+        largest.transpose(0, 2, 1),
+        jnp.sum(source_total * source_factor, axis=0).transpose(0, 2, 1),
+        jnp.sum(source_out * spread_factor, axis=0).reshape(local_req, tree, head_local, HD),
     )
     tree_query = query.reshape(local_req, tree, head_local, HD)
     tree_key = key_new.reshape(local_req, tree, head_local, HD)

time: 178 us -> 137 us (0.77)
  waiting for transfers between devices: 69.8 us -> 46.7 us
  local copies, waits for them, and re-layouts: 41.2 us -> 29.7 us
  other arithmetic: 16.6 us -> 12.1 us
  matrix products: 12.2 us -> 8.03 us
  starting transfers between devices: 35.6 us -> 37.7 us
    all_to_all x1, waiting for transfers between devices: 46.4 us -> 22.8 us  [shards(): lax.all_to_all(packed, 'req', split_axis=0, concat_axis=0, tiled=True)]
    broadcast_in_dim x2 -> x11, local copies, waits for them, and re-layouts: 3.49 us -> 11.2 us  [the longest x3 10.4 us: shards(): jnp.broadcast_to(source_factor.transpose(0, 1, 3, 2)[..., None], (sources...]
    reshape x3, local copies, waits for them, and re-layouts: 5.82 us -> 0.27 us  [the longest x2 0.18 us: shards(): jnp.sum(source_out * spread_factor, axis=0)]
    dot_general x2 -> x0, local copies, waits for them, and re-layouts: 4.98 us -> none  [the longest x1 2.9 us: shards(): jnp.dot(member_float, (page_total * factor).reshape(pool, -1), precision=...]
    concatenate x1 -> x0, other arithmetic: 4 us -> none  [shards(): jnp.concatenate([request_out, request_total[..., None], request_max[...,...]
    slice x3 -> x0, local copies, waits for them, and re-layouts: 3.58 us -> none  [the longest x2 2.49 us: shards(): cache_values = page_cache[1].reshape(pool, page, head_local, HD)]
    dot_general x4, matrix products: 6.97 us -> 3.98 us  [the longest x1 1.61 us: shards(): jnp.einsum('prk,pkc->prc', weights, page_cache[1], preferred_element_type...]
    concatenate x1 -> x0, local copies, waits for them, and re-layouts: 2.95 us -> none  [shards(): jnp.concatenate([request_out, request_total[..., None], request_max[...,...]
where the time goes in v3:
time: 137 us; the launch traced here: 135 us
  waiting for transfers between devices  46.7 us (34%)
  starting transfers between devices  37.7 us (28%)
  local copies, waits for them, and re-layouts  29.7 us (22%)
  other arithmetic  12.1 us (9%)
  matrix products  8.03 us (6%)
    all_to_all x3, starting transfers between devices, gather_rows(): return lax.all_to_all(spread, axis_name, 0, 0, tiled=True)  25.8 us
    all_to_all x1, waiting for transfers between devices, shards(): lax.all_to_all(packed, 'req', split_axis=0, concat_axis=0, tiled=True)  22.8 us
    all_to_all x3, waiting for transfers between devices, gather_rows(): return lax.all_to_all(spread, axis_name, 0, 0, tiled=True)  19.3 us
    broadcast_in_dim x3, local copies, waits for them, and re-layouts, shards(): jnp.broadcast_to(source_factor.transpose(0, 1, 3, 2)[..., None], (sources...  10.4 us
    all_to_all x1, starting transfers between devices, shards(): lax.all_to_all(packed, 'req', split_axis=0, concat_axis=0, tiled=True)  7.7 us
    all_to_all x1, waiting for transfers between devices, shards(): lax.all_to_all(down_part.reshape(head_parts, own_rows, -1), 'head', 0, 0,...  4.48 us
    all_to_all x1, starting transfers between devices, shards(): lax.all_to_all(down_part.reshape(head_parts, own_rows, -1), 'head', 0, 0,...  4.14 us
    broadcast_in_dim x4, local copies, waits for them, and re-layouts, gather_rows(): spread = jnp.broadcast_to(rows[None], (parts,) + rows.shape)  3.17 us
  transfers between devices with their start and end apart: 5, of which 4 were waited for; matrix products, arithmetic and copies ran while one was open for 9% of the time, Pallas kernels for 0%

profile of v3, /device:TPU:1, one launch (start us, length us, event | category | flops | bytes accessed | tf_op | source)
XLA Modules:
  0.0 135.4 jit_solution(17632088751638423890)
XLA Ops:
  0.7 1.5 %broadcast_in_dim.273 = bf16[8,8,1024]{2,1,0:T(8,128)(2,1)} broadcast(bf16[8,1024]{1,0:T(8,128)(2,1)} %param.14), dimensions={1,2} | broadcast | bytes 147456 | tf_op jit(solution)/shard_map/broadcast_in_dim | solution.py:36
  2.2 6.5 %all-to-all-start = ((bf16[8,8,1024]{2,1,0:T(8,128)(2,1)}), bf16[8,8,1024]{2,1,0:T(8,128)(2,1)S(1)}, u32[]{:S(2)}, u32[]{:S(2)}) async-start(bf16[8,8,1024]{2,1,0:T(8,128)(2,1)} %broadcast_in_dim.273), calls=%async_computation | async-start | bytes 262144 | tf_op jit(solution)/shard_map/all_to_all | solution.py:37
  8.7 2.3 %fusion.22 = (s32[20]{0:T(128)S(1)}, s32[20]{0:T(128)S(1)}, s32[20]{0:T(128)S(1)}, s32[20]{0:T(128)S(1)}) fusion(s32[32,32]{1,0:T(8,128)} %param.25, s32[20]{0:T(128)S(1)} %iota_add_fusion, s32[32]{0:T(128)} %param.24), kind=kLoop, calls=%fused_computation.52 | loop fusion | flops 184240 | bytes 4624 | tf_op jit(solution)/shard_map/reduce_sum | solution.py:83
  11.1 1.4 %fusion.78 = (f32[1,1024]{1,0:T(1,128)}, f32[1,1024]{1,0:T(1,128)S(1)}) fusion(f32[2,1024]{1,0:T(2,128)} %param.15), kind=kLoop, calls=%fused_computation.146 | loop fusion | bytes 16384 | tf_op jit(solution)/shard_map/slice | solution.py:196
  12.4 0.8 reshape.549
  13.2 0.8 constant_dynamic-slice_fusion
  14.0 0.6 gather_fusion.1
  14.6 0.9 broadcast_compare_fusion
  16.0 0.4 copy.53
  16.9 0.6 fusion.77
  17.6 0.9 broadcast_in_dim.281
  18.5 10.5 %all-to-all-start.1 = ((bf16[32,64,128]{2,1,0:T(8,128)(2,1)}), bf16[32,64,128]{2,1,0:T(8,128)(2,1)S(1)}, u32[]{:S(2)}, u32[]{:S(2)}) async-start(bf16[32,64,128]{2,1,0:T(8,128)(2,1)} %broadcast_in_dim.281), calls=%async_computation.1 | async-start | bytes 1048576 | tf_op jit(solution)/shard_map/all_to_all | solution.py:37
  29.2 0.7 fusion.54
  29.8 14.1 %all-to-all-done.1 = bf16[32,64,128]{2,1,0:T(8,128)(2,1)S(1)} async-done(((bf16[32,64,128]{2,1,0:T(8,128)(2,1)}), bf16[32,64,128]{2,1,0:T(8,128)(2,1)S(1)}, u32[]{:S(2)}, u32[]{:S(2)}) %all-to-all-start.1) | async-done | bytes 524320 | tf_op jit(solution)/shard_map/all_to_all | solution.py:37
  43.9 0.6 gather_fusion
  44.8 1.1 copy-done.3
  45.9 0.7 select_reduce_fusion.1
  46.6 1.2 convert_reduce_fusion
  47.7 1.6 %fusion.13 = f32[20,128,128]{2,1,0:T(8,128)S(1)} fusion(bf16[2,20,128,128]{3,2,1,0:T(8,128)(2,1)S(1)} %copy-done.3, f32[20,128,128]{1,2,0:T(8,128)S(1)} %get-tuple-element.33, f32[20,128]{1,0:T(8,128)S(1)} %get-tuple-element.32, pred[20,128]{1,0:T(8,128)(4,1)S(1)} %iota_compare_fusion), kind=kOutput, calls=%fused_computation.34 | convolution fusion | flops 84869120 | bytes 3292160 | tf_op jit(solution)/shard_map/prk,pkc->prc/dot_general | solution.py:113
  49.4 0.7 reduce_max.43
  50.0 0.9 select_reduce_fusion.2
  50.9 1.3 gather_fusion.2
  52.2 1.4 %gather.17 = f32[20,2,64]{2,1,0:T(2,128)} reshape(f32[20,128]{1,0:T(8,128)} %gather_fusion.2) | data formatting | bytes 20480 | tf_op jit(solution)/shard_map/jit(_take)/gather | solution.py:120
  53.6 1.0 fusion.48
  54.6 0.9 exponential_select_fusion
  55.5 1.1 select_reduce_fusion
  56.7 0.5 copy.71
  57.3 0.7 fusion.75
  58.1 2.1 %copy.55 = f32[32,1,8448]{2,1,0:T(1,128)} copy(f32[32,1,8448]{2,0,1:T(8,128)S(1)} %maximum_bitcast_fusion) | data formatting | bytes 2162688 | tf_op jit(solution)/shard_map/all_to_all | solution.py:136
  60.2 7.7 %all-to-all-start.2 = ((f32[32,1,8448]{2,1,0:T(1,128)}), f32[32,1,8448]{2,1,0:T(1,128)S(1)}, u32[]{:S(2)}, u32[]{:S(2)}) async-start(f32[32,1,8448]{2,1,0:T(1,128)} %copy.55), calls=%async_computation.2 | async-start | bytes 2162688 | tf_op jit(solution)/shard_map/all_to_all | solution.py:136
  67.9 0.8 dynamic_slice.10
  69.8 0.7 copy.69
  70.8 22.8 %all-to-all-done.2 = f32[32,1,8448]{2,1,0:T(1,128)S(1)} async-done(((f32[32,1,8448]{2,1,0:T(1,128)}), f32[32,1,8448]{2,1,0:T(1,128)S(1)}, u32[]{:S(2)}, u32[]{:S(2)}) %all-to-all-start.2) | async-done | bytes 1081376 | tf_op jit(solution)/shard_map/all_to_all | solution.py:136
  94.1 1.4 %copy.56 = f32[32,64,2]{2,1,0:T(8,128)} copy(f32[32,64,2]{1,2,0:T(2,128)S(1)} %exponential_bitcast_fusion) | data formatting | bytes 32768 | tf_op jit(solution)/shard_map/broadcast_in_dim | solution.py:148
  95.5 4.8 %broadcast_in_dim.313 = f32[32,64,2,64]{3,2,1,0:T(2,128)} broadcast(f32[32,64,2]{2,1,0:T(8,128)} %copy.56), dimensions={0,1,2} | broadcast | bytes 1064960 | tf_op jit(solution)/shard_map/broadcast_in_dim | solution.py:148
  100.3 4.2 %broadcast_in_dim.314 = f32[32,1,8192]{2,1,0:T(1,128)} reshape(f32[32,64,2,64]{3,2,1,0:T(2,128)} %broadcast_in_dim.313) | data formatting | bytes 2097152 | tf_op jit(solution)/shard_map/broadcast_in_dim | solution.py:148
  104.5 2.5 %fusion.12 = f32[8192]{0:T(1024)S(1)} fusion(f32[32,1,8192]{2,1,0:T(1,128)} %broadcast_in_dim.314, f32[32,1,8448]{2,1,0:T(1,128)S(1)} %all-to-all-done.2), kind=kLoop, calls=%fused_computation.33 | loop fusion | flops 516096 | bytes 2129920 | tf_op jit(solution)/shard_map/reduce_sum | solution.py:154
  107.5 0.7 broadcast_in_dim.322
  108.2 8.8 %all-to-all-start.3 = ((bf16[8,64,128]{2,1,0:T(8,128)(2,1)}), bf16[8,64,128]{2,1,0:T(8,128)(2,1)S(1)}, u32[]{:S(2)}, u32[]{:S(2)}) async-start(bf16[8,64,128]{2,1,0:T(8,128)(2,1)} %broadcast_in_dim.322), calls=%async_computation.3 | async-start | bytes 262144 | tf_op jit(solution)/shard_map/all_to_all | solution.py:37
  117.0 5.2 %all-to-all-done.3 = bf16[8,64,128]{2,1,0:T(8,128)(2,1)S(1)} async-done(((bf16[8,64,128]{2,1,0:T(8,128)(2,1)}), bf16[8,64,128]{2,1,0:T(8,128)(2,1)S(1)}, u32[]{:S(2)}, u32[]{:S(2)}) %all-to-all-start.3) | async-done | bytes 131104 | tf_op jit(solution)/shard_map/all_to_all | solution.py:37
  122.3 0.6 fusion.23
  122.9 1.0 copy-done.1
  123.9 0.5 convolution_bitcast_fusion
  124.4 0.9 fusion.2
  125.3 4.1 %all-to-all-start.4 = ((bf16[8,8,1024]{2,1,0:T(8,128)(2,1)}), bf16[8,8,1024]{2,1,0:T(8,128)(2,1)S(1)}, u32[]{:S(2)}, u32[]{:S(2)}) async-start(bf16[8,8,1024]{2,1,0:T(8,128)(2,1)} %fusion.2), calls=%async_computation.4 | async-start | bytes 262144 | tf_op jit(solution)/shard_map/all_to_all | solution.py:208
  129.5 0.8 fusion.11
  130.3 4.5 %all-to-all-done.4 = bf16[8,8,1024]{2,1,0:T(8,128)(2,1)S(1)} async-done(((bf16[8,8,1024]{2,1,0:T(8,128)(2,1)}), bf16[8,8,1024]{2,1,0:T(8,128)(2,1)S(1)}, u32[]{:S(2)}, u32[]{:S(2)}) %all-to-all-start.4) | async-done | bytes 131104 | tf_op jit(solution)/shard_map/all_to_all | solution.py:208
  134.8 0.6 add_convert_fusion
  (103 shorter events, 3.9 us)
Async XLA Ops:
  0.6 121.6 %copy-start = (bf16[1024,1024]{1,0:T(8,128)(2,1)S(1)}, bf16[1024,1024]{1,0:T(8,128)(2,1)}, u32[]{:S(2)}) copy-start(bf16[1024,1024]{1,0:T(8,128)(2,1)} %param.17) | copy-start | bytes 6291460
  0.6 16.0 %copy-start.2 = (bf16[3,1024,128]{2,1,0:T(8,128)(2,1)S(1)}, bf16[3,1024,128]{2,1,0:T(8,128)(2,1)}, u32[]{:S(2)}) copy-start(bf16[3,1024,128]{2,1,0:T(8,128)(2,1)} %param.16) | copy-start | bytes 2359300
  2.2 14.2 %all-to-all-start = ((bf16[8,8,1024]{2,1,0:T(8,128)(2,1)}), bf16[8,8,1024]{2,1,0:T(8,128)(2,1)S(1)}, u32[]{:S(2)}, u32[]{:S(2)}) async-start(bf16[8,8,1024]{2,1,0:T(8,128)(2,1)} %broadcast_in_dim.273), calls=%async_computation | async-start | bytes 262144 | tf_op jit(solution)/shard_map/all_to_all | solution.py:37
  11.0 18.2 %copy-start.16 = (s32[20]{0:T(128)}, s32[20]{0:T(128)S(1)}, u32[]{:S(2)}) copy-start(s32[20]{0:T(128)S(1)} %get-tuple-element.20) | copy-start | bytes 244
  11.0 33.5 %copy-start.18 = (pred[20]{0:T(512)(128)(4,1)}, pred[20]{0:T(512)(128)(4,1)S(1)}, u32[]{:S(2)}) copy-start(pred[20]{0:T(512)(128)(4,1)S(1)} %compare_and_fusion) | copy-start | bytes 64
  11.1 32.9 %copy-start.13 = (s32[1024]{0:T(1024)}, s32[1024]{0:T(1024)S(1)}, u32[]{:S(2)}) copy-start(s32[1024]{0:T(1024)S(1)} %pad_clamp_fusion) | copy-start | bytes 12292
  15.6 1.1 copy-start.23
  15.6 2.9 %copy-start.21 = (f32[2]{0:T(128)}, f32[2]{0:T(128)S(1)}, u32[]{:S(2)}) copy-start(f32[2]{0:T(128)S(1)} %get-tuple-element.30) | copy-start | bytes 28
  16.9 12.9 %copy-start.5 = (bf16[3,64,128]{2,1,0:T(8,128)(2,1)}, bf16[3,64,128]{2,1,0:T(8,128)(2,1)S(1)}, u32[]{:S(2)}) copy-start(bf16[3,64,128]{2,1,0:T(8,128)(2,1)S(1)} %fusion.9) | copy-start | bytes 147460
  18.5 25.4 %all-to-all-start.1 = ((bf16[32,64,128]{2,1,0:T(8,128)(2,1)}), bf16[32,64,128]{2,1,0:T(8,128)(2,1)S(1)}, u32[]{:S(2)}, u32[]{:S(2)}) async-start(bf16[32,64,128]{2,1,0:T(8,128)(2,1)} %broadcast_in_dim.281), calls=%async_computation.1 | async-start | bytes 1048576 | tf_op jit(solution)/shard_map/all_to_all | solution.py:37
  29.0 17.5 %copy-start.19 = (pred[2,128]{1,0:T(4,128)(4,1)}, pred[2,128]{1,0:T(4,128)(4,1)S(1)}, u32[]{:S(2)}) copy-start(pred[2,128]{1,0:T(4,128)(4,1)S(1)} %iota_compare_fusion.3) | copy-start | bytes 772
  29.1 15.6 %copy-start.14 = (pred[20]{0:T(512)(128)(4,1)}, pred[20]{0:T(512)(128)(4,1)S(1)}, u32[]{:S(2)}) copy-start(pred[20]{0:T(512)(128)(4,1)S(1)} %broadcast_compare_fusion.2) | copy-start | bytes 64
  44.6 1.3 copy-start.3
  46.6 2.8 %copy-start.4 = (f32[20,128]{1,0:T(8,128)}, f32[20,128]{1,0:T(8,128)S(1)}, u32[]{:S(2)}) copy-start(f32[20,128]{1,0:T(8,128)S(1)} %get-tuple-element.32) | copy-start | bytes 30724
  56.6 0.6 copy-start.15
  56.6 0.7 copy-start.17
  60.2 8.5 %copy-start.20 = (s32[1,64]{1,0:T(1,128)S(1)}, s32[1,64]{1,0:T(1,128)}, u32[]{:S(2)}) copy-start(s32[1,64]{1,0:T(1,128)} %param.26) | copy-start | bytes 772
  60.2 9.5 %copy-start.9 = (bf16[1,64,128]{2,1,0:T(8,128)(2,1)S(1)}, bf16[1,64,128]{2,1,0:T(8,128)(2,1)}, u32[]{:S(2)}) copy-start(bf16[1,64,128]{2,1,0:T(8,128)(2,1)} %get-tuple-element.21) | copy-start | bytes 49156
  60.2 9.6 %copy-start.8 = (bf16[1,64,128]{2,1,0:T(8,128)(2,1)S(1)}, bf16[1,64,128]{2,1,0:T(8,128)(2,1)}, u32[]{:S(2)}) copy-start(bf16[1,64,128]{2,1,0:T(8,128)(2,1)} %get-tuple-element.23) | copy-start | bytes 49156
  60.2 10.3 %copy-start.7 = (bf16[1,64,128]{2,1,0:T(8,128)(2,1)S(1)}, bf16[1,64,128]{2,1,0:T(8,128)(2,1)}, u32[]{:S(2)}) copy-start(bf16[1,64,128]{2,1,0:T(8,128)(2,1)} %get-tuple-element.24) | copy-start | bytes 49156
  60.2 10.4 %copy-start.22 = (f32[2]{0:T(128)S(1)}, f32[2]{0:T(128)}, u32[]{:S(2)}) copy-start(f32[2]{0:T(128)} %copy-done.21) | copy-start | bytes 28
  60.2 10.4 %copy-start.24 = (f32[2]{0:T(128)S(1)}, f32[2]{0:T(128)}, u32[]{:S(2)}) copy-start(f32[2]{0:T(128)} %copy-done.23) | copy-start | bytes 28
  60.2 33.4 %all-to-all-start.2 = ((f32[32,1,8448]{2,1,0:T(1,128)}), f32[32,1,8448]{2,1,0:T(1,128)S(1)}, u32[]{:S(2)}, u32[]{:S(2)}) async-start(f32[32,1,8448]{2,1,0:T(1,128)} %copy.55), calls=%async_computation.2 | async-start | bytes 2162688 | tf_op jit(solution)/shard_map/all_to_all | solution.py:136
  104.5 2.8 %copy-start.11 = (bf16[1,64,128]{1,2,0:T(8,128)(2,1)S(1)}, bf16[1,64,128]{1,2,0:T(8,128)(2,1)}, u32[]{:S(2)}) copy-start(bf16[1,64,128]{1,2,0:T(8,128)(2,1)} %copy.69) | copy-start | bytes 49156
  107.5 15.3 %copy-start.10 = (bf16[64,128]{1,0:T(8,128)(2,1)}, bf16[64,128]{1,0:T(8,128)(2,1)S(1)}, u32[]{:S(2)}) copy-start(bf16[64,128]{1,0:T(8,128)(2,1)S(1)} %copy.63) | copy-start | bytes 49156
  108.2 14.1 %all-to-all-start.3 = ((bf16[8,64,128]{2,1,0:T(8,128)(2,1)}), bf16[8,64,128]{2,1,0:T(8,128)(2,1)S(1)}, u32[]{:S(2)}, u32[]{:S(2)}) async-start(bf16[8,64,128]{2,1,0:T(8,128)(2,1)} %broadcast_in_dim.322), calls=%async_computation.3 | async-start | bytes 262144 | tf_op jit(solution)/shard_map/all_to_all | solution.py:37
  117.0 5.9 %copy-start.12 = (f32[1,1024]{1,0:T(1,128)S(1)}, f32[1,1024]{1,0:T(1,128)}, u32[]{:S(2)}) copy-start(f32[1,1024]{1,0:T(1,128)} %get-tuple-element.25) | copy-start | bytes 12292
  122.3 1.6 %copy-start.1 = (bf16[2,1024,512]{2,1,0:T(8,128)(2,1)S(1)}, bf16[2,1024,512]{2,1,0:T(8,128)(2,1)}, u32[]{:S(2)}) copy-start(bf16[2,1024,512]{2,1,0:T(8,128)(2,1)} %param.18) | copy-start | bytes 6291460
  122.9 1.5 %copy-start.25 = (bf16[512,1024]{1,0:T(8,128)(2,1)S(1)}, bf16[512,1024]{1,0:T(8,128)(2,1)}, u32[]{:S(2)}) copy-start(bf16[512,1024]{1,0:T(8,128)(2,1)} %param.19) | copy-start | bytes 3145732
  124.4 5.1 %copy-start.6 = (bf16[3,64,128]{2,1,0:T(8,128)(2,1)S(1)}, bf16[3,64,128]{2,1,0:T(8,128)(2,1)}, u32[]{:S(2)}) copy-start(bf16[3,64,128]{2,1,0:T(8,128)(2,1)} %copy-done.5) | copy-start | bytes 147460
  124.4 5.1 %copy-start.26 = (s32[1,8]{1,0:T(1,128)S(1)}, s32[1,8]{1,0:T(1,128)}, u32[]{:S(2)}) copy-start(s32[1,8]{1,0:T(1,128)} %param.27) | copy-start | bytes 100
  125.3 9.4 %all-to-all-start.4 = ((bf16[8,8,1024]{2,1,0:T(8,128)(2,1)}), bf16[8,8,1024]{2,1,0:T(8,128)(2,1)S(1)}, u32[]{:S(2)}, u32[]{:S(2)}) async-start(bf16[8,8,1024]{2,1,0:T(8,128)(2,1)} %fusion.2), calls=%async_computation.4 | async-start | bytes 262144 | tf_op jit(solution)/shard_map/all_to_all | solution.py:208

commit v4 on v3

--- a/solution.py
+++ b/solution.py
@@ -30,6 +30,18 @@
         total_one * factor_one + total_two * factor_two,
         out_one * factor_one[..., None] + out_two * factor_two[..., None],
     )
+
+
+def split_three(values):
+    high = lax.reduce_precision(values, exponent_bits=8, mantissa_bits=7)
+    rest = values - high
+    middle = lax.reduce_precision(rest, exponent_bits=8, mantissa_bits=7)
+    low = rest - middle
+    return [part.astype(jnp.bfloat16) for part in (high, middle, low)]
+
+
+def join_three(high, middle, low):
+    return (high.astype(jnp.float32) + middle.astype(jnp.float32)) + low.astype(jnp.float32)
 
 
 def gather_rows(rows, axis_name, parts):
@@ -132,26 +144,32 @@
     request_out = jnp.dot(member_float, scaled_out.reshape(pool, -1), precision=highest)
     out_width = tree * qdl
     stat_width = tree * head_local
-    packed = jnp.concatenate([request_out, request_total, request_max], axis=-1)
+    stats = jnp.concatenate([request_total, request_max], axis=-1)
+    packed = jnp.concatenate([request_out.astype(jnp.bfloat16)] + split_three(stats), axis=-1)
     received = lax.all_to_all(packed, "req", split_axis=0, concat_axis=0, tiled=True)
     sources = lax.axis_size("req")
     received = received.reshape(sources, local_req, -1)
-    source_out = received[..., :out_width]
-    source_total = received[..., out_width : out_width + stat_width].reshape(
-        sources, local_req, head_local, tree
-    )
-    source_max = received[..., out_width + stat_width :].reshape(
-        sources, local_req, head_local, tree
-    )
+    source_out = received[..., :out_width].astype(jnp.float32).reshape(
+        sources, local_req, tree, qdl
+    )
+    both_width = 2 * stat_width
+    got_stats = join_three(
+        *[
+            received[..., out_width + part * both_width : out_width + (part + 1) * both_width]
+            for part in range(3)
+        ]
+    )
+    source_total = got_stats[..., :stat_width].reshape(sources, local_req, head_local, tree)
+    source_max = got_stats[..., stat_width:].reshape(sources, local_req, head_local, tree)
     largest = jnp.max(source_max, axis=0)
     source_factor = jnp.exp(source_max - largest[None])
-    spread_factor = jnp.broadcast_to(
-        source_factor.transpose(0, 1, 3, 2)[..., None], (sources, local_req, tree, head_local, HD)
-    ).reshape(sources, local_req, out_width)
+    column_factor = jnp.sum(
+        jnp.where(head_mask[None, None, :, None, :], source_factor[..., None], 0.0), axis=2
+    )
     cached_part = (
         largest.transpose(0, 2, 1),
         jnp.sum(source_total * source_factor, axis=0).transpose(0, 2, 1),
-        jnp.sum(source_out * spread_factor, axis=0).reshape(local_req, tree, head_local, HD),
+        jnp.sum(source_out * column_factor, axis=0).reshape(local_req, tree, head_local, HD),
     )
     tree_query = query.reshape(local_req, tree, head_local, HD)
     tree_key = key_new.reshape(local_req, tree, head_local, HD)

time: 137 us -> 125 us (0.912)
  waiting for transfers between devices: 46.7 us -> 35.7 us
  local copies, waits for them, and re-layouts: 29.7 us -> 27.1 us
  other arithmetic: 12.1 us -> 14.1 us
    broadcast_in_dim x3 -> x0, local copies, waits for them, and re-layouts: 10.4 us -> none  [shards(): jnp.broadcast_to(source_factor.transpose(0, 1, 3, 2)[..., None], (sources...]
    all_to_all x1, waiting for transfers between devices: 22.8 us -> 12.7 us  [shards(): lax.all_to_all(packed, 'req', split_axis=0, concat_axis=0, tiled=True)]
    unnamed x56 -> x65, local copies, waits for them, and re-layouts: 2.84 us -> 7.55 us
    reduce_sum x0 -> x1, local copies, waits for them, and re-layouts: none -> 2.54 us  [shards(): jnp.sum(jnp.where(head_mask[None, None, :, None, :], source_factor[..., N...]
    slice x0 -> x1, local copies, waits for them, and re-layouts: none -> 2.07 us  [shards(): received[..., :out_width].astype(jnp.float32)]
    all_to_all x1, local copies, waits for them, and re-layouts: 2.1 us -> 0.59 us  [shards(): lax.all_to_all(packed, 'req', split_axis=0, concat_axis=0, tiled=True)]
    reduce_sum x1 -> x2, other arithmetic: 2.54 us -> 3.48 us  [the longest x1 1.89 us: shards(): jnp.sum(source_out * column_factor, axis=0)]
  transfers between devices with their start and end apart: 5 -> 5, of which waited for: 4 -> 4; matrix products, arithmetic and copies ran while one was open for 9% -> 10% of each run, Pallas kernels for 0% -> 0%
where the time goes in v4:
time: 125 us; the launch traced here: 123 us
  starting transfers between devices  36.6 us (29%)
  waiting for transfers between devices  35.7 us (29%)
  local copies, waits for them, and re-layouts  27.1 us (22%)
  other arithmetic  14.1 us (11%)
  matrix products  8.64 us (7%)
  between operations  1.32 us (1%)
    all_to_all x3, starting transfers between devices, gather_rows(): return lax.all_to_all(spread, axis_name, 0, 0, tiled=True)  24.9 us
    all_to_all x3, waiting for transfers between devices, gather_rows(): return lax.all_to_all(spread, axis_name, 0, 0, tiled=True)  18.5 us
    all_to_all x1, waiting for transfers between devices, shards(): lax.all_to_all(packed, 'req', split_axis=0, concat_axis=0, tiled=True)  12.7 us
    unnamed x65, local copies, waits for them, and re-layouts  7.55 us
    all_to_all x1, starting transfers between devices, shards(): lax.all_to_all(packed, 'req', split_axis=0, concat_axis=0, tiled=True)  7.5 us
    all_to_all x1, waiting for transfers between devices, shards(): lax.all_to_all(down_part.reshape(head_parts, own_rows, -1), 'head', 0, 0,...  4.48 us
    all_to_all x1, starting transfers between devices, shards(): lax.all_to_all(down_part.reshape(head_parts, own_rows, -1), 'head', 0, 0,...  4.14 us
    broadcast_in_dim x4, local copies, waits for them, and re-layouts, gather_rows(): spread = jnp.broadcast_to(rows[None], (parts,) + rows.shape)  3.17 us
  transfers between devices with their start and end apart: 5, of which 4 were waited for; matrix products, arithmetic and copies ran while one was open for 10% of the time, Pallas kernels for 0%

profile of v4, /device:TPU:1, one launch (start us, length us, event | category | flops | bytes accessed | tf_op | source)
XLA Modules:
  0.0 123.4 jit_solution(9567257074658267667)
XLA Ops:
  0.7 1.5 %broadcast_in_dim.285 = bf16[8,8,1024]{2,1,0:T(8,128)(2,1)} broadcast(bf16[8,1024]{1,0:T(8,128)(2,1)} %param.14), dimensions={1,2} | broadcast | bytes 147456 | tf_op jit(solution)/shard_map/broadcast_in_dim | solution.py:48
  2.2 6.5 %all-to-all-start = ((bf16[8,8,1024]{2,1,0:T(8,128)(2,1)}), bf16[8,8,1024]{2,1,0:T(8,128)(2,1)S(1)}, u32[]{:S(2)}, u32[]{:S(2)}) async-start(bf16[8,8,1024]{2,1,0:T(8,128)(2,1)} %broadcast_in_dim.285), calls=%async_computation | async-start | bytes 262144 | tf_op jit(solution)/shard_map/all_to_all | solution.py:49
  8.7 2.3 %fusion.21 = (s32[20]{0:T(128)S(1)}, s32[20]{0:T(128)S(1)}, s32[20]{0:T(128)S(1)}, s32[20]{0:T(128)S(1)}) fusion(s32[32,32]{1,0:T(8,128)} %param.25, s32[20]{0:T(128)S(1)} %iota_add_fusion, s32[32]{0:T(128)} %param.24), kind=kLoop, calls=%fused_computation.53 | loop fusion | flops 184240 | bytes 4624 | tf_op jit(solution)/shard_map/reduce_sum | solution.py:95
  11.0 0.8 constant_dynamic-slice_fusion
  11.8 1.4 %fusion.79 = (f32[1,1024]{1,0:T(1,128)}, f32[1,1024]{1,0:T(1,128)S(1)}) fusion(f32[2,1024]{1,0:T(2,128)} %param.15), kind=kLoop, calls=%fused_computation.157 | loop fusion | bytes 16384 | tf_op jit(solution)/shard_map/slice | solution.py:214
  13.2 0.8 reshape.574
  14.6 0.9 broadcast_compare_fusion
  17.0 0.6 fusion.78
  17.6 0.9 broadcast_in_dim.293
  18.5 10.5 %all-to-all-start.1 = ((bf16[32,64,128]{2,1,0:T(8,128)(2,1)}), bf16[32,64,128]{2,1,0:T(8,128)(2,1)S(1)}, u32[]{:S(2)}, u32[]{:S(2)}) async-start(bf16[32,64,128]{2,1,0:T(8,128)(2,1)} %broadcast_in_dim.293), calls=%async_computation.1 | async-start | bytes 1048576 | tf_op jit(solution)/shard_map/all_to_all | solution.py:49
  29.2 0.7 fusion.56
  30.0 0.8 convolution_minimum_fusion.3
  30.7 13.2 %all-to-all-done.1 = bf16[32,64,128]{2,1,0:T(8,128)(2,1)S(1)} async-done(((bf16[32,64,128]{2,1,0:T(8,128)(2,1)}), bf16[32,64,128]{2,1,0:T(8,128)(2,1)S(1)}, u32[]{:S(2)}, u32[]{:S(2)}) %all-to-all-start.1) | async-done | bytes 524320 | tf_op jit(solution)/shard_map/all_to_all | solution.py:49
  44.0 0.6 gather_fusion
  44.8 1.1 copy-done.4
  45.9 0.7 select_reduce_fusion.2
  46.6 1.2 convert_reduce_fusion
  47.8 1.6 %fusion.12 = f32[20,128,128]{2,1,0:T(8,128)S(1)} fusion(bf16[2,20,128,128]{3,2,1,0:T(8,128)(2,1)S(1)} %copy-done.4, f32[20,128,128]{1,2,0:T(8,128)S(1)} %get-tuple-element.39, f32[20,128]{1,0:T(8,128)S(1)} %get-tuple-element.38, pred[20,128]{1,0:T(8,128)(4,1)S(1)} %iota_compare_fusion), kind=kOutput, calls=%fused_computation.34 | convolution fusion | flops 84869120 | bytes 3292160 | tf_op jit(solution)/shard_map/prk,pkc->prc/dot_general | solution.py:125
  49.4 0.7 reduce_max.43
  50.1 0.9 select_reduce_fusion.3
  50.9 1.3 %gather_fusion.2 = f32[20,128]{1,0:T(8,128)} fusion(f32[32,128]{1,0:T(8,128)S(1)} %select_reduce_fusion.3, s32[1024]{0:T(1024)} %copy-done.15), kind=kCustom, calls=%fused_computation.2 | custom fusion | bytes 20560 | tf_op jit(solution)/shard_map/jit(_take)/gather | solution.py:132
  52.2 1.4 %gather.17 = f32[20,2,64]{2,1,0:T(2,128)} reshape(f32[20,128]{1,0:T(8,128)} %gather_fusion.2) | data formatting | bytes 20480 | tf_op jit(solution)/shard_map/jit(_take)/gather | solution.py:132
  53.6 1.0 fusion.50
  54.6 0.9 exponential_select_fusion
  55.5 1.1 select_reduce_fusion.1
  57.3 0.7 convolution_convert_fusion
  58.0 0.6 broadcast.474
  58.6 1.1 reduce.14
  59.8 1.0 reshape.620
  60.8 7.5 %all-to-all-start.2 = ((bf16[32,2,4480]{2,1,0:T(2,128)(2,1)}), bf16[32,2,4480]{2,1,0:T(2,128)(2,1)}, u32[]{:S(2)}, u32[]{:S(2)}) async-start(bf16[32,2,4480]{2,1,0:T(2,128)(2,1)} %reshape.620), calls=%async_computation.2 | async-start | bytes 1146880 | tf_op jit(solution)/shard_map/all_to_all | solution.py:149
  68.4 0.8 dynamic_slice.10
  69.8 0.7 copy.80
  70.8 12.7 %all-to-all-done.2 = bf16[32,2,4480]{2,1,0:T(2,128)(2,1)} async-done(((bf16[32,2,4480]{2,1,0:T(2,128)(2,1)}), bf16[32,2,4480]{2,1,0:T(2,128)(2,1)}, u32[]{:S(2)}, u32[]{:S(2)}) %all-to-all-start.2) | async-done | bytes 573472 | tf_op jit(solution)/shard_map/all_to_all | solution.py:149
  83.6 3.7 %reshape.621 = bf16[32,1,8960]{2,1,0:T(2,128)(2,1)S(1)} reshape(bf16[32,2,4480]{2,1,0:T(2,128)(2,1)} %all-to-all-done.2) | data formatting | bytes 1146880
  87.4 2.1 %slice.76 = bf16[32,1,8192]{2,1,0:T(2,128)(2,1)} slice(bf16[32,1,8960]{2,1,0:T(2,128)(2,1)S(1)} %reshape.621), slice={[0:32], [0:1], [0:8192]} | slice | bytes 1048576 | tf_op jit(solution)/shard_map/slice | solution.py:152
  90.0 1.6 %select_reduce_fusion = f32[32,64,128]{2,1,0:T(8,128)} fusion(f32[32,2,64]{2,1,0:T(2,128)S(1)} %bitcast.174, pred[2,128]{1,0:T(4,128)(4,1)S(1)} %copy-done.17), kind=kLoop, calls=%fused_computation.4 | loop fusion | flops 786432 | bytes 1065216 | tf_op jit(solution)/shard_map/reduce_sum | solution.py:166
  91.6 2.5 %reduce_sum.134 = f32[32,1,8192]{2,0,1:T(8,128)} reshape(f32[32,64,128]{2,1,0:T(8,128)} %select_reduce_fusion) | data formatting | bytes 2097152 | tf_op jit(solution)/shard_map/reduce_sum | solution.py:166
  94.1 1.9 %multiply_reduce_fusion = f32[8192]{0:T(1024)S(1)} fusion(f32[32,1,8192]{2,0,1:T(8,128)} %reduce_sum.134, bf16[32,1,8192]{2,1,0:T(2,128)(2,1)S(1)} %copy-done.1), kind=kLoop, calls=%fused_computation.33 | loop fusion | flops 778240 | bytes 1605632 | tf_op jit(solution)/shard_map/reduce_sum | solution.py:172
  96.5 0.7 broadcast_in_dim.334
  97.1 7.9 %all-to-all-start.3 = ((bf16[8,64,128]{2,1,0:T(8,128)(2,1)}), bf16[8,64,128]{2,1,0:T(8,128)(2,1)S(1)}, u32[]{:S(2)}, u32[]{:S(2)}) async-start(bf16[8,64,128]{2,1,0:T(8,128)(2,1)} %broadcast_in_dim.334), calls=%async_computation.3 | async-start | bytes 262144 | tf_op jit(solution)/shard_map/all_to_all | solution.py:49
  105.1 5.2 %all-to-all-done.3 = bf16[8,64,128]{2,1,0:T(8,128)(2,1)S(1)} async-done(((bf16[8,64,128]{2,1,0:T(8,128)(2,1)}), bf16[8,64,128]{2,1,0:T(8,128)(2,1)S(1)}, u32[]{:S(2)}, u32[]{:S(2)}) %all-to-all-start.3) | async-done | bytes 131104 | tf_op jit(solution)/shard_map/all_to_all | solution.py:49
  110.3 0.6 fusion.22
  111.0 1.0 copy-done.2
  112.5 0.9 fusion.2
  113.4 4.1 %all-to-all-start.4 = ((bf16[8,8,1024]{2,1,0:T(8,128)(2,1)}), bf16[8,8,1024]{2,1,0:T(8,128)(2,1)S(1)}, u32[]{:S(2)}, u32[]{:S(2)}) async-start(bf16[8,8,1024]{2,1,0:T(8,128)(2,1)} %fusion.2), calls=%async_computation.4 | async-start | bytes 262144 | tf_op jit(solution)/shard_map/all_to_all | solution.py:226
  117.5 0.8 fusion.11
  118.3 4.5 %all-to-all-done.4 = bf16[8,8,1024]{2,1,0:T(8,128)(2,1)S(1)} async-done(((bf16[8,8,1024]{2,1,0:T(8,128)(2,1)}), bf16[8,8,1024]{2,1,0:T(8,128)(2,1)S(1)}, u32[]{:S(2)}, u32[]{:S(2)}) %all-to-all-start.4) | async-done | bytes 131104 | tf_op jit(solution)/shard_map/all_to_all | solution.py:226
  122.8 0.6 add_convert_fusion
  (115 shorter events, 5.7 us)
Async XLA Ops:
  0.6 109.7 %copy-start = (bf16[1024,1024]{1,0:T(8,128)(2,1)S(1)}, bf16[1024,1024]{1,0:T(8,128)(2,1)}, u32[]{:S(2)}) copy-start(bf16[1024,1024]{1,0:T(8,128)(2,1)} %param.17) | copy-start | bytes 6291460
  0.6 16.0 %copy-start.3 = (bf16[3,1024,128]{2,1,0:T(8,128)(2,1)S(1)}, bf16[3,1024,128]{2,1,0:T(8,128)(2,1)}, u32[]{:S(2)}) copy-start(bf16[3,1024,128]{2,1,0:T(8,128)(2,1)} %param.16) | copy-start | bytes 2359300
  2.2 14.3 %all-to-all-start = ((bf16[8,8,1024]{2,1,0:T(8,128)(2,1)}), bf16[8,8,1024]{2,1,0:T(8,128)(2,1)S(1)}, u32[]{:S(2)}, u32[]{:S(2)}) async-start(bf16[8,8,1024]{2,1,0:T(8,128)(2,1)} %broadcast_in_dim.285), calls=%async_computation | async-start | bytes 262144 | tf_op jit(solution)/shard_map/all_to_all | solution.py:49
  11.0 18.2 %copy-start.20 = (s32[20]{0:T(128)}, s32[20]{0:T(128)S(1)}, u32[]{:S(2)}) copy-start(s32[20]{0:T(128)S(1)} %get-tuple-element.23) | copy-start | bytes 244
  11.0 33.6 %copy-start.22 = (pred[20]{0:T(512)(128)(4,1)}, pred[20]{0:T(512)(128)(4,1)S(1)}, u32[]{:S(2)}) copy-start(pred[20]{0:T(512)(128)(4,1)S(1)} %compare_and_fusion) | copy-start | bytes 64
  11.8 4.8 %copy-start.24 = (f32[2]{0:T(128)}, f32[2]{0:T(128)S(1)}, u32[]{:S(2)}) copy-start(f32[2]{0:T(128)S(1)} %get-tuple-element.36) | copy-start | bytes 28
  11.8 4.8 %copy-start.26 = (f32[2]{0:T(128)}, f32[2]{0:T(128)S(1)}, u32[]{:S(2)}) copy-start(f32[2]{0:T(128)S(1)} %get-tuple-element.37) | copy-start | bytes 28
  11.8 32.2 %copy-start.15 = (s32[1024]{0:T(1024)}, s32[1024]{0:T(1024)S(1)}, u32[]{:S(2)}) copy-start(s32[1024]{0:T(1024)S(1)} %pad_clamp_fusion) | copy-start | bytes 12292
  15.6 13.6 %copy-start.18 = (pred[20]{0:T(512)(128)(4,1)}, pred[20]{0:T(512)(128)(4,1)S(1)}, u32[]{:S(2)}) copy-start(pred[20]{0:T(512)(128)(4,1)S(1)} %broadcast_compare_fusion.2) | copy-start | bytes 64
  16.7 13.2 %copy-start.23 = (s32[1,64]{1,0:T(1,128)S(1)}, s32[1,64]{1,0:T(1,128)}, u32[]{:S(2)}) copy-start(s32[1,64]{1,0:T(1,128)} %param.26) | copy-start | bytes 772
  17.0 13.8 %copy-start.7 = (bf16[3,64,128]{2,1,0:T(8,128)(2,1)}, bf16[3,64,128]{2,1,0:T(8,128)(2,1)S(1)}, u32[]{:S(2)}) copy-start(bf16[3,64,128]{2,1,0:T(8,128)(2,1)S(1)} %fusion.9) | copy-start | bytes 147460
  18.5 25.4 %all-to-all-start.1 = ((bf16[32,64,128]{2,1,0:T(8,128)(2,1)}), bf16[32,64,128]{2,1,0:T(8,128)(2,1)S(1)}, u32[]{:S(2)}, u32[]{:S(2)}) async-start(bf16[32,64,128]{2,1,0:T(8,128)(2,1)} %broadcast_in_dim.293), calls=%async_computation.1 | async-start | bytes 1048576 | tf_op jit(solution)/shard_map/all_to_all | solution.py:49
  29.1 15.7 %copy-start.16 = (pred[2,128]{1,0:T(4,128)(4,1)}, pred[2,128]{1,0:T(4,128)(4,1)S(1)}, u32[]{:S(2)}) copy-start(pred[2,128]{1,0:T(4,128)(4,1)S(1)} %iota_compare_fusion.3) | copy-start | bytes 772
  44.6 1.3 %copy-start.4 = (bf16[2,20,128,128]{3,2,1,0:T(8,128)(2,1)S(1)}, bf16[2,20,128,128]{3,2,1,0:T(8,128)(2,1)}, u32[]{:S(2)}) copy-start(bf16[2,20,128,128]{3,2,1,0:T(8,128)(2,1)} %param.21) | copy-start | bytes 3932164
  46.6 2.8 %copy-start.6 = (f32[20,128]{1,0:T(8,128)}, f32[20,128]{1,0:T(8,128)S(1)}, u32[]{:S(2)}) copy-start(f32[20,128]{1,0:T(8,128)S(1)} %get-tuple-element.38) | copy-start | bytes 30724
  56.6 0.6 copy-start.19
  56.6 0.7 copy-start.21
  59.7 8.5 %copy-start.5 = (f32[64,64]{1,0:T(8,128)S(1)}, f32[64,64]{1,0:T(8,128)}, u32[]{:S(2)}) copy-start(f32[64,64]{1,0:T(8,128)} %convolution_minimum_fusion.3) | copy-start | bytes 49156
  59.7 10.0 %copy-start.11 = (bf16[1,64,128]{2,1,0:T(8,128)(2,1)S(1)}, bf16[1,64,128]{2,1,0:T(8,128)(2,1)}, u32[]{:S(2)}) copy-start(bf16[1,64,128]{2,1,0:T(8,128)(2,1)} %get-tuple-element.24) | copy-start | bytes 49156
  59.8 10.1 %copy-start.10 = (bf16[1,64,128]{2,1,0:T(8,128)(2,1)S(1)}, bf16[1,64,128]{2,1,0:T(8,128)(2,1)}, u32[]{:S(2)}) copy-start(bf16[1,64,128]{2,1,0:T(8,128)(2,1)} %get-tuple-element.26) | copy-start | bytes 49156
  59.8 10.8 %copy-start.9 = (bf16[1,64,128]{2,1,0:T(8,128)(2,1)S(1)}, bf16[1,64,128]{2,1,0:T(8,128)(2,1)}, u32[]{:S(2)}) copy-start(bf16[1,64,128]{2,1,0:T(8,128)(2,1)} %get-tuple-element.27) | copy-start | bytes 49156
  59.8 10.9 %copy-start.25 = (f32[2]{0:T(128)S(1)}, f32[2]{0:T(128)}, u32[]{:S(2)}) copy-start(f32[2]{0:T(128)} %copy-done.24) | copy-start | bytes 28
  59.8 10.9 %copy-start.27 = (f32[2]{0:T(128)S(1)}, f32[2]{0:T(128)}, u32[]{:S(2)}) copy-start(f32[2]{0:T(128)} %copy-done.26) | copy-start | bytes 28
  60.8 22.8 %all-to-all-start.2 = ((bf16[32,2,4480]{2,1,0:T(2,128)(2,1)}), bf16[32,2,4480]{2,1,0:T(2,128)(2,1)}, u32[]{:S(2)}, u32[]{:S(2)}) async-start(bf16[32,2,4480]{2,1,0:T(2,128)(2,1)} %reshape.620), calls=%async_computation.2 | async-start | bytes 1146880 | tf_op jit(solution)/shard_map/all_to_all | solution.py:149
  87.3 2.7 %copy-start.17 = (pred[2,128]{1,0:T(4,128)(4,1)S(1)}, pred[2,128]{1,0:T(4,128)(4,1)}, u32[]{:S(2)}) copy-start(pred[2,128]{1,0:T(4,128)(4,1)} %copy-done.16) | copy-start | bytes 772
  91.6 2.5 %copy-start.1 = (bf16[32,1,8192]{2,1,0:T(2,128)(2,1)S(1)}, bf16[32,1,8192]{2,1,0:T(2,128)(2,1)}, u32[]{:S(2)}) copy-start(bf16[32,1,8192]{2,1,0:T(2,128)(2,1)} %slice.76) | copy-start | bytes 1572868
  94.1 2.1 %copy-start.13 = (bf16[1,64,128]{1,2,0:T(8,128)(2,1)S(1)}, bf16[1,64,128]{1,2,0:T(8,128)(2,1)}, u32[]{:S(2)}) copy-start(bf16[1,64,128]{1,2,0:T(8,128)(2,1)} %copy.80) | copy-start | bytes 49156
  96.5 14.4 %copy-start.12 = (bf16[64,128]{1,0:T(8,128)(2,1)}, bf16[64,128]{1,0:T(8,128)(2,1)S(1)}, u32[]{:S(2)}) copy-start(bf16[64,128]{1,0:T(8,128)(2,1)S(1)} %copy.74) | copy-start | bytes 49156
  97.1 13.2 %all-to-all-start.3 = ((bf16[8,64,128]{2,1,0:T(8,128)(2,1)}), bf16[8,64,128]{2,1,0:T(8,128)(2,1)S(1)}, u32[]{:S(2)}, u32[]{:S(2)}) async-start(bf16[8,64,128]{2,1,0:T(8,128)(2,1)} %broadcast_in_dim.334), calls=%async_computation.3 | async-start | bytes 262144 | tf_op jit(solution)/shard_map/all_to_all | solution.py:49
  105.1 5.9 %copy-start.14 = (f32[1,1024]{1,0:T(1,128)S(1)}, f32[1,1024]{1,0:T(1,128)}, u32[]{:S(2)}) copy-start(f32[1,1024]{1,0:T(1,128)} %get-tuple-element.31) | copy-start | bytes 12292
  110.3 1.6 %copy-start.2 = (bf16[2,1024,512]{2,1,0:T(8,128)(2,1)S(1)}, bf16[2,1024,512]{2,1,0:T(8,128)(2,1)}, u32[]{:S(2)}) copy-start(bf16[2,1024,512]{2,1,0:T(8,128)(2,1)} %param.18) | copy-start | bytes 6291460
  110.9 1.5 %copy-start.28 = (bf16[512,1024]{1,0:T(8,128)(2,1)S(1)}, bf16[512,1024]{1,0:T(8,128)(2,1)}, u32[]{:S(2)}) copy-start(bf16[512,1024]{1,0:T(8,128)(2,1)} %param.19) | copy-start | bytes 3145732
  112.4 5.1 %copy-start.8 = (bf16[3,64,128]{2,1,0:T(8,128)(2,1)S(1)}, bf16[3,64,128]{2,1,0:T(8,128)(2,1)}, u32[]{:S(2)}) copy-start(bf16[3,64,128]{2,1,0:T(8,128)(2,1)} %copy-done.7) | copy-start | bytes 147460
  112.5 5.1 %copy-start.29 = (s32[1,8]{1,0:T(1,128)S(1)}, s32[1,8]{1,0:T(1,128)}, u32[]{:S(2)}) copy-start(s32[1,8]{1,0:T(1,128)} %param.27) | copy-start | bytes 100
  113.4 9.4 %all-to-all-start.4 = ((bf16[8,8,1024]{2,1,0:T(8,128)(2,1)}), bf16[8,8,1024]{2,1,0:T(8,128)(2,1)S(1)}, u32[]{:S(2)}, u32[]{:S(2)}) async-start(bf16[8,8,1024]{2,1,0:T(8,128)(2,1)} %fusion.2), calls=%async_computation.4 | async-start | bytes 262144 | tf_op jit(solution)/shard_map/all_to_all | solution.py:226

commit v5 on v4

--- a/solution.py
+++ b/solution.py
@@ -142,25 +142,20 @@
         axis=1,
     )
     request_out = jnp.dot(member_float, scaled_out.reshape(pool, -1), precision=highest)
-    out_width = tree * qdl
-    stat_width = tree * head_local
-    stats = jnp.concatenate([request_total, request_max], axis=-1)
-    packed = jnp.concatenate([request_out.astype(jnp.bfloat16)] + split_three(stats), axis=-1)
+    stats = jnp.stack([request_total, request_max], axis=1)
+    packed = jnp.concatenate(
+        [request_out.astype(jnp.bfloat16).reshape(requests, tree, qdl)] + split_three(stats),
+        axis=1,
+    )
     received = lax.all_to_all(packed, "req", split_axis=0, concat_axis=0, tiled=True)
     sources = lax.axis_size("req")
-    received = received.reshape(sources, local_req, -1)
-    source_out = received[..., :out_width].astype(jnp.float32).reshape(
-        sources, local_req, tree, qdl
-    )
-    both_width = 2 * stat_width
+    received = received.reshape((sources, local_req) + packed.shape[1:])
+    source_out = received[:, :, :tree].astype(jnp.float32)
     got_stats = join_three(
-        *[
-            received[..., out_width + part * both_width : out_width + (part + 1) * both_width]
-            for part in range(3)
-        ]
-    )
-    source_total = got_stats[..., :stat_width].reshape(sources, local_req, head_local, tree)
-    source_max = got_stats[..., stat_width:].reshape(sources, local_req, head_local, tree)
+        *[received[:, :, tree + 2 * part : tree + 2 * part + 2] for part in range(3)]
+    )
+    source_total = got_stats[:, :, 0].reshape(sources, local_req, head_local, tree)
+    source_max = got_stats[:, :, 1].reshape(sources, local_req, head_local, tree)
     largest = jnp.max(source_max, axis=0)
     source_factor = jnp.exp(source_max - largest[None])
     column_factor = jnp.sum(

time: 125 us -> 114 us (0.912)
  local copies, waits for them, and re-layouts: 27.1 us -> 17.9 us
  other arithmetic: 14.1 us -> 11.2 us
    unnamed x65 -> x62, local copies, waits for them, and re-layouts: 7.55 us -> 3.51 us
    reduce_sum x1, local copies, waits for them, and re-layouts: 2.54 us -> 0.09 us  [shards(): jnp.sum(source_out * column_factor, axis=0)]
    slice x1 -> x0, local copies, waits for them, and re-layouts: 2.07 us -> none  [shards(): received[..., :out_width].astype(jnp.float32)]
    reduce_sum x1, other arithmetic: 1.89 us -> 0.17 us  [shards(): jnp.sum(source_out * column_factor, axis=0)]
  transfers between devices with their start and end apart: 5 -> 5, of which waited for: 4 -> 4; matrix products, arithmetic and copies ran while one was open for 10% -> 11% of each run, Pallas kernels for 0% -> 0%
where the time goes in v5:
time: 114 us; the launch traced here: 112 us
  starting transfers between devices  36.7 us (32%)
  waiting for transfers between devices  36.5 us (32%)
  local copies, waits for them, and re-layouts  17.9 us (16%)
  other arithmetic  11.2 us (10%)
  matrix products  8.65 us (8%)
  between operations  1.32 us (1%)
    all_to_all x3, starting transfers between devices, gather_rows(): return lax.all_to_all(spread, axis_name, 0, 0, tiled=True)  25 us
    all_to_all x3, waiting for transfers between devices, gather_rows(): return lax.all_to_all(spread, axis_name, 0, 0, tiled=True)  18.5 us
    all_to_all x1, waiting for transfers between devices, shards(): lax.all_to_all(packed, 'req', split_axis=0, concat_axis=0, tiled=True)  13.6 us
    all_to_all x1, starting transfers between devices, shards(): lax.all_to_all(packed, 'req', split_axis=0, concat_axis=0, tiled=True)  7.51 us
    all_to_all x1, waiting for transfers between devices, shards(): lax.all_to_all(down_part.reshape(head_parts, own_rows, -1), 'head', 0, 0,...  4.48 us
    all_to_all x1, starting transfers between devices, shards(): lax.all_to_all(down_part.reshape(head_parts, own_rows, -1), 'head', 0, 0,...  4.14 us
    unnamed x62, local copies, waits for them, and re-layouts  3.51 us
    broadcast_in_dim x4, local copies, waits for them, and re-layouts, gather_rows(): spread = jnp.broadcast_to(rows[None], (parts,) + rows.shape)  3.17 us
  transfers between devices with their start and end apart: 5, of which 4 were waited for; matrix products, arithmetic and copies ran while one was open for 11% of the time, Pallas kernels for 0%

profile of v5, /device:TPU:1, one launch (start us, length us, event | category | flops | bytes accessed | tf_op | source)
XLA Modules:
  0.0 112.3 jit_solution(4258463416796722758)
XLA Ops:
  0.7 1.5 %broadcast_in_dim.285 = bf16[8,8,1024]{2,1,0:T(8,128)(2,1)} broadcast(bf16[8,1024]{1,0:T(8,128)(2,1)} %param.14), dimensions={1,2} | broadcast | bytes 147456 | tf_op jit(solution)/shard_map/broadcast_in_dim | solution.py:48
  2.2 6.5 %all-to-all-start = ((bf16[8,8,1024]{2,1,0:T(8,128)(2,1)}), bf16[8,8,1024]{2,1,0:T(8,128)(2,1)S(1)}, u32[]{:S(2)}, u32[]{:S(2)}) async-start(bf16[8,8,1024]{2,1,0:T(8,128)(2,1)} %broadcast_in_dim.285), calls=%async_computation | async-start | bytes 262144 | tf_op jit(solution)/shard_map/all_to_all | solution.py:49
  8.7 2.3 %fusion.23 = (s32[20]{0:T(128)S(1)}, s32[20]{0:T(128)S(1)}, s32[20]{0:T(128)S(1)}, s32[20]{0:T(128)S(1)}) fusion(s32[32,32]{1,0:T(8,128)} %param.25, s32[20]{0:T(128)S(1)} %iota_add_fusion, s32[32]{0:T(128)} %param.24), kind=kLoop, calls=%fused_computation.56 | loop fusion | flops 184240 | bytes 4624 | tf_op jit(solution)/shard_map/reduce_sum | solution.py:95
  11.0 0.8 constant_dynamic-slice_fusion
  11.8 1.4 %fusion.78 = (f32[1,1024]{1,0:T(1,128)}, f32[1,1024]{1,0:T(1,128)S(1)}) fusion(f32[2,1024]{1,0:T(2,128)} %param.15), kind=kLoop, calls=%fused_computation.155 | loop fusion | bytes 16384 | tf_op jit(solution)/shard_map/slice | solution.py:209
  13.2 0.8 reshape.563
  14.0 0.6 gather_fusion.1
  14.6 0.9 broadcast_compare_fusion
  16.0 1.1 %copy.57 = pred[20,128,128]{1,2,0:T(32,128)(4,1)} copy(pred[20,128,128]{2,1,0:T(32,128)(4,1)S(1)} %bitcast.185) | data formatting | bytes 655360 | tf_op jit(solution)/shard_map/jit(_where)/broadcast_in_dim | solution.py:117
  17.4 0.3 fusion.10
  17.7 0.6 copy-done.7
  18.3 0.6 fusion.77
  18.9 0.9 broadcast_in_dim.293
  19.8 10.5 %all-to-all-start.1 = ((bf16[32,64,128]{2,1,0:T(8,128)(2,1)}), bf16[32,64,128]{2,1,0:T(8,128)(2,1)S(1)}, u32[]{:S(2)}, u32[]{:S(2)}) async-start(bf16[32,64,128]{2,1,0:T(8,128)(2,1)} %broadcast_in_dim.293), calls=%async_computation.1 | async-start | bytes 1048576 | tf_op jit(solution)/shard_map/all_to_all | solution.py:49
  30.5 0.7 fusion.55
  31.3 0.8 convolution_minimum_fusion.3
  32.1 13.2 %all-to-all-done.1 = bf16[32,64,128]{2,1,0:T(8,128)(2,1)S(1)} async-done(((bf16[32,64,128]{2,1,0:T(8,128)(2,1)}), bf16[32,64,128]{2,1,0:T(8,128)(2,1)S(1)}, u32[]{:S(2)}, u32[]{:S(2)}) %all-to-all-start.1) | async-done | bytes 524320 | tf_op jit(solution)/shard_map/all_to_all | solution.py:49
  45.3 0.6 gather_fusion
  46.1 1.1 copy-done.4
  47.2 0.7 select_reduce_fusion.2
  47.9 1.2 %convert_reduce_fusion = f32[20,128]{1,0:T(8,128)} fusion(f32[20,128,128]{1,2,0:T(8,128)S(1)} %get-tuple-element.36, f32[20,128]{1,0:T(8,128)S(1)} %get-tuple-element.35, pred[20,128]{1,0:T(8,128)(4,1)S(1)} %iota_compare_fusion), kind=kLoop, calls=%fused_computation.7 | loop fusion | flops 1635840 | bytes 1333760 | tf_op jit(solution)/shard_map/reduce_sum | solution.py:124
  49.1 1.6 %fusion.14 = f32[20,128,128]{2,1,0:T(8,128)S(1)} fusion(bf16[2,20,128,128]{3,2,1,0:T(8,128)(2,1)S(1)} %copy-done.4, f32[20,128,128]{1,2,0:T(8,128)S(1)} %get-tuple-element.36, f32[20,128]{1,0:T(8,128)S(1)} %get-tuple-element.35, pred[20,128]{1,0:T(8,128)(4,1)S(1)} %iota_compare_fusion), kind=kOutput, calls=%fused_computation.37 | convolution fusion | flops 84869120 | bytes 3292160 | tf_op jit(solution)/shard_map/prk,pkc->prc/dot_general | solution.py:125
  50.7 0.7 reduce_max.43
  51.4 0.9 select_reduce_fusion.3
  52.2 1.3 %gather_fusion.2 = f32[20,128]{1,0:T(8,128)} fusion(f32[32,128]{1,0:T(8,128)S(1)} %select_reduce_fusion.3, s32[1024]{0:T(1024)} %copy-done.14), kind=kCustom, calls=%fused_computation.2 | custom fusion | bytes 20560 | tf_op jit(solution)/shard_map/jit(_take)/gather | solution.py:132
  53.5 1.4 %gather.17 = f32[20,2,64]{2,1,0:T(2,128)} reshape(f32[20,128]{1,0:T(8,128)} %gather_fusion.2) | data formatting | bytes 20480 | tf_op jit(solution)/shard_map/jit(_take)/gather | solution.py:132
  54.9 1.0 convolution_bitcast_fusion.2
  56.0 0.9 exponential_select_fusion
  56.9 1.1 %select_reduce_fusion.1 = f32[20,64,128]{2,1,0:T(8,128)S(1)} fusion(f32[20,2,64,128]{3,2,1,0:T(8,128)S(1)} %bitcast.179, f32[20,2,64]{2,1,0:T(2,128)S(1)} %exponential_select_fusion, pred[2,128]{1,0:T(4,128)(4,1)} %copy-done.15), kind=kLoop, calls=%fused_computation.8 | loop fusion | flops 819200 | bytes 1976576 | tf_op jit(solution)/shard_map/reduce_sum | solution.py:136
  58.1 0.5 copy.76
  58.7 0.7 fusion.1
  59.5 0.9 pad_maximum_fusion
  60.5 7.5 %all-to-all-start.2 = ((bf16[32,70,128]{2,1,0:T(8,128)(2,1)}), bf16[32,70,128]{2,1,0:T(8,128)(2,1)S(1)}, u32[]{:S(2)}, u32[]{:S(2)}) async-start(bf16[32,70,128]{2,1,0:T(8,128)(2,1)} %pad_maximum_fusion), calls=%async_computation.2 | async-start | bytes 1179648 | tf_op jit(solution)/shard_map/all_to_all | solution.py:150
  68.2 0.8 dynamic_slice.10
  69.1 0.2 fusion.11
  70.0 13.6 %all-to-all-done.2 = bf16[32,70,128]{2,1,0:T(8,128)(2,1)S(1)} async-done(((bf16[32,70,128]{2,1,0:T(8,128)(2,1)}), bf16[32,70,128]{2,1,0:T(8,128)(2,1)S(1)}, u32[]{:S(2)}, u32[]{:S(2)}) %all-to-all-start.2) | async-done | bytes 573472 | tf_op jit(solution)/shard_map/all_to_all | solution.py:150
  84.1 0.6 select_reduce_fusion
  85.3 0.7 broadcast_in_dim.334
  85.9 8.0 %all-to-all-start.3 = ((bf16[8,64,128]{2,1,0:T(8,128)(2,1)}), bf16[8,64,128]{2,1,0:T(8,128)(2,1)S(1)}, u32[]{:S(2)}, u32[]{:S(2)}) async-start(bf16[8,64,128]{2,1,0:T(8,128)(2,1)} %broadcast_in_dim.334), calls=%async_computation.3 | async-start | bytes 262144 | tf_op jit(solution)/shard_map/all_to_all | solution.py:49
  94.0 5.2 %all-to-all-done.3 = bf16[8,64,128]{2,1,0:T(8,128)(2,1)S(1)} async-done(((bf16[8,64,128]{2,1,0:T(8,128)(2,1)}), bf16[8,64,128]{2,1,0:T(8,128)(2,1)S(1)}, u32[]{:S(2)}, u32[]{:S(2)}) %all-to-all-start.3) | async-done | bytes 131104 | tf_op jit(solution)/shard_map/all_to_all | solution.py:49
  99.2 0.6 fusion.24
  99.8 1.0 copy-done.1
  100.8 0.5 convolution_bitcast_fusion
  101.4 0.9 fusion.3
  102.3 4.1 %all-to-all-start.4 = ((bf16[8,8,1024]{2,1,0:T(8,128)(2,1)}), bf16[8,8,1024]{2,1,0:T(8,128)(2,1)S(1)}, u32[]{:S(2)}, u32[]{:S(2)}) async-start(bf16[8,8,1024]{2,1,0:T(8,128)(2,1)} %fusion.3), calls=%async_computation.4 | async-start | bytes 262144 | tf_op jit(solution)/shard_map/all_to_all | solution.py:221
  106.4 0.8 fusion.12
  107.2 4.5 %all-to-all-done.4 = bf16[8,8,1024]{2,1,0:T(8,128)(2,1)S(1)} async-done(((bf16[8,8,1024]{2,1,0:T(8,128)(2,1)}), bf16[8,8,1024]{2,1,0:T(8,128)(2,1)S(1)}, u32[]{:S(2)}, u32[]{:S(2)}) %all-to-all-start.4) | async-done | bytes 131104 | tf_op jit(solution)/shard_map/all_to_all | solution.py:221
  111.7 0.6 add_convert_fusion
  (110 shorter events, 3.5 us)
Async XLA Ops:
  0.6 98.6 %copy-start = (bf16[1024,1024]{1,0:T(8,128)(2,1)S(1)}, bf16[1024,1024]{1,0:T(8,128)(2,1)}, u32[]{:S(2)}) copy-start(bf16[1024,1024]{1,0:T(8,128)(2,1)} %param.17) | copy-start | bytes 6291460
  0.6 16.7 %copy-start.2 = (bf16[3,1024,128]{2,1,0:T(8,128)(2,1)S(1)}, bf16[3,1024,128]{2,1,0:T(8,128)(2,1)}, u32[]{:S(2)}) copy-start(bf16[3,1024,128]{2,1,0:T(8,128)(2,1)} %param.16) | copy-start | bytes 2359300
  2.2 15.0 %all-to-all-start = ((bf16[8,8,1024]{2,1,0:T(8,128)(2,1)}), bf16[8,8,1024]{2,1,0:T(8,128)(2,1)S(1)}, u32[]{:S(2)}, u32[]{:S(2)}) async-start(bf16[8,8,1024]{2,1,0:T(8,128)(2,1)} %broadcast_in_dim.285), calls=%async_computation | async-start | bytes 262144 | tf_op jit(solution)/shard_map/all_to_all | solution.py:49
  11.0 19.5 %copy-start.19 = (s32[20]{0:T(128)}, s32[20]{0:T(128)S(1)}, u32[]{:S(2)}) copy-start(s32[20]{0:T(128)S(1)} %get-tuple-element.20) | copy-start | bytes 244
  11.0 34.9 %copy-start.21 = (pred[20]{0:T(512)(128)(4,1)}, pred[20]{0:T(512)(128)(4,1)S(1)}, u32[]{:S(2)}) copy-start(pred[20]{0:T(512)(128)(4,1)S(1)} %compare_and_fusion) | copy-start | bytes 64
  11.8 5.9 %copy-start.23 = (f32[2]{0:T(128)}, f32[2]{0:T(128)S(1)}, u32[]{:S(2)}) copy-start(f32[2]{0:T(128)S(1)} %get-tuple-element.33) | copy-start | bytes 28
  11.8 5.9 %copy-start.25 = (f32[2]{0:T(128)}, f32[2]{0:T(128)S(1)}, u32[]{:S(2)}) copy-start(f32[2]{0:T(128)S(1)} %get-tuple-element.34) | copy-start | bytes 28
  11.8 33.5 %copy-start.14 = (s32[1024]{0:T(1024)}, s32[1024]{0:T(1024)S(1)}, u32[]{:S(2)}) copy-start(s32[1024]{0:T(1024)S(1)} %pad_clamp_fusion) | copy-start | bytes 12292
  15.6 14.9 %copy-start.17 = (pred[20]{0:T(512)(128)(4,1)}, pred[20]{0:T(512)(128)(4,1)S(1)}, u32[]{:S(2)}) copy-start(pred[20]{0:T(512)(128)(4,1)S(1)} %broadcast_compare_fusion.2) | copy-start | bytes 64
  17.4 13.8 %copy-start.22 = (s32[1,64]{1,0:T(1,128)S(1)}, s32[1,64]{1,0:T(1,128)}, u32[]{:S(2)}) copy-start(s32[1,64]{1,0:T(1,128)} %param.26) | copy-start | bytes 772
  17.7 0.6 copy-start.7
  19.8 25.4 %all-to-all-start.1 = ((bf16[32,64,128]{2,1,0:T(8,128)(2,1)}), bf16[32,64,128]{2,1,0:T(8,128)(2,1)S(1)}, u32[]{:S(2)}, u32[]{:S(2)}) async-start(bf16[32,64,128]{2,1,0:T(8,128)(2,1)} %broadcast_in_dim.293), calls=%async_computation.1 | async-start | bytes 1048576 | tf_op jit(solution)/shard_map/all_to_all | solution.py:49
  30.4 15.7 %copy-start.3 = (pred[20,128,128]{1,2,0:T(32,128)(4,1)S(1)}, pred[20,128,128]{1,2,0:T(32,128)(4,1)}, u32[]{:S(2)}) copy-start(pred[20,128,128]{1,2,0:T(32,128)(4,1)} %copy.57) | copy-start | bytes 983044
  30.4 17.5 %copy-start.15 = (pred[2,128]{1,0:T(4,128)(4,1)}, pred[2,128]{1,0:T(4,128)(4,1)S(1)}, u32[]{:S(2)}) copy-start(pred[2,128]{1,0:T(4,128)(4,1)S(1)} %iota_compare_fusion.3) | copy-start | bytes 772
  45.9 1.3 %copy-start.4 = (bf16[2,20,128,128]{3,2,1,0:T(8,128)(2,1)S(1)}, bf16[2,20,128,128]{3,2,1,0:T(8,128)(2,1)}, u32[]{:S(2)}) copy-start(bf16[2,20,128,128]{3,2,1,0:T(8,128)(2,1)} %param.21) | copy-start | bytes 3932164
  47.9 2.8 %copy-start.6 = (f32[20,128]{1,0:T(8,128)}, f32[20,128]{1,0:T(8,128)S(1)}, u32[]{:S(2)}) copy-start(f32[20,128]{1,0:T(8,128)S(1)} %get-tuple-element.35) | copy-start | bytes 30724
  58.0 0.6 copy-start.18
  58.1 0.6 copy-start.20
  59.5 8.5 %copy-start.5 = (f32[64,64]{1,0:T(8,128)S(1)}, f32[64,64]{1,0:T(8,128)}, u32[]{:S(2)}) copy-start(f32[64,64]{1,0:T(8,128)} %convolution_minimum_fusion.3) | copy-start | bytes 49156
  59.5 10.0 %copy-start.11 = (bf16[1,64,128]{2,1,0:T(8,128)(2,1)S(1)}, bf16[1,64,128]{2,1,0:T(8,128)(2,1)}, u32[]{:S(2)}) copy-start(bf16[1,64,128]{2,1,0:T(8,128)(2,1)} %get-tuple-element.21) | copy-start | bytes 49156
  59.5 10.0 %copy-start.10 = (bf16[1,64,128]{2,1,0:T(8,128)(2,1)S(1)}, bf16[1,64,128]{2,1,0:T(8,128)(2,1)}, u32[]{:S(2)}) copy-start(bf16[1,64,128]{2,1,0:T(8,128)(2,1)} %get-tuple-element.23) | copy-start | bytes 49156
  59.5 10.1 %copy-start.9 = (bf16[1,64,128]{2,1,0:T(8,128)(2,1)S(1)}, bf16[1,64,128]{2,1,0:T(8,128)(2,1)}, u32[]{:S(2)}) copy-start(bf16[1,64,128]{2,1,0:T(8,128)(2,1)} %get-tuple-element.24) | copy-start | bytes 49156
  59.5 10.2 %copy-start.24 = (f32[2]{0:T(128)S(1)}, f32[2]{0:T(128)}, u32[]{:S(2)}) copy-start(f32[2]{0:T(128)} %copy-done.23) | copy-start | bytes 28
  59.5 10.2 %copy-start.26 = (f32[2]{0:T(128)S(1)}, f32[2]{0:T(128)}, u32[]{:S(2)}) copy-start(f32[2]{0:T(128)} %copy-done.25) | copy-start | bytes 28
  60.5 23.7 %copy-start.16 = (pred[2,128]{1,0:T(4,128)(4,1)S(1)}, pred[2,128]{1,0:T(4,128)(4,1)}, u32[]{:S(2)}) copy-start(pred[2,128]{1,0:T(4,128)(4,1)} %copy-done.15) | copy-start | bytes 772
  60.5 23.1 %all-to-all-start.2 = ((bf16[32,70,128]{2,1,0:T(8,128)(2,1)}), bf16[32,70,128]{2,1,0:T(8,128)(2,1)S(1)}, u32[]{:S(2)}, u32[]{:S(2)}) async-start(bf16[32,70,128]{2,1,0:T(8,128)(2,1)} %pad_maximum_fusion), calls=%async_computation.2 | async-start | bytes 1179648 | tf_op jit(solution)/shard_map/all_to_all | solution.py:150
  85.3 14.6 %copy-start.12 = (bf16[64,128]{1,0:T(8,128)(2,1)}, bf16[64,128]{1,0:T(8,128)(2,1)S(1)}, u32[]{:S(2)}) copy-start(bf16[64,128]{1,0:T(8,128)(2,1)S(1)} %copy.68) | copy-start | bytes 49156
  85.9 13.3 %all-to-all-start.3 = ((bf16[8,64,128]{2,1,0:T(8,128)(2,1)}), bf16[8,64,128]{2,1,0:T(8,128)(2,1)S(1)}, u32[]{:S(2)}, u32[]{:S(2)}) async-start(bf16[8,64,128]{2,1,0:T(8,128)(2,1)} %broadcast_in_dim.334), calls=%async_computation.3 | async-start | bytes 262144 | tf_op jit(solution)/shard_map/all_to_all | solution.py:49
  94.0 5.9 %copy-start.13 = (f32[1,1024]{1,0:T(1,128)S(1)}, f32[1,1024]{1,0:T(1,128)}, u32[]{:S(2)}) copy-start(f32[1,1024]{1,0:T(1,128)} %get-tuple-element.28) | copy-start | bytes 12292
  99.2 1.6 %copy-start.1 = (bf16[2,1024,512]{2,1,0:T(8,128)(2,1)S(1)}, bf16[2,1024,512]{2,1,0:T(8,128)(2,1)}, u32[]{:S(2)}) copy-start(bf16[2,1024,512]{2,1,0:T(8,128)(2,1)} %param.18) | copy-start | bytes 6291460
  99.8 1.5 %copy-start.27 = (bf16[512,1024]{1,0:T(8,128)(2,1)S(1)}, bf16[512,1024]{1,0:T(8,128)(2,1)}, u32[]{:S(2)}) copy-start(bf16[512,1024]{1,0:T(8,128)(2,1)} %param.19) | copy-start | bytes 3145732
  101.3 5.1 %copy-start.8 = (bf16[3,64,128]{2,1,0:T(8,128)(2,1)S(1)}, bf16[3,64,128]{2,1,0:T(8,128)(2,1)}, u32[]{:S(2)}) copy-start(bf16[3,64,128]{2,1,0:T(8,128)(2,1)} %copy-done.7) | copy-start | bytes 147460
  101.4 5.1 %copy-start.28 = (s32[1,8]{1,0:T(1,128)S(1)}, s32[1,8]{1,0:T(1,128)}, u32[]{:S(2)}) copy-start(s32[1,8]{1,0:T(1,128)} %param.27) | copy-start | bytes 100
  102.3 9.4 %all-to-all-start.4 = ((bf16[8,8,1024]{2,1,0:T(8,128)(2,1)}), bf16[8,8,1024]{2,1,0:T(8,128)(2,1)S(1)}, u32[]{:S(2)}, u32[]{:S(2)}) async-start(bf16[8,8,1024]{2,1,0:T(8,128)(2,1)} %fusion.3), calls=%async_computation.4 | async-start | bytes 262144 | tf_op jit(solution)/shard_map/all_to_all | solution.py:221

commit v6 on v5

--- a/solution.py
+++ b/solution.py
@@ -3,9 +3,11 @@
 import jax
 import jax.numpy as jnp
 from jax import lax
+from jax.sharding import Mesh
 from jax.sharding import PartitionSpec as P
 
 HD = 64
+REQ = ("req_y", "req_z")
 LEVELS = 8
 
 
@@ -72,7 +74,7 @@
     qdl = qkv_weight.shape[2]
     head_local = qdl // HD
     head_slot = lax.axis_index("head")
-    req_slot = lax.axis_index("req")
+    req_slot = lax.axis_index(REQ)
     bias_local = lax.dynamic_slice_in_dim(variate_bias, head_slot * head_local, head_local, 1)
     same_bias = bias_local[0]
     other_bias = bias_local[1]
@@ -88,7 +90,9 @@
     query = projected[0]
     key_new = projected[1]
     value_new = projected[2]
-    all_queries = gather_rows(query, "req", requests // local_req)
+    req_z_parts = lax.axis_size("req_z")
+    req_y_parts = lax.axis_size("req_y")
+    all_queries = gather_rows(gather_rows(query, "req_z", req_z_parts), "req_y", req_y_parts)
     global_ids = req_slot * pool + jnp.arange(pool, dtype=jnp.int32)
     matching = (page_table[:, :, None] == global_ids[None, None, :]).astype(jnp.int32)
     owner = jnp.sum(matching * jnp.arange(requests, dtype=jnp.int32)[:, None, None], axis=(0, 1))
@@ -147,8 +151,8 @@
         [request_out.astype(jnp.bfloat16).reshape(requests, tree, qdl)] + split_three(stats),
         axis=1,
     )
-    received = lax.all_to_all(packed, "req", split_axis=0, concat_axis=0, tiled=True)
-    sources = lax.axis_size("req")
+    received = lax.all_to_all(packed, REQ, split_axis=0, concat_axis=0, tiled=True)
+    sources = lax.axis_size(REQ)
     received = received.reshape((sources, local_req) + packed.shape[1:])
     source_out = received[:, :, :tree].astype(jnp.float32)
     got_stats = join_three(
@@ -232,26 +236,35 @@
     return (mixed, attended, new_kv)
 
 
+def split_req_mesh(mesh):
+    column = mesh.devices[:, 0]
+    y_parts = len({device.coords[1] for device in column})
+    return Mesh(
+        mesh.devices.reshape(y_parts, column.size // y_parts, mesh.devices.shape[1]),
+        REQ + ("head",),
+    )
+
+
 def solution(mesh):
     return jax.shard_map(
         shards,
-        mesh=mesh,
+        mesh=split_req_mesh(mesh),
         in_specs=(
-            P(("req", "head"), None),
+            P((REQ + ("head",)), None),
             P(),
             P(None, None, "head"),
             P(),
             P(None, None, "head"),
             P("head", None),
             P(),
-            P(None, "req", None, "head"),
-            P("req", None),
-            P(),
-            P(),
-            P(),
-            P("req", None),
-            P("req", None),
+            P(None, REQ, None, "head"),
+            P(REQ, None),
+            P(),
+            P(),
+            P(),
+            P(REQ, None),
+            P(REQ, None),
         ),
-        out_specs=(P(("req", "head"), None), P("req", "head"), P(None, "req", None, "head")),
+        out_specs=(P((REQ + ("head",)), None), P(REQ, "head"), P(None, REQ, None, "head")),
         check_vma=False,
     )

time: 114 us -> 113 us (level)
  waiting for transfers between devices: 36.5 us -> 33.9 us
  matrix products: 8.65 us -> 10.5 us
    all_to_all x1, starting transfers between devices: 7.51 us -> 4.03 us  [shards(): lax.all_to_all(packed, REQ, split_axis=0, concat_axis=0, tiled=True)]
    all_to_all x3 -> x4, starting transfers between devices: 25 us -> 28.2 us  [gather_rows(): return lax.all_to_all(spread, axis_name, 0, 0, tiled=True)]
    all_to_all x1, waiting for transfers between devices: 13.6 us -> 11.2 us  [shards(): lax.all_to_all(packed, REQ, split_axis=0, concat_axis=0, tiled=True)]
    dot_general x1, matrix products: 0.29 us -> 1.44 us  [shards(): jnp.einsum('td,cdq->ctq', normed, qkv_weight, preferred_element_type=jnp....]
    broadcast_in_dim x4 -> x5, local copies, waits for them, and re-layouts: 3.17 us -> 3.81 us  [gather_rows(): spread = jnp.broadcast_to(rows[None], (parts,) + rows.shape)]
    unnamed x62 -> x58, local copies, waits for them, and re-layouts: 3.51 us -> 2.97 us
    all_to_all x3 -> x4, waiting for transfers between devices: 18.5 us -> 18.3 us  [gather_rows(): return lax.all_to_all(spread, axis_name, 0, 0, tiled=True)]
  transfers between devices with their start and end apart: 5 -> 6, of which waited for: 4 -> 5; matrix products, arithmetic and copies ran while one was open for 11% -> 12% of each run, Pallas kernels for 0% -> 0%
where the time goes in v6:
time: 113 us; the launch traced here: 112 us
  starting transfers between devices  36.4 us (32%)
  waiting for transfers between devices  33.9 us (30%)
  local copies, waits for them, and re-layouts  18.4 us (16%)
  other arithmetic  11.1 us (10%)
  matrix products  10.5 us (9%)
  between operations  1.32 us (1%)
    all_to_all x4, starting transfers between devices, gather_rows(): return lax.all_to_all(spread, axis_name, 0, 0, tiled=True)  28.2 us
    all_to_all x4, waiting for transfers between devices, gather_rows(): return lax.all_to_all(spread, axis_name, 0, 0, tiled=True)  18.3 us
    all_to_all x1, waiting for transfers between devices, shards(): lax.all_to_all(packed, REQ, split_axis=0, concat_axis=0, tiled=True)  11.2 us
    all_to_all x1, waiting for transfers between devices, shards(): lax.all_to_all(down_part.reshape(head_parts, own_rows, -1), 'head', 0, 0,...  4.48 us
    all_to_all x1, starting transfers between devices, shards(): lax.all_to_all(down_part.reshape(head_parts, own_rows, -1), 'head', 0, 0,...  4.14 us
    all_to_all x1, starting transfers between devices, shards(): lax.all_to_all(packed, REQ, split_axis=0, concat_axis=0, tiled=True)  4.03 us
    broadcast_in_dim x5, local copies, waits for them, and re-layouts, gather_rows(): spread = jnp.broadcast_to(rows[None], (parts,) + rows.shape)  3.81 us
    unnamed x58, local copies, waits for them, and re-layouts  2.97 us
  transfers between devices with their start and end apart: 6, of which 5 were waited for; matrix products, arithmetic and copies ran while one was open for 12% of the time, Pallas kernels for 0%

profile of v6, /device:TPU:1, one launch (start us, length us, event | category | flops | bytes accessed | tf_op | source)
XLA Modules:
  0.0 111.6 jit_solution(140408564235122485)
XLA Ops:
  0.6 1.5 %broadcast_in_dim.291 = bf16[8,8,1024]{2,1,0:T(8,128)(2,1)} broadcast(bf16[8,1024]{1,0:T(8,128)(2,1)} %param.14), dimensions={1,2} | broadcast | bytes 147456 | tf_op jit(solution)/shard_map/broadcast_in_dim | solution.py:50
  2.2 6.5 %all-to-all-start = ((bf16[8,8,1024]{2,1,0:T(8,128)(2,1)}), bf16[8,8,1024]{2,1,0:T(8,128)(2,1)S(1)}, u32[]{:S(2)}, u32[]{:S(2)}) async-start(bf16[8,8,1024]{2,1,0:T(8,128)(2,1)} %broadcast_in_dim.291), calls=%async_computation | async-start | bytes 262144 | tf_op jit(solution)/shard_map/all_to_all | solution.py:51
  8.6 2.3 %fusion.23 = (s32[20]{0:T(128)S(1)}, s32[20]{0:T(128)S(1)}, s32[20]{0:T(128)S(1)}, s32[20]{0:T(128)S(1)}) fusion(s32[32,32]{1,0:T(8,128)} %param.25, s32[20]{0:T(128)S(1)} %iota_add_fusion, s32[32]{0:T(128)} %param.24), kind=kLoop, calls=%fused_computation.56 | loop fusion | flops 184240 | bytes 4624 | tf_op jit(solution)/shard_map/reduce_sum | solution.py:99
  11.1 0.7 fusion.55
  11.8 1.4 %fusion.78 = (f32[1,1024]{1,0:T(1,128)}, f32[1,1024]{1,0:T(1,128)S(1)}) fusion(f32[2,1024]{1,0:T(2,128)} %param.15), kind=kLoop, calls=%fused_computation.155 | loop fusion | bytes 16384 | tf_op jit(solution)/shard_map/slice | solution.py:213
  13.2 0.8 reshape.568
  13.9 0.8 constant_dynamic-slice_fusion
  14.7 0.6 gather_fusion.1
  15.3 0.9 broadcast_compare_fusion
  16.5 1.4 %fusion.10 = bf16[3,64,128]{2,1,0:T(8,128)(2,1)S(1)} fusion(bf16[3,1024,128]{2,1,0:T(8,128)(2,1)} %param.16, bf16[8,8,1024]{2,1,0:T(8,128)(2,1)S(1)} %all-to-all-done, f32[1024]{0:T(1024)S(1)} %bitcast.197, f32[64]{0:T(128)S(1)} %rsqrt.20), kind=kOutput, calls=%fused_computation.26 | convolution fusion | flops 50618368 | bytes 971008 | tf_op jit(solution)/shard_map/td,cdq->ctq/dot_general | solution.py:84
  18.0 0.6 fusion.77
  18.6 0.7 broadcast_in_dim.299
  19.3 7.5 %all-to-all-start.1 = ((bf16[8,64,128]{2,1,0:T(8,128)(2,1)}), bf16[8,64,128]{2,1,0:T(8,128)(2,1)S(1)}, u32[]{:S(2)}, u32[]{:S(2)}) async-start(bf16[8,64,128]{2,1,0:T(8,128)(2,1)} %broadcast_in_dim.299), calls=%async_computation.1 | async-start | bytes 262144 | tf_op jit(solution)/shard_map/all_to_all | solution.py:51
  26.9 0.6 broadcast_in_dim.311
  27.5 0.7 broadcast_in_dim.315
  28.9 6.4 %all-to-all-done.1 = bf16[8,64,128]{2,1,0:T(8,128)(2,1)S(1)} async-done(((bf16[8,64,128]{2,1,0:T(8,128)(2,1)}), bf16[8,64,128]{2,1,0:T(8,128)(2,1)S(1)}, u32[]{:S(2)}, u32[]{:S(2)}) %all-to-all-start.1) | async-done | bytes 131104 | tf_op jit(solution)/shard_map/all_to_all | solution.py:51
  35.3 0.9 broadcast_in_dim.300
  36.2 4.2 %all-to-all-start.2 = ((bf16[4,8,64,128]{3,2,1,0:T(8,128)(2,1)}), bf16[4,8,64,128]{3,2,1,0:T(8,128)(2,1)S(1)}, u32[]{:S(2)}, u32[]{:S(2)}) async-start(bf16[4,8,64,128]{3,2,1,0:T(8,128)(2,1)} %broadcast_in_dim.300), calls=%async_computation.2 | async-start | bytes 1048576 | tf_op jit(solution)/shard_map/all_to_all | solution.py:51
  40.4 0.8 convolution_minimum_fusion.3
  41.1 6.7 %all-to-all-done.2 = bf16[4,8,64,128]{3,2,1,0:T(8,128)(2,1)S(1)} async-done(((bf16[4,8,64,128]{3,2,1,0:T(8,128)(2,1)}), bf16[4,8,64,128]{3,2,1,0:T(8,128)(2,1)S(1)}, u32[]{:S(2)}, u32[]{:S(2)}) %all-to-all-start.2) | async-done | bytes 524320 | tf_op jit(solution)/shard_map/all_to_all | solution.py:51
  47.8 0.6 gather_fusion
  48.6 1.1 %copy-done.2 = bf16[2,20,128,128]{3,2,1,0:T(8,128)(2,1)S(1)} copy-done((bf16[2,20,128,128]{3,2,1,0:T(8,128)(2,1)S(1)}, bf16[2,20,128,128]{3,2,1,0:T(8,128)(2,1)}, u32[]{:S(2)}) %copy-start.2) | copy-done | bytes 1310744
  49.7 1.3 %select_reduce_fusion.2 = (f32[20,128]{1,0:T(8,128)S(1)}, f32[20,128,128]{1,2,0:T(8,128)S(1)}) fusion(pred[20,128]{1,0:T(8,128)(4,1)S(1)} %iota_compare_fusion, pred[20,128,128]{1,2,0:T(32,128)(4,1)S(1)} %copy.57, f32[128]{0:T(128)} %broadcast_in_dim.315, f32[128]{0:T(128)} %broadcast_in_dim.311, bf16[20,128,128]{2,1,0:T(8,128)(2,1)S(1)} %bitcast_select_fusion, ...), kind=kOutput, calls=%fused_computation.10 | convolution fusion | flops 85521920 | bytes 2963456 | tf_op jit(solution)/shard_map/prd,pkd->prk/dot_general | solution.py:115
  51.1 1.2 %convert_reduce_fusion = f32[20,128]{1,0:T(8,128)} fusion(f32[20,128,128]{1,2,0:T(8,128)S(1)} %get-tuple-element.36, f32[20,128]{1,0:T(8,128)S(1)} %get-tuple-element.35, pred[20,128]{1,0:T(8,128)(4,1)S(1)} %iota_compare_fusion), kind=kLoop, calls=%fused_computation.7 | loop fusion | flops 1635840 | bytes 1333760 | tf_op jit(solution)/shard_map/reduce_sum | solution.py:128
  52.3 1.6 %fusion.14 = f32[20,128,128]{2,1,0:T(8,128)S(1)} fusion(bf16[2,20,128,128]{3,2,1,0:T(8,128)(2,1)S(1)} %copy-done.2, f32[20,128,128]{1,2,0:T(8,128)S(1)} %get-tuple-element.36, f32[20,128]{1,0:T(8,128)S(1)} %get-tuple-element.35, pred[20,128]{1,0:T(8,128)(4,1)S(1)} %iota_compare_fusion), kind=kOutput, calls=%fused_computation.37 | convolution fusion | flops 84869120 | bytes 3292160 | tf_op jit(solution)/shard_map/prk,pkc->prc/dot_general | solution.py:129
  53.9 0.7 reduce_max.43
  54.6 0.9 select_reduce_fusion.3
  55.4 1.3 %gather_fusion.2 = f32[20,128]{1,0:T(8,128)} fusion(f32[32,128]{1,0:T(8,128)S(1)} %select_reduce_fusion.3, s32[1024]{0:T(1024)} %copy-done.12), kind=kCustom, calls=%fused_computation.2 | custom fusion | bytes 20560 | tf_op jit(solution)/shard_map/jit(_take)/gather | solution.py:136
  56.7 1.4 %gather.17 = f32[20,2,64]{2,1,0:T(2,128)} reshape(f32[20,128]{1,0:T(8,128)} %gather_fusion.2) | data formatting | bytes 20480 | tf_op jit(solution)/shard_map/jit(_take)/gather | solution.py:136
  58.1 1.0 convolution_bitcast_fusion.2
  59.2 0.9 exponential_select_fusion
  60.1 1.1 select_reduce_fusion.1
  61.8 0.7 fusion.1
  62.7 0.9 pad_maximum_fusion
  63.6 4.0 %all-to-all-start.3 = ((bf16[32,70,128]{2,1,0:T(8,128)(2,1)}), bf16[32,70,128]{2,1,0:T(8,128)(2,1)S(1)}, u32[]{:S(2)}, u32[]{:S(2)}) async-start(bf16[32,70,128]{2,1,0:T(8,128)(2,1)} %pad_maximum_fusion), calls=%async_computation.3 | async-start | bytes 1179648 | tf_op jit(solution)/shard_map/all_to_all | solution.py:154
  67.8 0.8 dynamic_slice.10
  69.7 11.2 %all-to-all-done.3 = bf16[32,70,128]{2,1,0:T(8,128)(2,1)S(1)} async-done(((bf16[32,70,128]{2,1,0:T(8,128)(2,1)}), bf16[32,70,128]{2,1,0:T(8,128)(2,1)S(1)}, u32[]{:S(2)}, u32[]{:S(2)}) %all-to-all-start.3) | async-done | bytes 573472 | tf_op jit(solution)/shard_map/all_to_all | solution.py:154
  81.4 0.6 select_reduce_fusion
  82.5 0.7 broadcast_in_dim.341
  83.2 10.1 %all-to-all-start.4 = ((bf16[8,64,128]{2,1,0:T(8,128)(2,1)}), bf16[8,64,128]{2,1,0:T(8,128)(2,1)S(1)}, u32[]{:S(2)}, u32[]{:S(2)}) async-start(bf16[8,64,128]{2,1,0:T(8,128)(2,1)} %broadcast_in_dim.341), calls=%async_computation.4 | async-start | bytes 262144 | tf_op jit(solution)/shard_map/all_to_all | solution.py:51
  93.2 5.2 %all-to-all-done.4 = bf16[8,64,128]{2,1,0:T(8,128)(2,1)S(1)} async-done(((bf16[8,64,128]{2,1,0:T(8,128)(2,1)}), bf16[8,64,128]{2,1,0:T(8,128)(2,1)S(1)}, u32[]{:S(2)}, u32[]{:S(2)}) %all-to-all-start.4) | async-done | bytes 131104 | tf_op jit(solution)/shard_map/all_to_all | solution.py:51
  98.5 0.6 fusion.24
  99.1 1.0 copy-done.1
  100.6 0.9 fusion.3
  101.6 4.1 %all-to-all-start.5 = ((bf16[8,8,1024]{2,1,0:T(8,128)(2,1)}), bf16[8,8,1024]{2,1,0:T(8,128)(2,1)S(1)}, u32[]{:S(2)}, u32[]{:S(2)}) async-start(bf16[8,8,1024]{2,1,0:T(8,128)(2,1)} %fusion.3), calls=%async_computation.5 | async-start | bytes 262144 | tf_op jit(solution)/shard_map/all_to_all | solution.py:225
  105.7 0.8 fusion.12
  106.5 4.5 %all-to-all-done.5 = bf16[8,8,1024]{2,1,0:T(8,128)(2,1)S(1)} async-done(((bf16[8,8,1024]{2,1,0:T(8,128)(2,1)}), bf16[8,8,1024]{2,1,0:T(8,128)(2,1)S(1)}, u32[]{:S(2)}, u32[]{:S(2)}) %all-to-all-start.5) | async-done | bytes 131104 | tf_op jit(solution)/shard_map/all_to_all | solution.py:225
  111.0 0.6 add_convert_fusion
  (109 shorter events, 5.0 us)
Async XLA Ops:
  0.6 97.8 %copy-start = (bf16[1024,1024]{1,0:T(8,128)(2,1)S(1)}, bf16[1024,1024]{1,0:T(8,128)(2,1)}, u32[]{:S(2)}) copy-start(bf16[1024,1024]{1,0:T(8,128)(2,1)} %param.17) | copy-start | bytes 6291460
  2.2 14.2 %all-to-all-start = ((bf16[8,8,1024]{2,1,0:T(8,128)(2,1)}), bf16[8,8,1024]{2,1,0:T(8,128)(2,1)S(1)}, u32[]{:S(2)}, u32[]{:S(2)}) async-start(bf16[8,8,1024]{2,1,0:T(8,128)(2,1)} %broadcast_in_dim.291), calls=%async_computation | async-start | bytes 262144 | tf_op jit(solution)/shard_map/all_to_all | solution.py:51
  11.0 5.3 %copy-start.17 = (s32[20]{0:T(128)}, s32[20]{0:T(128)S(1)}, u32[]{:S(2)}) copy-start(s32[20]{0:T(128)S(1)} %get-tuple-element.20) | copy-start | bytes 244
  11.0 37.4 %copy-start.19 = (pred[20]{0:T(512)(128)(4,1)}, pred[20]{0:T(512)(128)(4,1)S(1)}, u32[]{:S(2)}) copy-start(pred[20]{0:T(512)(128)(4,1)S(1)} %compare_and_fusion) | copy-start | bytes 64
  11.0 0.8 copy-start.15
  11.8 36.0 %copy-start.12 = (s32[1024]{0:T(1024)}, s32[1024]{0:T(1024)S(1)}, u32[]{:S(2)}) copy-start(s32[1024]{0:T(1024)S(1)} %pad_clamp_fusion) | copy-start | bytes 12292
  16.3 12.4 %copy-start.21 = (f32[2]{0:T(128)}, f32[2]{0:T(128)S(1)}, u32[]{:S(2)}) copy-start(f32[2]{0:T(128)S(1)} %get-tuple-element.33) | copy-start | bytes 28
  16.3 12.4 %copy-start.23 = (f32[2]{0:T(128)}, f32[2]{0:T(128)S(1)}, u32[]{:S(2)}) copy-start(f32[2]{0:T(128)S(1)} %get-tuple-element.34) | copy-start | bytes 28
  16.5 12.2 %copy-start.20 = (s32[1,64]{1,0:T(1,128)S(1)}, s32[1,64]{1,0:T(1,128)}, u32[]{:S(2)}) copy-start(s32[1,64]{1,0:T(1,128)} %param.26) | copy-start | bytes 772
  18.0 9.5 %copy-start.5 = (bf16[3,64,128]{2,1,0:T(8,128)(2,1)}, bf16[3,64,128]{2,1,0:T(8,128)(2,1)S(1)}, u32[]{:S(2)}) copy-start(bf16[3,64,128]{2,1,0:T(8,128)(2,1)S(1)} %fusion.10) | copy-start | bytes 147460
  19.3 16.0 %all-to-all-start.1 = ((bf16[8,64,128]{2,1,0:T(8,128)(2,1)}), bf16[8,64,128]{2,1,0:T(8,128)(2,1)S(1)}, u32[]{:S(2)}, u32[]{:S(2)}) async-start(bf16[8,64,128]{2,1,0:T(8,128)(2,1)} %broadcast_in_dim.299), calls=%async_computation.1 | async-start | bytes 262144 | tf_op jit(solution)/shard_map/all_to_all | solution.py:51
  36.2 11.6 %all-to-all-start.2 = ((bf16[4,8,64,128]{3,2,1,0:T(8,128)(2,1)}), bf16[4,8,64,128]{3,2,1,0:T(8,128)(2,1)S(1)}, u32[]{:S(2)}, u32[]{:S(2)}) async-start(bf16[4,8,64,128]{3,2,1,0:T(8,128)(2,1)} %broadcast_in_dim.300), calls=%async_computation.2 | async-start | bytes 1048576 | tf_op jit(solution)/shard_map/all_to_all | solution.py:51
  40.4 8.2 %copy-start.13 = (pred[2,128]{1,0:T(4,128)(4,1)}, pred[2,128]{1,0:T(4,128)(4,1)S(1)}, u32[]{:S(2)}) copy-start(pred[2,128]{1,0:T(4,128)(4,1)S(1)} %iota_compare_fusion.3) | copy-start | bytes 772
  48.4 1.3 %copy-start.2 = (bf16[2,20,128,128]{3,2,1,0:T(8,128)(2,1)S(1)}, bf16[2,20,128,128]{3,2,1,0:T(8,128)(2,1)}, u32[]{:S(2)}) copy-start(bf16[2,20,128,128]{3,2,1,0:T(8,128)(2,1)} %param.21) | copy-start | bytes 3932164
  51.1 2.8 %copy-start.4 = (f32[20,128]{1,0:T(8,128)}, f32[20,128]{1,0:T(8,128)S(1)}, u32[]{:S(2)}) copy-start(f32[20,128]{1,0:T(8,128)S(1)} %get-tuple-element.35) | copy-start | bytes 30724
  61.2 0.6 copy-start.16
  61.2 0.7 copy-start.18
  62.7 5.0 %copy-start.3 = (f32[64,64]{1,0:T(8,128)S(1)}, f32[64,64]{1,0:T(8,128)}, u32[]{:S(2)}) copy-start(f32[64,64]{1,0:T(8,128)} %convolution_minimum_fusion.3) | copy-start | bytes 49156
  62.7 6.5 %copy-start.9 = (bf16[1,64,128]{2,1,0:T(8,128)(2,1)S(1)}, bf16[1,64,128]{2,1,0:T(8,128)(2,1)}, u32[]{:S(2)}) copy-start(bf16[1,64,128]{2,1,0:T(8,128)(2,1)} %get-tuple-element.21) | copy-start | bytes 49156
  62.7 6.5 %copy-start.8 = (bf16[1,64,128]{2,1,0:T(8,128)(2,1)S(1)}, bf16[1,64,128]{2,1,0:T(8,128)(2,1)}, u32[]{:S(2)}) copy-start(bf16[1,64,128]{2,1,0:T(8,128)(2,1)} %get-tuple-element.23) | copy-start | bytes 49156
  62.7 6.7 %copy-start.7 = (bf16[1,64,128]{2,1,0:T(8,128)(2,1)S(1)}, bf16[1,64,128]{2,1,0:T(8,128)(2,1)}, u32[]{:S(2)}) copy-start(bf16[1,64,128]{2,1,0:T(8,128)(2,1)} %get-tuple-element.24) | copy-start | bytes 49156
  62.7 6.7 %copy-start.22 = (f32[2]{0:T(128)S(1)}, f32[2]{0:T(128)}, u32[]{:S(2)}) copy-start(f32[2]{0:T(128)} %copy-done.21) | copy-start | bytes 28
  62.7 6.7 %copy-start.24 = (f32[2]{0:T(128)S(1)}, f32[2]{0:T(128)}, u32[]{:S(2)}) copy-start(f32[2]{0:T(128)} %copy-done.23) | copy-start | bytes 28
  63.6 17.7 %copy-start.14 = (pred[2,128]{1,0:T(4,128)(4,1)S(1)}, pred[2,128]{1,0:T(4,128)(4,1)}, u32[]{:S(2)}) copy-start(pred[2,128]{1,0:T(4,128)(4,1)} %copy-done.13) | copy-start | bytes 772
  63.6 17.2 %all-to-all-start.3 = ((bf16[32,70,128]{2,1,0:T(8,128)(2,1)}), bf16[32,70,128]{2,1,0:T(8,128)(2,1)S(1)}, u32[]{:S(2)}, u32[]{:S(2)}) async-start(bf16[32,70,128]{2,1,0:T(8,128)(2,1)} %pad_maximum_fusion), calls=%async_computation.3 | async-start | bytes 1179648 | tf_op jit(solution)/shard_map/all_to_all | solution.py:154
  82.5 16.6 %copy-start.10 = (bf16[64,128]{1,0:T(8,128)(2,1)}, bf16[64,128]{1,0:T(8,128)(2,1)S(1)}, u32[]{:S(2)}) copy-start(bf16[64,128]{1,0:T(8,128)(2,1)S(1)} %copy.68) | copy-start | bytes 49156
  83.2 15.3 %all-to-all-start.4 = ((bf16[8,64,128]{2,1,0:T(8,128)(2,1)}), bf16[8,64,128]{2,1,0:T(8,128)(2,1)S(1)}, u32[]{:S(2)}, u32[]{:S(2)}) async-start(bf16[8,64,128]{2,1,0:T(8,128)(2,1)} %broadcast_in_dim.341), calls=%async_computation.4 | async-start | bytes 262144 | tf_op jit(solution)/shard_map/all_to_all | solution.py:51
  93.2 5.9 %copy-start.11 = (f32[1,1024]{1,0:T(1,128)S(1)}, f32[1,1024]{1,0:T(1,128)}, u32[]{:S(2)}) copy-start(f32[1,1024]{1,0:T(1,128)} %get-tuple-element.28) | copy-start | bytes 12292
  98.5 1.6 %copy-start.1 = (bf16[2,1024,512]{2,1,0:T(8,128)(2,1)S(1)}, bf16[2,1024,512]{2,1,0:T(8,128)(2,1)}, u32[]{:S(2)}) copy-start(bf16[2,1024,512]{2,1,0:T(8,128)(2,1)} %param.18) | copy-start | bytes 6291460
  99.1 1.5 %copy-start.25 = (bf16[512,1024]{1,0:T(8,128)(2,1)S(1)}, bf16[512,1024]{1,0:T(8,128)(2,1)}, u32[]{:S(2)}) copy-start(bf16[512,1024]{1,0:T(8,128)(2,1)} %param.19) | copy-start | bytes 3145732
  100.6 5.1 %copy-start.6 = (bf16[3,64,128]{2,1,0:T(8,128)(2,1)S(1)}, bf16[3,64,128]{2,1,0:T(8,128)(2,1)}, u32[]{:S(2)}) copy-start(bf16[3,64,128]{2,1,0:T(8,128)(2,1)} %copy-done.5) | copy-start | bytes 147460
  100.6 5.1 %copy-start.26 = (s32[1,8]{1,0:T(1,128)S(1)}, s32[1,8]{1,0:T(1,128)}, u32[]{:S(2)}) copy-start(s32[1,8]{1,0:T(1,128)} %param.27) | copy-start | bytes 100
  101.6 9.4 %all-to-all-start.5 = ((bf16[8,8,1024]{2,1,0:T(8,128)(2,1)}), bf16[8,8,1024]{2,1,0:T(8,128)(2,1)S(1)}, u32[]{:S(2)}, u32[]{:S(2)}) async-start(bf16[8,8,1024]{2,1,0:T(8,128)(2,1)} %fusion.3), calls=%async_computation.5 | async-start | bytes 262144 | tf_op jit(solution)/shard_map/all_to_all | solution.py:225

commit v7 on v5

--- a/solution.py
+++ b/solution.py
@@ -1,8 +1,11 @@
+import functools
 import math
 
 import jax
 import jax.numpy as jnp
 from jax import lax
+from jax.experimental import pallas as pl
+from jax.experimental.pallas import tpu as pltpu
 from jax.sharding import PartitionSpec as P
 
 HD = 64
@@ -30,6 +33,86 @@
         total_one * factor_one + total_two * factor_two,
         out_one * factor_one[..., None] + out_two * factor_two[..., None],
     )
+
+
+def page_kernel(owner_ref, filled_ref, q_ref, qv_ref, k_ref, v_ref, pv_ref, bias_ref,
+                out_ref, max_ref, total_ref, *, head_local, scale):
+    step = pl.program_id(0)
+
+    @pl.when(step == 0)
+    def _():
+        out_ref[...] = jnp.zeros(out_ref.shape, jnp.float32)
+        max_ref[...] = jnp.full(max_ref.shape, masked_score, jnp.float32)
+        total_ref[...] = jnp.zeros(total_ref.shape, jnp.float32)
+
+    count = filled_ref[step]
+
+    @pl.when(count > 0)
+    def _():
+        row = owner_ref[step]
+        query = q_ref[row]
+        same = qv_ref[row] == pv_ref[...]
+        keys = k_ref[...]
+        values = v_ref[...]
+        valid = lax.broadcasted_iota(jnp.int32, same.shape, 1) < count
+        for head in range(head_local):
+            cols = slice(head * HD, (head + 1) * HD)
+            scores = lax.dot_general(
+                query[:, cols], keys[:, cols], (((1,), (1,)), ((), ())),
+                preferred_element_type=jnp.float32,
+            ) * scale
+            scores = scores + jnp.where(same, bias_ref[0, head], bias_ref[1, head])
+            block_max = jnp.max(jnp.where(valid, scores, masked_score), axis=1, keepdims=True)
+            weights = jnp.where(valid, jnp.exp(scores - block_max), 0.0).astype(jnp.bfloat16)
+            block_total = jnp.sum(weights.astype(jnp.float32), axis=1, keepdims=True)
+            block_out = jnp.dot(weights, values[:, cols], preferred_element_type=jnp.float32)
+            old_max = max_ref[row, :, head : head + 1]
+            new_max = jnp.maximum(old_max, block_max)
+            keep_old = jnp.exp(old_max - new_max)
+            keep_new = jnp.exp(block_max - new_max)
+            max_ref[row, :, head : head + 1] = new_max
+            total_ref[row, :, head : head + 1] = (
+                total_ref[row, :, head : head + 1] * keep_old + block_total * keep_new
+            )
+            out_ref[row, :, cols] = out_ref[row, :, cols] * keep_old + block_out * keep_new
+
+
+def page_attention(owner, filled, queries, query_variates, page_cache, page_variates, bias,
+                   interpret=False):
+    requests, tree, qdl = queries.shape
+    pool, page = page_variates.shape
+    head_local = qdl // HD
+    kernel = functools.partial(page_kernel, head_local=head_local, scale=1.0 / math.sqrt(HD))
+    whole3 = lambda shape: pl.BlockSpec(shape, lambda step, *_: (0, 0, 0))
+    grid_spec = pltpu.PrefetchScalarGridSpec(
+        num_scalar_prefetch=2,
+        grid=(pool,),
+        in_specs=[
+            whole3((requests, tree, qdl)),
+            whole3((requests, tree, 1)),
+            pl.BlockSpec((None, None, page, qdl), lambda step, *_: (0, step, 0, 0)),
+            pl.BlockSpec((None, None, page, qdl), lambda step, *_: (1, step, 0, 0)),
+            pl.BlockSpec((None, 1, page), lambda step, *_: (step, 0, 0)),
+            pl.BlockSpec(memory_space=pltpu.SMEM),
+        ],
+        out_specs=[
+            whole3((requests, tree, qdl)),
+            whole3((requests, tree, head_local)),
+            whole3((requests, tree, head_local)),
+        ],
+    )
+    return pl.pallas_call(
+        kernel,
+        grid_spec=grid_spec,
+        out_shape=[
+            jax.ShapeDtypeStruct((requests, tree, qdl), jnp.float32),
+            jax.ShapeDtypeStruct((requests, tree, head_local), jnp.float32),
+            jax.ShapeDtypeStruct((requests, tree, head_local), jnp.float32),
+        ],
+        compiler_params=pltpu.CompilerParams(dimension_semantics=("arbitrary",)),
+        interpret=interpret,
+    )(owner, filled, queries, query_variates[..., None], page_cache,
+      page_cache, page_variates[:, None, :], bias)
 
 
 def split_three(values):
@@ -101,47 +184,17 @@
     valid = jnp.arange(page, dtype=jnp.int32)[None, :] < filled[:, None]
     head_of_column = jnp.arange(qdl, dtype=jnp.int32) // HD
     head_mask = jnp.arange(head_local, dtype=jnp.int32)[:, None] == head_of_column[None, :]
-    split_rows = head_local * tree
-    page_queries = jnp.take(all_queries.reshape(requests, tree, qdl), owner, axis=0)
-    split_queries = jnp.where(
-        head_mask[None, :, None, :], page_queries[:, None], jnp.zeros((), page_queries.dtype)
-    ).reshape(pool, split_rows, qdl)
-    query_variates = jnp.take(token_variates.reshape(requests, tree), owner, axis=0)
-    scores = (
-        jnp.einsum(
-            "prd,pkd->prk", split_queries, page_cache[0], preferred_element_type=jnp.float32
-        )
-        * scale
-    )
-    same_page = query_variates[:, :, None] == page_variates[:, None, :]
-    page_bias = jnp.where(
-        same_page[:, None], same_bias[None, :, None, None], other_bias[None, :, None, None]
-    ).reshape(pool, split_rows, page)
-    scores = scores + page_bias
-    keep = valid[:, None, :]
-    page_max = jnp.max(jnp.where(keep, scores, masked_score), axis=-1)
-    weights = jnp.where(keep, jnp.exp(scores - page_max[..., None]), 0.0).astype(jnp.bfloat16)
-    page_total = jnp.sum(weights, axis=-1, dtype=jnp.float32)
-    crossed_out = jnp.einsum(
-        "prk,pkc->prc", weights, page_cache[1], preferred_element_type=jnp.float32
-    ).reshape(pool, head_local, tree, qdl)
-    member = (owner[None, :] == jnp.arange(requests, dtype=jnp.int32)[:, None]) & (
-        in_use[None, :] > 0
-    )
-    request_max = jnp.max(jnp.where(member[:, :, None], page_max[None], masked_score), axis=1)
-    owner_max = jnp.take(request_max, owner, axis=0)
-    factor = jnp.where(in_use[:, None] > 0, jnp.exp(page_max - owner_max), 0.0)
-    member_float = member.astype(jnp.float32)
-    request_total = jnp.dot(member_float, page_total * factor, precision=highest)
-    scaled_out = jnp.sum(
-        jnp.where(
-            head_mask[None, :, None, :],
-            crossed_out * factor.reshape(pool, head_local, tree)[..., None],
-            0.0,
-        ),
-        axis=1,
-    )
-    request_out = jnp.dot(member_float, scaled_out.reshape(pool, -1), precision=highest)
+    request_out, acc_max, acc_total = page_attention(
+        jnp.clip(owner, 0, requests - 1),
+        filled,
+        all_queries.reshape(requests, tree, qdl),
+        token_variates.reshape(requests, tree),
+        page_cache,
+        page_variates,
+        bias_local,
+    )
+    request_max = acc_max.transpose(0, 2, 1).reshape(requests, head_local * tree)
+    request_total = acc_total.transpose(0, 2, 1).reshape(requests, head_local * tree)
     stats = jnp.stack([request_total, request_max], axis=1)
     packed = jnp.concatenate(
         [request_out.astype(jnp.bfloat16).reshape(requests, tree, qdl)] + split_three(stats),

time: 114 us -> 120 us (1.053)
  Pallas kernels: 0 us -> 15.3 us
  other arithmetic: 11.2 us -> 5.82 us
  matrix products: 8.65 us -> 5.2 us
  starting transfers between devices: 36.7 us -> 40 us
  local copies, waits for them, and re-layouts: 17.9 us -> 15.5 us
    pallas_call x0 -> x1, Pallas kernels: none -> 15.3 us  [page_attention(): pl.pallas_call(kernel, grid_spec=grid_spec, out_shape=[jax.ShapeDtypeStru...]
    dot_general x4 -> x0, matrix products: 3.99 us -> none  [the longest x1 1.61 us: shards(): jnp.einsum('prk,pkc->prc', weights, page_cache[1], preferred_element_type...]
    gather x4 -> x0, local copies, waits for them, and re-layouts: 3.83 us -> none  [the longest x2 2.66 us: shards(): owner_max = jnp.take(request_max, owner, axis=0)]
    transpose x0 -> x2, local copies, waits for them, and re-layouts: none -> 3.31 us  [the longest x1 1.69 us: shards(): acc_total.transpose(0, 2, 1).reshape(requests, head_local * tree)]
    another operation x3 -> x6, local copies, waits for them, and re-layouts: 0.28 us -> 3.08 us  [the longest x1 2.6 us: page_attention(): query_variates[..., None]]
    reduce_sum x2 -> x0, other arithmetic: 2.31 us -> none  [the longest x1 1.17 us: shards(): page_total = jnp.sum(weights, axis=-1, dtype=jnp.float32)]
    all_to_all x1, starting transfers between devices: 7.51 us -> 9.66 us  [shards(): lax.all_to_all(packed, 'req', split_axis=0, concat_axis=0, tiled=True)]
    unnamed x62 -> x23, local copies, waits for them, and re-layouts: 3.51 us -> 1.82 us
  transfers between devices with their start and end apart: 5 -> 5, of which waited for: 4 -> 4; matrix products, arithmetic and copies ran while one was open for 11% -> 9% of each run, Pallas kernels for 0% -> 0%
where the time goes in v7:
time: 120 us; the launch traced here: 119 us
  starting transfers between devices  40 us (33%)
  waiting for transfers between devices  35.8 us (30%)
  local copies, waits for them, and re-layouts  15.5 us (13%)
  Pallas kernels  15.3 us (13%)
  other arithmetic  5.82 us (5%)
  matrix products  5.2 us (4%)
    all_to_all x3, starting transfers between devices, gather_rows(): return lax.all_to_all(spread, axis_name, 0, 0, tiled=True)  26.1 us
    all_to_all x3, waiting for transfers between devices, gather_rows(): return lax.all_to_all(spread, axis_name, 0, 0, tiled=True)  16.9 us
    pallas_call x1, Pallas kernels, page_attention(): pl.pallas_call(kernel, grid_spec=grid_spec, out_shape=[jax.ShapeDtypeStru...  15.3 us
    all_to_all x1, waiting for transfers between devices, shards(): lax.all_to_all(packed, 'req', split_axis=0, concat_axis=0, tiled=True)  14.5 us
    all_to_all x1, starting transfers between devices, shards(): lax.all_to_all(packed, 'req', split_axis=0, concat_axis=0, tiled=True)  9.66 us
    all_to_all x1, waiting for transfers between devices, shards(): lax.all_to_all(down_part.reshape(head_parts, own_rows, -1), 'head', 0, 0,...  4.48 us
    all_to_all x1, starting transfers between devices, shards(): lax.all_to_all(down_part.reshape(head_parts, own_rows, -1), 'head', 0, 0,...  4.14 us
    broadcast_in_dim x4, local copies, waits for them, and re-layouts, gather_rows(): spread = jnp.broadcast_to(rows[None], (parts,) + rows.shape)  3.2 us
  transfers between devices with their start and end apart: 5, of which 4 were waited for; matrix products, arithmetic and copies ran while one was open for 9% of the time, Pallas kernels for 0%

profile of v7, /device:TPU:1, one launch (start us, length us, event | category | flops | bytes accessed | tf_op | source)
XLA Modules:
  0.0 118.5 jit_solution(10191562880468538093)
XLA Ops:
  0.6 1.5 %broadcast_in_dim.112 = bf16[8,8,1024]{2,1,0:T(8,128)(2,1)} broadcast(bf16[8,1024]{1,0:T(8,128)(2,1)} %param.14), dimensions={1,2} | broadcast | bytes 147456 | tf_op jit(solution)/shard_map/broadcast_in_dim | solution.py:131
  2.2 6.5 %all-to-all-start = ((bf16[8,8,1024]{2,1,0:T(8,128)(2,1)}), bf16[8,8,1024]{2,1,0:T(8,128)(2,1)S(1)}, u32[]{:S(2)}, u32[]{:S(2)}) async-start(bf16[8,8,1024]{2,1,0:T(8,128)(2,1)} %broadcast_in_dim.112), calls=%async_computation | async-start | bytes 262144 | tf_op jit(solution)/shard_map/all_to_all | solution.py:132
  8.6 2.6 %broadcast_in_dim_reshape.3.qv_ref = s32[32,64,1]{2,1,0:T(8,128)} reshape(s32[2048]{0:T(1024)} %param.23) | data formatting | bytes 16384 | tf_op jit(solution)/shard_map/broadcast_in_dim;reshape | solution.py:114
  11.2 1.3 %broadcast_in_dim.115.pv_ref = s32[20,1,128]{2,1,0:T(1,128)} reshape(s32[20,128]{1,0:T(8,128)} %param.22) | data formatting | bytes 20480 | tf_op jit(solution)/shard_map/broadcast_in_dim | solution.py:115
  12.6 0.8 dynamic_slice.10
  13.3 0.8 fusion.38
  14.1 0.2 convolution_minimum_fusion.3
  14.3 0.2 convolution_minimum_fusion.2
  14.5 0.8 fusion.55
  15.2 0.1 fusion.22
  15.4 1.4 %fusion.8 = bf16[3,64,128]{2,1,0:T(8,128)(2,1)S(1)} fusion(bf16[3,1024,128]{2,1,0:T(8,128)(2,1)} %param.16, bf16[8,8,1024]{2,1,0:T(8,128)(2,1)S(1)} %all-to-all-done, f32[1024]{0:T(1024)S(1)} %bitcast.168, f32[64]{0:T(128)S(1)} %rsqrt.20), kind=kOutput, calls=%fused_computation.15 | convolution fusion | flops 50618368 | bytes 971008 | tf_op jit(solution)/shard_map/td,cdq->ctq/dot_general | solution.py:165
  16.9 0.9 broadcast_in_dim.114
  17.8 10.5 %all-to-all-start.1 = ((bf16[32,64,128]{2,1,0:T(8,128)(2,1)}), bf16[32,64,128]{2,1,0:T(8,128)(2,1)S(1)}, u32[]{:S(2)}, u32[]{:S(2)}) async-start(bf16[32,64,128]{2,1,0:T(8,128)(2,1)} %broadcast_in_dim.114), calls=%async_computation.1 | async-start | bytes 1048576 | tf_op jit(solution)/shard_map/all_to_all | solution.py:132
  28.4 0.2 convolution_minimum_fusion.1
  28.5 0.2 fusion.9
  28.7 0.1 copy.74
  28.8 0.6 constant_dynamic-slice_fusion.bias_ref
  29.5 1.6 %fusion.15 = (s32[20]{0:T(128)S(1)}, s32[20]{0:T(128)S(1)}, s32[20]{0:T(128)S(1)}, s32[20]{0:T(128)S(1)}) fusion(s32[32,32]{1,0:T(8,128)S(1)} %copy-done.5, s32[20]{0:T(128)S(1)} %iota_add_fusion, s32[32]{0:T(128)S(1)} %copy-done.8), kind=kLoop, calls=%fused_computation.37 | loop fusion | flops 184240 | bytes 4624 | tf_op jit(solution)/shard_map/reduce_sum | solution.py:178
  31.1 0.5 clamp_multiply_fusion
  31.6 11.6 %all-to-all-done.1.q_ref = bf16[32,64,128]{2,1,0:T(8,128)(2,1)S(1)} async-done(((bf16[32,64,128]{2,1,0:T(8,128)(2,1)}), bf16[32,64,128]{2,1,0:T(8,128)(2,1)S(1)}, u32[]{:S(2)}, u32[]{:S(2)}) %all-to-all-start.1) | async-done | bytes 524320 | tf_op jit(solution)/shard_map/all_to_all | solution.py:132
  43.3 0.8 copy-done.1
  44.0 15.3 %shard_map.160 = (f32[32,64,128]{2,1,0:T(8,128)}, f32[32,64,2]{2,1,0:T(8,128)}, f32[32,64,2]{2,1,0:T(8,128)}) custom-call(s32[20]{0:T(128)} %get-tuple-element.49.owner_ref, s32[20]{0:T(128)} %get-tuple-element.48.filled_ref, bf16[32,64,128]{2,1,0:T(8,128)(2,1)} %copy-done.1, s32[32,64,1]{2,1,0:T(8,128)} %broadcast_in_dim_reshape.3.qv_ref, ...), custom_call_target="tpu_custom_call" | custom-call | tf_op jit(solution)/shard_map/pallas_call | solution.py:104
  59.3 1.7 %copy.69 = f32[32,2,64]{2,1,0:T(2,128)S(1)} copy(f32[32,2,64]{1,2,0:T(8,128)} %bitcast.158) | data formatting | bytes 32768 | tf_op jit(solution)/shard_map/transpose | solution.py:197
  61.0 0.1 stack_reshape.6
  61.1 1.6 %copy.70 = f32[32,2,64]{2,1,0:T(2,128)S(1)} copy(f32[32,2,64]{1,2,0:T(8,128)} %bitcast.157) | data formatting | bytes 32768 | tf_op jit(solution)/shard_map/transpose | solution.py:196
  62.8 0.1 stack_reshape.7
  62.9 0.1 convert_element_type.143
  63.0 0.9 pad_maximum_fusion
  63.9 9.7 %all-to-all-start.2 = ((bf16[32,70,128]{2,1,0:T(8,128)(2,1)}), bf16[32,70,128]{2,1,0:T(8,128)(2,1)S(1)}, u32[]{:S(2)}, u32[]{:S(2)}) async-start(bf16[32,70,128]{2,1,0:T(8,128)(2,1)} %pad_maximum_fusion), calls=%async_computation.2 | async-start | bytes 1179648 | tf_op jit(solution)/shard_map/all_to_all | solution.py:203
  73.9 0.1 copy.84
  74.0 0.2 select_reduce_fusion.1
  74.2 14.5 %all-to-all-done.2 = bf16[32,70,128]{2,1,0:T(8,128)(2,1)S(1)} async-done(((bf16[32,70,128]{2,1,0:T(8,128)(2,1)}), bf16[32,70,128]{2,1,0:T(8,128)(2,1)S(1)}, u32[]{:S(2)}, u32[]{:S(2)}) %all-to-all-start.2) | async-done | bytes 573472 | tf_op jit(solution)/shard_map/all_to_all | solution.py:203
  89.1 0.1 reshape_squeeze.2
  89.2 0.6 select_reduce_fusion
  89.8 0.2 fusion.11
  90.0 0.1 copy.73
  90.1 0.1 fusion.7
  90.4 0.7 broadcast_in_dim.128
  91.0 9.2 %all-to-all-start.3 = ((bf16[8,64,128]{2,1,0:T(8,128)(2,1)}), bf16[8,64,128]{2,1,0:T(8,128)(2,1)S(1)}, u32[]{:S(2)}, u32[]{:S(2)}) async-start(bf16[8,64,128]{2,1,0:T(8,128)(2,1)} %broadcast_in_dim.128), calls=%async_computation.3 | async-start | bytes 262144 | tf_op jit(solution)/shard_map/all_to_all | solution.py:132
  100.2 5.2 %all-to-all-done.3 = bf16[8,64,128]{2,1,0:T(8,128)(2,1)S(1)} async-done(((bf16[8,64,128]{2,1,0:T(8,128)(2,1)}), bf16[8,64,128]{2,1,0:T(8,128)(2,1)S(1)}, u32[]{:S(2)}, u32[]{:S(2)}) %all-to-all-start.3) | async-done | bytes 131104 | tf_op jit(solution)/shard_map/all_to_all | solution.py:132
  105.4 0.6 fusion.17
  106.0 1.0 copy-done.2
  107.0 0.5 convolution_bitcast_fusion
  107.6 0.9 fusion.1
  108.5 4.1 %all-to-all-start.4 = ((bf16[8,8,1024]{2,1,0:T(8,128)(2,1)}), bf16[8,8,1024]{2,1,0:T(8,128)(2,1)S(1)}, u32[]{:S(2)}, u32[]{:S(2)}) async-start(bf16[8,8,1024]{2,1,0:T(8,128)(2,1)} %fusion.1), calls=%async_computation.4 | async-start | bytes 262144 | tf_op jit(solution)/shard_map/all_to_all | solution.py:274
  112.6 0.8 fusion.10
  113.4 4.5 %all-to-all-done.4 = bf16[8,8,1024]{2,1,0:T(8,128)(2,1)S(1)} async-done(((bf16[8,8,1024]{2,1,0:T(8,128)(2,1)}), bf16[8,8,1024]{2,1,0:T(8,128)(2,1)S(1)}, u32[]{:S(2)}, u32[]{:S(2)}) %all-to-all-start.4) | async-done | bytes 131104 | tf_op jit(solution)/shard_map/all_to_all | solution.py:274
  117.9 0.6 add_convert_fusion
  (45 shorter events, 1.1 us)
Async XLA Ops:
  0.6 104.8 %copy-start = (bf16[1024,1024]{1,0:T(8,128)(2,1)S(1)}, bf16[1024,1024]{1,0:T(8,128)(2,1)}, u32[]{:S(2)}) copy-start(bf16[1024,1024]{1,0:T(8,128)(2,1)} %param.17) | copy-start | bytes 6291460
  2.2 13.1 %all-to-all-start = ((bf16[8,8,1024]{2,1,0:T(8,128)(2,1)}), bf16[8,8,1024]{2,1,0:T(8,128)(2,1)S(1)}, u32[]{:S(2)}, u32[]{:S(2)}) async-start(bf16[8,8,1024]{2,1,0:T(8,128)(2,1)} %broadcast_in_dim.112), calls=%async_computation | async-start | bytes 262144 | tf_op jit(solution)/shard_map/all_to_all | solution.py:132
  8.6 20.2 %copy-start.7 = (f32[2,16]{1,0:T(2,128)S(1)}, f32[2,16]{1,0:T(2,128)}, u32[]{:S(2)}) copy-start(f32[2,16]{1,0:T(2,128)} %param.20) | copy-start | bytes 388
  8.6 20.8 %copy-start.5 = (s32[32,32]{1,0:T(8,128)S(1)}, s32[32,32]{1,0:T(8,128)}, u32[]{:S(2)}) copy-start(s32[32,32]{1,0:T(8,128)} %param.25) | copy-start | bytes 12292
  8.6 20.8 %copy-start.8 = (s32[32]{0:T(128)S(1)}, s32[32]{0:T(128)}, u32[]{:S(2)}) copy-start(s32[32]{0:T(128)} %param.24) | copy-start | bytes 388
  17.8 25.4 %all-to-all-start.1 = ((bf16[32,64,128]{2,1,0:T(8,128)(2,1)}), bf16[32,64,128]{2,1,0:T(8,128)(2,1)S(1)}, u32[]{:S(2)}, u32[]{:S(2)}) async-start(bf16[32,64,128]{2,1,0:T(8,128)(2,1)} %broadcast_in_dim.114), calls=%async_computation.1 | async-start | bytes 1048576 | tf_op jit(solution)/shard_map/all_to_all | solution.py:132
  43.2 0.8 copy-start.1
  59.3 3.5 %copy-start.3 = (f32[32,64,128]{2,1,0:T(8,128)S(1)}, f32[32,64,128]{2,1,0:T(8,128)}, u32[]{:S(2)}) copy-start(f32[32,64,128]{2,1,0:T(8,128)} %get-tuple-element.6) | copy-start | bytes 3145732
  62.8 10.9 %copy-start.6 = (f32[2,2]{1,0:T(2,128)S(1)}, f32[2,2]{1,0:T(2,128)}, u32[]{:S(2)}) copy-start(f32[2,2]{1,0:T(2,128)} %constant_dynamic-slice_fusion.bias_ref) | copy-start | bytes 52
  63.9 24.8 %all-to-all-start.2 = ((bf16[32,70,128]{2,1,0:T(8,128)(2,1)}), bf16[32,70,128]{2,1,0:T(8,128)(2,1)S(1)}, u32[]{:S(2)}, u32[]{:S(2)}) async-start(bf16[32,70,128]{2,1,0:T(8,128)(2,1)} %pad_maximum_fusion), calls=%async_computation.2 | async-start | bytes 1179648 | tf_op jit(solution)/shard_map/all_to_all | solution.py:203
  90.4 17.2 %copy-start.4 = (bf16[64,128]{1,0:T(8,128)(2,1)}, bf16[64,128]{1,0:T(8,128)(2,1)S(1)}, u32[]{:S(2)}) copy-start(bf16[64,128]{1,0:T(8,128)(2,1)S(1)} %copy.79) | copy-start | bytes 49156
  91.0 14.4 %all-to-all-start.3 = ((bf16[8,64,128]{2,1,0:T(8,128)(2,1)}), bf16[8,64,128]{2,1,0:T(8,128)(2,1)S(1)}, u32[]{:S(2)}, u32[]{:S(2)}) async-start(bf16[8,64,128]{2,1,0:T(8,128)(2,1)} %broadcast_in_dim.128), calls=%async_computation.3 | async-start | bytes 262144 | tf_op jit(solution)/shard_map/all_to_all | solution.py:132
  105.4 1.6 %copy-start.2 = (bf16[2,1024,512]{2,1,0:T(8,128)(2,1)S(1)}, bf16[2,1024,512]{2,1,0:T(8,128)(2,1)}, u32[]{:S(2)}) copy-start(bf16[2,1024,512]{2,1,0:T(8,128)(2,1)} %param.18) | copy-start | bytes 6291460
  105.4 2.1 %copy-start.9 = (bf16[512,1024]{1,0:T(8,128)(2,1)S(1)}, bf16[512,1024]{1,0:T(8,128)(2,1)}, u32[]{:S(2)}) copy-start(bf16[512,1024]{1,0:T(8,128)(2,1)} %param.19) | copy-start | bytes 3145732
  106.0 6.6 %copy-start.10 = (s32[1,8]{1,0:T(1,128)S(1)}, s32[1,8]{1,0:T(1,128)}, u32[]{:S(2)}) copy-start(s32[1,8]{1,0:T(1,128)} %param.27) | copy-start | bytes 100
  108.5 9.4 %all-to-all-start.4 = ((bf16[8,8,1024]{2,1,0:T(8,128)(2,1)}), bf16[8,8,1024]{2,1,0:T(8,128)(2,1)S(1)}, u32[]{:S(2)}, u32[]{:S(2)}) async-start(bf16[8,8,1024]{2,1,0:T(8,128)(2,1)} %fusion.1), calls=%async_computation.4 | async-start | bytes 262144 | tf_op jit(solution)/shard_map/all_to_all | solution.py:274

commit v8 on v7

--- a/solution.py
+++ b/solution.py
@@ -35,46 +35,51 @@
     )
 
 
-def page_kernel(owner_ref, filled_ref, q_ref, qv_ref, k_ref, v_ref, pv_ref, bias_ref,
-                out_ref, max_ref, total_ref, *, head_local, scale):
-    step = pl.program_id(0)
-
-    @pl.when(step == 0)
-    def _():
-        out_ref[...] = jnp.zeros(out_ref.shape, jnp.float32)
-        max_ref[...] = jnp.full(max_ref.shape, masked_score, jnp.float32)
-        total_ref[...] = jnp.zeros(total_ref.shape, jnp.float32)
-
-    count = filled_ref[step]
-
-    @pl.when(count > 0)
-    def _():
-        row = owner_ref[step]
-        query = q_ref[row]
-        same = qv_ref[row] == pv_ref[...]
-        keys = k_ref[...]
-        values = v_ref[...]
-        valid = lax.broadcasted_iota(jnp.int32, same.shape, 1) < count
-        for head in range(head_local):
-            cols = slice(head * HD, (head + 1) * HD)
-            scores = lax.dot_general(
-                query[:, cols], keys[:, cols], (((1,), (1,)), ((), ())),
-                preferred_element_type=jnp.float32,
-            ) * scale
-            scores = scores + jnp.where(same, bias_ref[0, head], bias_ref[1, head])
-            block_max = jnp.max(jnp.where(valid, scores, masked_score), axis=1, keepdims=True)
-            weights = jnp.where(valid, jnp.exp(scores - block_max), 0.0).astype(jnp.bfloat16)
-            block_total = jnp.sum(weights.astype(jnp.float32), axis=1, keepdims=True)
-            block_out = jnp.dot(weights, values[:, cols], preferred_element_type=jnp.float32)
-            old_max = max_ref[row, :, head : head + 1]
-            new_max = jnp.maximum(old_max, block_max)
-            keep_old = jnp.exp(old_max - new_max)
-            keep_new = jnp.exp(block_max - new_max)
-            max_ref[row, :, head : head + 1] = new_max
-            total_ref[row, :, head : head + 1] = (
-                total_ref[row, :, head : head + 1] * keep_old + block_total * keep_new
-            )
-            out_ref[row, :, cols] = out_ref[row, :, cols] * keep_old + block_out * keep_new
+def page_kernel(owner_ref, filled_ref, q_ref, qv_ref, cache_ref, pv_ref, bias_ref,
+                out_ref, max_ref, total_ref, *, head_local, scale, pool):
+    out_ref[...] = jnp.zeros(out_ref.shape, jnp.float32)
+    max_ref[...] = jnp.full(max_ref.shape, masked_score, jnp.float32)
+    total_ref[...] = jnp.zeros(total_ref.shape, jnp.float32)
+
+    def one_page(step, carry):
+        count = filled_ref[step]
+
+        @pl.when(count > 0)
+        def _():
+            row = owner_ref[step]
+            query = q_ref[row]
+            same = qv_ref[row] == pv_ref[step]
+            keys = cache_ref[0, step]
+            values = cache_ref[1, step]
+            valid = lax.broadcasted_iota(jnp.int32, same.shape, 1) < count
+            for head in range(head_local):
+                cols = slice(head * HD, (head + 1) * HD)
+                scores = lax.dot_general(
+                    query[:, cols], keys[:, cols], (((1,), (1,)), ((), ())),
+                    preferred_element_type=jnp.float32,
+                ) * scale
+                scores = scores + jnp.where(same, bias_ref[0, head], bias_ref[1, head])
+                block_max = jnp.max(
+                    jnp.where(valid, scores, masked_score), axis=1, keepdims=True
+                )
+                weights = jnp.where(valid, jnp.exp(scores - block_max), 0.0).astype(
+                    jnp.bfloat16
+                )
+                block_total = jnp.sum(weights.astype(jnp.float32), axis=1, keepdims=True)
+                block_out = jnp.dot(weights, values[:, cols], preferred_element_type=jnp.float32)
+                old_max = max_ref[row, :, head : head + 1]
+                new_max = jnp.maximum(old_max, block_max)
+                keep_old = jnp.exp(old_max - new_max)
+                keep_new = jnp.exp(block_max - new_max)
+                max_ref[row, :, head : head + 1] = new_max
+                total_ref[row, :, head : head + 1] = (
+                    total_ref[row, :, head : head + 1] * keep_old + block_total * keep_new
+                )
+                out_ref[row, :, cols] = out_ref[row, :, cols] * keep_old + block_out * keep_new
+
+        return carry
+
+    lax.fori_loop(0, pool, one_page, 0)
 
 
 def page_attention(owner, filled, queries, query_variates, page_cache, page_variates, bias,
@@ -82,23 +87,27 @@
     requests, tree, qdl = queries.shape
     pool, page = page_variates.shape
     head_local = qdl // HD
-    kernel = functools.partial(page_kernel, head_local=head_local, scale=1.0 / math.sqrt(HD))
-    whole3 = lambda shape: pl.BlockSpec(shape, lambda step, *_: (0, 0, 0))
+    kernel = functools.partial(
+        page_kernel, head_local=head_local, scale=1.0 / math.sqrt(HD), pool=pool
+    )
+
+    def whole(shape):
+        return pl.BlockSpec(shape, lambda step, *_: (0,) * len(shape))
+
     grid_spec = pltpu.PrefetchScalarGridSpec(
         num_scalar_prefetch=2,
-        grid=(pool,),
+        grid=(1,),
         in_specs=[
-            whole3((requests, tree, qdl)),
-            whole3((requests, tree, 1)),
-            pl.BlockSpec((None, None, page, qdl), lambda step, *_: (0, step, 0, 0)),
-            pl.BlockSpec((None, None, page, qdl), lambda step, *_: (1, step, 0, 0)),
-            pl.BlockSpec((None, 1, page), lambda step, *_: (step, 0, 0)),
+            whole((requests, tree, qdl)),
+            whole((requests, tree, 1)),
+            whole(page_cache.shape),
+            whole((pool, 1, page)),
             pl.BlockSpec(memory_space=pltpu.SMEM),
         ],
         out_specs=[
-            whole3((requests, tree, qdl)),
-            whole3((requests, tree, head_local)),
-            whole3((requests, tree, head_local)),
+            whole((requests, tree, qdl)),
+            whole((requests, tree, head_local)),
+            whole((requests, tree, head_local)),
         ],
     )
     return pl.pallas_call(
@@ -112,7 +121,7 @@
         compiler_params=pltpu.CompilerParams(dimension_semantics=("arbitrary",)),
         interpret=interpret,
     )(owner, filled, queries, query_variates[..., None], page_cache,
-      page_cache, page_variates[:, None, :], bias)
+      page_variates[:, None, :], bias)
 
 
 def split_three(values):

time: 120 us -> 115 us (0.958)
  Pallas kernels: 15.3 us -> 11.8 us
  starting transfers between devices: 40 us -> 37.6 us
    pallas_call x1, Pallas kernels: 15.3 us -> 11.8 us  [page_attention(): pl.pallas_call(kernel, grid_spec=grid_spec, out_shape=[jax.ShapeDtypeStru...]
    all_to_all x3, starting transfers between devices: 26.1 us -> 24.9 us  [gather_rows(): return lax.all_to_all(spread, axis_name, 0, 0, tiled=True)]
  transfers between devices with their start and end apart: 5 -> 5, of which waited for: 4 -> 4; matrix products, arithmetic and copies ran while one was open for 9% -> 10% of each run, Pallas kernels for 0% -> 0%
where the time goes in v8:
time: 115 us; the launch traced here: 113 us
  starting transfers between devices  37.6 us (33%)
  waiting for transfers between devices  36.5 us (32%)
  local copies, waits for them, and re-layouts  15.5 us (13%)
  Pallas kernels  11.8 us (10%)
  other arithmetic  5.82 us (5%)
  matrix products  5.2 us (5%)
    all_to_all x3, starting transfers between devices, gather_rows(): return lax.all_to_all(spread, axis_name, 0, 0, tiled=True)  24.9 us
    all_to_all x3, waiting for transfers between devices, gather_rows(): return lax.all_to_all(spread, axis_name, 0, 0, tiled=True)  16.9 us
    all_to_all x1, waiting for transfers between devices, shards(): lax.all_to_all(packed, 'req', split_axis=0, concat_axis=0, tiled=True)  15.1 us
    pallas_call x1, Pallas kernels, page_attention(): pl.pallas_call(kernel, grid_spec=grid_spec, out_shape=[jax.ShapeDtypeStru...  11.8 us
    all_to_all x1, starting transfers between devices, shards(): lax.all_to_all(packed, 'req', split_axis=0, concat_axis=0, tiled=True)  8.66 us
    all_to_all x1, waiting for transfers between devices, shards(): lax.all_to_all(down_part.reshape(head_parts, own_rows, -1), 'head', 0, 0,...  4.48 us
    all_to_all x1, starting transfers between devices, shards(): lax.all_to_all(down_part.reshape(head_parts, own_rows, -1), 'head', 0, 0,...  4.13 us
    broadcast_in_dim x4, local copies, waits for them, and re-layouts, gather_rows(): spread = jnp.broadcast_to(rows[None], (parts,) + rows.shape)  3.2 us
  transfers between devices with their start and end apart: 5, of which 4 were waited for; matrix products, arithmetic and copies ran while one was open for 10% of the time, Pallas kernels for 0%

profile of v8, /device:TPU:1, one launch (start us, length us, event | category | flops | bytes accessed | tf_op | source)
XLA Modules:
  0.0 113.4 jit_solution(14853953358964350216)
XLA Ops:
  0.6 1.5 %broadcast_in_dim.112 = bf16[8,8,1024]{2,1,0:T(8,128)(2,1)} broadcast(bf16[8,1024]{1,0:T(8,128)(2,1)} %param.14), dimensions={1,2} | broadcast | bytes 147456 | tf_op jit(solution)/shard_map/broadcast_in_dim | solution.py:140
  2.2 6.5 %all-to-all-start = ((bf16[8,8,1024]{2,1,0:T(8,128)(2,1)}), bf16[8,8,1024]{2,1,0:T(8,128)(2,1)S(1)}, u32[]{:S(2)}, u32[]{:S(2)}) async-start(bf16[8,8,1024]{2,1,0:T(8,128)(2,1)} %broadcast_in_dim.112), calls=%async_computation | async-start | bytes 262144 | tf_op jit(solution)/shard_map/all_to_all | solution.py:141
  8.6 2.6 %broadcast_in_dim_reshape.3.qv_ref = s32[32,64,1]{2,1,0:T(8,128)} reshape(s32[2048]{0:T(1024)} %param.23) | data formatting | bytes 16384 | tf_op jit(solution)/shard_map/broadcast_in_dim;reshape | solution.py:123
  11.2 1.3 %broadcast_in_dim.115.pv_ref = s32[20,1,128]{2,1,0:T(1,128)} reshape(s32[20,128]{1,0:T(8,128)} %param.22) | data formatting | bytes 20480 | tf_op jit(solution)/shard_map/broadcast_in_dim | solution.py:124
  12.6 0.8 dynamic_slice.10
  13.3 0.8 fusion.38
  14.1 0.2 convolution_minimum_fusion.3
  14.3 0.2 convolution_minimum_fusion.2
  14.5 0.8 fusion.55
  15.2 0.1 fusion.22
  15.4 1.4 %fusion.8 = bf16[3,64,128]{2,1,0:T(8,128)(2,1)S(1)} fusion(bf16[3,1024,128]{2,1,0:T(8,128)(2,1)} %param.16, bf16[8,8,1024]{2,1,0:T(8,128)(2,1)S(1)} %all-to-all-done, f32[1024]{0:T(1024)S(1)} %bitcast.168, f32[64]{0:T(128)S(1)} %rsqrt.20), kind=kOutput, calls=%fused_computation.15 | convolution fusion | flops 50618368 | bytes 971008 | tf_op jit(solution)/shard_map/td,cdq->ctq/dot_general | solution.py:174
  16.9 0.9 broadcast_in_dim.114
  17.8 10.5 %all-to-all-start.1 = ((bf16[32,64,128]{2,1,0:T(8,128)(2,1)}), bf16[32,64,128]{2,1,0:T(8,128)(2,1)S(1)}, u32[]{:S(2)}, u32[]{:S(2)}) async-start(bf16[32,64,128]{2,1,0:T(8,128)(2,1)} %broadcast_in_dim.114), calls=%async_computation.1 | async-start | bytes 1048576 | tf_op jit(solution)/shard_map/all_to_all | solution.py:141
  28.4 0.2 convolution_minimum_fusion.1
  28.5 0.2 fusion.9
  28.7 0.1 copy.74
  28.8 0.6 constant_dynamic-slice_fusion.bias_ref
  29.5 1.6 %fusion.15 = (s32[20]{0:T(128)S(1)}, s32[20]{0:T(128)S(1)}, s32[20]{0:T(128)S(1)}, s32[20]{0:T(128)S(1)}) fusion(s32[32,32]{1,0:T(8,128)S(1)} %copy-done.5, s32[20]{0:T(128)S(1)} %iota_add_fusion, s32[32]{0:T(128)S(1)} %copy-done.8), kind=kLoop, calls=%fused_computation.37 | loop fusion | flops 184240 | bytes 4624 | tf_op jit(solution)/shard_map/reduce_sum | solution.py:187
  31.1 0.5 clamp_multiply_fusion
  31.6 11.6 %all-to-all-done.1.q_ref = bf16[32,64,128]{2,1,0:T(8,128)(2,1)S(1)} async-done(((bf16[32,64,128]{2,1,0:T(8,128)(2,1)}), bf16[32,64,128]{2,1,0:T(8,128)(2,1)S(1)}, u32[]{:S(2)}, u32[]{:S(2)}) %all-to-all-start.1) | async-done | bytes 524320 | tf_op jit(solution)/shard_map/all_to_all | solution.py:141
  43.3 0.8 copy-done.2
  44.0 11.8 %shard_map.160 = (f32[32,64,128]{2,1,0:T(8,128)}, f32[32,64,2]{2,1,0:T(8,128)}, f32[32,64,2]{2,1,0:T(8,128)}) custom-call(s32[20]{0:T(128)} %get-tuple-element.49.owner_ref, s32[20]{0:T(128)} %get-tuple-element.48.filled_ref, bf16[32,64,128]{2,1,0:T(8,128)(2,1)} %copy-done.2, s32[32,64,1]{2,1,0:T(8,128)} %broadcast_in_dim_reshape.3.qv_ref, ...), custom_call_target="tpu_custom_call" | custom-call | tf_op jit(solution)/shard_map/pallas_call | solution.py:113
  55.8 1.7 %copy.69 = f32[32,2,64]{2,1,0:T(2,128)S(1)} copy(f32[32,2,64]{1,2,0:T(8,128)} %bitcast.158) | data formatting | bytes 32768 | tf_op jit(solution)/shard_map/transpose | solution.py:206
  57.5 0.1 stack_reshape.6
  57.6 1.6 %copy.70 = f32[32,2,64]{2,1,0:T(2,128)S(1)} copy(f32[32,2,64]{1,2,0:T(8,128)} %bitcast.157) | data formatting | bytes 32768 | tf_op jit(solution)/shard_map/transpose | solution.py:205
  59.2 0.1 stack_reshape.7
  59.5 0.9 pad_maximum_fusion
  60.4 8.7 %all-to-all-start.2 = ((bf16[32,70,128]{2,1,0:T(8,128)(2,1)}), bf16[32,70,128]{2,1,0:T(8,128)(2,1)S(1)}, u32[]{:S(2)}, u32[]{:S(2)}) async-start(bf16[32,70,128]{2,1,0:T(8,128)(2,1)} %pad_maximum_fusion), calls=%async_computation.2 | async-start | bytes 1179648 | tf_op jit(solution)/shard_map/all_to_all | solution.py:212
  69.4 0.1 copy.84
  69.5 0.2 select_reduce_fusion.1
  69.7 15.1 %all-to-all-done.2 = bf16[32,70,128]{2,1,0:T(8,128)(2,1)S(1)} async-done(((bf16[32,70,128]{2,1,0:T(8,128)(2,1)}), bf16[32,70,128]{2,1,0:T(8,128)(2,1)S(1)}, u32[]{:S(2)}, u32[]{:S(2)}) %all-to-all-start.2) | async-done | bytes 573472 | tf_op jit(solution)/shard_map/all_to_all | solution.py:212
  85.2 0.1 reshape_squeeze.2
  85.4 0.6 select_reduce_fusion
  86.0 0.2 fusion.11
  86.1 0.1 copy.73
  86.3 0.1 fusion.7
  86.4 0.1 copy.79
  86.5 0.7 broadcast_in_dim.128
  87.2 7.9 %all-to-all-start.3 = ((bf16[8,64,128]{2,1,0:T(8,128)(2,1)}), bf16[8,64,128]{2,1,0:T(8,128)(2,1)S(1)}, u32[]{:S(2)}, u32[]{:S(2)}) async-start(bf16[8,64,128]{2,1,0:T(8,128)(2,1)} %broadcast_in_dim.128), calls=%async_computation.3 | async-start | bytes 262144 | tf_op jit(solution)/shard_map/all_to_all | solution.py:141
  95.0 5.2 %all-to-all-done.3 = bf16[8,64,128]{2,1,0:T(8,128)(2,1)S(1)} async-done(((bf16[8,64,128]{2,1,0:T(8,128)(2,1)}), bf16[8,64,128]{2,1,0:T(8,128)(2,1)S(1)}, u32[]{:S(2)}, u32[]{:S(2)}) %all-to-all-start.3) | async-done | bytes 131104 | tf_op jit(solution)/shard_map/all_to_all | solution.py:141
  100.3 0.6 fusion.17
  100.9 1.0 copy-done.1
  101.9 0.5 convolution_bitcast_fusion
  102.4 0.9 fusion.1
  103.3 4.1 %all-to-all-start.4 = ((bf16[8,8,1024]{2,1,0:T(8,128)(2,1)}), bf16[8,8,1024]{2,1,0:T(8,128)(2,1)S(1)}, u32[]{:S(2)}, u32[]{:S(2)}) async-start(bf16[8,8,1024]{2,1,0:T(8,128)(2,1)} %fusion.1), calls=%async_computation.4 | async-start | bytes 262144 | tf_op jit(solution)/shard_map/all_to_all | solution.py:283
  107.5 0.8 fusion.10
  108.3 4.5 %all-to-all-done.4 = bf16[8,8,1024]{2,1,0:T(8,128)(2,1)S(1)} async-done(((bf16[8,8,1024]{2,1,0:T(8,128)(2,1)}), bf16[8,8,1024]{2,1,0:T(8,128)(2,1)S(1)}, u32[]{:S(2)}, u32[]{:S(2)}) %all-to-all-start.4) | async-done | bytes 131104 | tf_op jit(solution)/shard_map/all_to_all | solution.py:283
  112.8 0.6 add_convert_fusion
  (45 shorter events, 1.1 us)
Async XLA Ops:
  0.6 99.6 %copy-start = (bf16[1024,1024]{1,0:T(8,128)(2,1)S(1)}, bf16[1024,1024]{1,0:T(8,128)(2,1)}, u32[]{:S(2)}) copy-start(bf16[1024,1024]{1,0:T(8,128)(2,1)} %param.17) | copy-start | bytes 6291460
  2.2 13.1 %all-to-all-start = ((bf16[8,8,1024]{2,1,0:T(8,128)(2,1)}), bf16[8,8,1024]{2,1,0:T(8,128)(2,1)S(1)}, u32[]{:S(2)}, u32[]{:S(2)}) async-start(bf16[8,8,1024]{2,1,0:T(8,128)(2,1)} %broadcast_in_dim.112), calls=%async_computation | async-start | bytes 262144 | tf_op jit(solution)/shard_map/all_to_all | solution.py:141
  8.6 20.2 %copy-start.7 = (f32[2,16]{1,0:T(2,128)S(1)}, f32[2,16]{1,0:T(2,128)}, u32[]{:S(2)}) copy-start(f32[2,16]{1,0:T(2,128)} %param.20) | copy-start | bytes 388
  8.6 20.8 %copy-start.5 = (s32[32,32]{1,0:T(8,128)S(1)}, s32[32,32]{1,0:T(8,128)}, u32[]{:S(2)}) copy-start(s32[32,32]{1,0:T(8,128)} %param.25) | copy-start | bytes 12292
  8.6 20.8 %copy-start.8 = (s32[32]{0:T(128)S(1)}, s32[32]{0:T(128)}, u32[]{:S(2)}) copy-start(s32[32]{0:T(128)} %param.24) | copy-start | bytes 388
  17.8 25.4 %all-to-all-start.1 = ((bf16[32,64,128]{2,1,0:T(8,128)(2,1)}), bf16[32,64,128]{2,1,0:T(8,128)(2,1)S(1)}, u32[]{:S(2)}, u32[]{:S(2)}) async-start(bf16[32,64,128]{2,1,0:T(8,128)(2,1)} %broadcast_in_dim.114), calls=%async_computation.1 | async-start | bytes 1048576 | tf_op jit(solution)/shard_map/all_to_all | solution.py:141
  43.2 0.8 copy-start.2
  55.8 3.5 %copy-start.3 = (f32[32,64,128]{2,1,0:T(8,128)S(1)}, f32[32,64,128]{2,1,0:T(8,128)}, u32[]{:S(2)}) copy-start(f32[32,64,128]{2,1,0:T(8,128)} %get-tuple-element.6) | copy-start | bytes 3145732
  59.2 9.9 %copy-start.6 = (f32[2,2]{1,0:T(2,128)S(1)}, f32[2,2]{1,0:T(2,128)}, u32[]{:S(2)}) copy-start(f32[2,2]{1,0:T(2,128)} %constant_dynamic-slice_fusion.bias_ref) | copy-start | bytes 52
  60.4 24.4 %all-to-all-start.2 = ((bf16[32,70,128]{2,1,0:T(8,128)(2,1)}), bf16[32,70,128]{2,1,0:T(8,128)(2,1)S(1)}, u32[]{:S(2)}, u32[]{:S(2)}) async-start(bf16[32,70,128]{2,1,0:T(8,128)(2,1)} %pad_maximum_fusion), calls=%async_computation.2 | async-start | bytes 1179648 | tf_op jit(solution)/shard_map/all_to_all | solution.py:212
  86.5 15.9 %copy-start.4 = (bf16[64,128]{1,0:T(8,128)(2,1)}, bf16[64,128]{1,0:T(8,128)(2,1)S(1)}, u32[]{:S(2)}) copy-start(bf16[64,128]{1,0:T(8,128)(2,1)S(1)} %copy.79) | copy-start | bytes 49156
  87.2 13.1 %all-to-all-start.3 = ((bf16[8,64,128]{2,1,0:T(8,128)(2,1)}), bf16[8,64,128]{2,1,0:T(8,128)(2,1)S(1)}, u32[]{:S(2)}, u32[]{:S(2)}) async-start(bf16[8,64,128]{2,1,0:T(8,128)(2,1)} %broadcast_in_dim.128), calls=%async_computation.3 | async-start | bytes 262144 | tf_op jit(solution)/shard_map/all_to_all | solution.py:141
  100.3 1.6 %copy-start.1 = (bf16[2,1024,512]{2,1,0:T(8,128)(2,1)S(1)}, bf16[2,1024,512]{2,1,0:T(8,128)(2,1)}, u32[]{:S(2)}) copy-start(bf16[2,1024,512]{2,1,0:T(8,128)(2,1)} %param.18) | copy-start | bytes 6291460
  100.3 2.1 %copy-start.9 = (bf16[512,1024]{1,0:T(8,128)(2,1)S(1)}, bf16[512,1024]{1,0:T(8,128)(2,1)}, u32[]{:S(2)}) copy-start(bf16[512,1024]{1,0:T(8,128)(2,1)} %param.19) | copy-start | bytes 3145732
  100.9 6.6 %copy-start.10 = (s32[1,8]{1,0:T(1,128)S(1)}, s32[1,8]{1,0:T(1,128)}, u32[]{:S(2)}) copy-start(s32[1,8]{1,0:T(1,128)} %param.27) | copy-start | bytes 100
  103.3 9.4 %all-to-all-start.4 = ((bf16[8,8,1024]{2,1,0:T(8,128)(2,1)}), bf16[8,8,1024]{2,1,0:T(8,128)(2,1)S(1)}, u32[]{:S(2)}, u32[]{:S(2)}) async-start(bf16[8,8,1024]{2,1,0:T(8,128)(2,1)} %fusion.1), calls=%async_computation.4 | async-start | bytes 262144 | tf_op jit(solution)/shard_map/all_to_all | solution.py:283

commit v9 on v8

--- a/solution.py
+++ b/solution.py
@@ -36,10 +36,22 @@
 
 
 def page_kernel(owner_ref, filled_ref, q_ref, qv_ref, cache_ref, pv_ref, bias_ref,
-                out_ref, max_ref, total_ref, *, head_local, scale, pool):
+                out_ref, total_ref, max_ref, max_acc, total_acc,
+                *, head_local, tree, scale, pool):
+    rows, page = q_ref.shape[1], cache_ref.shape[2]
     out_ref[...] = jnp.zeros(out_ref.shape, jnp.float32)
-    max_ref[...] = jnp.full(max_ref.shape, masked_score, jnp.float32)
-    total_ref[...] = jnp.zeros(total_ref.shape, jnp.float32)
+    max_acc[...] = jnp.full(max_acc.shape, masked_score, jnp.float32)
+    total_acc[...] = jnp.zeros(total_acc.shape, jnp.float32)
+    request_lane = lax.broadcasted_iota(jnp.int32, max_acc.shape, 1)
+    column_head = lax.broadcasted_iota(jnp.int32, out_ref.shape[1:], 1) // HD
+
+    def pick_heads(values):
+        picked = jnp.zeros(out_ref.shape[1:], jnp.float32)
+        for head in range(head_local):
+            picked = picked + jnp.where(
+                column_head == head, values[head * tree : (head + 1) * tree], 0.0
+            )
+        return picked
 
     def one_page(step, carry):
         count = filled_ref[step]
@@ -47,48 +59,48 @@
         @pl.when(count > 0)
         def _():
             row = owner_ref[step]
-            query = q_ref[row]
             same = qv_ref[row] == pv_ref[step]
-            keys = cache_ref[0, step]
-            values = cache_ref[1, step]
-            valid = lax.broadcasted_iota(jnp.int32, same.shape, 1) < count
-            for head in range(head_local):
-                cols = slice(head * HD, (head + 1) * HD)
-                scores = lax.dot_general(
-                    query[:, cols], keys[:, cols], (((1,), (1,)), ((), ())),
-                    preferred_element_type=jnp.float32,
-                ) * scale
-                scores = scores + jnp.where(same, bias_ref[0, head], bias_ref[1, head])
-                block_max = jnp.max(
-                    jnp.where(valid, scores, masked_score), axis=1, keepdims=True
-                )
-                weights = jnp.where(valid, jnp.exp(scores - block_max), 0.0).astype(
-                    jnp.bfloat16
-                )
-                block_total = jnp.sum(weights.astype(jnp.float32), axis=1, keepdims=True)
-                block_out = jnp.dot(weights, values[:, cols], preferred_element_type=jnp.float32)
-                old_max = max_ref[row, :, head : head + 1]
-                new_max = jnp.maximum(old_max, block_max)
-                keep_old = jnp.exp(old_max - new_max)
-                keep_new = jnp.exp(block_max - new_max)
-                max_ref[row, :, head : head + 1] = new_max
-                total_ref[row, :, head : head + 1] = (
-                    total_ref[row, :, head : head + 1] * keep_old + block_total * keep_new
-                )
-                out_ref[row, :, cols] = out_ref[row, :, cols] * keep_old + block_out * keep_new
+            valid = lax.broadcasted_iota(jnp.int32, (rows, page), 1) < count
+            scores = lax.dot_general(
+                q_ref[row], cache_ref[0, step], (((1,), (1,)), ((), ())),
+                preferred_element_type=jnp.float32,
+            ) * scale
+            scores = scores + jnp.where(same, bias_ref[0], bias_ref[1])
+            block_max = jnp.max(jnp.where(valid, scores, masked_score), axis=1, keepdims=True)
+            weights = jnp.where(valid, jnp.exp(scores - block_max), 0.0).astype(jnp.bfloat16)
+            block_total = jnp.sum(weights.astype(jnp.float32), axis=1, keepdims=True)
+            crossed = jnp.dot(weights, cache_ref[1, step], preferred_element_type=jnp.float32)
+            is_row = request_lane == row
+            old_max = jnp.sum(jnp.where(is_row, max_acc[...], 0.0), axis=1, keepdims=True)
+            old_total = jnp.sum(jnp.where(is_row, total_acc[...], 0.0), axis=1, keepdims=True)
+            new_max = jnp.maximum(old_max, block_max)
+            keep_old = jnp.exp(old_max - new_max)
+            keep_new = jnp.exp(block_max - new_max)
+            max_acc[...] = jnp.where(is_row, new_max, max_acc[...])
+            total_acc[...] = jnp.where(
+                is_row, old_total * keep_old + block_total * keep_new, total_acc[...]
+            )
+            out_ref[row] = out_ref[row] * pick_heads(
+                jnp.broadcast_to(keep_old, crossed.shape)
+            ) + pick_heads(crossed * keep_new)
 
         return carry
 
     lax.fori_loop(0, pool, one_page, 0)
-
-
-def page_attention(owner, filled, queries, query_variates, page_cache, page_variates, bias,
-                   interpret=False):
-    requests, tree, qdl = queries.shape
+    requests = out_ref.shape[0]
+    total_ref[...] = jnp.transpose(total_acc[...])[:requests]
+    max_ref[...] = jnp.transpose(max_acc[...])[:requests]
+
+
+def page_attention(owner, filled, split_queries, row_variates, page_cache, page_variates,
+                   row_bias, interpret=False):
+    requests, rows, qdl = split_queries.shape
     pool, page = page_variates.shape
     head_local = qdl // HD
+    tree = rows // head_local
+    lanes = 128 * ((requests + 127) // 128)
     kernel = functools.partial(
-        page_kernel, head_local=head_local, scale=1.0 / math.sqrt(HD), pool=pool
+        page_kernel, head_local=head_local, tree=tree, scale=1.0 / math.sqrt(HD), pool=pool
     )
 
     def whole(shape):
@@ -98,30 +110,31 @@
         num_scalar_prefetch=2,
         grid=(1,),
         in_specs=[
-            whole((requests, tree, qdl)),
-            whole((requests, tree, 1)),
+            whole((requests, rows, qdl)),
+            whole((requests, rows, 1)),
             whole(page_cache.shape),
             whole((pool, 1, page)),
-            pl.BlockSpec(memory_space=pltpu.SMEM),
+            whole((2, rows, 1)),
         ],
         out_specs=[
             whole((requests, tree, qdl)),
-            whole((requests, tree, head_local)),
-            whole((requests, tree, head_local)),
+            whole((requests, rows)),
+            whole((requests, rows)),
         ],
+        scratch_shapes=[pltpu.VMEM((rows, lanes), jnp.float32)] * 2,
     )
     return pl.pallas_call(
         kernel,
         grid_spec=grid_spec,
         out_shape=[
             jax.ShapeDtypeStruct((requests, tree, qdl), jnp.float32),
-            jax.ShapeDtypeStruct((requests, tree, head_local), jnp.float32),
-            jax.ShapeDtypeStruct((requests, tree, head_local), jnp.float32),
+            jax.ShapeDtypeStruct((requests, rows), jnp.float32),
+            jax.ShapeDtypeStruct((requests, rows), jnp.float32),
         ],
         compiler_params=pltpu.CompilerParams(dimension_semantics=("arbitrary",)),
         interpret=interpret,
-    )(owner, filled, queries, query_variates[..., None], page_cache,
-      page_variates[:, None, :], bias)
+    )(owner, filled, split_queries, row_variates[..., None], page_cache,
+      page_variates[:, None, :], row_bias[..., None])
 
 
 def split_three(values):
@@ -193,17 +206,27 @@
     valid = jnp.arange(page, dtype=jnp.int32)[None, :] < filled[:, None]
     head_of_column = jnp.arange(qdl, dtype=jnp.int32) // HD
     head_mask = jnp.arange(head_local, dtype=jnp.int32)[:, None] == head_of_column[None, :]
-    request_out, acc_max, acc_total = page_attention(
+    split_rows = head_local * tree
+    split_queries = jnp.where(
+        head_mask[None, :, None, :],
+        all_queries.reshape(requests, 1, tree, qdl),
+        jnp.zeros((), all_queries.dtype),
+    ).reshape(requests, split_rows, qdl)
+    row_variates = jnp.broadcast_to(
+        token_variates.reshape(requests, 1, tree), (requests, head_local, tree)
+    ).reshape(requests, split_rows)
+    row_bias = jnp.broadcast_to(bias_local[:, :, None], (2, head_local, tree)).reshape(
+        2, split_rows
+    )
+    request_out, request_total, request_max = page_attention(
         jnp.clip(owner, 0, requests - 1),
         filled,
-        all_queries.reshape(requests, tree, qdl),
-        token_variates.reshape(requests, tree),
+        split_queries,
+        row_variates,
         page_cache,
         page_variates,
-        bias_local,
-    )
-    request_max = acc_max.transpose(0, 2, 1).reshape(requests, head_local * tree)
-    request_total = acc_total.transpose(0, 2, 1).reshape(requests, head_local * tree)
+        row_bias,
+    )
     stats = jnp.stack([request_total, request_max], axis=1)
     packed = jnp.concatenate(
         [request_out.astype(jnp.bfloat16).reshape(requests, tree, qdl)] + split_three(stats),

time: 115 us -> 110 us (0.957)
  Pallas kernels: 11.8 us -> 9.38 us
  other arithmetic: 5.82 us -> 8.14 us
  local copies, waits for them, and re-layouts: 15.5 us -> 13.2 us
  waiting for transfers between devices: 36.5 us -> 35.3 us
    transpose x2 -> x0, local copies, waits for them, and re-layouts: 3.31 us -> none  [the longest x1 1.69 us: shards(): acc_total.transpose(0, 2, 1).reshape(requests, head_local * tree)]
    pallas_call x1, Pallas kernels: 11.8 us -> 9.38 us  [page_attention(): pl.pallas_call(kernel, grid_spec=grid_spec, out_shape=[jax.ShapeDtypeStru...]
    all_to_all x1, waiting for transfers between devices: 15.1 us -> 13.3 us  [shards(): lax.all_to_all(packed, 'req', split_axis=0, concat_axis=0, tiled=True)]
    another operation x6 -> x5, local copies, waits for them, and re-layouts: 3.08 us -> 4.58 us  [the longest x1 3.51 us: page_attention(): row_variates[..., None]]
    convert_element_type x1, other arithmetic: 0.08 us -> 1.3 us  [shards(): request_out.astype(jnp.bfloat16).reshape(requests, tree, qdl)]
  transfers between devices with their start and end apart: 5 -> 5, of which waited for: 4 -> 4; matrix products, arithmetic and copies ran while one was open for 10% -> 11% of each run, Pallas kernels for 0% -> 0%
where the time goes in v9:
time: 110 us; the launch traced here: 109 us
  starting transfers between devices  37.5 us (34%)
  waiting for transfers between devices  35.3 us (32%)
  local copies, waits for them, and re-layouts  13.2 us (12%)
  Pallas kernels  9.38 us (9%)
  other arithmetic  8.14 us (7%)
  matrix products  4.07 us (4%)
    all_to_all x3, starting transfers between devices, gather_rows(): return lax.all_to_all(spread, axis_name, 0, 0, tiled=True)  25.1 us
    all_to_all x3, waiting for transfers between devices, gather_rows(): return lax.all_to_all(spread, axis_name, 0, 0, tiled=True)  17.5 us
    all_to_all x1, waiting for transfers between devices, shards(): lax.all_to_all(packed, 'req', split_axis=0, concat_axis=0, tiled=True)  13.3 us
    pallas_call x1, Pallas kernels, page_attention(): pl.pallas_call(kernel, grid_spec=grid_spec, out_shape=[jax.ShapeDtypeStru...  9.38 us
    all_to_all x1, starting transfers between devices, shards(): lax.all_to_all(packed, 'req', split_axis=0, concat_axis=0, tiled=True)  8.24 us
    all_to_all x1, waiting for transfers between devices, shards(): lax.all_to_all(down_part.reshape(head_parts, own_rows, -1), 'head', 0, 0,...  4.48 us
    all_to_all x1, starting transfers between devices, shards(): lax.all_to_all(down_part.reshape(head_parts, own_rows, -1), 'head', 0, 0,...  4.14 us
    another operation x1, local copies, waits for them, and re-layouts, page_attention(): row_variates[..., None]  3.51 us
  transfers between devices with their start and end apart: 5, of which 4 were waited for; matrix products, arithmetic and copies ran while one was open for 11% of the time, Pallas kernels for 0%

profile of v9, /device:TPU:1, one launch (start us, length us, event | category | flops | bytes accessed | tf_op | source)
XLA Modules:
  0.0 108.5 jit_solution(6689283817607828980)
XLA Ops:
  0.7 1.5 %broadcast_in_dim.152 = bf16[8,8,1024]{2,1,0:T(8,128)(2,1)} broadcast(bf16[8,1024]{1,0:T(8,128)(2,1)} %param.14), dimensions={1,2} | broadcast | bytes 147456 | tf_op jit(solution)/shard_map/broadcast_in_dim | solution.py:153
  2.2 6.5 %all-to-all-start = ((bf16[8,8,1024]{2,1,0:T(8,128)(2,1)}), bf16[8,8,1024]{2,1,0:T(8,128)(2,1)S(1)}, u32[]{:S(2)}, u32[]{:S(2)}) async-start(bf16[8,8,1024]{2,1,0:T(8,128)(2,1)} %broadcast_in_dim.152), calls=%async_computation | async-start | bytes 262144 | tf_op jit(solution)/shard_map/all_to_all | solution.py:154
  8.7 0.8 fusion.55
  9.5 0.8 constant_dynamic-slice_fusion
  10.3 0.8 broadcast_in_dim_reshape.12.bias_ref
  11.1 0.8 broadcast_in_dim.161
  11.9 3.5 %broadcast_in_dim_reshape.11.qv_ref = s32[32,128,1]{2,1,0:T(8,128)} reshape(s32[32,2,64]{2,1,0:T(2,128)S(1)} %broadcast_in_dim.162) | data formatting | bytes 32768 | tf_op jit(solution)/shard_map/broadcast_in_dim;reshape | solution.py:136
  15.4 0.6 broadcast_in_dim.163.pv_ref
  16.0 0.1 fusion.22
  16.2 0.3 fusion.8
  16.6 0.9 broadcast_in_dim.157
  17.5 10.5 %all-to-all-start.1 = ((bf16[32,64,128]{2,1,0:T(8,128)(2,1)}), bf16[32,64,128]{2,1,0:T(8,128)(2,1)S(1)}, u32[]{:S(2)}, u32[]{:S(2)}) async-start(bf16[32,64,128]{2,1,0:T(8,128)(2,1)} %broadcast_in_dim.157), calls=%async_computation.1 | async-start | bytes 1048576 | tf_op jit(solution)/shard_map/all_to_all | solution.py:154
  28.0 1.6 %fusion.15 = (s32[20]{0:T(128)S(1)}, s32[20]{0:T(128)S(1)}, s32[20]{0:T(128)S(1)}, s32[20]{0:T(128)S(1)}) fusion(s32[32,32]{1,0:T(8,128)S(1)} %copy-done.4, s32[20]{0:T(128)S(1)} %iota_add_fusion, s32[32]{0:T(128)S(1)} %copy-done.7), kind=kLoop, calls=%fused_computation.38 | loop fusion | flops 184240 | bytes 4624 | tf_op jit(solution)/shard_map/reduce_sum | solution.py:200
  29.6 0.5 clamp_multiply_fusion
  30.2 0.1 fusion.38
  30.3 0.2 convolution_minimum_fusion.3
  30.5 0.2 convolution_minimum_fusion.2
  30.7 12.3 %all-to-all-done.1 = bf16[32,64,128]{2,1,0:T(8,128)(2,1)S(1)} async-done(((bf16[32,64,128]{2,1,0:T(8,128)(2,1)}), bf16[32,64,128]{2,1,0:T(8,128)(2,1)S(1)}, u32[]{:S(2)}, u32[]{:S(2)}) %all-to-all-start.1) | async-done | bytes 524320 | tf_op jit(solution)/shard_map/all_to_all | solution.py:154
  43.0 1.1 bitcast_select_fusion.q_ref
  44.0 9.4 %shard_map.160 = (f32[32,64,128]{2,1,0:T(8,128)}, f32[32,128]{1,0:T(8,128)}, f32[32,128]{1,0:T(8,128)}) custom-call(s32[20]{0:T(128)} %get-tuple-element.46.owner_ref, s32[20]{0:T(128)} %get-tuple-element.45.filled_ref, bf16[32,128,128]{2,1,0:T(8,128)(2,1)} %bitcast_select_fusion.q_ref, s32[32,128,1]{2,1,0:T(8,128)} %broadcast_in_dim_reshape.11.qv_ref, ...), custom_call_target="tpu_custom_call" | custom-call | tf_op jit(solution)/shard_map/pallas_call | solution.py:126
  53.4 0.7 reduce-precision_convert_fusion.1
  54.2 1.3 %convert_element_type.143 = bf16[32,64,128]{2,1,0:T(8,128)(2,1)S(1)} convert(f32[32,64,128]{2,1,0:T(8,128)} %get-tuple-element.6) | non-fusion elementwise | flops 262144 | bytes 1572864 | tf_op jit(solution)/shard_map/convert_element_type | solution.py:232
  55.5 0.9 pad_maximum_fusion
  56.4 8.2 %all-to-all-start.2 = ((bf16[32,70,128]{2,1,0:T(8,128)(2,1)}), bf16[32,70,128]{2,1,0:T(8,128)(2,1)S(1)}, u32[]{:S(2)}, u32[]{:S(2)}) async-start(bf16[32,70,128]{2,1,0:T(8,128)(2,1)} %pad_maximum_fusion), calls=%async_computation.2 | async-start | bytes 1179648 | tf_op jit(solution)/shard_map/all_to_all | solution.py:235
  64.7 0.2 convolution_minimum_fusion.1
  64.8 0.8 dynamic_slice.10
  65.6 0.2 fusion.9
  65.8 0.1 copy.62
  66.0 0.1 reshape.426
  66.1 0.1 copy.72
  66.2 0.2 select_reduce_fusion.1
  66.5 13.3 %all-to-all-done.2 = bf16[32,70,128]{2,1,0:T(8,128)(2,1)S(1)} async-done(((bf16[32,70,128]{2,1,0:T(8,128)(2,1)}), bf16[32,70,128]{2,1,0:T(8,128)(2,1)S(1)}, u32[]{:S(2)}, u32[]{:S(2)}) %all-to-all-start.2) | async-done | bytes 573472 | tf_op jit(solution)/shard_map/all_to_all | solution.py:235
  80.1 0.1 reshape_squeeze.2
  80.2 0.6 select_reduce_fusion
  80.9 0.2 fusion.11
  81.0 0.1 copy.61
  81.1 0.1 fusion.7
  81.4 0.7 broadcast_in_dim.177
  82.1 8.1 %all-to-all-start.3 = ((bf16[8,64,128]{2,1,0:T(8,128)(2,1)}), bf16[8,64,128]{2,1,0:T(8,128)(2,1)S(1)}, u32[]{:S(2)}, u32[]{:S(2)}) async-start(bf16[8,64,128]{2,1,0:T(8,128)(2,1)} %broadcast_in_dim.177), calls=%async_computation.3 | async-start | bytes 262144 | tf_op jit(solution)/shard_map/all_to_all | solution.py:154
  90.1 5.3 %all-to-all-done.3 = bf16[8,64,128]{2,1,0:T(8,128)(2,1)S(1)} async-done(((bf16[8,64,128]{2,1,0:T(8,128)(2,1)}), bf16[8,64,128]{2,1,0:T(8,128)(2,1)S(1)}, u32[]{:S(2)}, u32[]{:S(2)}) %all-to-all-start.3) | async-done | bytes 131104 | tf_op jit(solution)/shard_map/all_to_all | solution.py:154
  95.4 0.6 fusion.17
  96.0 1.0 copy-done.1
  97.0 0.5 convolution_bitcast_fusion
  97.5 0.9 fusion.1
  98.5 4.1 %all-to-all-start.4 = ((bf16[8,8,1024]{2,1,0:T(8,128)(2,1)}), bf16[8,8,1024]{2,1,0:T(8,128)(2,1)S(1)}, u32[]{:S(2)}, u32[]{:S(2)}) async-start(bf16[8,8,1024]{2,1,0:T(8,128)(2,1)} %fusion.1), calls=%async_computation.4 | async-start | bytes 262144 | tf_op jit(solution)/shard_map/all_to_all | solution.py:306
  102.6 0.8 fusion.10
  103.4 4.5 %all-to-all-done.4 = bf16[8,8,1024]{2,1,0:T(8,128)(2,1)S(1)} async-done(((bf16[8,8,1024]{2,1,0:T(8,128)(2,1)}), bf16[8,8,1024]{2,1,0:T(8,128)(2,1)S(1)}, u32[]{:S(2)}, u32[]{:S(2)}) %all-to-all-start.4) | async-done | bytes 131104 | tf_op jit(solution)/shard_map/all_to_all | solution.py:306
  107.9 0.6 add_convert_fusion
  (48 shorter events, 1.1 us)
Async XLA Ops:
  0.6 94.8 %copy-start = (bf16[1024,1024]{1,0:T(8,128)(2,1)S(1)}, bf16[1024,1024]{1,0:T(8,128)(2,1)}, u32[]{:S(2)}) copy-start(bf16[1024,1024]{1,0:T(8,128)(2,1)} %param.17) | copy-start | bytes 6291460
  0.6 14.8 %copy-start.5 = (s32[20,128]{1,0:T(8,128)S(1)}, s32[20,128]{1,0:T(8,128)}, u32[]{:S(2)}) copy-start(s32[20,128]{1,0:T(8,128)} %param.22) | copy-start | bytes 30724
  0.7 15.6 %copy-start.2 = (bf16[3,1024,128]{2,1,0:T(8,128)(2,1)S(1)}, bf16[3,1024,128]{2,1,0:T(8,128)(2,1)}, u32[]{:S(2)}) copy-start(bf16[3,1024,128]{2,1,0:T(8,128)(2,1)} %param.16) | copy-start | bytes 2359300
  2.2 13.8 %all-to-all-start = ((bf16[8,8,1024]{2,1,0:T(8,128)(2,1)}), bf16[8,8,1024]{2,1,0:T(8,128)(2,1)S(1)}, u32[]{:S(2)}, u32[]{:S(2)}) async-start(bf16[8,8,1024]{2,1,0:T(8,128)(2,1)} %broadcast_in_dim.152), calls=%async_computation | async-start | bytes 262144 | tf_op jit(solution)/shard_map/all_to_all | solution.py:154
  11.9 16.1 %copy-start.4 = (s32[32,32]{1,0:T(8,128)S(1)}, s32[32,32]{1,0:T(8,128)}, u32[]{:S(2)}) copy-start(s32[32,32]{1,0:T(8,128)} %param.25) | copy-start | bytes 12292
  11.9 16.1 %copy-start.7 = (s32[32]{0:T(128)S(1)}, s32[32]{0:T(128)}, u32[]{:S(2)}) copy-start(s32[32]{0:T(128)} %param.24) | copy-start | bytes 388
  11.9 18.3 %copy-start.6 = (s32[1,64]{1,0:T(1,128)S(1)}, s32[1,64]{1,0:T(1,128)}, u32[]{:S(2)}) copy-start(s32[1,64]{1,0:T(1,128)} %param.26) | copy-start | bytes 772
  17.5 25.5 %all-to-all-start.1 = ((bf16[32,64,128]{2,1,0:T(8,128)(2,1)}), bf16[32,64,128]{2,1,0:T(8,128)(2,1)S(1)}, u32[]{:S(2)}, u32[]{:S(2)}) async-start(bf16[32,64,128]{2,1,0:T(8,128)(2,1)} %broadcast_in_dim.157), calls=%async_computation.1 | async-start | bytes 1048576 | tf_op jit(solution)/shard_map/all_to_all | solution.py:154
  56.4 23.3 %all-to-all-start.2 = ((bf16[32,70,128]{2,1,0:T(8,128)(2,1)}), bf16[32,70,128]{2,1,0:T(8,128)(2,1)S(1)}, u32[]{:S(2)}, u32[]{:S(2)}) async-start(bf16[32,70,128]{2,1,0:T(8,128)(2,1)} %pad_maximum_fusion), calls=%async_computation.2 | async-start | bytes 1179648 | tf_op jit(solution)/shard_map/all_to_all | solution.py:235
  81.4 16.1 %copy-start.3 = (bf16[64,128]{1,0:T(8,128)(2,1)}, bf16[64,128]{1,0:T(8,128)(2,1)S(1)}, u32[]{:S(2)}) copy-start(bf16[64,128]{1,0:T(8,128)(2,1)S(1)} %copy.67) | copy-start | bytes 49156
  82.1 13.4 %all-to-all-start.3 = ((bf16[8,64,128]{2,1,0:T(8,128)(2,1)}), bf16[8,64,128]{2,1,0:T(8,128)(2,1)S(1)}, u32[]{:S(2)}, u32[]{:S(2)}) async-start(bf16[8,64,128]{2,1,0:T(8,128)(2,1)} %broadcast_in_dim.177), calls=%async_computation.3 | async-start | bytes 262144 | tf_op jit(solution)/shard_map/all_to_all | solution.py:154
  95.4 1.6 %copy-start.1 = (bf16[2,1024,512]{2,1,0:T(8,128)(2,1)S(1)}, bf16[2,1024,512]{2,1,0:T(8,128)(2,1)}, u32[]{:S(2)}) copy-start(bf16[2,1024,512]{2,1,0:T(8,128)(2,1)} %param.18) | copy-start | bytes 6291460
  95.4 2.1 %copy-start.8 = (bf16[512,1024]{1,0:T(8,128)(2,1)S(1)}, bf16[512,1024]{1,0:T(8,128)(2,1)}, u32[]{:S(2)}) copy-start(bf16[512,1024]{1,0:T(8,128)(2,1)} %param.19) | copy-start | bytes 3145732
  96.0 6.6 %copy-start.9 = (s32[1,8]{1,0:T(1,128)S(1)}, s32[1,8]{1,0:T(1,128)}, u32[]{:S(2)}) copy-start(s32[1,8]{1,0:T(1,128)} %param.27) | copy-start | bytes 100
  98.5 9.4 %all-to-all-start.4 = ((bf16[8,8,1024]{2,1,0:T(8,128)(2,1)}), bf16[8,8,1024]{2,1,0:T(8,128)(2,1)S(1)}, u32[]{:S(2)}, u32[]{:S(2)}) async-start(bf16[8,8,1024]{2,1,0:T(8,128)(2,1)} %fusion.1), calls=%async_computation.4 | async-start | bytes 262144 | tf_op jit(solution)/shard_map/all_to_all | solution.py:306

commit v10 on v9

--- a/solution.py
+++ b/solution.py
@@ -35,18 +35,26 @@
     )
 
 
-def page_kernel(owner_ref, filled_ref, q_ref, qv_ref, cache_ref, pv_ref, bias_ref,
-                out_ref, total_ref, max_ref, max_acc, total_acc,
+def page_kernel(owner_ref, filled_ref, q_ref, aux_ref, cache_ref, pv_ref,
+                out_ref, total_ref, max_ref, out_acc, max_acc, total_acc,
                 *, head_local, tree, scale, pool):
     rows, page = q_ref.shape[1], cache_ref.shape[2]
-    out_ref[...] = jnp.zeros(out_ref.shape, jnp.float32)
+    lanes = aux_ref.shape[0]
+    out_acc[...] = jnp.zeros(out_acc.shape, jnp.float32)
     max_acc[...] = jnp.full(max_acc.shape, masked_score, jnp.float32)
     total_acc[...] = jnp.zeros(total_acc.shape, jnp.float32)
     request_lane = lax.broadcasted_iota(jnp.int32, max_acc.shape, 1)
-    column_head = lax.broadcasted_iota(jnp.int32, out_ref.shape[1:], 1) // HD
+    column_head = lax.broadcasted_iota(jnp.int32, out_acc.shape[1:], 1) // HD
+    aux_columns = jnp.transpose(aux_ref[...])
+
+    def column_of(index):
+        return jnp.sum(jnp.where(request_lane == index, aux_columns, 0.0), axis=1, keepdims=True)
+
+    same_bias = column_of(lanes - 2)
+    other_bias = column_of(lanes - 1)
 
     def pick_heads(values):
-        picked = jnp.zeros(out_ref.shape[1:], jnp.float32)
+        picked = jnp.zeros(out_acc.shape[1:], jnp.float32)
         for head in range(head_local):
             picked = picked + jnp.where(
                 column_head == head, values[head * tree : (head + 1) * tree], 0.0
@@ -59,13 +67,13 @@
         @pl.when(count > 0)
         def _():
             row = owner_ref[step]
-            same = qv_ref[row] == pv_ref[step]
+            same = column_of(row) == pv_ref[step]
             valid = lax.broadcasted_iota(jnp.int32, (rows, page), 1) < count
             scores = lax.dot_general(
                 q_ref[row], cache_ref[0, step], (((1,), (1,)), ((), ())),
                 preferred_element_type=jnp.float32,
             ) * scale
-            scores = scores + jnp.where(same, bias_ref[0], bias_ref[1])
+            scores = scores + jnp.where(same, same_bias, other_bias)
             block_max = jnp.max(jnp.where(valid, scores, masked_score), axis=1, keepdims=True)
             weights = jnp.where(valid, jnp.exp(scores - block_max), 0.0).astype(jnp.bfloat16)
             block_total = jnp.sum(weights.astype(jnp.float32), axis=1, keepdims=True)
@@ -80,7 +88,7 @@
             total_acc[...] = jnp.where(
                 is_row, old_total * keep_old + block_total * keep_new, total_acc[...]
             )
-            out_ref[row] = out_ref[row] * pick_heads(
+            out_acc[row] = out_acc[row] * pick_heads(
                 jnp.broadcast_to(keep_old, crossed.shape)
             ) + pick_heads(crossed * keep_new)
 
@@ -88,6 +96,7 @@
 
     lax.fori_loop(0, pool, one_page, 0)
     requests = out_ref.shape[0]
+    out_ref[...] = out_acc[...].astype(out_ref.dtype)
     total_ref[...] = jnp.transpose(total_acc[...])[:requests]
     max_ref[...] = jnp.transpose(max_acc[...])[:requests]
 
@@ -98,7 +107,15 @@
     pool, page = page_variates.shape
     head_local = qdl // HD
     tree = rows // head_local
-    lanes = 128 * ((requests + 127) // 128)
+    lanes = 128 * ((requests + 2 + 127) // 128)
+    aux = jnp.concatenate(
+        [
+            row_variates.astype(jnp.float32),
+            jnp.zeros((lanes - requests - 2, rows), jnp.float32),
+            row_bias,
+        ],
+        axis=0,
+    )
     kernel = functools.partial(
         page_kernel, head_local=head_local, tree=tree, scale=1.0 / math.sqrt(HD), pool=pool
     )
@@ -111,30 +128,32 @@
         grid=(1,),
         in_specs=[
             whole((requests, rows, qdl)),
-            whole((requests, rows, 1)),
+            whole((lanes, rows)),
             whole(page_cache.shape),
             whole((pool, 1, page)),
-            whole((2, rows, 1)),
         ],
         out_specs=[
             whole((requests, tree, qdl)),
             whole((requests, rows)),
             whole((requests, rows)),
         ],
-        scratch_shapes=[pltpu.VMEM((rows, lanes), jnp.float32)] * 2,
+        scratch_shapes=[
+            pltpu.VMEM((requests, tree, qdl), jnp.float32),
+            pltpu.VMEM((rows, lanes), jnp.float32),
+            pltpu.VMEM((rows, lanes), jnp.float32),
+        ],
     )
     return pl.pallas_call(
         kernel,
         grid_spec=grid_spec,
         out_shape=[
-            jax.ShapeDtypeStruct((requests, tree, qdl), jnp.float32),
+            jax.ShapeDtypeStruct((requests, tree, qdl), jnp.bfloat16),
             jax.ShapeDtypeStruct((requests, rows), jnp.float32),
             jax.ShapeDtypeStruct((requests, rows), jnp.float32),
         ],
         compiler_params=pltpu.CompilerParams(dimension_semantics=("arbitrary",)),
         interpret=interpret,
-    )(owner, filled, split_queries, row_variates[..., None], page_cache,
-      page_variates[:, None, :], row_bias[..., None])
+    )(owner, filled, split_queries, aux, page_cache, page_variates[:, None, :])
 
 
 def split_three(values):

time: 110 us -> 107 us (0.973)
  local copies, waits for them, and re-layouts: 13.2 us -> 7.07 us
  waiting for transfers between devices: 35.3 us -> 37.8 us
  Pallas kernels: 9.38 us -> 8.05 us
  other arithmetic: 8.14 us -> 9.38 us
  matrix products: 4.07 us -> 5.2 us
    another operation x5 -> x3, local copies, waits for them, and re-layouts: 4.58 us -> 0.28 us  [the longest x1 3.51 us: page_attention(): row_variates[..., None]]
    all_to_all x3, waiting for transfers between devices: 17.5 us -> 19.1 us  [gather_rows(): return lax.all_to_all(spread, axis_name, 0, 0, tiled=True)]
    pallas_call x1, Pallas kernels: 9.38 us -> 8.05 us  [page_attention(): pl.pallas_call(kernel, grid_spec=grid_spec, out_shape=[jax.ShapeDtypeStru...]
    convert_element_type x1, other arithmetic: 1.3 us -> 0.01 us  [page_attention(): row_variates.astype(jnp.float32)]
    all_to_all x3, starting transfers between devices: 25.1 us -> 23.8 us  [gather_rows(): return lax.all_to_all(spread, axis_name, 0, 0, tiled=True)]
    dot_general x1, matrix products: 0.29 us -> 1.42 us  [shards(): jnp.einsum('td,cdq->ctq', normed, qkv_weight, preferred_element_type=jnp....]
  transfers between devices with their start and end apart: 5 -> 5, of which waited for: 4 -> 5; matrix products, arithmetic and copies ran while one was open for 11% -> 7% of each run, Pallas kernels for 0% -> 0%
where the time goes in v10:
time: 107 us; the launch traced here: 105 us
  waiting for transfers between devices  37.8 us (35%)
  starting transfers between devices  37 us (35%)
  other arithmetic  9.38 us (9%)
  Pallas kernels  8.05 us (8%)
  local copies, waits for them, and re-layouts  7.07 us (7%)
  matrix products  5.2 us (5%)
    all_to_all x3, starting transfers between devices, gather_rows(): return lax.all_to_all(spread, axis_name, 0, 0, tiled=True)  23.8 us
    all_to_all x3, waiting for transfers between devices, gather_rows(): return lax.all_to_all(spread, axis_name, 0, 0, tiled=True)  19.1 us
    all_to_all x1, waiting for transfers between devices, shards(): lax.all_to_all(packed, 'req', split_axis=0, concat_axis=0, tiled=True)  14.2 us
    all_to_all x1, starting transfers between devices, shards(): lax.all_to_all(packed, 'req', split_axis=0, concat_axis=0, tiled=True)  9.1 us
    pallas_call x1, Pallas kernels, page_attention(): pl.pallas_call(kernel, grid_spec=grid_spec, out_shape=[jax.ShapeDtypeStru...  8.05 us
    all_to_all x1, waiting for transfers between devices, shards(): lax.all_to_all(down_part.reshape(head_parts, own_rows, -1), 'head', 0, 0,...  4.48 us
    all_to_all x1, starting transfers between devices, shards(): lax.all_to_all(down_part.reshape(head_parts, own_rows, -1), 'head', 0, 0,...  4.13 us
    broadcast_in_dim x4, local copies, waits for them, and re-layouts, gather_rows(): spread = jnp.broadcast_to(rows[None], (parts,) + rows.shape)  3.15 us
  transfers between devices with their start and end apart: 5, of which 5 were waited for; matrix products, arithmetic and copies ran while one was open for 7% of the time, Pallas kernels for 0%

profile of v10, /device:TPU:1, one launch (start us, length us, event | category | flops | bytes accessed | tf_op | source)
XLA Modules:
  0.0 105.5 jit_solution(9046106253819923591)
XLA Ops:
  0.7 1.5 %broadcast_in_dim.153 = bf16[8,8,1024]{2,1,0:T(8,128)(2,1)} broadcast(bf16[8,1024]{1,0:T(8,128)(2,1)} %param.14), dimensions={1,2} | broadcast | bytes 147456 | tf_op jit(solution)/shard_map/broadcast_in_dim | solution.py:172
  2.2 6.5 %all-to-all-start = ((bf16[8,8,1024]{2,1,0:T(8,128)(2,1)}), bf16[8,8,1024]{2,1,0:T(8,128)(2,1)S(1)}, u32[]{:S(2)}, u32[]{:S(2)}) async-start(bf16[8,8,1024]{2,1,0:T(8,128)(2,1)} %broadcast_in_dim.153), calls=%async_computation | async-start | bytes 262144 | tf_op jit(solution)/shard_map/all_to_all | solution.py:173
  8.7 0.8 fusion.55
  9.5 2.3 %fusion.15 = (s32[20]{0:T(128)S(1)}, s32[20]{0:T(128)S(1)}, s32[20]{0:T(128)S(1)}, s32[20]{0:T(128)S(1)}) fusion(s32[32,32]{1,0:T(8,128)} %param.25, s32[20]{0:T(128)S(1)} %iota_add_fusion, s32[32]{0:T(128)} %param.24), kind=kLoop, calls=%fused_computation.38 | loop fusion | flops 184240 | bytes 4624 | tf_op jit(solution)/shard_map/reduce_sum | solution.py:219
  11.8 0.6 clamp_multiply_fusion
  12.4 1.5 %all-to-all-done = bf16[8,8,1024]{2,1,0:T(8,128)(2,1)S(1)} async-done(((bf16[8,8,1024]{2,1,0:T(8,128)(2,1)}), bf16[8,8,1024]{2,1,0:T(8,128)(2,1)S(1)}, u32[]{:S(2)}, u32[]{:S(2)}) %all-to-all-start) | async-done | bytes 131104 | tf_op jit(solution)/shard_map/all_to_all | solution.py:173
  13.9 0.1 fusion.22
  14.1 1.4 %fusion.8 = bf16[3,64,128]{2,1,0:T(8,128)(2,1)S(1)} fusion(bf16[3,1024,128]{2,1,0:T(8,128)(2,1)} %param.16, bf16[8,8,1024]{2,1,0:T(8,128)(2,1)S(1)} %all-to-all-done, f32[1024]{0:T(1024)S(1)} %bitcast.166, f32[64]{0:T(128)S(1)} %rsqrt.20), kind=kOutput, calls=%fused_computation.15 | convolution fusion | flops 50618368 | bytes 971008 | tf_op jit(solution)/shard_map/td,cdq->ctq/dot_general | solution.py:206
  15.6 0.9 broadcast_in_dim.158
  16.5 10.5 %all-to-all-start.1 = ((bf16[32,64,128]{2,1,0:T(8,128)(2,1)}), bf16[32,64,128]{2,1,0:T(8,128)(2,1)S(1)}, u32[]{:S(2)}, u32[]{:S(2)}) async-start(bf16[32,64,128]{2,1,0:T(8,128)(2,1)} %broadcast_in_dim.158), calls=%async_computation.1 | async-start | bytes 1048576 | tf_op jit(solution)/shard_map/all_to_all | solution.py:173
  27.2 0.1 reshape.429
  27.3 0.6 broadcast_in_dim.165.pv_ref
  27.9 0.1 convert_element_type.152
  28.1 0.1 fusion.38
  28.3 0.7 pad_maximum_fusion.1.aux_ref
  29.0 0.2 convolution_minimum_fusion.3
  29.1 0.2 convolution_minimum_fusion.2
  29.3 12.3 %all-to-all-done.1 = bf16[32,64,128]{2,1,0:T(8,128)(2,1)S(1)} async-done(((bf16[32,64,128]{2,1,0:T(8,128)(2,1)}), bf16[32,64,128]{2,1,0:T(8,128)(2,1)S(1)}, u32[]{:S(2)}, u32[]{:S(2)}) %all-to-all-start.1) | async-done | bytes 524320 | tf_op jit(solution)/shard_map/all_to_all | solution.py:173
  41.6 1.1 %bitcast_select_fusion.q_ref = bf16[32,128,128]{2,1,0:T(8,128)(2,1)} fusion(pred[128,128]{1,0:T(8,128)(4,1)S(1)} %bitcast.161, bf16[32,64,128]{2,1,0:T(8,128)(2,1)S(1)} %all-to-all-done.1), kind=kLoop, calls=%fused_computation.25 | loop fusion | flops 524288 | bytes 1589248 | tf_op jit(solution)/shard_map/jit(_where)/select_n | solution.py:229
  42.6 8.0 %shard_map.160 = (bf16[32,64,128]{2,1,0:T(8,128)(2,1)}, f32[32,128]{1,0:T(8,128)}, f32[32,128]{1,0:T(8,128)}) custom-call(s32[20]{0:T(128)} %get-tuple-element.46.owner_ref, s32[20]{0:T(128)} %get-tuple-element.45.filled_ref, bf16[32,128,128]{2,1,0:T(8,128)(2,1)} %bitcast_select_fusion.q_ref, f32[128,128]{1,0:T(8,128)} %pad_maximum_fusion.1.aux_ref, ...), custom_call_target="tpu_custom_call" | custom-call | tf_op jit(solution)/shard_map/pallas_call | solution.py:146
  50.7 0.7 reduce-precision_convert_fusion.1
  51.5 1.9 %pad_maximum_fusion = bf16[32,70,128]{2,1,0:T(8,128)(2,1)} fusion(bf16[32,2,128]{2,1,0:T(2,128)(2,1)S(1)} %copy.54, bf16[32,2,128]{2,1,0:T(2,128)(2,1)S(1)} %copy.53, bf16[32,2,128]{2,1,0:T(2,128)(2,1)S(1)} %copy.52, bf16[32,64,128]{2,1,0:T(8,128)(2,1)} %get-tuple-element.6), kind=kLoop, calls=%fused_computation.26 | loop fusion | flops 2293760 | bytes 1146880 | tf_op jit(solution)/shard_map/concatenate | solution.py:250
  53.4 9.1 %all-to-all-start.2 = ((bf16[32,70,128]{2,1,0:T(8,128)(2,1)}), bf16[32,70,128]{2,1,0:T(8,128)(2,1)S(1)}, u32[]{:S(2)}, u32[]{:S(2)}) async-start(bf16[32,70,128]{2,1,0:T(8,128)(2,1)} %pad_maximum_fusion), calls=%async_computation.2 | async-start | bytes 1179648 | tf_op jit(solution)/shard_map/all_to_all | solution.py:254
  62.6 0.2 convolution_minimum_fusion.1
  62.8 0.2 fusion.9
  63.0 0.1 copy.56
  63.2 0.1 reshape.432
  63.2 0.1 copy.66
  63.4 0.1 reshape.433
  63.5 0.2 select_reduce_fusion.1
  63.7 14.2 %all-to-all-done.2 = bf16[32,70,128]{2,1,0:T(8,128)(2,1)S(1)} async-done(((bf16[32,70,128]{2,1,0:T(8,128)(2,1)}), bf16[32,70,128]{2,1,0:T(8,128)(2,1)S(1)}, u32[]{:S(2)}, u32[]{:S(2)}) %all-to-all-start.2) | async-done | bytes 573472 | tf_op jit(solution)/shard_map/all_to_all | solution.py:254
  78.3 0.1 reshape_squeeze.2
  78.4 0.6 select_reduce_fusion
  79.0 0.2 fusion.11
  79.2 0.1 copy.55
  79.3 0.1 fusion.7
  79.5 0.1 copy.61
  79.6 0.7 broadcast_in_dim.178
  80.2 6.8 %all-to-all-start.3 = ((bf16[8,64,128]{2,1,0:T(8,128)(2,1)}), bf16[8,64,128]{2,1,0:T(8,128)(2,1)S(1)}, u32[]{:S(2)}, u32[]{:S(2)}) async-start(bf16[8,64,128]{2,1,0:T(8,128)(2,1)} %broadcast_in_dim.178), calls=%async_computation.3 | async-start | bytes 262144 | tf_op jit(solution)/shard_map/all_to_all | solution.py:173
  87.1 5.3 %all-to-all-done.3 = bf16[8,64,128]{2,1,0:T(8,128)(2,1)S(1)} async-done(((bf16[8,64,128]{2,1,0:T(8,128)(2,1)}), bf16[8,64,128]{2,1,0:T(8,128)(2,1)S(1)}, u32[]{:S(2)}, u32[]{:S(2)}) %all-to-all-start.3) | async-done | bytes 131104 | tf_op jit(solution)/shard_map/all_to_all | solution.py:173
  92.3 0.6 fusion.17
  93.0 1.0 copy-done.1
  93.9 0.5 convolution_bitcast_fusion
  94.5 0.9 fusion.1
  95.4 4.1 %all-to-all-start.4 = ((bf16[8,8,1024]{2,1,0:T(8,128)(2,1)}), bf16[8,8,1024]{2,1,0:T(8,128)(2,1)S(1)}, u32[]{:S(2)}, u32[]{:S(2)}) async-start(bf16[8,8,1024]{2,1,0:T(8,128)(2,1)} %fusion.1), calls=%async_computation.4 | async-start | bytes 262144 | tf_op jit(solution)/shard_map/all_to_all | solution.py:325
  99.5 0.8 fusion.10
  100.3 4.5 %all-to-all-done.4 = bf16[8,8,1024]{2,1,0:T(8,128)(2,1)S(1)} async-done(((bf16[8,8,1024]{2,1,0:T(8,128)(2,1)}), bf16[8,8,1024]{2,1,0:T(8,128)(2,1)S(1)}, u32[]{:S(2)}, u32[]{:S(2)}) %all-to-all-start.4) | async-done | bytes 131104 | tf_op jit(solution)/shard_map/all_to_all | solution.py:325
  104.8 0.6 add_convert_fusion
  (49 shorter events, 1.2 us)
Async XLA Ops:
  0.6 91.7 %copy-start = (bf16[1024,1024]{1,0:T(8,128)(2,1)S(1)}, bf16[1024,1024]{1,0:T(8,128)(2,1)}, u32[]{:S(2)}) copy-start(bf16[1024,1024]{1,0:T(8,128)(2,1)} %param.17) | copy-start | bytes 6291460
  0.6 26.3 %copy-start.5 = (f32[2,16]{1,0:T(2,128)S(1)}, f32[2,16]{1,0:T(2,128)}, u32[]{:S(2)}) copy-start(f32[2,16]{1,0:T(2,128)} %param.20) | copy-start | bytes 388
  0.7 26.6 %copy-start.4 = (s32[2048]{0:T(1024)S(1)}, s32[2048]{0:T(1024)}, u32[]{:S(2)}) copy-start(s32[2048]{0:T(1024)} %param.23) | copy-start | bytes 24580
  0.7 26.7 %copy-start.3 = (s32[20,128]{1,0:T(8,128)S(1)}, s32[20,128]{1,0:T(8,128)}, u32[]{:S(2)}) copy-start(s32[20,128]{1,0:T(8,128)} %param.22) | copy-start | bytes 30724
  0.7 27.4 %copy-start.6 = (s32[1,64]{1,0:T(1,128)S(1)}, s32[1,64]{1,0:T(1,128)}, u32[]{:S(2)}) copy-start(s32[1,64]{1,0:T(1,128)} %param.26) | copy-start | bytes 772
  2.2 11.7 %all-to-all-start = ((bf16[8,8,1024]{2,1,0:T(8,128)(2,1)}), bf16[8,8,1024]{2,1,0:T(8,128)(2,1)S(1)}, u32[]{:S(2)}, u32[]{:S(2)}) async-start(bf16[8,8,1024]{2,1,0:T(8,128)(2,1)} %broadcast_in_dim.153), calls=%async_computation | async-start | bytes 262144 | tf_op jit(solution)/shard_map/all_to_all | solution.py:173
  16.5 25.1 %all-to-all-start.1 = ((bf16[32,64,128]{2,1,0:T(8,128)(2,1)}), bf16[32,64,128]{2,1,0:T(8,128)(2,1)S(1)}, u32[]{:S(2)}, u32[]{:S(2)}) async-start(bf16[32,64,128]{2,1,0:T(8,128)(2,1)} %broadcast_in_dim.158), calls=%async_computation.1 | async-start | bytes 1048576 | tf_op jit(solution)/shard_map/all_to_all | solution.py:173
  53.4 24.5 %all-to-all-start.2 = ((bf16[32,70,128]{2,1,0:T(8,128)(2,1)}), bf16[32,70,128]{2,1,0:T(8,128)(2,1)S(1)}, u32[]{:S(2)}, u32[]{:S(2)}) async-start(bf16[32,70,128]{2,1,0:T(8,128)(2,1)} %pad_maximum_fusion), calls=%async_computation.2 | async-start | bytes 1179648 | tf_op jit(solution)/shard_map/all_to_all | solution.py:254
  79.6 14.9 %copy-start.2 = (bf16[64,128]{1,0:T(8,128)(2,1)}, bf16[64,128]{1,0:T(8,128)(2,1)S(1)}, u32[]{:S(2)}) copy-start(bf16[64,128]{1,0:T(8,128)(2,1)S(1)} %copy.61) | copy-start | bytes 49156
  80.2 12.1 %all-to-all-start.3 = ((bf16[8,64,128]{2,1,0:T(8,128)(2,1)}), bf16[8,64,128]{2,1,0:T(8,128)(2,1)S(1)}, u32[]{:S(2)}, u32[]{:S(2)}) async-start(bf16[8,64,128]{2,1,0:T(8,128)(2,1)} %broadcast_in_dim.178), calls=%async_computation.3 | async-start | bytes 262144 | tf_op jit(solution)/shard_map/all_to_all | solution.py:173
  92.3 1.6 %copy-start.1 = (bf16[2,1024,512]{2,1,0:T(8,128)(2,1)S(1)}, bf16[2,1024,512]{2,1,0:T(8,128)(2,1)}, u32[]{:S(2)}) copy-start(bf16[2,1024,512]{2,1,0:T(8,128)(2,1)} %param.18) | copy-start | bytes 6291460
  92.3 2.1 %copy-start.7 = (bf16[512,1024]{1,0:T(8,128)(2,1)S(1)}, bf16[512,1024]{1,0:T(8,128)(2,1)}, u32[]{:S(2)}) copy-start(bf16[512,1024]{1,0:T(8,128)(2,1)} %param.19) | copy-start | bytes 3145732
  92.9 6.6 %copy-start.8 = (s32[1,8]{1,0:T(1,128)S(1)}, s32[1,8]{1,0:T(1,128)}, u32[]{:S(2)}) copy-start(s32[1,8]{1,0:T(1,128)} %param.27) | copy-start | bytes 100
  95.4 9.4 %all-to-all-start.4 = ((bf16[8,8,1024]{2,1,0:T(8,128)(2,1)}), bf16[8,8,1024]{2,1,0:T(8,128)(2,1)S(1)}, u32[]{:S(2)}, u32[]{:S(2)}) async-start(bf16[8,8,1024]{2,1,0:T(8,128)(2,1)} %fusion.1), calls=%async_computation.4 | async-start | bytes 262144 | tf_op jit(solution)/shard_map/all_to_all | solution.py:325

commit v11 on v10

--- a/solution.py
+++ b/solution.py
@@ -36,7 +36,7 @@
 
 
 def page_kernel(owner_ref, filled_ref, q_ref, aux_ref, cache_ref, pv_ref,
-                out_ref, total_ref, max_ref, out_acc, max_acc, total_acc,
+                out_ref, out_acc, max_acc, total_acc,
                 *, head_local, tree, scale, pool):
     rows, page = q_ref.shape[1], cache_ref.shape[2]
     lanes = aux_ref.shape[0]
@@ -96,9 +96,16 @@
 
     lax.fori_loop(0, pool, one_page, 0)
     requests = out_ref.shape[0]
-    out_ref[...] = out_acc[...].astype(out_ref.dtype)
-    total_ref[...] = jnp.transpose(total_acc[...])[:requests]
-    max_ref[...] = jnp.transpose(max_acc[...])[:requests]
+    out_ref[:, :tree, :] = out_acc[...].astype(out_ref.dtype)
+    stats = (
+        jnp.transpose(total_acc[...])[:requests],
+        jnp.transpose(max_acc[...])[:requests],
+    )
+    for kind, values in enumerate(stats):
+        for part in range(3):
+            rounded = values.astype(out_ref.dtype)
+            out_ref[:, tree + 2 * part + kind, :] = rounded
+            values = values - rounded.astype(jnp.float32)
 
 
 def page_attention(owner, filled, split_queries, row_variates, page_cache, page_variates,
@@ -132,11 +139,7 @@
             whole(page_cache.shape),
             whole((pool, 1, page)),
         ],
-        out_specs=[
-            whole((requests, tree, qdl)),
-            whole((requests, rows)),
-            whole((requests, rows)),
-        ],
+        out_specs=whole((requests, tree + 6, qdl)),
         scratch_shapes=[
             pltpu.VMEM((requests, tree, qdl), jnp.float32),
             pltpu.VMEM((rows, lanes), jnp.float32),
@@ -146,22 +149,10 @@
     return pl.pallas_call(
         kernel,
         grid_spec=grid_spec,
-        out_shape=[
-            jax.ShapeDtypeStruct((requests, tree, qdl), jnp.bfloat16),
-            jax.ShapeDtypeStruct((requests, rows), jnp.float32),
-            jax.ShapeDtypeStruct((requests, rows), jnp.float32),
-        ],
+        out_shape=jax.ShapeDtypeStruct((requests, tree + 6, qdl), jnp.bfloat16),
         compiler_params=pltpu.CompilerParams(dimension_semantics=("arbitrary",)),
         interpret=interpret,
     )(owner, filled, split_queries, aux, page_cache, page_variates[:, None, :])
-
-
-def split_three(values):
-    high = lax.reduce_precision(values, exponent_bits=8, mantissa_bits=7)
-    rest = values - high
-    middle = lax.reduce_precision(rest, exponent_bits=8, mantissa_bits=7)
-    low = rest - middle
-    return [part.astype(jnp.bfloat16) for part in (high, middle, low)]
 
 
 def join_three(high, middle, low):
@@ -237,7 +228,7 @@
     row_bias = jnp.broadcast_to(bias_local[:, :, None], (2, head_local, tree)).reshape(
         2, split_rows
     )
-    request_out, request_total, request_max = page_attention(
+    packed = page_attention(
         jnp.clip(owner, 0, requests - 1),
         filled,
         split_queries,
@@ -245,11 +236,6 @@
         page_cache,
         page_variates,
         row_bias,
-    )
-    stats = jnp.stack([request_total, request_max], axis=1)
-    packed = jnp.concatenate(
-        [request_out.astype(jnp.bfloat16).reshape(requests, tree, qdl)] + split_three(stats),
-        axis=1,
     )
     received = lax.all_to_all(packed, "req", split_axis=0, concat_axis=0, tiled=True)
     sources = lax.axis_size("req")

time: 107 us -> 103 us (0.963)
  other arithmetic: 9.38 us -> 6.61 us
  waiting for transfers between devices: 37.8 us -> 36.2 us
  starting transfers between devices: 37 us -> 38.1 us
    all_to_all x3, starting transfers between devices: 23.8 us -> 26.5 us  [gather_rows(): return lax.all_to_all(spread, axis_name, 0, 0, tiled=True)]
    concatenate x1 -> x0, other arithmetic: 1.94 us -> none  [shards(): jnp.concatenate([request_out.astype(jnp.bfloat16).reshape(requests, tree,...]
    all_to_all x1, starting transfers between devices: 9.1 us -> 7.38 us  [shards(): lax.all_to_all(packed, 'req', split_axis=0, concat_axis=0, tiled=True)]
    all_to_all x1, waiting for transfers between devices: 14.2 us -> 12.6 us  [shards(): lax.all_to_all(packed, 'req', split_axis=0, concat_axis=0, tiled=True)]
  transfers between devices with their start and end apart: 5 -> 5, of which waited for: 5 -> 5; matrix products, arithmetic and copies ran while one was open for 7% -> 8% of each run, Pallas kernels for 0% -> 0%
where the time goes in v11:
time: 103 us; the launch traced here: 102 us
  starting transfers between devices  38.1 us (37%)
  waiting for transfers between devices  36.2 us (35%)
  Pallas kernels  7.89 us (8%)
  local copies, waits for them, and re-layouts  7.03 us (7%)
  other arithmetic  6.61 us (6%)
  matrix products  5.2 us (5%)
    all_to_all x3, starting transfers between devices, gather_rows(): return lax.all_to_all(spread, axis_name, 0, 0, tiled=True)  26.5 us
    all_to_all x3, waiting for transfers between devices, gather_rows(): return lax.all_to_all(spread, axis_name, 0, 0, tiled=True)  19.1 us
    all_to_all x1, waiting for transfers between devices, shards(): lax.all_to_all(packed, 'req', split_axis=0, concat_axis=0, tiled=True)  12.6 us
    pallas_call x1, Pallas kernels, page_attention(): pl.pallas_call(kernel, grid_spec=grid_spec, out_shape=jax.ShapeDtypeStruc...  7.89 us
    all_to_all x1, starting transfers between devices, shards(): lax.all_to_all(packed, 'req', split_axis=0, concat_axis=0, tiled=True)  7.38 us
    all_to_all x1, waiting for transfers between devices, shards(): lax.all_to_all(down_part.reshape(head_parts, own_rows, -1), 'head', 0, 0,...  4.48 us
    all_to_all x1, starting transfers between devices, shards(): lax.all_to_all(down_part.reshape(head_parts, own_rows, -1), 'head', 0, 0,...  4.14 us
    broadcast_in_dim x4, local copies, waits for them, and re-layouts, gather_rows(): spread = jnp.broadcast_to(rows[None], (parts,) + rows.shape)  3.15 us
  transfers between devices with their start and end apart: 5, of which 5 were waited for; matrix products, arithmetic and copies ran while one was open for 8% of the time, Pallas kernels for 0%

profile of v11, /device:TPU:1, one launch (start us, length us, event | category | flops | bytes accessed | tf_op | source)
XLA Modules:
  0.0 101.9 jit_solution(1765925329382146715)
XLA Ops:
  0.7 1.5 %broadcast_in_dim.153 = bf16[8,8,1024]{2,1,0:T(8,128)(2,1)} broadcast(bf16[8,1024]{1,0:T(8,128)(2,1)} %param.14), dimensions={1,2} | broadcast | bytes 147456 | tf_op jit(solution)/shard_map/broadcast_in_dim | solution.py:163
  2.2 6.5 %all-to-all-start = ((bf16[8,8,1024]{2,1,0:T(8,128)(2,1)}), bf16[8,8,1024]{2,1,0:T(8,128)(2,1)S(1)}, u32[]{:S(2)}, u32[]{:S(2)}) async-start(bf16[8,8,1024]{2,1,0:T(8,128)(2,1)} %broadcast_in_dim.153), calls=%async_computation | async-start | bytes 262144 | tf_op jit(solution)/shard_map/all_to_all | solution.py:164
  8.7 0.8 fusion.54
  9.5 2.3 %fusion.15 = (s32[20]{0:T(128)S(1)}, s32[20]{0:T(128)S(1)}, s32[20]{0:T(128)S(1)}, s32[20]{0:T(128)S(1)}) fusion(s32[32,32]{1,0:T(8,128)} %param.25, s32[20]{0:T(128)S(1)} %iota_add_fusion, s32[32]{0:T(128)} %param.24), kind=kLoop, calls=%fused_computation.37 | loop fusion | flops 184240 | bytes 4624 | tf_op jit(solution)/shard_map/reduce_sum | solution.py:210
  11.8 0.5 clamp_multiply_fusion
  12.3 1.6 %all-to-all-done = bf16[8,8,1024]{2,1,0:T(8,128)(2,1)S(1)} async-done(((bf16[8,8,1024]{2,1,0:T(8,128)(2,1)}), bf16[8,8,1024]{2,1,0:T(8,128)(2,1)S(1)}, u32[]{:S(2)}, u32[]{:S(2)}) %all-to-all-start) | async-done | bytes 131104 | tf_op jit(solution)/shard_map/all_to_all | solution.py:164
  13.9 0.1 fusion.22
  14.0 0.1 rsqrt.20
  14.1 1.4 %fusion.8 = bf16[3,64,128]{2,1,0:T(8,128)(2,1)S(1)} fusion(bf16[3,1024,128]{2,1,0:T(8,128)(2,1)} %param.16, bf16[8,8,1024]{2,1,0:T(8,128)(2,1)S(1)} %all-to-all-done, f32[1024]{0:T(1024)S(1)} %bitcast.164, f32[64]{0:T(128)S(1)} %rsqrt.20), kind=kOutput, calls=%fused_computation.15 | convolution fusion | flops 50618368 | bytes 971008 | tf_op jit(solution)/shard_map/td,cdq->ctq/dot_general | solution.py:197
  15.6 0.9 broadcast_in_dim.158
  16.5 10.5 %all-to-all-start.1 = ((bf16[32,64,128]{2,1,0:T(8,128)(2,1)}), bf16[32,64,128]{2,1,0:T(8,128)(2,1)S(1)}, u32[]{:S(2)}, u32[]{:S(2)}) async-start(bf16[32,64,128]{2,1,0:T(8,128)(2,1)} %broadcast_in_dim.158), calls=%async_computation.1 | async-start | bytes 1048576 | tf_op jit(solution)/shard_map/all_to_all | solution.py:164
  27.2 0.1 reshape.429
  27.3 0.1 convert_element_type.143
  27.4 0.6 broadcast_in_dim.165.pv_ref
  28.1 0.1 fusion.37
  28.3 0.7 pad_maximum_fusion.aux_ref
  29.0 0.2 convolution_minimum_fusion.3
  29.1 0.2 convolution_minimum_fusion.2
  29.3 12.3 %all-to-all-done.1 = bf16[32,64,128]{2,1,0:T(8,128)(2,1)S(1)} async-done(((bf16[32,64,128]{2,1,0:T(8,128)(2,1)}), bf16[32,64,128]{2,1,0:T(8,128)(2,1)S(1)}, u32[]{:S(2)}, u32[]{:S(2)}) %all-to-all-start.1) | async-done | bytes 524320 | tf_op jit(solution)/shard_map/all_to_all | solution.py:164
  41.6 1.1 %bitcast_select_fusion.q_ref = bf16[32,128,128]{2,1,0:T(8,128)(2,1)} fusion(pred[128,128]{1,0:T(8,128)(4,1)S(1)} %bitcast.159, bf16[32,64,128]{2,1,0:T(8,128)(2,1)S(1)} %all-to-all-done.1), kind=kLoop, calls=%fused_computation.25 | loop fusion | flops 524288 | bytes 1589248 | tf_op jit(solution)/shard_map/jit(_where)/select_n | solution.py:220
  42.6 7.9 %shard_map.160 = bf16[32,70,128]{2,1,0:T(8,128)(2,1)} custom-call(s32[20]{0:T(128)} %get-tuple-element.37.owner_ref, s32[20]{0:T(128)} %get-tuple-element.36.filled_ref, bf16[32,128,128]{2,1,0:T(8,128)(2,1)} %bitcast_select_fusion.q_ref, f32[128,128]{1,0:T(8,128)} %pad_maximum_fusion.aux_ref, bf16[2,20,128,128]{3,2,1,0:T(8,128)(2,1)} %cache_ref.1, ...), custom_call_target="tpu_custom_call" | custom-call | tf_op jit(solution)/shard_map/pallas_call | solution.py:149
  50.5 7.4 %all-to-all-start.2 = ((bf16[32,70,128]{2,1,0:T(8,128)(2,1)}), bf16[32,70,128]{2,1,0:T(8,128)(2,1)S(1)}, u32[]{:S(2)}, u32[]{:S(2)}) async-start(bf16[32,70,128]{2,1,0:T(8,128)(2,1)} %shard_map.160), calls=%async_computation.2 | async-start | bytes 1179648 | tf_op jit(solution)/shard_map/all_to_all | solution.py:240
  57.9 0.2 convolution_minimum_fusion.1
  58.2 0.2 fusion.9
  58.3 0.1 copy.44
  58.5 0.1 reshape.432
  58.6 0.1 reshape.433
  58.7 0.1 copy.54
  58.8 0.2 select_reduce_fusion.1
  59.0 12.6 %all-to-all-done.2 = bf16[32,70,128]{2,1,0:T(8,128)(2,1)S(1)} async-done(((bf16[32,70,128]{2,1,0:T(8,128)(2,1)}), bf16[32,70,128]{2,1,0:T(8,128)(2,1)S(1)}, u32[]{:S(2)}, u32[]{:S(2)}) %all-to-all-start.2) | async-done | bytes 573472 | tf_op jit(solution)/shard_map/all_to_all | solution.py:240
  71.8 0.1 reduce_max.23
  72.1 0.1 reshape_squeeze.2
  72.2 0.6 select_reduce_fusion
  72.8 0.2 fusion.11
  73.0 0.1 copy.43
  73.1 0.1 fusion.7
  73.3 0.1 copy.49
  73.4 0.7 broadcast_in_dim.178
  74.0 9.6 %all-to-all-start.3 = ((bf16[8,64,128]{2,1,0:T(8,128)(2,1)}), bf16[8,64,128]{2,1,0:T(8,128)(2,1)S(1)}, u32[]{:S(2)}, u32[]{:S(2)}) async-start(bf16[8,64,128]{2,1,0:T(8,128)(2,1)} %broadcast_in_dim.178), calls=%async_computation.3 | async-start | bytes 262144 | tf_op jit(solution)/shard_map/all_to_all | solution.py:164
  83.6 5.2 %all-to-all-done.3 = bf16[8,64,128]{2,1,0:T(8,128)(2,1)S(1)} async-done(((bf16[8,64,128]{2,1,0:T(8,128)(2,1)}), bf16[8,64,128]{2,1,0:T(8,128)(2,1)S(1)}, u32[]{:S(2)}, u32[]{:S(2)}) %all-to-all-start.3) | async-done | bytes 131104 | tf_op jit(solution)/shard_map/all_to_all | solution.py:164
  88.8 0.6 fusion.17
  89.4 1.0 copy-done.1
  90.4 0.5 convolution_bitcast_fusion
  91.0 0.9 fusion.1
  91.9 4.1 %all-to-all-start.4 = ((bf16[8,8,1024]{2,1,0:T(8,128)(2,1)}), bf16[8,8,1024]{2,1,0:T(8,128)(2,1)S(1)}, u32[]{:S(2)}, u32[]{:S(2)}) async-start(bf16[8,8,1024]{2,1,0:T(8,128)(2,1)} %fusion.1), calls=%async_computation.4 | async-start | bytes 262144 | tf_op jit(solution)/shard_map/all_to_all | solution.py:311
  96.0 0.8 fusion.10
  96.8 4.5 %all-to-all-done.4 = bf16[8,8,1024]{2,1,0:T(8,128)(2,1)S(1)} async-done(((bf16[8,8,1024]{2,1,0:T(8,128)(2,1)}), bf16[8,8,1024]{2,1,0:T(8,128)(2,1)S(1)}, u32[]{:S(2)}, u32[]{:S(2)}) %all-to-all-start.4) | async-done | bytes 131104 | tf_op jit(solution)/shard_map/all_to_all | solution.py:311
  101.3 0.6 add_convert_fusion
  (44 shorter events, 1.0 us)
Async XLA Ops:
  0.6 88.2 %copy-start = (bf16[1024,1024]{1,0:T(8,128)(2,1)S(1)}, bf16[1024,1024]{1,0:T(8,128)(2,1)}, u32[]{:S(2)}) copy-start(bf16[1024,1024]{1,0:T(8,128)(2,1)} %param.17) | copy-start | bytes 6291460
  0.6 26.3 %copy-start.5 = (f32[2,16]{1,0:T(2,128)S(1)}, f32[2,16]{1,0:T(2,128)}, u32[]{:S(2)}) copy-start(f32[2,16]{1,0:T(2,128)} %param.20) | copy-start | bytes 388
  0.7 26.6 %copy-start.4 = (s32[2048]{0:T(1024)S(1)}, s32[2048]{0:T(1024)}, u32[]{:S(2)}) copy-start(s32[2048]{0:T(1024)} %param.23) | copy-start | bytes 24580
  0.7 26.8 %copy-start.3 = (s32[20,128]{1,0:T(8,128)S(1)}, s32[20,128]{1,0:T(8,128)}, u32[]{:S(2)}) copy-start(s32[20,128]{1,0:T(8,128)} %param.22) | copy-start | bytes 30724
  0.7 27.4 %copy-start.6 = (s32[1,64]{1,0:T(1,128)S(1)}, s32[1,64]{1,0:T(1,128)}, u32[]{:S(2)}) copy-start(s32[1,64]{1,0:T(1,128)} %param.26) | copy-start | bytes 772
  2.2 11.7 %all-to-all-start = ((bf16[8,8,1024]{2,1,0:T(8,128)(2,1)}), bf16[8,8,1024]{2,1,0:T(8,128)(2,1)S(1)}, u32[]{:S(2)}, u32[]{:S(2)}) async-start(bf16[8,8,1024]{2,1,0:T(8,128)(2,1)} %broadcast_in_dim.153), calls=%async_computation | async-start | bytes 262144 | tf_op jit(solution)/shard_map/all_to_all | solution.py:164
  16.5 25.1 %all-to-all-start.1 = ((bf16[32,64,128]{2,1,0:T(8,128)(2,1)}), bf16[32,64,128]{2,1,0:T(8,128)(2,1)S(1)}, u32[]{:S(2)}, u32[]{:S(2)}) async-start(bf16[32,64,128]{2,1,0:T(8,128)(2,1)} %broadcast_in_dim.158), calls=%async_computation.1 | async-start | bytes 1048576 | tf_op jit(solution)/shard_map/all_to_all | solution.py:164
  50.5 21.1 %all-to-all-start.2 = ((bf16[32,70,128]{2,1,0:T(8,128)(2,1)}), bf16[32,70,128]{2,1,0:T(8,128)(2,1)S(1)}, u32[]{:S(2)}, u32[]{:S(2)}) async-start(bf16[32,70,128]{2,1,0:T(8,128)(2,1)} %shard_map.160), calls=%async_computation.2 | async-start | bytes 1179648 | tf_op jit(solution)/shard_map/all_to_all | solution.py:240
  73.3 17.6 %copy-start.2 = (bf16[64,128]{1,0:T(8,128)(2,1)}, bf16[64,128]{1,0:T(8,128)(2,1)S(1)}, u32[]{:S(2)}) copy-start(bf16[64,128]{1,0:T(8,128)(2,1)S(1)} %copy.49) | copy-start | bytes 49156
  74.0 14.8 %all-to-all-start.3 = ((bf16[8,64,128]{2,1,0:T(8,128)(2,1)}), bf16[8,64,128]{2,1,0:T(8,128)(2,1)S(1)}, u32[]{:S(2)}, u32[]{:S(2)}) async-start(bf16[8,64,128]{2,1,0:T(8,128)(2,1)} %broadcast_in_dim.178), calls=%async_computation.3 | async-start | bytes 262144 | tf_op jit(solution)/shard_map/all_to_all | solution.py:164
  88.8 1.6 %copy-start.1 = (bf16[2,1024,512]{2,1,0:T(8,128)(2,1)S(1)}, bf16[2,1024,512]{2,1,0:T(8,128)(2,1)}, u32[]{:S(2)}) copy-start(bf16[2,1024,512]{2,1,0:T(8,128)(2,1)} %param.18) | copy-start | bytes 6291460
  88.8 2.1 %copy-start.7 = (bf16[512,1024]{1,0:T(8,128)(2,1)S(1)}, bf16[512,1024]{1,0:T(8,128)(2,1)}, u32[]{:S(2)}) copy-start(bf16[512,1024]{1,0:T(8,128)(2,1)} %param.19) | copy-start | bytes 3145732
  89.4 6.6 %copy-start.8 = (s32[1,8]{1,0:T(1,128)S(1)}, s32[1,8]{1,0:T(1,128)}, u32[]{:S(2)}) copy-start(s32[1,8]{1,0:T(1,128)} %param.27) | copy-start | bytes 100
  91.9 9.4 %all-to-all-start.4 = ((bf16[8,8,1024]{2,1,0:T(8,128)(2,1)}), bf16[8,8,1024]{2,1,0:T(8,128)(2,1)S(1)}, u32[]{:S(2)}, u32[]{:S(2)}) async-start(bf16[8,8,1024]{2,1,0:T(8,128)(2,1)} %fusion.1), calls=%async_computation.4 | async-start | bytes 262144 | tf_op jit(solution)/shard_map/all_to_all | solution.py:311

commit v12 on v11

--- a/solution.py
+++ b/solution.py
@@ -38,7 +38,7 @@
 def page_kernel(owner_ref, filled_ref, q_ref, aux_ref, cache_ref, pv_ref,
                 out_ref, out_acc, max_acc, total_acc,
                 *, head_local, tree, scale, pool):
-    rows, page = q_ref.shape[1], cache_ref.shape[2]
+    rows, page = head_local * tree, cache_ref.shape[2]
     lanes = aux_ref.shape[0]
     out_acc[...] = jnp.zeros(out_acc.shape, jnp.float32)
     max_acc[...] = jnp.full(max_acc.shape, masked_score, jnp.float32)
@@ -69,8 +69,16 @@
             row = owner_ref[step]
             same = column_of(row) == pv_ref[step]
             valid = lax.broadcasted_iota(jnp.int32, (rows, page), 1) < count
+            query = q_ref[row]
+            stacked = jnp.concatenate(
+                [
+                    jnp.where(column_head == head, query, jnp.zeros_like(query))
+                    for head in range(head_local)
+                ],
+                axis=0,
+            )
             scores = lax.dot_general(
-                q_ref[row], cache_ref[0, step], (((1,), (1,)), ((), ())),
+                stacked, cache_ref[0, step], (((1,), (1,)), ((), ())),
                 preferred_element_type=jnp.float32,
             ) * scale
             scores = scores + jnp.where(same, same_bias, other_bias)
@@ -108,12 +116,12 @@
             values = values - rounded.astype(jnp.float32)
 
 
-def page_attention(owner, filled, split_queries, row_variates, page_cache, page_variates,
+def page_attention(owner, filled, queries, row_variates, page_cache, page_variates,
                    row_bias, interpret=False):
-    requests, rows, qdl = split_queries.shape
+    requests, tree, qdl = queries.shape
     pool, page = page_variates.shape
     head_local = qdl // HD
-    tree = rows // head_local
+    rows = head_local * tree
     lanes = 128 * ((requests + 2 + 127) // 128)
     aux = jnp.concatenate(
         [
@@ -134,7 +142,7 @@
         num_scalar_prefetch=2,
         grid=(1,),
         in_specs=[
-            whole((requests, rows, qdl)),
+            whole((requests, tree, qdl)),
             whole((lanes, rows)),
             whole(page_cache.shape),
             whole((pool, 1, page)),
@@ -152,7 +160,7 @@
         out_shape=jax.ShapeDtypeStruct((requests, tree + 6, qdl), jnp.bfloat16),
         compiler_params=pltpu.CompilerParams(dimension_semantics=("arbitrary",)),
         interpret=interpret,
-    )(owner, filled, split_queries, aux, page_cache, page_variates[:, None, :])
+    )(owner, filled, queries, aux, page_cache, page_variates[:, None, :])
 
 
 def join_three(high, middle, low):
@@ -217,11 +225,6 @@
     head_of_column = jnp.arange(qdl, dtype=jnp.int32) // HD
     head_mask = jnp.arange(head_local, dtype=jnp.int32)[:, None] == head_of_column[None, :]
     split_rows = head_local * tree
-    split_queries = jnp.where(
-        head_mask[None, :, None, :],
-        all_queries.reshape(requests, 1, tree, qdl),
-        jnp.zeros((), all_queries.dtype),
-    ).reshape(requests, split_rows, qdl)
     row_variates = jnp.broadcast_to(
         token_variates.reshape(requests, 1, tree), (requests, head_local, tree)
     ).reshape(requests, split_rows)
@@ -231,7 +234,7 @@
     packed = page_attention(
         jnp.clip(owner, 0, requests - 1),
         filled,
-        split_queries,
+        all_queries.reshape(requests, tree, qdl),
         row_variates,
         page_cache,
         page_variates,

time: 103 us -> 104 us (level)
  local copies, waits for them, and re-layouts: 7.03 us -> 8.49 us
    all_to_all x1, starting transfers between devices: 7.38 us -> 10.2 us  [shards(): lax.all_to_all(packed, 'req', split_axis=0, concat_axis=0, tiled=True)]
    all_to_all x3, starting transfers between devices: 26.5 us -> 23.8 us  [gather_rows(): return lax.all_to_all(spread, axis_name, 0, 0, tiled=True)]
    all_to_all x1, waiting for transfers between devices: 12.6 us -> 14.7 us  [shards(): lax.all_to_all(packed, 'req', split_axis=0, concat_axis=0, tiled=True)]
    all_to_all x3, waiting for transfers between devices: 19.1 us -> 17.3 us  [gather_rows(): return lax.all_to_all(spread, axis_name, 0, 0, tiled=True)]
    select_n x1 -> x0, other arithmetic: 1.06 us -> none  [shards(): jnp.where(head_mask[None, :, None, :], all_queries.reshape(requests, 1, t...]
  transfers between devices with their start and end apart: 5 -> 5, of which waited for: 5 -> 5; matrix products, arithmetic and copies ran while one was open for 8% -> 9% of each run, Pallas kernels for 0% -> 0%
where the time goes in v12:
time: 104 us; the launch traced here: 103 us
  starting transfers between devices  38.1 us (37%)
  waiting for transfers between devices  36.5 us (35%)
  local copies, waits for them, and re-layouts  8.49 us (8%)
  Pallas kernels  7.34 us (7%)
  other arithmetic  6.17 us (6%)
  matrix products  5.2 us (5%)
    all_to_all x3, starting transfers between devices, gather_rows(): return lax.all_to_all(spread, axis_name, 0, 0, tiled=True)  23.8 us
    all_to_all x3, waiting for transfers between devices, gather_rows(): return lax.all_to_all(spread, axis_name, 0, 0, tiled=True)  17.3 us
    all_to_all x1, waiting for transfers between devices, shards(): lax.all_to_all(packed, 'req', split_axis=0, concat_axis=0, tiled=True)  14.7 us
    all_to_all x1, starting transfers between devices, shards(): lax.all_to_all(packed, 'req', split_axis=0, concat_axis=0, tiled=True)  10.2 us
    pallas_call x1, Pallas kernels, page_attention(): pl.pallas_call(kernel, grid_spec=grid_spec, out_shape=jax.ShapeDtypeStruc...  7.34 us
    all_to_all x1, waiting for transfers between devices, shards(): lax.all_to_all(down_part.reshape(head_parts, own_rows, -1), 'head', 0, 0,...  4.48 us
    all_to_all x1, starting transfers between devices, shards(): lax.all_to_all(down_part.reshape(head_parts, own_rows, -1), 'head', 0, 0,...  4.14 us
    broadcast_in_dim x4, local copies, waits for them, and re-layouts, gather_rows(): spread = jnp.broadcast_to(rows[None], (parts,) + rows.shape)  3.15 us
  transfers between devices with their start and end apart: 5, of which 5 were waited for; matrix products, arithmetic and copies ran while one was open for 9% of the time, Pallas kernels for 0%

profile of v12, /device:TPU:1, one launch (start us, length us, event | category | flops | bytes accessed | tf_op | source)
XLA Modules:
  0.0 102.8 jit_solution(11665898455398764397)
XLA Ops:
  0.7 1.5 %broadcast_in_dim.126 = bf16[8,8,1024]{2,1,0:T(8,128)(2,1)} broadcast(bf16[8,1024]{1,0:T(8,128)(2,1)} %param.14), dimensions={1,2} | broadcast | bytes 147456 | tf_op jit(solution)/shard_map/broadcast_in_dim | solution.py:171
  2.2 6.5 %all-to-all-start = ((bf16[8,8,1024]{2,1,0:T(8,128)(2,1)}), bf16[8,8,1024]{2,1,0:T(8,128)(2,1)S(1)}, u32[]{:S(2)}, u32[]{:S(2)}) async-start(bf16[8,8,1024]{2,1,0:T(8,128)(2,1)} %broadcast_in_dim.126), calls=%async_computation | async-start | bytes 262144 | tf_op jit(solution)/shard_map/all_to_all | solution.py:172
  8.7 0.7 convert_element_type.141
  9.4 0.8 dynamic_slice.10
  10.1 0.8 fusion.37
  10.9 0.2 convolution_minimum_fusion.3
  11.1 0.2 convolution_minimum_fusion.2
  11.3 0.2 convolution_minimum_fusion.1
  11.4 0.8 fusion.54
  12.2 1.7 %all-to-all-done = bf16[8,8,1024]{2,1,0:T(8,128)(2,1)S(1)} async-done(((bf16[8,8,1024]{2,1,0:T(8,128)(2,1)}), bf16[8,8,1024]{2,1,0:T(8,128)(2,1)S(1)}, u32[]{:S(2)}, u32[]{:S(2)}) %all-to-all-start) | async-done | bytes 131104 | tf_op jit(solution)/shard_map/all_to_all | solution.py:172
  13.9 0.1 fusion.22
  14.1 1.4 %fusion.8 = bf16[3,64,128]{2,1,0:T(8,128)(2,1)S(1)} fusion(bf16[3,1024,128]{2,1,0:T(8,128)(2,1)} %param.16, bf16[8,8,1024]{2,1,0:T(8,128)(2,1)S(1)} %all-to-all-done, f32[1024]{0:T(1024)S(1)} %bitcast.160, f32[64]{0:T(128)S(1)} %rsqrt.20), kind=kOutput, calls=%fused_computation.15 | convolution fusion | flops 50618368 | bytes 971008 | tf_op jit(solution)/shard_map/td,cdq->ctq/dot_general | solution.py:205
  15.6 0.9 broadcast_in_dim.128
  16.5 10.5 %all-to-all-start.1 = ((bf16[32,64,128]{2,1,0:T(8,128)(2,1)}), bf16[32,64,128]{2,1,0:T(8,128)(2,1)S(1)}, u32[]{:S(2)}, u32[]{:S(2)}) async-start(bf16[32,64,128]{2,1,0:T(8,128)(2,1)} %broadcast_in_dim.128), calls=%async_computation.1 | async-start | bytes 1048576 | tf_op jit(solution)/shard_map/all_to_all | solution.py:172
  27.2 0.1 reshape.404
  27.3 0.6 broadcast_in_dim.132.pv_ref
  27.9 0.1 convert_element_type.143
  28.0 0.2 fusion.9
  28.2 0.1 copy.44
  28.4 1.6 %fusion.15 = (s32[20]{0:T(128)S(1)}, s32[20]{0:T(128)S(1)}, s32[20]{0:T(128)S(1)}, s32[20]{0:T(128)S(1)}) fusion(s32[32,32]{1,0:T(8,128)S(1)} %copy-done.4, s32[20]{0:T(128)S(1)} %iota_add_fusion, s32[32]{0:T(128)S(1)} %copy-done.7), kind=kLoop, calls=%fused_computation.36 | loop fusion | flops 184240 | bytes 4624 | tf_op jit(solution)/shard_map/reduce_sum | solution.py:218
  30.0 0.5 clamp_multiply_fusion
  30.5 0.7 pad_maximum_fusion.aux_ref
  31.2 10.3 %all-to-all-done.1.q_ref = bf16[32,64,128]{2,1,0:T(8,128)(2,1)S(1)} async-done(((bf16[32,64,128]{2,1,0:T(8,128)(2,1)}), bf16[32,64,128]{2,1,0:T(8,128)(2,1)S(1)}, u32[]{:S(2)}, u32[]{:S(2)}) %all-to-all-start.1) | async-done | bytes 524320 | tf_op jit(solution)/shard_map/all_to_all | solution.py:172
  41.6 0.8 copy-done.2
  42.3 7.3 %shard_map.160 = bf16[32,70,128]{2,1,0:T(8,128)(2,1)} custom-call(s32[20]{0:T(128)} %get-tuple-element.37.owner_ref, s32[20]{0:T(128)} %get-tuple-element.36.filled_ref, bf16[32,64,128]{2,1,0:T(8,128)(2,1)} %copy-done.2, f32[128,128]{1,0:T(8,128)} %pad_maximum_fusion.aux_ref, bf16[2,20,128,128]{3,2,1,0:T(8,128)(2,1)} %cache_ref.1, ...), custom_call_target="tpu_custom_call" | custom-call | tf_op jit(solution)/shard_map/pallas_call | solution.py:157
  49.7 10.2 %all-to-all-start.2 = ((bf16[32,70,128]{2,1,0:T(8,128)(2,1)}), bf16[32,70,128]{2,1,0:T(8,128)(2,1)S(1)}, u32[]{:S(2)}, u32[]{:S(2)}) async-start(bf16[32,70,128]{2,1,0:T(8,128)(2,1)} %shard_map.160), calls=%async_computation.2 | async-start | bytes 1179648 | tf_op jit(solution)/shard_map/all_to_all | solution.py:243
  60.0 0.1 reshape.407
  60.1 0.1 copy.54
  60.2 0.1 reshape.408
  60.3 0.2 select_reduce_fusion.1
  60.5 14.7 %all-to-all-done.2 = bf16[32,70,128]{2,1,0:T(8,128)(2,1)S(1)} async-done(((bf16[32,70,128]{2,1,0:T(8,128)(2,1)}), bf16[32,70,128]{2,1,0:T(8,128)(2,1)S(1)}, u32[]{:S(2)}, u32[]{:S(2)}) %all-to-all-start.2) | async-done | bytes 573472 | tf_op jit(solution)/shard_map/all_to_all | solution.py:243
  75.7 0.1 reshape_squeeze.2
  75.8 0.6 select_reduce_fusion
  76.4 0.2 fusion.11
  76.6 0.1 copy.43
  76.7 0.1 fusion.7
  76.8 0.1 copy.49
  76.9 0.7 broadcast_in_dim.145
  77.6 6.8 %all-to-all-start.3 = ((bf16[8,64,128]{2,1,0:T(8,128)(2,1)}), bf16[8,64,128]{2,1,0:T(8,128)(2,1)S(1)}, u32[]{:S(2)}, u32[]{:S(2)}) async-start(bf16[8,64,128]{2,1,0:T(8,128)(2,1)} %broadcast_in_dim.145), calls=%async_computation.3 | async-start | bytes 262144 | tf_op jit(solution)/shard_map/all_to_all | solution.py:172
  84.4 5.3 %all-to-all-done.3 = bf16[8,64,128]{2,1,0:T(8,128)(2,1)S(1)} async-done(((bf16[8,64,128]{2,1,0:T(8,128)(2,1)}), bf16[8,64,128]{2,1,0:T(8,128)(2,1)S(1)}, u32[]{:S(2)}, u32[]{:S(2)}) %all-to-all-start.3) | async-done | bytes 131104 | tf_op jit(solution)/shard_map/all_to_all | solution.py:172
  89.7 0.6 fusion.17
  90.3 1.0 copy-done.1
  91.3 0.5 convolution_bitcast_fusion
  91.8 0.9 fusion.1
  92.8 4.1 %all-to-all-start.4 = ((bf16[8,8,1024]{2,1,0:T(8,128)(2,1)}), bf16[8,8,1024]{2,1,0:T(8,128)(2,1)S(1)}, u32[]{:S(2)}, u32[]{:S(2)}) async-start(bf16[8,8,1024]{2,1,0:T(8,128)(2,1)} %fusion.1), calls=%async_computation.4 | async-start | bytes 262144 | tf_op jit(solution)/shard_map/all_to_all | solution.py:314
  96.9 0.8 fusion.10
  97.7 4.5 %all-to-all-done.4 = bf16[8,8,1024]{2,1,0:T(8,128)(2,1)S(1)} async-done(((bf16[8,8,1024]{2,1,0:T(8,128)(2,1)}), bf16[8,8,1024]{2,1,0:T(8,128)(2,1)S(1)}, u32[]{:S(2)}, u32[]{:S(2)}) %all-to-all-start.4) | async-done | bytes 131104 | tf_op jit(solution)/shard_map/all_to_all | solution.py:314
  102.2 0.6 add_convert_fusion
  (44 shorter events, 1.0 us)
Async XLA Ops:
  0.6 89.1 %copy-start = (bf16[1024,1024]{1,0:T(8,128)(2,1)S(1)}, bf16[1024,1024]{1,0:T(8,128)(2,1)}, u32[]{:S(2)}) copy-start(bf16[1024,1024]{1,0:T(8,128)(2,1)} %param.17) | copy-start | bytes 6291460
  0.6 26.3 %copy-start.6 = (f32[2,16]{1,0:T(2,128)S(1)}, f32[2,16]{1,0:T(2,128)}, u32[]{:S(2)}) copy-start(f32[2,16]{1,0:T(2,128)} %param.20) | copy-start | bytes 388
  0.7 26.7 %copy-start.5 = (s32[20,128]{1,0:T(8,128)S(1)}, s32[20,128]{1,0:T(8,128)}, u32[]{:S(2)}) copy-start(s32[20,128]{1,0:T(8,128)} %param.22) | copy-start | bytes 30724
  0.7 27.7 %copy-start.4 = (s32[32,32]{1,0:T(8,128)S(1)}, s32[32,32]{1,0:T(8,128)}, u32[]{:S(2)}) copy-start(s32[32,32]{1,0:T(8,128)} %param.25) | copy-start | bytes 12292
  0.7 27.7 %copy-start.7 = (s32[32]{0:T(128)S(1)}, s32[32]{0:T(128)}, u32[]{:S(2)}) copy-start(s32[32]{0:T(128)} %param.24) | copy-start | bytes 388
  2.2 11.7 %all-to-all-start = ((bf16[8,8,1024]{2,1,0:T(8,128)(2,1)}), bf16[8,8,1024]{2,1,0:T(8,128)(2,1)S(1)}, u32[]{:S(2)}, u32[]{:S(2)}) async-start(bf16[8,8,1024]{2,1,0:T(8,128)(2,1)} %broadcast_in_dim.126), calls=%async_computation | async-start | bytes 262144 | tf_op jit(solution)/shard_map/all_to_all | solution.py:172
  16.5 25.1 %all-to-all-start.1 = ((bf16[32,64,128]{2,1,0:T(8,128)(2,1)}), bf16[32,64,128]{2,1,0:T(8,128)(2,1)S(1)}, u32[]{:S(2)}, u32[]{:S(2)}) async-start(bf16[32,64,128]{2,1,0:T(8,128)(2,1)} %broadcast_in_dim.128), calls=%async_computation.1 | async-start | bytes 1048576 | tf_op jit(solution)/shard_map/all_to_all | solution.py:172
  41.6 0.8 copy-start.2
  49.7 25.5 %all-to-all-start.2 = ((bf16[32,70,128]{2,1,0:T(8,128)(2,1)}), bf16[32,70,128]{2,1,0:T(8,128)(2,1)S(1)}, u32[]{:S(2)}, u32[]{:S(2)}) async-start(bf16[32,70,128]{2,1,0:T(8,128)(2,1)} %shard_map.160), calls=%async_computation.2 | async-start | bytes 1179648 | tf_op jit(solution)/shard_map/all_to_all | solution.py:243
  76.9 14.9 %copy-start.3 = (bf16[64,128]{1,0:T(8,128)(2,1)}, bf16[64,128]{1,0:T(8,128)(2,1)S(1)}, u32[]{:S(2)}) copy-start(bf16[64,128]{1,0:T(8,128)(2,1)S(1)} %copy.49) | copy-start | bytes 49156
  77.6 12.1 %all-to-all-start.3 = ((bf16[8,64,128]{2,1,0:T(8,128)(2,1)}), bf16[8,64,128]{2,1,0:T(8,128)(2,1)S(1)}, u32[]{:S(2)}, u32[]{:S(2)}) async-start(bf16[8,64,128]{2,1,0:T(8,128)(2,1)} %broadcast_in_dim.145), calls=%async_computation.3 | async-start | bytes 262144 | tf_op jit(solution)/shard_map/all_to_all | solution.py:172
  89.7 1.6 %copy-start.1 = (bf16[2,1024,512]{2,1,0:T(8,128)(2,1)S(1)}, bf16[2,1024,512]{2,1,0:T(8,128)(2,1)}, u32[]{:S(2)}) copy-start(bf16[2,1024,512]{2,1,0:T(8,128)(2,1)} %param.18) | copy-start | bytes 6291460
  89.7 2.1 %copy-start.8 = (bf16[512,1024]{1,0:T(8,128)(2,1)S(1)}, bf16[512,1024]{1,0:T(8,128)(2,1)}, u32[]{:S(2)}) copy-start(bf16[512,1024]{1,0:T(8,128)(2,1)} %param.19) | copy-start | bytes 3145732
  90.3 6.6 %copy-start.9 = (s32[1,8]{1,0:T(1,128)S(1)}, s32[1,8]{1,0:T(1,128)}, u32[]{:S(2)}) copy-start(s32[1,8]{1,0:T(1,128)} %param.27) | copy-start | bytes 100
  92.8 9.4 %all-to-all-start.4 = ((bf16[8,8,1024]{2,1,0:T(8,128)(2,1)}), bf16[8,8,1024]{2,1,0:T(8,128)(2,1)S(1)}, u32[]{:S(2)}, u32[]{:S(2)}) async-start(bf16[8,8,1024]{2,1,0:T(8,128)(2,1)} %fusion.1), calls=%async_computation.4 | async-start | bytes 262144 | tf_op jit(solution)/shard_map/all_to_all | solution.py:314

commit v13 on v12

--- a/solution.py
+++ b/solution.py
@@ -200,7 +200,10 @@
     same_bias = bias_local[0]
     other_bias = bias_local[1]
     head_parts = lax.axis_size("head")
-    group_tokens = gather_rows(tokens, "head", head_parts).reshape(-1, tokens.shape[1])
+    lane_rows = tokens.shape[0] * tokens.shape[1] // 128
+    group_tokens = gather_rows(tokens.reshape(lane_rows, 128), "head", head_parts).reshape(
+        -1, tokens.shape[1]
+    )
     normed = rms_scaled(group_tokens, gains[0]).astype(jnp.bfloat16)
     projected = jnp.einsum(
         "td,cdq->ctq",
@@ -312,9 +315,9 @@
     )
     own_rows = tokens.shape[0]
     down_parts = lax.all_to_all(
-        down_part.reshape(head_parts, own_rows, -1), "head", 0, 0, tiled=True
-    )
-    ffn_rows = jnp.sum(down_parts.astype(jnp.float32), axis=0)
+        down_part.reshape(head_parts, lane_rows, 128), "head", 0, 0, tiled=True
+    )
+    ffn_rows = jnp.sum(down_parts.astype(jnp.float32), axis=0).reshape(own_rows, -1)
     own_hidden = lax.dynamic_slice_in_dim(hidden_state, head_slot * own_rows, own_rows, 0)
     mixed = (own_hidden.astype(jnp.float32) + ffn_rows).astype(jnp.bfloat16)
     chosen = (accepted[:, :, None] == nodes[None, None, :]).astype(jnp.bfloat16)

time: 104 us -> 103 us (level)
  starting transfers between devices: 38.1 us -> 35.3 us
  Pallas kernels: 7.34 us -> 9.91 us
    all_to_all x1, starting transfers between devices: 10.2 us -> 5.81 us  [shards(): lax.all_to_all(packed, 'req', split_axis=0, concat_axis=0, tiled=True)]
    pallas_call x1, Pallas kernels: 7.34 us -> 9.91 us  [page_attention(): pl.pallas_call(kernel, grid_spec=grid_spec, out_shape=jax.ShapeDtypeStruc...]
    all_to_all x3, starting transfers between devices: 23.8 us -> 25.3 us  [gather_rows(): return lax.all_to_all(spread, axis_name, 0, 0, tiled=True)]
    broadcast_in_dim x4 -> x5, local copies, waits for them, and re-layouts: 3.15 us -> 3.18 us  [gather_rows(): spread = jnp.broadcast_to(rows[None], (parts,) + rows.shape)]
where the time goes in v13:
time: 103 us; the launch traced here: 102 us
  waiting for transfers between devices  36 us (35%)
  starting transfers between devices  35.3 us (34%)
  Pallas kernels  9.91 us (10%)
  local copies, waits for them, and re-layouts  9.3 us (9%)
  other arithmetic  6.32 us (6%)
  matrix products  4.54 us (4%)
    all_to_all x3, starting transfers between devices, gather_rows(): return lax.all_to_all(spread, axis_name, 0, 0, tiled=True)  25.3 us
    all_to_all x3, waiting for transfers between devices, gather_rows(): return lax.all_to_all(spread, axis_name, 0, 0, tiled=True)  17.3 us
    all_to_all x1, waiting for transfers between devices, shards(): lax.all_to_all(packed, 'req', split_axis=0, concat_axis=0, tiled=True)  14.2 us
    pallas_call x1, Pallas kernels, page_attention(): pl.pallas_call(kernel, grid_spec=grid_spec, out_shape=jax.ShapeDtypeStruc...  9.91 us
    all_to_all x1, starting transfers between devices, shards(): lax.all_to_all(packed, 'req', split_axis=0, concat_axis=0, tiled=True)  5.81 us
    all_to_all x1, waiting for transfers between devices, shards(): lax.all_to_all(down_part.reshape(head_parts, lane_rows, 128), 'head', 0,...  4.48 us
    all_to_all x1, starting transfers between devices, shards(): lax.all_to_all(down_part.reshape(head_parts, lane_rows, 128), 'head', 0,...  4.14 us
    broadcast_in_dim x5, local copies, waits for them, and re-layouts, gather_rows(): spread = jnp.broadcast_to(rows[None], (parts,) + rows.shape)  3.18 us
  transfers between devices with their start and end apart: 5, of which 5 were waited for; matrix products, arithmetic and copies ran while one was open for 9% of the time, Pallas kernels for 0%

profile of v13, /device:TPU:1, one launch (start us, length us, event | category | flops | bytes accessed | tf_op | source)
XLA Modules:
  0.0 102.3 jit_solution(13550157481137113490)
XLA Ops:
  0.6 0.9 broadcast_in_dim.127
  1.5 0.7 broadcast_in_dim.128
  2.2 6.6 %all-to-all-start = ((bf16[8,64,128]{2,1,0:T(8,128)(2,1)}), bf16[8,64,128]{2,1,0:T(8,128)(2,1)S(1)}, u32[]{:S(2)}, u32[]{:S(2)}) async-start(bf16[8,64,128]{2,1,0:T(8,128)(2,1)} %broadcast_in_dim.128), calls=%async_computation | async-start | bytes 262144 | tf_op jit(solution)/shard_map/all_to_all | solution.py:172
  8.8 0.7 convert_element_type.141
  9.5 0.8 dynamic_slice.10
  10.3 0.8 fusion.32
  11.1 0.2 convolution_minimum_fusion.3
  11.2 0.2 convolution_minimum_fusion.2
  11.4 0.2 convolution_minimum_fusion.1
  11.6 0.8 fusion.49
  12.4 1.7 %all-to-all-done = bf16[8,64,128]{2,1,0:T(8,128)(2,1)S(1)} async-done(((bf16[8,64,128]{2,1,0:T(8,128)(2,1)}), bf16[8,64,128]{2,1,0:T(8,128)(2,1)S(1)}, u32[]{:S(2)}, u32[]{:S(2)}) %all-to-all-start) | async-done | bytes 131104 | tf_op jit(solution)/shard_map/all_to_all | solution.py:172
  14.1 0.1 multiply_reduce_fusion
  14.3 0.1 reduce_sum.118
  14.5 1.4 %fusion.7 = bf16[3,64,128]{2,1,0:T(8,128)(2,1)S(1)} fusion(bf16[3,1024,128]{2,1,0:T(8,128)(2,1)} %param.16, f32[64,1024]{1,0:T(8,128)S(1)} %reshape.409, f32[1024]{0:T(1024)S(1)} %bitcast.145, f32[64]{0:T(128)S(1)} %add_rsqrt_fusion.1), kind=kOutput, calls=%fused_computation.14 | convolution fusion | flops 50552832 | bytes 1102080 | tf_op jit(solution)/shard_map/td,cdq->ctq/dot_general | solution.py:208
  15.9 0.9 broadcast_in_dim.130
  16.9 10.5 %all-to-all-start.1 = ((bf16[32,64,128]{2,1,0:T(8,128)(2,1)}), bf16[32,64,128]{2,1,0:T(8,128)(2,1)S(1)}, u32[]{:S(2)}, u32[]{:S(2)}) async-start(bf16[32,64,128]{2,1,0:T(8,128)(2,1)} %broadcast_in_dim.130), calls=%async_computation.1 | async-start | bytes 1048576 | tf_op jit(solution)/shard_map/all_to_all | solution.py:172
  27.5 0.1 reshape.399
  27.7 0.6 broadcast_in_dim.134.pv_ref
  28.3 0.1 convert_element_type.143
  28.4 0.2 fusion.8
  28.6 0.1 copy.44
  28.8 1.6 %fusion.13 = (s32[20]{0:T(128)S(1)}, s32[20]{0:T(128)S(1)}, s32[20]{0:T(128)S(1)}, s32[20]{0:T(128)S(1)}) fusion(s32[32,32]{1,0:T(8,128)S(1)} %copy-done.4, s32[20]{0:T(128)S(1)} %iota_add_fusion, s32[32]{0:T(128)S(1)} %copy-done.7), kind=kLoop, calls=%fused_computation.32 | loop fusion | flops 184240 | bytes 4624 | tf_op jit(solution)/shard_map/reduce_sum | solution.py:221
  30.4 0.5 clamp_multiply_fusion
  30.9 0.7 pad_maximum_fusion.aux_ref
  31.6 10.3 %all-to-all-done.1.q_ref = bf16[32,64,128]{2,1,0:T(8,128)(2,1)S(1)} async-done(((bf16[32,64,128]{2,1,0:T(8,128)(2,1)}), bf16[32,64,128]{2,1,0:T(8,128)(2,1)S(1)}, u32[]{:S(2)}, u32[]{:S(2)}) %all-to-all-start.1) | async-done | bytes 524320 | tf_op jit(solution)/shard_map/all_to_all | solution.py:172
  41.9 0.8 copy-done.2
  42.7 9.9 %shard_map.160 = bf16[32,70,128]{2,1,0:T(8,128)(2,1)} custom-call(s32[20]{0:T(128)} %get-tuple-element.37.owner_ref, s32[20]{0:T(128)} %get-tuple-element.36.filled_ref, bf16[32,64,128]{2,1,0:T(8,128)(2,1)} %copy-done.2, f32[128,128]{1,0:T(8,128)} %pad_maximum_fusion.aux_ref, bf16[2,20,128,128]{3,2,1,0:T(8,128)(2,1)} %cache_ref.1, ...), custom_call_target="tpu_custom_call" | custom-call | tf_op jit(solution)/shard_map/pallas_call | solution.py:157
  52.6 5.8 %all-to-all-start.2 = ((bf16[32,70,128]{2,1,0:T(8,128)(2,1)}), bf16[32,70,128]{2,1,0:T(8,128)(2,1)S(1)}, u32[]{:S(2)}, u32[]{:S(2)}) async-start(bf16[32,70,128]{2,1,0:T(8,128)(2,1)} %shard_map.160), calls=%async_computation.2 | async-start | bytes 1179648 | tf_op jit(solution)/shard_map/all_to_all | solution.py:246
  58.6 0.1 copy.54
  58.8 0.2 select_reduce_fusion.1
  59.1 14.2 %all-to-all-done.2 = bf16[32,70,128]{2,1,0:T(8,128)(2,1)S(1)} async-done(((bf16[32,70,128]{2,1,0:T(8,128)(2,1)}), bf16[32,70,128]{2,1,0:T(8,128)(2,1)S(1)}, u32[]{:S(2)}, u32[]{:S(2)}) %all-to-all-start.2) | async-done | bytes 573472 | tf_op jit(solution)/shard_map/all_to_all | solution.py:246
  73.7 0.1 reshape_squeeze.2
  73.8 0.6 select_reduce_fusion
  74.4 0.2 fusion.10
  74.6 0.1 copy.43
  74.7 0.1 fusion.6
  75.0 0.7 broadcast_in_dim.147
  75.6 8.2 %all-to-all-start.3 = ((bf16[8,64,128]{2,1,0:T(8,128)(2,1)}), bf16[8,64,128]{2,1,0:T(8,128)(2,1)S(1)}, u32[]{:S(2)}, u32[]{:S(2)}) async-start(bf16[8,64,128]{2,1,0:T(8,128)(2,1)} %broadcast_in_dim.147), calls=%async_computation.3 | async-start | bytes 262144 | tf_op jit(solution)/shard_map/all_to_all | solution.py:172
  83.9 5.3 %all-to-all-done.3 = bf16[8,64,128]{2,1,0:T(8,128)(2,1)S(1)} async-done(((bf16[8,64,128]{2,1,0:T(8,128)(2,1)}), bf16[8,64,128]{2,1,0:T(8,128)(2,1)S(1)}, u32[]{:S(2)}, u32[]{:S(2)}) %all-to-all-start.3) | async-done | bytes 131104 | tf_op jit(solution)/shard_map/all_to_all | solution.py:172
  89.1 0.6 fusion.15
  89.7 1.0 copy-done.1
  90.7 0.5 convolution_bitcast_fusion
  91.3 0.3 convolution_convert_fusion
  91.6 0.7 reshape.407
  92.3 4.1 %all-to-all-start.4 = ((bf16[8,64,128]{2,1,0:T(8,128)(2,1)}), bf16[8,64,128]{2,1,0:T(8,128)(2,1)S(1)}, u32[]{:S(2)}, u32[]{:S(2)}) async-start(bf16[8,64,128]{2,1,0:T(8,128)(2,1)} %reshape.407), calls=%async_computation.4 | async-start | bytes 262144 | tf_op jit(solution)/shard_map/all_to_all | solution.py:317
  96.4 0.8 fusion.9
  97.2 4.5 %all-to-all-done.4 = bf16[8,64,128]{2,1,0:T(8,128)(2,1)S(1)} async-done(((bf16[8,64,128]{2,1,0:T(8,128)(2,1)}), bf16[8,64,128]{2,1,0:T(8,128)(2,1)S(1)}, u32[]{:S(2)}, u32[]{:S(2)}) %all-to-all-start.4) | async-done | bytes 131104 | tf_op jit(solution)/shard_map/all_to_all | solution.py:317
  101.7 0.6 add_convert_fusion
  (49 shorter events, 1.4 us)
Async XLA Ops:
  0.6 88.5 %copy-start = (bf16[1024,1024]{1,0:T(8,128)(2,1)S(1)}, bf16[1024,1024]{1,0:T(8,128)(2,1)}, u32[]{:S(2)}) copy-start(bf16[1024,1024]{1,0:T(8,128)(2,1)} %param.17) | copy-start | bytes 6291460
  1.5 25.8 %copy-start.6 = (f32[2,16]{1,0:T(2,128)S(1)}, f32[2,16]{1,0:T(2,128)}, u32[]{:S(2)}) copy-start(f32[2,16]{1,0:T(2,128)} %param.20) | copy-start | bytes 388
  1.5 26.1 %copy-start.5 = (s32[20,128]{1,0:T(8,128)S(1)}, s32[20,128]{1,0:T(8,128)}, u32[]{:S(2)}) copy-start(s32[20,128]{1,0:T(8,128)} %param.22) | copy-start | bytes 30724
  2.2 26.6 %copy-start.4 = (s32[32,32]{1,0:T(8,128)S(1)}, s32[32,32]{1,0:T(8,128)}, u32[]{:S(2)}) copy-start(s32[32,32]{1,0:T(8,128)} %param.25) | copy-start | bytes 12292
  2.2 26.6 %copy-start.7 = (s32[32]{0:T(128)S(1)}, s32[32]{0:T(128)}, u32[]{:S(2)}) copy-start(s32[32]{0:T(128)} %param.24) | copy-start | bytes 388
  2.2 11.9 %all-to-all-start = ((bf16[8,64,128]{2,1,0:T(8,128)(2,1)}), bf16[8,64,128]{2,1,0:T(8,128)(2,1)S(1)}, u32[]{:S(2)}, u32[]{:S(2)}) async-start(bf16[8,64,128]{2,1,0:T(8,128)(2,1)} %broadcast_in_dim.128), calls=%async_computation | async-start | bytes 262144 | tf_op jit(solution)/shard_map/all_to_all | solution.py:172
  16.9 25.1 %all-to-all-start.1 = ((bf16[32,64,128]{2,1,0:T(8,128)(2,1)}), bf16[32,64,128]{2,1,0:T(8,128)(2,1)S(1)}, u32[]{:S(2)}, u32[]{:S(2)}) async-start(bf16[32,64,128]{2,1,0:T(8,128)(2,1)} %broadcast_in_dim.130), calls=%async_computation.1 | async-start | bytes 1048576 | tf_op jit(solution)/shard_map/all_to_all | solution.py:172
  41.9 0.8 copy-start.2
  52.6 20.7 %all-to-all-start.2 = ((bf16[32,70,128]{2,1,0:T(8,128)(2,1)}), bf16[32,70,128]{2,1,0:T(8,128)(2,1)S(1)}, u32[]{:S(2)}, u32[]{:S(2)}) async-start(bf16[32,70,128]{2,1,0:T(8,128)(2,1)} %shard_map.160), calls=%async_computation.2 | async-start | bytes 1179648 | tf_op jit(solution)/shard_map/all_to_all | solution.py:246
  75.0 16.3 %copy-start.3 = (bf16[64,128]{1,0:T(8,128)(2,1)}, bf16[64,128]{1,0:T(8,128)(2,1)S(1)}, u32[]{:S(2)}) copy-start(bf16[64,128]{1,0:T(8,128)(2,1)S(1)} %copy.49) | copy-start | bytes 49156
  75.6 13.5 %all-to-all-start.3 = ((bf16[8,64,128]{2,1,0:T(8,128)(2,1)}), bf16[8,64,128]{2,1,0:T(8,128)(2,1)S(1)}, u32[]{:S(2)}, u32[]{:S(2)}) async-start(bf16[8,64,128]{2,1,0:T(8,128)(2,1)} %broadcast_in_dim.147), calls=%async_computation.3 | async-start | bytes 262144 | tf_op jit(solution)/shard_map/all_to_all | solution.py:172
  89.1 1.6 %copy-start.1 = (bf16[2,1024,512]{2,1,0:T(8,128)(2,1)S(1)}, bf16[2,1024,512]{2,1,0:T(8,128)(2,1)}, u32[]{:S(2)}) copy-start(bf16[2,1024,512]{2,1,0:T(8,128)(2,1)} %param.18) | copy-start | bytes 6291460
  89.1 2.1 %copy-start.8 = (bf16[512,1024]{1,0:T(8,128)(2,1)S(1)}, bf16[512,1024]{1,0:T(8,128)(2,1)}, u32[]{:S(2)}) copy-start(bf16[512,1024]{1,0:T(8,128)(2,1)} %param.19) | copy-start | bytes 3145732
  90.7 5.7 %copy-start.9 = (s32[1,8]{1,0:T(1,128)S(1)}, s32[1,8]{1,0:T(1,128)}, u32[]{:S(2)}) copy-start(s32[1,8]{1,0:T(1,128)} %param.27) | copy-start | bytes 100
  92.3 9.4 %all-to-all-start.4 = ((bf16[8,64,128]{2,1,0:T(8,128)(2,1)}), bf16[8,64,128]{2,1,0:T(8,128)(2,1)S(1)}, u32[]{:S(2)}, u32[]{:S(2)}) async-start(bf16[8,64,128]{2,1,0:T(8,128)(2,1)} %reshape.407), calls=%async_computation.4 | async-start | bytes 262144 | tf_op jit(solution)/shard_map/all_to_all | solution.py:317

commit v14 on v12

--- a/solution.py
+++ b/solution.py
@@ -64,45 +64,43 @@
     def one_page(step, carry):
         count = filled_ref[step]
 
-        @pl.when(count > 0)
-        def _():
-            row = owner_ref[step]
-            same = column_of(row) == pv_ref[step]
-            valid = lax.broadcasted_iota(jnp.int32, (rows, page), 1) < count
-            query = q_ref[row]
-            stacked = jnp.concatenate(
-                [
-                    jnp.where(column_head == head, query, jnp.zeros_like(query))
-                    for head in range(head_local)
-                ],
-                axis=0,
-            )
-            scores = lax.dot_general(
-                stacked, cache_ref[0, step], (((1,), (1,)), ((), ())),
-                preferred_element_type=jnp.float32,
-            ) * scale
-            scores = scores + jnp.where(same, same_bias, other_bias)
-            block_max = jnp.max(jnp.where(valid, scores, masked_score), axis=1, keepdims=True)
-            weights = jnp.where(valid, jnp.exp(scores - block_max), 0.0).astype(jnp.bfloat16)
-            block_total = jnp.sum(weights.astype(jnp.float32), axis=1, keepdims=True)
-            crossed = jnp.dot(weights, cache_ref[1, step], preferred_element_type=jnp.float32)
-            is_row = request_lane == row
-            old_max = jnp.sum(jnp.where(is_row, max_acc[...], 0.0), axis=1, keepdims=True)
-            old_total = jnp.sum(jnp.where(is_row, total_acc[...], 0.0), axis=1, keepdims=True)
-            new_max = jnp.maximum(old_max, block_max)
-            keep_old = jnp.exp(old_max - new_max)
-            keep_new = jnp.exp(block_max - new_max)
-            max_acc[...] = jnp.where(is_row, new_max, max_acc[...])
-            total_acc[...] = jnp.where(
-                is_row, old_total * keep_old + block_total * keep_new, total_acc[...]
-            )
-            out_acc[row] = out_acc[row] * pick_heads(
-                jnp.broadcast_to(keep_old, crossed.shape)
-            ) + pick_heads(crossed * keep_new)
+        row = owner_ref[step]
+        same = column_of(row) == pv_ref[step]
+        valid = lax.broadcasted_iota(jnp.int32, (rows, page), 1) < count
+        query = q_ref[row]
+        stacked = jnp.concatenate(
+            [
+                jnp.where(column_head == head, query, jnp.zeros_like(query))
+                for head in range(head_local)
+            ],
+            axis=0,
+        )
+        scores = lax.dot_general(
+            stacked, cache_ref[0, step], (((1,), (1,)), ((), ())),
+            preferred_element_type=jnp.float32,
+        ) * scale
+        scores = scores + jnp.where(same, same_bias, other_bias)
+        block_max = jnp.max(jnp.where(valid, scores, masked_score), axis=1, keepdims=True)
+        weights = jnp.where(valid, jnp.exp(scores - block_max), 0.0).astype(jnp.bfloat16)
+        block_total = jnp.sum(weights.astype(jnp.float32), axis=1, keepdims=True)
+        crossed = jnp.dot(weights, cache_ref[1, step], preferred_element_type=jnp.float32)
+        is_row = request_lane == row
+        old_max = jnp.sum(jnp.where(is_row, max_acc[...], 0.0), axis=1, keepdims=True)
+        old_total = jnp.sum(jnp.where(is_row, total_acc[...], 0.0), axis=1, keepdims=True)
+        new_max = jnp.maximum(old_max, block_max)
+        keep_old = jnp.exp(old_max - new_max)
+        keep_new = jnp.exp(block_max - new_max)
+        max_acc[...] = jnp.where(is_row, new_max, max_acc[...])
+        total_acc[...] = jnp.where(
+            is_row, old_total * keep_old + block_total * keep_new, total_acc[...]
+        )
+        out_acc[row] = out_acc[row] * pick_heads(
+            jnp.broadcast_to(keep_old, crossed.shape)
+        ) + pick_heads(crossed * keep_new)
 
         return carry
 
-    lax.fori_loop(0, pool, one_page, 0)
+    lax.fori_loop(0, pool, one_page, 0, unroll=True)
     requests = out_ref.shape[0]
     out_ref[:, :tree, :] = out_acc[...].astype(out_ref.dtype)
     stats = (

time: 104 us -> 103 us (level)
  starting transfers between devices: 38.1 us -> 36.4 us
    all_to_all x1, starting transfers between devices: 10.2 us -> 7.27 us  [shards(): lax.all_to_all(packed, 'req', split_axis=0, concat_axis=0, tiled=True)]
    all_to_all x3, starting transfers between devices: 23.8 us -> 25 us  [gather_rows(): return lax.all_to_all(spread, axis_name, 0, 0, tiled=True)]
where the time goes in v14:
time: 103 us; the launch traced here: 102 us
  starting transfers between devices  36.4 us (35%)
  waiting for transfers between devices  36.3 us (35%)
  local copies, waits for them, and re-layouts  8.49 us (8%)
  Pallas kernels  8.3 us (8%)
  other arithmetic  6.17 us (6%)
  matrix products  5.2 us (5%)
    all_to_all x3, starting transfers between devices, gather_rows(): return lax.all_to_all(spread, axis_name, 0, 0, tiled=True)  25 us
    all_to_all x3, waiting for transfers between devices, gather_rows(): return lax.all_to_all(spread, axis_name, 0, 0, tiled=True)  17.3 us
    all_to_all x1, waiting for transfers between devices, shards(): lax.all_to_all(packed, 'req', split_axis=0, concat_axis=0, tiled=True)  14.5 us
    pallas_call x1, Pallas kernels, page_attention(): pl.pallas_call(kernel, grid_spec=grid_spec, out_shape=jax.ShapeDtypeStruc...  8.3 us
    all_to_all x1, starting transfers between devices, shards(): lax.all_to_all(packed, 'req', split_axis=0, concat_axis=0, tiled=True)  7.27 us
    all_to_all x1, waiting for transfers between devices, shards(): lax.all_to_all(down_part.reshape(head_parts, own_rows, -1), 'head', 0, 0,...  4.48 us
    all_to_all x1, starting transfers between devices, shards(): lax.all_to_all(down_part.reshape(head_parts, own_rows, -1), 'head', 0, 0,...  4.14 us
    broadcast_in_dim x4, local copies, waits for them, and re-layouts, gather_rows(): spread = jnp.broadcast_to(rows[None], (parts,) + rows.shape)  3.15 us
  transfers between devices with their start and end apart: 5, of which 5 were waited for; matrix products, arithmetic and copies ran while one was open for 9% of the time, Pallas kernels for 0%

profile of v14, /device:TPU:1, one launch (start us, length us, event | category | flops | bytes accessed | tf_op | source)
XLA Modules:
  0.0 101.8 jit_solution(12299908768620074953)
XLA Ops:
  0.7 1.5 %broadcast_in_dim.126 = bf16[8,8,1024]{2,1,0:T(8,128)(2,1)} broadcast(bf16[8,1024]{1,0:T(8,128)(2,1)} %param.14), dimensions={1,2} | broadcast | bytes 147456 | tf_op jit(solution)/shard_map/broadcast_in_dim | solution.py:169
  2.2 6.5 %all-to-all-start = ((bf16[8,8,1024]{2,1,0:T(8,128)(2,1)}), bf16[8,8,1024]{2,1,0:T(8,128)(2,1)S(1)}, u32[]{:S(2)}, u32[]{:S(2)}) async-start(bf16[8,8,1024]{2,1,0:T(8,128)(2,1)} %broadcast_in_dim.126), calls=%async_computation | async-start | bytes 262144 | tf_op jit(solution)/shard_map/all_to_all | solution.py:170
  8.7 0.7 convert_element_type.141
  9.4 0.8 dynamic_slice.10
  10.1 0.8 fusion.37
  10.9 0.2 convolution_minimum_fusion.3
  11.1 0.2 convolution_minimum_fusion.2
  11.3 0.2 convolution_minimum_fusion.1
  11.4 0.8 fusion.54
  12.2 1.7 %all-to-all-done = bf16[8,8,1024]{2,1,0:T(8,128)(2,1)S(1)} async-done(((bf16[8,8,1024]{2,1,0:T(8,128)(2,1)}), bf16[8,8,1024]{2,1,0:T(8,128)(2,1)S(1)}, u32[]{:S(2)}, u32[]{:S(2)}) %all-to-all-start) | async-done | bytes 131104 | tf_op jit(solution)/shard_map/all_to_all | solution.py:170
  13.9 0.1 fusion.22
  14.1 1.4 %fusion.8 = bf16[3,64,128]{2,1,0:T(8,128)(2,1)S(1)} fusion(bf16[3,1024,128]{2,1,0:T(8,128)(2,1)} %param.16, bf16[8,8,1024]{2,1,0:T(8,128)(2,1)S(1)} %all-to-all-done, f32[1024]{0:T(1024)S(1)} %bitcast.160, f32[64]{0:T(128)S(1)} %rsqrt.20), kind=kOutput, calls=%fused_computation.15 | convolution fusion | flops 50618368 | bytes 971008 | tf_op jit(solution)/shard_map/td,cdq->ctq/dot_general | solution.py:203
  15.6 0.9 broadcast_in_dim.128
  16.5 10.5 %all-to-all-start.1 = ((bf16[32,64,128]{2,1,0:T(8,128)(2,1)}), bf16[32,64,128]{2,1,0:T(8,128)(2,1)S(1)}, u32[]{:S(2)}, u32[]{:S(2)}) async-start(bf16[32,64,128]{2,1,0:T(8,128)(2,1)} %broadcast_in_dim.128), calls=%async_computation.1 | async-start | bytes 1048576 | tf_op jit(solution)/shard_map/all_to_all | solution.py:170
  27.2 0.1 reshape.404
  27.3 0.6 broadcast_in_dim.132.pv_ref
  27.9 0.1 convert_element_type.143
  28.0 0.2 fusion.9
  28.2 0.1 copy.44
  28.4 1.6 %fusion.15 = (s32[20]{0:T(128)S(1)}, s32[20]{0:T(128)S(1)}, s32[20]{0:T(128)S(1)}, s32[20]{0:T(128)S(1)}) fusion(s32[32,32]{1,0:T(8,128)S(1)} %copy-done.4, s32[20]{0:T(128)S(1)} %iota_add_fusion, s32[32]{0:T(128)S(1)} %copy-done.7), kind=kLoop, calls=%fused_computation.36 | loop fusion | flops 184240 | bytes 4624 | tf_op jit(solution)/shard_map/reduce_sum | solution.py:216
  30.0 0.5 clamp_multiply_fusion
  30.5 0.7 pad_maximum_fusion.aux_ref
  31.2 10.3 %all-to-all-done.1.q_ref = bf16[32,64,128]{2,1,0:T(8,128)(2,1)S(1)} async-done(((bf16[32,64,128]{2,1,0:T(8,128)(2,1)}), bf16[32,64,128]{2,1,0:T(8,128)(2,1)S(1)}, u32[]{:S(2)}, u32[]{:S(2)}) %all-to-all-start.1) | async-done | bytes 524320 | tf_op jit(solution)/shard_map/all_to_all | solution.py:170
  41.6 0.8 copy-done.2
  42.3 8.3 %shard_map.160 = bf16[32,70,128]{2,1,0:T(8,128)(2,1)} custom-call(s32[20]{0:T(128)} %get-tuple-element.37.owner_ref, s32[20]{0:T(128)} %get-tuple-element.36.filled_ref, bf16[32,64,128]{2,1,0:T(8,128)(2,1)} %copy-done.2, f32[128,128]{1,0:T(8,128)} %pad_maximum_fusion.aux_ref, bf16[2,20,128,128]{3,2,1,0:T(8,128)(2,1)} %cache_ref.1, ...), custom_call_target="tpu_custom_call" | custom-call | tf_op jit(solution)/shard_map/pallas_call | solution.py:155
  50.6 7.3 %all-to-all-start.2 = ((bf16[32,70,128]{2,1,0:T(8,128)(2,1)}), bf16[32,70,128]{2,1,0:T(8,128)(2,1)S(1)}, u32[]{:S(2)}, u32[]{:S(2)}) async-start(bf16[32,70,128]{2,1,0:T(8,128)(2,1)} %shard_map.160), calls=%async_computation.2 | async-start | bytes 1179648 | tf_op jit(solution)/shard_map/all_to_all | solution.py:241
  58.0 0.1 reshape.407
  58.1 0.1 copy.54
  58.2 0.1 reshape.408
  58.3 0.2 select_reduce_fusion.1
  58.5 14.5 %all-to-all-done.2 = bf16[32,70,128]{2,1,0:T(8,128)(2,1)S(1)} async-done(((bf16[32,70,128]{2,1,0:T(8,128)(2,1)}), bf16[32,70,128]{2,1,0:T(8,128)(2,1)S(1)}, u32[]{:S(2)}, u32[]{:S(2)}) %all-to-all-start.2) | async-done | bytes 573472 | tf_op jit(solution)/shard_map/all_to_all | solution.py:241
  73.4 0.1 reshape_squeeze.2
  73.6 0.6 select_reduce_fusion
  74.2 0.2 fusion.11
  74.3 0.1 copy.43
  74.5 0.1 fusion.7
  74.6 0.1 copy.49
  74.7 0.7 broadcast_in_dim.145
  75.4 8.1 %all-to-all-start.3 = ((bf16[8,64,128]{2,1,0:T(8,128)(2,1)}), bf16[8,64,128]{2,1,0:T(8,128)(2,1)S(1)}, u32[]{:S(2)}, u32[]{:S(2)}) async-start(bf16[8,64,128]{2,1,0:T(8,128)(2,1)} %broadcast_in_dim.145), calls=%async_computation.3 | async-start | bytes 262144 | tf_op jit(solution)/shard_map/all_to_all | solution.py:170
  83.4 5.3 %all-to-all-done.3 = bf16[8,64,128]{2,1,0:T(8,128)(2,1)S(1)} async-done(((bf16[8,64,128]{2,1,0:T(8,128)(2,1)}), bf16[8,64,128]{2,1,0:T(8,128)(2,1)S(1)}, u32[]{:S(2)}, u32[]{:S(2)}) %all-to-all-start.3) | async-done | bytes 131104 | tf_op jit(solution)/shard_map/all_to_all | solution.py:170
  88.7 0.6 fusion.17
  89.3 1.0 copy-done.1
  90.3 0.5 convolution_bitcast_fusion
  90.8 0.9 fusion.1
  91.8 4.1 %all-to-all-start.4 = ((bf16[8,8,1024]{2,1,0:T(8,128)(2,1)}), bf16[8,8,1024]{2,1,0:T(8,128)(2,1)S(1)}, u32[]{:S(2)}, u32[]{:S(2)}) async-start(bf16[8,8,1024]{2,1,0:T(8,128)(2,1)} %fusion.1), calls=%async_computation.4 | async-start | bytes 262144 | tf_op jit(solution)/shard_map/all_to_all | solution.py:312
  95.9 0.8 fusion.10
  96.7 4.5 %all-to-all-done.4 = bf16[8,8,1024]{2,1,0:T(8,128)(2,1)S(1)} async-done(((bf16[8,8,1024]{2,1,0:T(8,128)(2,1)}), bf16[8,8,1024]{2,1,0:T(8,128)(2,1)S(1)}, u32[]{:S(2)}, u32[]{:S(2)}) %all-to-all-start.4) | async-done | bytes 131104 | tf_op jit(solution)/shard_map/all_to_all | solution.py:312
  101.2 0.6 add_convert_fusion
  (44 shorter events, 1.0 us)
Async XLA Ops:
  0.6 88.1 %copy-start = (bf16[1024,1024]{1,0:T(8,128)(2,1)S(1)}, bf16[1024,1024]{1,0:T(8,128)(2,1)}, u32[]{:S(2)}) copy-start(bf16[1024,1024]{1,0:T(8,128)(2,1)} %param.17) | copy-start | bytes 6291460
  0.6 26.3 %copy-start.6 = (f32[2,16]{1,0:T(2,128)S(1)}, f32[2,16]{1,0:T(2,128)}, u32[]{:S(2)}) copy-start(f32[2,16]{1,0:T(2,128)} %param.20) | copy-start | bytes 388
  0.7 26.7 %copy-start.5 = (s32[20,128]{1,0:T(8,128)S(1)}, s32[20,128]{1,0:T(8,128)}, u32[]{:S(2)}) copy-start(s32[20,128]{1,0:T(8,128)} %param.22) | copy-start | bytes 30724
  0.7 27.7 %copy-start.4 = (s32[32,32]{1,0:T(8,128)S(1)}, s32[32,32]{1,0:T(8,128)}, u32[]{:S(2)}) copy-start(s32[32,32]{1,0:T(8,128)} %param.25) | copy-start | bytes 12292
  0.7 27.7 %copy-start.7 = (s32[32]{0:T(128)S(1)}, s32[32]{0:T(128)}, u32[]{:S(2)}) copy-start(s32[32]{0:T(128)} %param.24) | copy-start | bytes 388
  2.2 11.7 %all-to-all-start = ((bf16[8,8,1024]{2,1,0:T(8,128)(2,1)}), bf16[8,8,1024]{2,1,0:T(8,128)(2,1)S(1)}, u32[]{:S(2)}, u32[]{:S(2)}) async-start(bf16[8,8,1024]{2,1,0:T(8,128)(2,1)} %broadcast_in_dim.126), calls=%async_computation | async-start | bytes 262144 | tf_op jit(solution)/shard_map/all_to_all | solution.py:170
  16.5 25.1 %all-to-all-start.1 = ((bf16[32,64,128]{2,1,0:T(8,128)(2,1)}), bf16[32,64,128]{2,1,0:T(8,128)(2,1)S(1)}, u32[]{:S(2)}, u32[]{:S(2)}) async-start(bf16[32,64,128]{2,1,0:T(8,128)(2,1)} %broadcast_in_dim.128), calls=%async_computation.1 | async-start | bytes 1048576 | tf_op jit(solution)/shard_map/all_to_all | solution.py:170
  41.6 0.8 copy-start.2
  50.6 22.4 %all-to-all-start.2 = ((bf16[32,70,128]{2,1,0:T(8,128)(2,1)}), bf16[32,70,128]{2,1,0:T(8,128)(2,1)S(1)}, u32[]{:S(2)}, u32[]{:S(2)}) async-start(bf16[32,70,128]{2,1,0:T(8,128)(2,1)} %shard_map.160), calls=%async_computation.2 | async-start | bytes 1179648 | tf_op jit(solution)/shard_map/all_to_all | solution.py:241
  74.7 16.1 %copy-start.3 = (bf16[64,128]{1,0:T(8,128)(2,1)}, bf16[64,128]{1,0:T(8,128)(2,1)S(1)}, u32[]{:S(2)}) copy-start(bf16[64,128]{1,0:T(8,128)(2,1)S(1)} %copy.49) | copy-start | bytes 49156
  75.4 13.3 %all-to-all-start.3 = ((bf16[8,64,128]{2,1,0:T(8,128)(2,1)}), bf16[8,64,128]{2,1,0:T(8,128)(2,1)S(1)}, u32[]{:S(2)}, u32[]{:S(2)}) async-start(bf16[8,64,128]{2,1,0:T(8,128)(2,1)} %broadcast_in_dim.145), calls=%async_computation.3 | async-start | bytes 262144 | tf_op jit(solution)/shard_map/all_to_all | solution.py:170
  88.7 1.6 %copy-start.1 = (bf16[2,1024,512]{2,1,0:T(8,128)(2,1)S(1)}, bf16[2,1024,512]{2,1,0:T(8,128)(2,1)}, u32[]{:S(2)}) copy-start(bf16[2,1024,512]{2,1,0:T(8,128)(2,1)} %param.18) | copy-start | bytes 6291460
  88.7 2.1 %copy-start.8 = (bf16[512,1024]{1,0:T(8,128)(2,1)S(1)}, bf16[512,1024]{1,0:T(8,128)(2,1)}, u32[]{:S(2)}) copy-start(bf16[512,1024]{1,0:T(8,128)(2,1)} %param.19) | copy-start | bytes 3145732
  89.3 6.6 %copy-start.9 = (s32[1,8]{1,0:T(1,128)S(1)}, s32[1,8]{1,0:T(1,128)}, u32[]{:S(2)}) copy-start(s32[1,8]{1,0:T(1,128)} %param.27) | copy-start | bytes 100
  91.8 9.4 %all-to-all-start.4 = ((bf16[8,8,1024]{2,1,0:T(8,128)(2,1)}), bf16[8,8,1024]{2,1,0:T(8,128)(2,1)S(1)}, u32[]{:S(2)}, u32[]{:S(2)}) async-start(bf16[8,8,1024]{2,1,0:T(8,128)(2,1)} %fusion.1), calls=%async_computation.4 | async-start | bytes 262144 | tf_op jit(solution)/shard_map/all_to_all | solution.py:312

commit v15 on v14

--- a/solution.py
+++ b/solution.py
@@ -43,7 +43,7 @@
     out_acc[...] = jnp.zeros(out_acc.shape, jnp.float32)
     max_acc[...] = jnp.full(max_acc.shape, masked_score, jnp.float32)
     total_acc[...] = jnp.zeros(total_acc.shape, jnp.float32)
-    request_lane = lax.broadcasted_iota(jnp.int32, max_acc.shape, 1)
+    request_lane = lax.broadcasted_iota(jnp.int32, (rows, lanes), 1)
     column_head = lax.broadcasted_iota(jnp.int32, out_acc.shape[1:], 1) // HD
     aux_columns = jnp.transpose(aux_ref[...])
 
@@ -84,16 +84,13 @@
         weights = jnp.where(valid, jnp.exp(scores - block_max), 0.0).astype(jnp.bfloat16)
         block_total = jnp.sum(weights.astype(jnp.float32), axis=1, keepdims=True)
         crossed = jnp.dot(weights, cache_ref[1, step], preferred_element_type=jnp.float32)
-        is_row = request_lane == row
-        old_max = jnp.sum(jnp.where(is_row, max_acc[...], 0.0), axis=1, keepdims=True)
-        old_total = jnp.sum(jnp.where(is_row, total_acc[...], 0.0), axis=1, keepdims=True)
+        old_max = max_acc[row]
+        old_total = total_acc[row]
         new_max = jnp.maximum(old_max, block_max)
         keep_old = jnp.exp(old_max - new_max)
         keep_new = jnp.exp(block_max - new_max)
-        max_acc[...] = jnp.where(is_row, new_max, max_acc[...])
-        total_acc[...] = jnp.where(
-            is_row, old_total * keep_old + block_total * keep_new, total_acc[...]
-        )
+        max_acc[row] = new_max
+        total_acc[row] = old_total * keep_old + block_total * keep_new
         out_acc[row] = out_acc[row] * pick_heads(
             jnp.broadcast_to(keep_old, crossed.shape)
         ) + pick_heads(crossed * keep_new)
@@ -103,10 +100,13 @@
     lax.fori_loop(0, pool, one_page, 0, unroll=True)
     requests = out_ref.shape[0]
     out_ref[:, :tree, :] = out_acc[...].astype(out_ref.dtype)
-    stats = (
-        jnp.transpose(total_acc[...])[:requests],
-        jnp.transpose(max_acc[...])[:requests],
-    )
+    def lane_table(columns, fill):
+        table = jnp.full((rows, lanes), fill, jnp.float32)
+        for request in range(requests):
+            table = jnp.where(request_lane == request, columns[request], table)
+        return jnp.transpose(table)[:requests]
+
+    stats = (lane_table(total_acc, 0.0), lane_table(max_acc, masked_score))
     for kind, values in enumerate(stats):
         for part in range(3):
             rounded = values.astype(out_ref.dtype)
@@ -148,8 +148,8 @@
         out_specs=whole((requests, tree + 6, qdl)),
         scratch_shapes=[
             pltpu.VMEM((requests, tree, qdl), jnp.float32),
-            pltpu.VMEM((rows, lanes), jnp.float32),
-            pltpu.VMEM((rows, lanes), jnp.float32),
+            pltpu.VMEM((requests, rows, 1), jnp.float32),
+            pltpu.VMEM((requests, rows, 1), jnp.float32),
         ],
     )
     return pl.pallas_call(

time: 103 us -> 105 us (1.019)
  Pallas kernels: 8.3 us -> 10.1 us
    pallas_call x1, Pallas kernels: 8.3 us -> 10.1 us  [page_attention(): pl.pallas_call(kernel, grid_spec=grid_spec, out_shape=jax.ShapeDtypeStruc...]
where the time goes in v15:
time: 105 us; the launch traced here: 104 us
  starting transfers between devices  36.4 us (35%)
  waiting for transfers between devices  36.3 us (35%)
  Pallas kernels  10.1 us (10%)
  local copies, waits for them, and re-layouts  8.49 us (8%)
  other arithmetic  6.17 us (6%)
  matrix products  5.2 us (5%)
    all_to_all x3, starting transfers between devices, gather_rows(): return lax.all_to_all(spread, axis_name, 0, 0, tiled=True)  25 us
    all_to_all x3, waiting for transfers between devices, gather_rows(): return lax.all_to_all(spread, axis_name, 0, 0, tiled=True)  17.3 us
    all_to_all x1, waiting for transfers between devices, shards(): lax.all_to_all(packed, 'req', split_axis=0, concat_axis=0, tiled=True)  14.5 us
    pallas_call x1, Pallas kernels, page_attention(): pl.pallas_call(kernel, grid_spec=grid_spec, out_shape=jax.ShapeDtypeStruc...  10.1 us
    all_to_all x1, starting transfers between devices, shards(): lax.all_to_all(packed, 'req', split_axis=0, concat_axis=0, tiled=True)  7.28 us
    all_to_all x1, waiting for transfers between devices, shards(): lax.all_to_all(down_part.reshape(head_parts, own_rows, -1), 'head', 0, 0,...  4.48 us
    all_to_all x1, starting transfers between devices, shards(): lax.all_to_all(down_part.reshape(head_parts, own_rows, -1), 'head', 0, 0,...  4.13 us
    broadcast_in_dim x4, local copies, waits for them, and re-layouts, gather_rows(): spread = jnp.broadcast_to(rows[None], (parts,) + rows.shape)  3.15 us
  transfers between devices with their start and end apart: 5, of which 5 were waited for; matrix products, arithmetic and copies ran while one was open for 9% of the time, Pallas kernels for 0%

profile of v15, /device:TPU:1, one launch (start us, length us, event | category | flops | bytes accessed | tf_op | source)
XLA Modules:
  0.0 103.6 jit_solution(1461384625881364093)
XLA Ops:
  0.7 1.5 %broadcast_in_dim.126 = bf16[8,8,1024]{2,1,0:T(8,128)(2,1)} broadcast(bf16[8,1024]{1,0:T(8,128)(2,1)} %param.14), dimensions={1,2} | broadcast | bytes 147456 | tf_op jit(solution)/shard_map/broadcast_in_dim | solution.py:169
  2.2 6.5 %all-to-all-start = ((bf16[8,8,1024]{2,1,0:T(8,128)(2,1)}), bf16[8,8,1024]{2,1,0:T(8,128)(2,1)S(1)}, u32[]{:S(2)}, u32[]{:S(2)}) async-start(bf16[8,8,1024]{2,1,0:T(8,128)(2,1)} %broadcast_in_dim.126), calls=%async_computation | async-start | bytes 262144 | tf_op jit(solution)/shard_map/all_to_all | solution.py:170
  8.7 0.7 convert_element_type.141
  9.4 0.8 dynamic_slice.10
  10.1 0.8 fusion.37
  10.9 0.2 convolution_minimum_fusion.3
  11.1 0.2 convolution_minimum_fusion.2
  11.3 0.2 convolution_minimum_fusion.1
  11.4 0.8 fusion.54
  12.2 1.7 %all-to-all-done = bf16[8,8,1024]{2,1,0:T(8,128)(2,1)S(1)} async-done(((bf16[8,8,1024]{2,1,0:T(8,128)(2,1)}), bf16[8,8,1024]{2,1,0:T(8,128)(2,1)S(1)}, u32[]{:S(2)}, u32[]{:S(2)}) %all-to-all-start) | async-done | bytes 131104 | tf_op jit(solution)/shard_map/all_to_all | solution.py:170
  13.9 0.1 fusion.22
  14.1 1.4 %fusion.8 = bf16[3,64,128]{2,1,0:T(8,128)(2,1)S(1)} fusion(bf16[3,1024,128]{2,1,0:T(8,128)(2,1)} %param.16, bf16[8,8,1024]{2,1,0:T(8,128)(2,1)S(1)} %all-to-all-done, f32[1024]{0:T(1024)S(1)} %bitcast.160, f32[64]{0:T(128)S(1)} %rsqrt.20), kind=kOutput, calls=%fused_computation.15 | convolution fusion | flops 50618368 | bytes 971008 | tf_op jit(solution)/shard_map/td,cdq->ctq/dot_general | solution.py:203
  15.6 0.9 broadcast_in_dim.128
  16.5 10.5 %all-to-all-start.1 = ((bf16[32,64,128]{2,1,0:T(8,128)(2,1)}), bf16[32,64,128]{2,1,0:T(8,128)(2,1)S(1)}, u32[]{:S(2)}, u32[]{:S(2)}) async-start(bf16[32,64,128]{2,1,0:T(8,128)(2,1)} %broadcast_in_dim.128), calls=%async_computation.1 | async-start | bytes 1048576 | tf_op jit(solution)/shard_map/all_to_all | solution.py:170
  27.2 0.1 reshape.404
  27.3 0.6 broadcast_in_dim.132.pv_ref
  27.9 0.1 convert_element_type.143
  28.0 0.2 fusion.9
  28.2 0.1 copy.44
  28.4 1.6 %fusion.15 = (s32[20]{0:T(128)S(1)}, s32[20]{0:T(128)S(1)}, s32[20]{0:T(128)S(1)}, s32[20]{0:T(128)S(1)}) fusion(s32[32,32]{1,0:T(8,128)S(1)} %copy-done.4, s32[20]{0:T(128)S(1)} %iota_add_fusion, s32[32]{0:T(128)S(1)} %copy-done.7), kind=kLoop, calls=%fused_computation.36 | loop fusion | flops 184240 | bytes 4624 | tf_op jit(solution)/shard_map/reduce_sum | solution.py:216
  30.0 0.5 clamp_multiply_fusion
  30.5 0.7 pad_maximum_fusion.aux_ref
  31.2 10.3 %all-to-all-done.1.q_ref = bf16[32,64,128]{2,1,0:T(8,128)(2,1)S(1)} async-done(((bf16[32,64,128]{2,1,0:T(8,128)(2,1)}), bf16[32,64,128]{2,1,0:T(8,128)(2,1)S(1)}, u32[]{:S(2)}, u32[]{:S(2)}) %all-to-all-start.1) | async-done | bytes 524320 | tf_op jit(solution)/shard_map/all_to_all | solution.py:170
  41.6 0.8 copy-done.2
  42.3 10.1 %shard_map.160 = bf16[32,70,128]{2,1,0:T(8,128)(2,1)} custom-call(s32[20]{0:T(128)} %get-tuple-element.37.owner_ref, s32[20]{0:T(128)} %get-tuple-element.36.filled_ref, bf16[32,64,128]{2,1,0:T(8,128)(2,1)} %copy-done.2, f32[128,128]{1,0:T(8,128)} %pad_maximum_fusion.aux_ref, bf16[2,20,128,128]{3,2,1,0:T(8,128)(2,1)} %cache_ref.1, ...), custom_call_target="tpu_custom_call" | custom-call | tf_op jit(solution)/shard_map/pallas_call | solution.py:155
  52.5 7.3 %all-to-all-start.2 = ((bf16[32,70,128]{2,1,0:T(8,128)(2,1)}), bf16[32,70,128]{2,1,0:T(8,128)(2,1)S(1)}, u32[]{:S(2)}, u32[]{:S(2)}) async-start(bf16[32,70,128]{2,1,0:T(8,128)(2,1)} %shard_map.160), calls=%async_computation.2 | async-start | bytes 1179648 | tf_op jit(solution)/shard_map/all_to_all | solution.py:241
  59.9 0.1 reshape.407
  59.9 0.1 copy.54
  60.1 0.1 reshape.408
  60.2 0.2 select_reduce_fusion.1
  60.4 14.5 %all-to-all-done.2 = bf16[32,70,128]{2,1,0:T(8,128)(2,1)S(1)} async-done(((bf16[32,70,128]{2,1,0:T(8,128)(2,1)}), bf16[32,70,128]{2,1,0:T(8,128)(2,1)S(1)}, u32[]{:S(2)}, u32[]{:S(2)}) %all-to-all-start.2) | async-done | bytes 573472 | tf_op jit(solution)/shard_map/all_to_all | solution.py:241
  75.3 0.1 reshape_squeeze.2
  75.4 0.6 select_reduce_fusion
  76.0 0.2 fusion.11
  76.2 0.1 copy.43
  76.3 0.1 fusion.7
  76.4 0.1 copy.49
  76.5 0.7 broadcast_in_dim.145
  77.2 8.1 %all-to-all-start.3 = ((bf16[8,64,128]{2,1,0:T(8,128)(2,1)}), bf16[8,64,128]{2,1,0:T(8,128)(2,1)S(1)}, u32[]{:S(2)}, u32[]{:S(2)}) async-start(bf16[8,64,128]{2,1,0:T(8,128)(2,1)} %broadcast_in_dim.145), calls=%async_computation.3 | async-start | bytes 262144 | tf_op jit(solution)/shard_map/all_to_all | solution.py:170
  85.3 5.3 %all-to-all-done.3 = bf16[8,64,128]{2,1,0:T(8,128)(2,1)S(1)} async-done(((bf16[8,64,128]{2,1,0:T(8,128)(2,1)}), bf16[8,64,128]{2,1,0:T(8,128)(2,1)S(1)}, u32[]{:S(2)}, u32[]{:S(2)}) %all-to-all-start.3) | async-done | bytes 131104 | tf_op jit(solution)/shard_map/all_to_all | solution.py:170
  90.5 0.6 fusion.17
  91.1 1.0 copy-done.1
  92.1 0.5 convolution_bitcast_fusion
  92.7 0.9 fusion.1
  93.6 4.1 %all-to-all-start.4 = ((bf16[8,8,1024]{2,1,0:T(8,128)(2,1)}), bf16[8,8,1024]{2,1,0:T(8,128)(2,1)S(1)}, u32[]{:S(2)}, u32[]{:S(2)}) async-start(bf16[8,8,1024]{2,1,0:T(8,128)(2,1)} %fusion.1), calls=%async_computation.4 | async-start | bytes 262144 | tf_op jit(solution)/shard_map/all_to_all | solution.py:312
  97.7 0.8 fusion.10
  98.5 4.5 %all-to-all-done.4 = bf16[8,8,1024]{2,1,0:T(8,128)(2,1)S(1)} async-done(((bf16[8,8,1024]{2,1,0:T(8,128)(2,1)}), bf16[8,8,1024]{2,1,0:T(8,128)(2,1)S(1)}, u32[]{:S(2)}, u32[]{:S(2)}) %all-to-all-start.4) | async-done | bytes 131104 | tf_op jit(solution)/shard_map/all_to_all | solution.py:312
  103.0 0.6 add_convert_fusion
  (44 shorter events, 1.0 us)
Async XLA Ops:
  0.6 89.9 %copy-start = (bf16[1024,1024]{1,0:T(8,128)(2,1)S(1)}, bf16[1024,1024]{1,0:T(8,128)(2,1)}, u32[]{:S(2)}) copy-start(bf16[1024,1024]{1,0:T(8,128)(2,1)} %param.17) | copy-start | bytes 6291460
  0.6 26.3 %copy-start.6 = (f32[2,16]{1,0:T(2,128)S(1)}, f32[2,16]{1,0:T(2,128)}, u32[]{:S(2)}) copy-start(f32[2,16]{1,0:T(2,128)} %param.20) | copy-start | bytes 388
  0.7 26.7 %copy-start.5 = (s32[20,128]{1,0:T(8,128)S(1)}, s32[20,128]{1,0:T(8,128)}, u32[]{:S(2)}) copy-start(s32[20,128]{1,0:T(8,128)} %param.22) | copy-start | bytes 30724
  0.7 27.7 %copy-start.4 = (s32[32,32]{1,0:T(8,128)S(1)}, s32[32,32]{1,0:T(8,128)}, u32[]{:S(2)}) copy-start(s32[32,32]{1,0:T(8,128)} %param.25) | copy-start | bytes 12292
  0.7 27.7 %copy-start.7 = (s32[32]{0:T(128)S(1)}, s32[32]{0:T(128)}, u32[]{:S(2)}) copy-start(s32[32]{0:T(128)} %param.24) | copy-start | bytes 388
  2.2 11.7 %all-to-all-start = ((bf16[8,8,1024]{2,1,0:T(8,128)(2,1)}), bf16[8,8,1024]{2,1,0:T(8,128)(2,1)S(1)}, u32[]{:S(2)}, u32[]{:S(2)}) async-start(bf16[8,8,1024]{2,1,0:T(8,128)(2,1)} %broadcast_in_dim.126), calls=%async_computation | async-start | bytes 262144 | tf_op jit(solution)/shard_map/all_to_all | solution.py:170
  16.5 25.1 %all-to-all-start.1 = ((bf16[32,64,128]{2,1,0:T(8,128)(2,1)}), bf16[32,64,128]{2,1,0:T(8,128)(2,1)S(1)}, u32[]{:S(2)}, u32[]{:S(2)}) async-start(bf16[32,64,128]{2,1,0:T(8,128)(2,1)} %broadcast_in_dim.128), calls=%async_computation.1 | async-start | bytes 1048576 | tf_op jit(solution)/shard_map/all_to_all | solution.py:170
  41.6 0.8 copy-start.2
  52.5 22.4 %all-to-all-start.2 = ((bf16[32,70,128]{2,1,0:T(8,128)(2,1)}), bf16[32,70,128]{2,1,0:T(8,128)(2,1)S(1)}, u32[]{:S(2)}, u32[]{:S(2)}) async-start(bf16[32,70,128]{2,1,0:T(8,128)(2,1)} %shard_map.160), calls=%async_computation.2 | async-start | bytes 1179648 | tf_op jit(solution)/shard_map/all_to_all | solution.py:241
  76.5 16.1 %copy-start.3 = (bf16[64,128]{1,0:T(8,128)(2,1)}, bf16[64,128]{1,0:T(8,128)(2,1)S(1)}, u32[]{:S(2)}) copy-start(bf16[64,128]{1,0:T(8,128)(2,1)S(1)} %copy.49) | copy-start | bytes 49156
  77.2 13.3 %all-to-all-start.3 = ((bf16[8,64,128]{2,1,0:T(8,128)(2,1)}), bf16[8,64,128]{2,1,0:T(8,128)(2,1)S(1)}, u32[]{:S(2)}, u32[]{:S(2)}) async-start(bf16[8,64,128]{2,1,0:T(8,128)(2,1)} %broadcast_in_dim.145), calls=%async_computation.3 | async-start | bytes 262144 | tf_op jit(solution)/shard_map/all_to_all | solution.py:170
  90.5 1.6 %copy-start.1 = (bf16[2,1024,512]{2,1,0:T(8,128)(2,1)S(1)}, bf16[2,1024,512]{2,1,0:T(8,128)(2,1)}, u32[]{:S(2)}) copy-start(bf16[2,1024,512]{2,1,0:T(8,128)(2,1)} %param.18) | copy-start | bytes 6291460
  90.5 2.1 %copy-start.8 = (bf16[512,1024]{1,0:T(8,128)(2,1)S(1)}, bf16[512,1024]{1,0:T(8,128)(2,1)}, u32[]{:S(2)}) copy-start(bf16[512,1024]{1,0:T(8,128)(2,1)} %param.19) | copy-start | bytes 3145732
  91.1 6.6 %copy-start.9 = (s32[1,8]{1,0:T(1,128)S(1)}, s32[1,8]{1,0:T(1,128)}, u32[]{:S(2)}) copy-start(s32[1,8]{1,0:T(1,128)} %param.27) | copy-start | bytes 100
  93.6 9.4 %all-to-all-start.4 = ((bf16[8,8,1024]{2,1,0:T(8,128)(2,1)}), bf16[8,8,1024]{2,1,0:T(8,128)(2,1)S(1)}, u32[]{:S(2)}, u32[]{:S(2)}) async-start(bf16[8,8,1024]{2,1,0:T(8,128)(2,1)} %fusion.1), calls=%async_computation.4 | async-start | bytes 262144 | tf_op jit(solution)/shard_map/all_to_all | solution.py:312

commit v16 on v14

--- a/solution.py
+++ b/solution.py
@@ -100,7 +100,7 @@
 
         return carry
 
-    lax.fori_loop(0, pool, one_page, 0, unroll=True)
+    lax.fori_loop(0, pool, one_page, 0, unroll=4)
     requests = out_ref.shape[0]
     out_ref[:, :tree, :] = out_acc[...].astype(out_ref.dtype)
     stats = (

time: 103 us -> 104 us (level)
  Pallas kernels: 8.3 us -> 9.36 us
    pallas_call x1, Pallas kernels: 8.3 us -> 9.36 us  [page_attention(): pl.pallas_call(kernel, grid_spec=grid_spec, out_shape=jax.ShapeDtypeStruc...]
where the time goes in v16:
time: 104 us; the launch traced here: 103 us
  starting transfers between devices  36.4 us (35%)
  waiting for transfers between devices  36.3 us (35%)
  Pallas kernels  9.36 us (9%)
  local copies, waits for them, and re-layouts  8.49 us (8%)
  other arithmetic  6.17 us (6%)
  matrix products  5.19 us (5%)
    all_to_all x3, starting transfers between devices, gather_rows(): return lax.all_to_all(spread, axis_name, 0, 0, tiled=True)  25 us
    all_to_all x3, waiting for transfers between devices, gather_rows(): return lax.all_to_all(spread, axis_name, 0, 0, tiled=True)  17.3 us
    all_to_all x1, waiting for transfers between devices, shards(): lax.all_to_all(packed, 'req', split_axis=0, concat_axis=0, tiled=True)  14.5 us
    pallas_call x1, Pallas kernels, page_attention(): pl.pallas_call(kernel, grid_spec=grid_spec, out_shape=jax.ShapeDtypeStruc...  9.36 us
    all_to_all x1, starting transfers between devices, shards(): lax.all_to_all(packed, 'req', split_axis=0, concat_axis=0, tiled=True)  7.27 us
    all_to_all x1, waiting for transfers between devices, shards(): lax.all_to_all(down_part.reshape(head_parts, own_rows, -1), 'head', 0, 0,...  4.48 us
    all_to_all x1, starting transfers between devices, shards(): lax.all_to_all(down_part.reshape(head_parts, own_rows, -1), 'head', 0, 0,...  4.14 us
    broadcast_in_dim x4, local copies, waits for them, and re-layouts, gather_rows(): spread = jnp.broadcast_to(rows[None], (parts,) + rows.shape)  3.15 us
  transfers between devices with their start and end apart: 5, of which 5 were waited for; matrix products, arithmetic and copies ran while one was open for 9% of the time, Pallas kernels for 0%

profile of v16, /device:TPU:1, one launch (start us, length us, event | category | flops | bytes accessed | tf_op | source)
XLA Modules:
  0.0 102.9 jit_solution(330081529329241136)
XLA Ops:
  0.7 1.5 %broadcast_in_dim.126 = bf16[8,8,1024]{2,1,0:T(8,128)(2,1)} broadcast(bf16[8,1024]{1,0:T(8,128)(2,1)} %param.14), dimensions={1,2} | broadcast | bytes 147456 | tf_op jit(solution)/shard_map/broadcast_in_dim | solution.py:169
  2.2 6.5 %all-to-all-start = ((bf16[8,8,1024]{2,1,0:T(8,128)(2,1)}), bf16[8,8,1024]{2,1,0:T(8,128)(2,1)S(1)}, u32[]{:S(2)}, u32[]{:S(2)}) async-start(bf16[8,8,1024]{2,1,0:T(8,128)(2,1)} %broadcast_in_dim.126), calls=%async_computation | async-start | bytes 262144 | tf_op jit(solution)/shard_map/all_to_all | solution.py:170
  8.7 0.7 convert_element_type.141
  9.4 0.8 dynamic_slice.10
  10.1 0.8 fusion.37
  10.9 0.2 convolution_minimum_fusion.3
  11.1 0.2 convolution_minimum_fusion.2
  11.3 0.2 convolution_minimum_fusion.1
  11.4 0.8 fusion.54
  12.2 1.7 %all-to-all-done = bf16[8,8,1024]{2,1,0:T(8,128)(2,1)S(1)} async-done(((bf16[8,8,1024]{2,1,0:T(8,128)(2,1)}), bf16[8,8,1024]{2,1,0:T(8,128)(2,1)S(1)}, u32[]{:S(2)}, u32[]{:S(2)}) %all-to-all-start) | async-done | bytes 131104 | tf_op jit(solution)/shard_map/all_to_all | solution.py:170
  13.9 0.1 fusion.22
  14.1 1.4 %fusion.8 = bf16[3,64,128]{2,1,0:T(8,128)(2,1)S(1)} fusion(bf16[3,1024,128]{2,1,0:T(8,128)(2,1)} %param.16, bf16[8,8,1024]{2,1,0:T(8,128)(2,1)S(1)} %all-to-all-done, f32[1024]{0:T(1024)S(1)} %bitcast.160, f32[64]{0:T(128)S(1)} %rsqrt.20), kind=kOutput, calls=%fused_computation.15 | convolution fusion | flops 50618368 | bytes 971008 | tf_op jit(solution)/shard_map/td,cdq->ctq/dot_general | solution.py:203
  15.6 0.9 broadcast_in_dim.128
  16.5 10.5 %all-to-all-start.1 = ((bf16[32,64,128]{2,1,0:T(8,128)(2,1)}), bf16[32,64,128]{2,1,0:T(8,128)(2,1)S(1)}, u32[]{:S(2)}, u32[]{:S(2)}) async-start(bf16[32,64,128]{2,1,0:T(8,128)(2,1)} %broadcast_in_dim.128), calls=%async_computation.1 | async-start | bytes 1048576 | tf_op jit(solution)/shard_map/all_to_all | solution.py:170
  27.2 0.1 reshape.404
  27.3 0.6 broadcast_in_dim.132.pv_ref
  27.9 0.1 convert_element_type.143
  28.0 0.2 fusion.9
  28.2 0.1 copy.44
  28.4 1.6 %fusion.15 = (s32[20]{0:T(128)S(1)}, s32[20]{0:T(128)S(1)}, s32[20]{0:T(128)S(1)}, s32[20]{0:T(128)S(1)}) fusion(s32[32,32]{1,0:T(8,128)S(1)} %copy-done.4, s32[20]{0:T(128)S(1)} %iota_add_fusion, s32[32]{0:T(128)S(1)} %copy-done.7), kind=kLoop, calls=%fused_computation.36 | loop fusion | flops 184240 | bytes 4624 | tf_op jit(solution)/shard_map/reduce_sum | solution.py:216
  30.0 0.5 clamp_multiply_fusion
  30.5 0.7 pad_maximum_fusion.aux_ref
  31.2 10.3 %all-to-all-done.1.q_ref = bf16[32,64,128]{2,1,0:T(8,128)(2,1)S(1)} async-done(((bf16[32,64,128]{2,1,0:T(8,128)(2,1)}), bf16[32,64,128]{2,1,0:T(8,128)(2,1)S(1)}, u32[]{:S(2)}, u32[]{:S(2)}) %all-to-all-start.1) | async-done | bytes 524320 | tf_op jit(solution)/shard_map/all_to_all | solution.py:170
  41.6 0.8 copy-done.2
  42.3 9.4 %shard_map.160 = bf16[32,70,128]{2,1,0:T(8,128)(2,1)} custom-call(s32[20]{0:T(128)} %get-tuple-element.37.owner_ref, s32[20]{0:T(128)} %get-tuple-element.36.filled_ref, bf16[32,64,128]{2,1,0:T(8,128)(2,1)} %copy-done.2, f32[128,128]{1,0:T(8,128)} %pad_maximum_fusion.aux_ref, bf16[2,20,128,128]{3,2,1,0:T(8,128)(2,1)} %cache_ref.1, ...), custom_call_target="tpu_custom_call" | custom-call | tf_op jit(solution)/shard_map/pallas_call | solution.py:155
  51.7 7.3 %all-to-all-start.2 = ((bf16[32,70,128]{2,1,0:T(8,128)(2,1)}), bf16[32,70,128]{2,1,0:T(8,128)(2,1)S(1)}, u32[]{:S(2)}, u32[]{:S(2)}) async-start(bf16[32,70,128]{2,1,0:T(8,128)(2,1)} %shard_map.160), calls=%async_computation.2 | async-start | bytes 1179648 | tf_op jit(solution)/shard_map/all_to_all | solution.py:241
  59.1 0.1 reshape.407
  59.2 0.1 copy.54
  59.3 0.1 reshape.408
  59.4 0.2 select_reduce_fusion.1
  59.6 14.5 %all-to-all-done.2 = bf16[32,70,128]{2,1,0:T(8,128)(2,1)S(1)} async-done(((bf16[32,70,128]{2,1,0:T(8,128)(2,1)}), bf16[32,70,128]{2,1,0:T(8,128)(2,1)S(1)}, u32[]{:S(2)}, u32[]{:S(2)}) %all-to-all-start.2) | async-done | bytes 573472 | tf_op jit(solution)/shard_map/all_to_all | solution.py:241
  74.5 0.1 reshape_squeeze.2
  74.6 0.6 select_reduce_fusion
  75.2 0.2 fusion.11
  75.4 0.1 copy.43
  75.5 0.1 fusion.7
  75.7 0.1 copy.49
  75.8 0.7 broadcast_in_dim.145
  76.4 8.1 %all-to-all-start.3 = ((bf16[8,64,128]{2,1,0:T(8,128)(2,1)}), bf16[8,64,128]{2,1,0:T(8,128)(2,1)S(1)}, u32[]{:S(2)}, u32[]{:S(2)}) async-start(bf16[8,64,128]{2,1,0:T(8,128)(2,1)} %broadcast_in_dim.145), calls=%async_computation.3 | async-start | bytes 262144 | tf_op jit(solution)/shard_map/all_to_all | solution.py:170
  84.5 5.3 %all-to-all-done.3 = bf16[8,64,128]{2,1,0:T(8,128)(2,1)S(1)} async-done(((bf16[8,64,128]{2,1,0:T(8,128)(2,1)}), bf16[8,64,128]{2,1,0:T(8,128)(2,1)S(1)}, u32[]{:S(2)}, u32[]{:S(2)}) %all-to-all-start.3) | async-done | bytes 131104 | tf_op jit(solution)/shard_map/all_to_all | solution.py:170
  89.8 0.6 fusion.17
  90.4 1.0 copy-done.1
  91.3 0.5 convolution_bitcast_fusion
  91.9 0.9 fusion.1
  92.8 4.1 %all-to-all-start.4 = ((bf16[8,8,1024]{2,1,0:T(8,128)(2,1)}), bf16[8,8,1024]{2,1,0:T(8,128)(2,1)S(1)}, u32[]{:S(2)}, u32[]{:S(2)}) async-start(bf16[8,8,1024]{2,1,0:T(8,128)(2,1)} %fusion.1), calls=%async_computation.4 | async-start | bytes 262144 | tf_op jit(solution)/shard_map/all_to_all | solution.py:312
  97.0 0.8 fusion.10
  97.7 4.5 %all-to-all-done.4 = bf16[8,8,1024]{2,1,0:T(8,128)(2,1)S(1)} async-done(((bf16[8,8,1024]{2,1,0:T(8,128)(2,1)}), bf16[8,8,1024]{2,1,0:T(8,128)(2,1)S(1)}, u32[]{:S(2)}, u32[]{:S(2)}) %all-to-all-start.4) | async-done | bytes 131104 | tf_op jit(solution)/shard_map/all_to_all | solution.py:312
  102.2 0.6 add_convert_fusion
  (44 shorter events, 1.0 us)
Async XLA Ops:
  0.6 89.1 %copy-start = (bf16[1024,1024]{1,0:T(8,128)(2,1)S(1)}, bf16[1024,1024]{1,0:T(8,128)(2,1)}, u32[]{:S(2)}) copy-start(bf16[1024,1024]{1,0:T(8,128)(2,1)} %param.17) | copy-start | bytes 6291460
  0.6 26.3 %copy-start.6 = (f32[2,16]{1,0:T(2,128)S(1)}, f32[2,16]{1,0:T(2,128)}, u32[]{:S(2)}) copy-start(f32[2,16]{1,0:T(2,128)} %param.20) | copy-start | bytes 388
  0.7 26.7 %copy-start.5 = (s32[20,128]{1,0:T(8,128)S(1)}, s32[20,128]{1,0:T(8,128)}, u32[]{:S(2)}) copy-start(s32[20,128]{1,0:T(8,128)} %param.22) | copy-start | bytes 30724
  0.7 27.7 %copy-start.4 = (s32[32,32]{1,0:T(8,128)S(1)}, s32[32,32]{1,0:T(8,128)}, u32[]{:S(2)}) copy-start(s32[32,32]{1,0:T(8,128)} %param.25) | copy-start | bytes 12292
  0.7 27.7 %copy-start.7 = (s32[32]{0:T(128)S(1)}, s32[32]{0:T(128)}, u32[]{:S(2)}) copy-start(s32[32]{0:T(128)} %param.24) | copy-start | bytes 388
  2.2 11.7 %all-to-all-start = ((bf16[8,8,1024]{2,1,0:T(8,128)(2,1)}), bf16[8,8,1024]{2,1,0:T(8,128)(2,1)S(1)}, u32[]{:S(2)}, u32[]{:S(2)}) async-start(bf16[8,8,1024]{2,1,0:T(8,128)(2,1)} %broadcast_in_dim.126), calls=%async_computation | async-start | bytes 262144 | tf_op jit(solution)/shard_map/all_to_all | solution.py:170
  16.5 25.1 %all-to-all-start.1 = ((bf16[32,64,128]{2,1,0:T(8,128)(2,1)}), bf16[32,64,128]{2,1,0:T(8,128)(2,1)S(1)}, u32[]{:S(2)}, u32[]{:S(2)}) async-start(bf16[32,64,128]{2,1,0:T(8,128)(2,1)} %broadcast_in_dim.128), calls=%async_computation.1 | async-start | bytes 1048576 | tf_op jit(solution)/shard_map/all_to_all | solution.py:170
  41.6 0.8 copy-start.2
  51.7 22.4 %all-to-all-start.2 = ((bf16[32,70,128]{2,1,0:T(8,128)(2,1)}), bf16[32,70,128]{2,1,0:T(8,128)(2,1)S(1)}, u32[]{:S(2)}, u32[]{:S(2)}) async-start(bf16[32,70,128]{2,1,0:T(8,128)(2,1)} %shard_map.160), calls=%async_computation.2 | async-start | bytes 1179648 | tf_op jit(solution)/shard_map/all_to_all | solution.py:241
  75.7 16.1 %copy-start.3 = (bf16[64,128]{1,0:T(8,128)(2,1)}, bf16[64,128]{1,0:T(8,128)(2,1)S(1)}, u32[]{:S(2)}) copy-start(bf16[64,128]{1,0:T(8,128)(2,1)S(1)} %copy.49) | copy-start | bytes 49156
  76.4 13.3 %all-to-all-start.3 = ((bf16[8,64,128]{2,1,0:T(8,128)(2,1)}), bf16[8,64,128]{2,1,0:T(8,128)(2,1)S(1)}, u32[]{:S(2)}, u32[]{:S(2)}) async-start(bf16[8,64,128]{2,1,0:T(8,128)(2,1)} %broadcast_in_dim.145), calls=%async_computation.3 | async-start | bytes 262144 | tf_op jit(solution)/shard_map/all_to_all | solution.py:170
  89.8 1.6 %copy-start.1 = (bf16[2,1024,512]{2,1,0:T(8,128)(2,1)S(1)}, bf16[2,1024,512]{2,1,0:T(8,128)(2,1)}, u32[]{:S(2)}) copy-start(bf16[2,1024,512]{2,1,0:T(8,128)(2,1)} %param.18) | copy-start | bytes 6291460
  89.8 2.1 %copy-start.8 = (bf16[512,1024]{1,0:T(8,128)(2,1)S(1)}, bf16[512,1024]{1,0:T(8,128)(2,1)}, u32[]{:S(2)}) copy-start(bf16[512,1024]{1,0:T(8,128)(2,1)} %param.19) | copy-start | bytes 3145732
  90.3 6.6 %copy-start.9 = (s32[1,8]{1,0:T(1,128)S(1)}, s32[1,8]{1,0:T(1,128)}, u32[]{:S(2)}) copy-start(s32[1,8]{1,0:T(1,128)} %param.27) | copy-start | bytes 100
  92.8 9.4 %all-to-all-start.4 = ((bf16[8,8,1024]{2,1,0:T(8,128)(2,1)}), bf16[8,8,1024]{2,1,0:T(8,128)(2,1)S(1)}, u32[]{:S(2)}, u32[]{:S(2)}) async-start(bf16[8,8,1024]{2,1,0:T(8,128)(2,1)} %fusion.1), calls=%async_computation.4 | async-start | bytes 262144 | tf_op jit(solution)/shard_map/all_to_all | solution.py:312
